TPU v7x, 512 devices: a whole 4x8x8 slice. The times are simulated.
512 devices in a mesh: grid: 64 (over x, z, core), orb: 8 (over y).
Axes of the slice: x: 4, y: 8, z: 8, core: 2. Of those that a mesh axis runs over, the one named last changes fastest.
Arguments:
- orbitals: float32 [256, 16, 16, 1024], P('grid', None, None, 'orb'), may hold values from -15 to 15
- potential: float32 [256, 16, 16], P('grid'), may hold values from -2 to 0
Outputs:
- filtered: float32 [256, 16, 16, 1024], P('grid', None, None, 'orb')
- hamiltonian_block: float32 [1024, 1024], P('orb', 'grid')
- margin_block: float32 [1024, 1024], P('orb', 'grid')
All inputs are finite; a program needn't handle non-finite values.
Results may differ from a plain program's by a relative error of at most 0.0039.
Values may be sent and summed in bfloat16 or wider, within the bound.
No kernel may reach another device: no remote copies, remote signals or barrier semaphores. Data moves between devices by JAX's collectives and lax.ppermute only.
A program may use at most 64 MiB of HBM per device.

v0:
```python
import jax
import jax.numpy as jnp
from jax import lax
from jax.sharding import PartitionSpec as P

DEGREE = 4


STENCIL = (-205.0 / 72.0, 8.0 / 5.0, -1.0 / 5.0, 8.0 / 315.0, -1.0 / 560.0)
LOWER_EDGE = -2.0
CUT_EDGE = 1.5
UPPER_EDGE = 10.0
EPSILON = 1e-06


def padded_2(shard, sides, width):
    for axis, dim in sides:
        size, length = (lax.axis_size(axis), shard.shape[dim])
        up = [(i, (i + 1) % size) for i in range(size - 1)]
        down = [(j, i) for i, j in up]
        last = lax.slice_in_dim(shard, length - width, length, axis=dim)
        initial = lax.slice_in_dim(shard, 0, width, axis=dim)
        before = lax.ppermute(last, axis, up)
        after = lax.ppermute(initial, axis, down)
        shard = jnp.concatenate([before, shard, after], axis=dim)
    return shard


def plane_matrix(rows_y, cols_x):
    flat_count = rows_y * cols_x
    index_all = jnp.arange(flat_count, dtype=jnp.int32)
    row_y = (index_all // cols_x)[:, None]
    row_x = (index_all % cols_x)[:, None]
    col_y = (index_all // cols_x)[None, :]
    col_x = (index_all % cols_x)[None, :]
    delta_y = jnp.mod(row_y - col_y, rows_y)
    delta_x = jnp.mod(row_x - col_x, cols_x)
    same_y = delta_y == 0
    same_x = delta_x == 0
    matrix = jnp.zeros((flat_count, flat_count), jnp.float32)
    for offset in range(1, 5):
        for signed in (offset, -offset):
            hit_y = jnp.logical_and(same_x, delta_y == signed % rows_y)
            hit_x = jnp.logical_and(same_y, delta_x == signed % cols_x)
            matrix = matrix + STENCIL[offset] * (
                hit_y.astype(jnp.float32) + hit_x.astype(jnp.float32)
            )
    return matrix


def apply_hamiltonian(current, potential, plane):
    layers, rows_y, cols_x, width = current.shape
    padded = padded_2(current.astype(jnp.bfloat16), (("grid", 0),), 4).astype(current.dtype)
    laplacian = 3.0 * STENCIL[0] * current
    for offset in range(1, 5):
        laplacian = laplacian + STENCIL[offset] * (
            padded[4 + offset : 4 + offset + layers] + padded[4 - offset : 4 - offset + layers]
        )
    flat = current.reshape(layers, rows_y * cols_x, width)
    in_plane = jnp.einsum(
        "pq,zqo->zpo",
        plane,
        flat,
        precision=lax.Precision.HIGHEST,
        preferred_element_type=jnp.float32,
    )
    laplacian = laplacian + in_plane.reshape(current.shape)
    return -0.5 * laplacian + potential[:, :, :, None] * current


def chebyshev(initial, potential, plane):
    half_width = (UPPER_EDGE - CUT_EDGE) / 2.0
    centre = (UPPER_EDGE + CUT_EDGE) / 2.0
    sigma_now = half_width / (LOWER_EDGE - centre)
    gamma_ratio = 2.0 / sigma_now
    previous = initial
    current = (
        sigma_now / half_width * (apply_hamiltonian(previous, potential, plane) - centre * previous)
    )
    for degree_step in range(DEGREE - 1):
        sigma_next = 1.0 / (gamma_ratio - sigma_now)
        following = (
            2.0
            * sigma_next
            / half_width
            * (apply_hamiltonian(current, potential, plane) - centre * current)
            - sigma_now * sigma_next * previous
        )
        previous, current, sigma_now = (current, following, sigma_next)
    return current


def contract_points(left_side, right_side):
    return lax.dot_general(
        left_side, right_side, (((0,), (0,)), ((), ())), preferred_element_type=jnp.float32
    )


def on_device(orbitals, potential):
    own_width = orbitals.shape[3]
    point_count = orbitals.shape[0] * orbitals.shape[1] * orbitals.shape[2]
    point_total = float(point_count * lax.axis_size("grid"))
    plane = plane_matrix(orbitals.shape[1], orbitals.shape[2])
    result_block = chebyshev(orbitals, potential, plane)
    own_squares = jnp.sum(result_block * result_block, axis=(0, 1, 2))
    rounded_orbitals = result_block.astype(jnp.bfloat16).reshape(point_count, own_width)
    rounded_image = (
        apply_hamiltonian(result_block, potential, plane)
        .astype(jnp.bfloat16)
        .reshape(point_count, own_width)
    )
    summed_own = lax.psum(own_squares, "grid")
    squares_all = lax.all_gather(summed_own, "orb", axis=0, tiled=True)
    scale_all = 1.0 / jnp.sqrt(squares_all / point_total + EPSILON)
    scale_own = lax.dynamic_slice_in_dim(scale_all, lax.axis_index("orb") * own_width, own_width)
    filtered = result_block * scale_own
    orbitals_all, images_all = (
        lax.all_gather(rounded_orbitals, "orb", axis=1, tiled=True),
        lax.all_gather(rounded_image, "orb", axis=1, tiled=True),
    )
    hamiltonian_part = contract_points(images_all, rounded_orbitals)
    margin_part = contract_points(orbitals_all, rounded_orbitals)
    combined = lax.psum_scatter(
        jnp.concatenate([hamiltonian_part, margin_part], axis=1),
        "grid",
        scatter_dimension=0,
        tiled=True,
    )
    column_count = combined.shape[0]
    column_scale = lax.dynamic_slice_in_dim(
        scale_all, lax.axis_index("grid") * column_count, column_count
    )
    pair_scale = scale_own[:, None] * column_scale[None, :] / point_total
    hamiltonian_block = combined[:, :own_width].T * pair_scale
    margin_block = combined[:, own_width:].T * pair_scale
    return (filtered, hamiltonian_block, margin_block)


def solution(mesh):
    placed = (P("grid", None, None, "orb"), P("grid", None, None))
    return jax.shard_map(
        on_device,
        mesh=mesh,
        in_specs=placed,
        out_specs=(P("grid", None, None, "orb"), P("orb", "grid"), P("orb", "grid")),
        check_vma=False,
    )
```

profile of v0, /device:TPU:6, one launch (start us, length us, event | category | flops | bytes accessed | tf_op | source)
XLA Modules:
  0.0 411.5 jit_solution(13175780743739567016)
XLA Ops:
  7.2 1.1 convert_element_type.210
  8.3 10.7 %collective-permute-start.1 = (bf16[4,16,16,128]{3,2,1,0:T(8,128)(2,1)S(1)}, bf16[4,16,16,128]{3,2,1,0:T(8,128)(2,1)S(1)}, u32[]{:S(2)}, u32[]{:S(2)}) collective-permute-start(bf16[4,16,16,128]{3,2,1,0:T(8,128)(2,1)S(1)} %convert_element_type.210), channel_id=1, source_target_pairs={{8,0},{16,8},{24,16},{32,24},{40,32},{48,40},{56,48},{64,56},{72,6... | collective-permute-start | bytes 786440 | tf_op jit(solution)/shard_map/ppermute | solution.py:24
  19.0 1.9 collective-permute-start
  20.9 0.8 broadcast_multiply_fusion.2
  21.7 2.7 fusion.72
  24.4 4.4 %collective-permute-done = bf16[4,16,16,128]{3,2,1,0:T(8,128)(2,1)S(1)} collective-permute-done((bf16[4,16,16,128]{3,2,1,0:T(8,128)(2,1)S(1)}, bf16[4,16,16,128]{3,2,1,0:T(8,128)(2,1)S(1)}, u32[]{:S(2)}, u32[]{:S(2)}) %collective-permute-start) | collective-permute-done | bytes 262176 | tf_op jit(solution)/shard_map/ppermute | solution.py:23
  29.3 2.2 collective-permute-start.3
  31.5 2.1 collective-permute-start.2
  33.7 1.9 convolution_bitcast_fusion.3
  35.9 5.5 %collective-permute-done.2 = bf16[4,16,16,128]{3,2,1,0:T(8,128)(2,1)S(1)} collective-permute-done((bf16[4,16,16,128]{3,2,1,0:T(8,128)(2,1)S(1)}, bf16[4,16,16,128]{3,2,1,0:T(8,128)(2,1)S(1)}, u32[]{:S(2)}, u32[]{:S(2)}) %collective-permute-start.2) | collective-permute-done | bytes 262176 | tf_op jit(solution)/shard_map/ppermute | solution.py:23
  41.9 1.9 collective-permute-start.5
  43.8 2.4 collective-permute-start.4
  46.2 1.9 convolution_bitcast_fusion.2
  48.4 5.2 %collective-permute-done.4 = bf16[4,16,16,128]{3,2,1,0:T(8,128)(2,1)S(1)} collective-permute-done((bf16[4,16,16,128]{3,2,1,0:T(8,128)(2,1)S(1)}, bf16[4,16,16,128]{3,2,1,0:T(8,128)(2,1)S(1)}, u32[]{:S(2)}, u32[]{:S(2)}) %collective-permute-start.4) | collective-permute-done | bytes 262176 | tf_op jit(solution)/shard_map/ppermute | solution.py:23
  54.2 1.9 collective-permute-start.7
  56.1 2.4 collective-permute-start.6
  58.5 1.9 convolution_bitcast_fusion.1
  60.7 5.2 %collective-permute-done.6 = bf16[4,16,16,128]{3,2,1,0:T(8,128)(2,1)S(1)} collective-permute-done((bf16[4,16,16,128]{3,2,1,0:T(8,128)(2,1)S(1)}, bf16[4,16,16,128]{3,2,1,0:T(8,128)(2,1)S(1)}, u32[]{:S(2)}, u32[]{:S(2)}) %collective-permute-start.6) | collective-permute-done | bytes 262176 | tf_op jit(solution)/shard_map/ppermute | solution.py:23
  66.0 1.2 fusion.156
  67.3 1.9 collective-permute-start.9
  69.2 2.6 collective-permute-start.8
  71.8 1.9 convolution_bitcast_fusion
  74.1 108.1 %psum.7 = f32[128]{0:T(128)S(1)} all-reduce(f32[128]{0:T(128)S(1)} %multiply_reduce_fusion), channel_id=1, replica_groups=mesh['grid'=64,'orb'=8] {'grid'}, use_global_device_ids=true, to_apply=%region_1.2 | all-reduce | flops 128 | bytes 1024 | tf_op jit(solution)/shard_map/psum | solution.py:112
  182.2 16.9 %all-gather = f32[8,1,128]{2,1,0:T(1,128)S(1)} all-gather(f32[1,1,128]{2,1,0:T(1,128)S(1)} %bitcast.65), channel_id=1, replica_groups=mesh['grid'=64,'orb'=8] {'orb'}, dimensions={0}, use_global_device_ids=true | all-gather | bytes 4608 | tf_op jit(solution)/shard_map/all_gather | solution.py:113
  199.3 1.3 fusion.5
  200.6 2.1 fusion.165
  202.7 47.9 %all-gather.4.cloned.1.call-done = bf16[1024,1024]{1,0:T(8,128)(2,1)} async-done(((bf16[1024,128]{1,0:T(8,128)(2,1)}), bf16[1024,1024]{1,0:T(8,128)(2,1)}) %all-gather.4.cloned.1.call-update) | async-done | bytes 2097168 | tf_op jit(solution)/shard_map/all_gather | solution.py:119
  250.6 2.1 fusion.164
  252.8 1.3 copy.39
  254.3 148.3 %reduce-scatter.4.cloned.1.call-done = f32[16,256]{1,0:T(8,128)} async-done(((f32[1024,256]{1,0:T(8,128)}), f32[16,256]{1,0:T(8,128)}) %reduce-scatter.4.cloned.1.call-update) | async-done | bytes 16400
  402.6 0.7 fusion.163
  403.6 0.7 copy.33
  (42 shorter events, 4.3 us)
Async XLA Ops:
  7.2 193.5 %all-gather.6.cloned.1.call-start = ((), (), s32[]{:S(2)}) async-start(), calls=%async_computation.2 | async-start | bytes 2359296 | tf_op jit(solution)/shard_map/all_gather | solution.py:118
  8.3 16.1 %collective-permute-start.1 = (bf16[4,16,16,128]{3,2,1,0:T(8,128)(2,1)S(1)}, bf16[4,16,16,128]{3,2,1,0:T(8,128)(2,1)S(1)}, u32[]{:S(2)}, u32[]{:S(2)}) collective-permute-start(bf16[4,16,16,128]{3,2,1,0:T(8,128)(2,1)S(1)} %convert_element_type.210), channel_id=1, source_target_pairs={{8,0},{16,8},{24,16},{32,24},{40,32},{48,40},{56,48},{64,56},{72,6... | collective-permute-start | bytes 786440 | tf_op jit(solution)/shard_map/ppermute | solution.py:24
  19.0 9.8 %collective-permute-start = (bf16[4,16,16,128]{3,2,1,0:T(8,128)(2,1)S(1)}, bf16[4,16,16,128]{3,2,1,0:T(8,128)(2,1)S(1)}, u32[]{:S(2)}, u32[]{:S(2)}) collective-permute-start(bf16[4,16,16,128]{3,2,1,0:T(8,128)(2,1)S(1)} %convert_element_type.210), channel_id=1, source_target_pairs={{0,8},{8,16},{16,24},{24,32},{32,40},{40,48},{48,56},{56,64},{64,7... | collective-permute-start | bytes 786440 | tf_op jit(solution)/shard_map/ppermute | solution.py:23
  24.3 4.6 %copy-start.1 = (f32[4,16,16,128]{3,2,1,0:T(8,128)S(1)}, f32[4,16,16,128]{3,2,1,0:T(8,128)}, u32[]{:S(2)}) copy-start(f32[4,16,16,128]{3,2,1,0:T(8,128)} %param.2) | copy-start | bytes 1572868
  24.3 4.5 %copy-start.2 = (f32[4,16,16]{2,1,0:T(8,128)S(1)}, f32[4,16,16]{2,1,0:T(8,128)}, u32[]{:S(2)}) copy-start(f32[4,16,16]{2,1,0:T(8,128)} %param.3) | copy-start | bytes 12292
  29.3 6.5 %collective-permute-start.3 = (bf16[4,16,16,128]{3,2,1,0:T(8,128)(2,1)S(1)}, bf16[4,16,16,128]{3,2,1,0:T(8,128)(2,1)S(1)}, u32[]{:S(2)}, u32[]{:S(2)}) collective-permute-start(bf16[4,16,16,128]{3,2,1,0:T(8,128)(2,1)S(1)} %get-tuple-element.18), channel_id=1, source_target_pairs={{8,0},{16,8},{24,16},{32,24},{40,32},{48,40},{56,48},{64,56},{72,6... | collective-permute-start | bytes 786440 | tf_op jit(solution)/shard_map/ppermute | solution.py:24
  31.5 9.8 %collective-permute-start.2 = (bf16[4,16,16,128]{3,2,1,0:T(8,128)(2,1)S(1)}, bf16[4,16,16,128]{3,2,1,0:T(8,128)(2,1)S(1)}, u32[]{:S(2)}, u32[]{:S(2)}) collective-permute-start(bf16[4,16,16,128]{3,2,1,0:T(8,128)(2,1)S(1)} %get-tuple-element.18), channel_id=1, source_target_pairs={{0,8},{8,16},{16,24},{24,32},{32,40},{40,48},{48,56},{56,64},{64,7... | collective-permute-start | bytes 786440 | tf_op jit(solution)/shard_map/ppermute | solution.py:23
  41.9 6.5 %collective-permute-start.5 = (bf16[4,16,16,128]{3,2,1,0:T(8,128)(2,1)S(1)}, bf16[4,16,16,128]{3,2,1,0:T(8,128)(2,1)S(1)}, u32[]{:S(2)}, u32[]{:S(2)}) collective-permute-start(bf16[4,16,16,128]{3,2,1,0:T(8,128)(2,1)S(1)} %get-tuple-element.16), channel_id=1, source_target_pairs={{8,0},{16,8},{24,16},{32,24},{40,32},{48,40},{56,48},{64,56},{72,6... | collective-permute-start | bytes 786440 | tf_op jit(solution)/shard_map/ppermute | solution.py:24
  43.8 9.8 %collective-permute-start.4 = (bf16[4,16,16,128]{3,2,1,0:T(8,128)(2,1)S(1)}, bf16[4,16,16,128]{3,2,1,0:T(8,128)(2,1)S(1)}, u32[]{:S(2)}, u32[]{:S(2)}) collective-permute-start(bf16[4,16,16,128]{3,2,1,0:T(8,128)(2,1)S(1)} %get-tuple-element.16), channel_id=1, source_target_pairs={{0,8},{8,16},{16,24},{24,32},{32,40},{40,48},{48,56},{56,64},{64,7... | collective-permute-start | bytes 786440 | tf_op jit(solution)/shard_map/ppermute | solution.py:23
  54.2 6.5 %collective-permute-start.7 = (bf16[4,16,16,128]{3,2,1,0:T(8,128)(2,1)S(1)}, bf16[4,16,16,128]{3,2,1,0:T(8,128)(2,1)S(1)}, u32[]{:S(2)}, u32[]{:S(2)}) collective-permute-start(bf16[4,16,16,128]{3,2,1,0:T(8,128)(2,1)S(1)} %get-tuple-element.14), channel_id=1, source_target_pairs={{8,0},{16,8},{24,16},{32,24},{40,32},{48,40},{56,48},{64,56},{72,6... | collective-permute-start | bytes 786440 | tf_op jit(solution)/shard_map/ppermute | solution.py:24
  56.1 9.8 %collective-permute-start.6 = (bf16[4,16,16,128]{3,2,1,0:T(8,128)(2,1)S(1)}, bf16[4,16,16,128]{3,2,1,0:T(8,128)(2,1)S(1)}, u32[]{:S(2)}, u32[]{:S(2)}) collective-permute-start(bf16[4,16,16,128]{3,2,1,0:T(8,128)(2,1)S(1)} %get-tuple-element.14), channel_id=1, source_target_pairs={{0,8},{8,16},{16,24},{24,32},{32,40},{40,48},{48,56},{56,64},{64,7... | collective-permute-start | bytes 786440 | tf_op jit(solution)/shard_map/ppermute | solution.py:23
  67.2 183.4 %all-gather.4.cloned.1.call-start = ((), (), s32[]{:S(2)}) async-start(), calls=%async_computation.1 | async-start | bytes 2359296 | tf_op jit(solution)/shard_map/all_gather | solution.py:119
  67.3 131.9 %collective-permute-start.9 = (bf16[4,16,16,128]{3,2,1,0:T(8,128)(2,1)}, bf16[4,16,16,128]{3,2,1,0:T(8,128)(2,1)S(1)}, u32[]{:S(2)}, u32[]{:S(2)}) collective-permute-start(bf16[4,16,16,128]{3,2,1,0:T(8,128)(2,1)} %get-tuple-element.12), channel_id=1, source_target_pairs={{8,0},{16,8},{24,16},{32,24},{40,32},{48,40},{56,48},{64,56},{72,6... | collective-permute-start | bytes 786440 | tf_op jit(solution)/shard_map/ppermute | solution.py:24
  69.2 129.9 %collective-permute-start.8 = (bf16[4,16,16,128]{3,2,1,0:T(8,128)(2,1)}, bf16[4,16,16,128]{3,2,1,0:T(8,128)(2,1)S(1)}, u32[]{:S(2)}, u32[]{:S(2)}) collective-permute-start(bf16[4,16,16,128]{3,2,1,0:T(8,128)(2,1)} %get-tuple-element.12), channel_id=1, source_target_pairs={{0,8},{8,16},{16,24},{24,32},{32,40},{40,48},{48,56},{56,64},{64,7... | collective-permute-start | bytes 786440 | tf_op jit(solution)/shard_map/ppermute | solution.py:23
  73.7 125.4 %copy-start = (bf16[4,16,16,128]{3,2,1,0:T(8,128)(2,1)S(1)}, bf16[4,16,16,128]{3,2,1,0:T(8,128)(2,1)}, u32[]{:S(2)}) copy-start(bf16[4,16,16,128]{3,2,1,0:T(8,128)(2,1)} %get-tuple-element.12) | copy-start | bytes 786436
  200.6 202.0 %reduce-scatter.4.cloned.1.call-start = ((), (), s32[]{:S(2)}) async-start(), calls=%async_computation.3 | async-start | bytes 1064960
Sparse Core Ops, SparseCore 0:
  67.3 45.8 all-gather.5
  200.7 49.8 all-gather.3
  255.2 147.3 reduce-scatter.3
where the time goes:
time: 413 us; the launch traced here: 411 us
  waiting for transfers between devices  217 us (53%)
  blocking collectives  125 us (30%)
  starting transfers between devices  30.2 us (7%)
  matrix products  14.5 us (4%)
  between operations  14.1 us (3%)
  other arithmetic  6.55 us (2%)
  local copies, waits for them, and re-layouts  4.51 us (1%)
    unnamed x4, waiting for transfers between devices  148 us
    psum x1, blocking collectives, on_device(): summed_own = lax.psum(own_squares, 'grid')  108 us
    all_gather x1, waiting for transfers between devices, on_device(): lax.all_gather(rounded_image, 'orb', axis=1, tiled=True)  47.9 us
    ppermute x5, waiting for transfers between devices, padded_2(): before = lax.ppermute(last, axis, up)  20.4 us
    ppermute x5, starting transfers between devices, padded_2(): after = lax.ppermute(initial, axis, down)  18.6 us
    all_gather x1, blocking collectives, on_device(): squares_all = lax.all_gather(summed_own, 'orb', axis=0, tiled=True)  16.9 us
    ppermute x5, starting transfers between devices, padded_2(): before = lax.ppermute(last, axis, up)  11.4 us
    dot_general x5, matrix products, apply_hamiltonian(): jnp.einsum('pq,zqo->zpo', plane, flat, precision=lax.Precision.HIGHEST, p...  10.4 us
  transfers between devices with their start and end apart: 13, of which 6 were waited for; matrix products, arithmetic and copies ran while one was open for 4% of the time, Pallas kernels for 0%

commit v1 on v0

--- a/solution.py
+++ b/solution.py
@@ -13,17 +13,16 @@
 EPSILON = 1e-06
 
 
-def padded_2(shard, sides, width):
-    for axis, dim in sides:
-        size, length = (lax.axis_size(axis), shard.shape[dim])
-        up = [(i, (i + 1) % size) for i in range(size - 1)]
-        down = [(j, i) for i, j in up]
-        last = lax.slice_in_dim(shard, length - width, length, axis=dim)
-        initial = lax.slice_in_dim(shard, 0, width, axis=dim)
-        before = lax.ppermute(last, axis, up)
-        after = lax.ppermute(initial, axis, down)
-        shard = jnp.concatenate([before, shard, after], axis=dim)
-    return shard
+def halo_layers(shard, width):
+    size = lax.axis_size("grid")
+    length = shard.shape[0]
+    up = [(i, i + 1) for i in range(size - 1)]
+    down = [(j, i) for i, j in up]
+    last = lax.slice_in_dim(shard, length - width, length, axis=0).astype(jnp.bfloat16)
+    initial = lax.slice_in_dim(shard, 0, width, axis=0).astype(jnp.bfloat16)
+    before = lax.ppermute(last, "grid", up).astype(shard.dtype)
+    after = lax.ppermute(initial, "grid", down).astype(shard.dtype)
+    return jnp.concatenate([before, shard, after], axis=0)
 
 
 def plane_matrix(rows_y, cols_x):
@@ -50,7 +49,7 @@
 
 def apply_hamiltonian(current, potential, plane):
     layers, rows_y, cols_x, width = current.shape
-    padded = padded_2(current.astype(jnp.bfloat16), (("grid", 0),), 4).astype(current.dtype)
+    padded = halo_layers(current, 4)
     laplacian = 3.0 * STENCIL[0] * current
     for offset in range(1, 5):
         laplacian = laplacian + STENCIL[offset] * (
@@ -96,10 +95,29 @@
     )
 
 
+def reduce_scatter_grid(slots):
+    size = slots.shape[0]
+    bits = size.bit_length() - 1
+    me = lax.axis_index("grid")
+    rest = slots.shape[1:]
+    buf = slots.reshape((2,) * bits + rest)
+    for bit in range(bits):
+        axis = bits - 1 - bit
+        mine = (me >> bit) & 1
+        low = lax.index_in_dim(buf, 0, axis=axis, keepdims=False)
+        high = lax.index_in_dim(buf, 1, axis=axis, keepdims=False)
+        keep = jnp.where(mine == 1, high, low)
+        send = jnp.where(mine == 1, low, high)
+        pairs = [(i, i ^ (1 << bit)) for i in range(size)]
+        buf = keep + lax.ppermute(send, "grid", pairs)
+    return buf
+
+
 def on_device(orbitals, potential):
     own_width = orbitals.shape[3]
     point_count = orbitals.shape[0] * orbitals.shape[1] * orbitals.shape[2]
-    point_total = float(point_count * lax.axis_size("grid"))
+    grid_size = lax.axis_size("grid")
+    point_total = float(point_count * grid_size)
     plane = plane_matrix(orbitals.shape[1], orbitals.shape[2])
     result_block = chebyshev(orbitals, potential, plane)
     own_squares = jnp.sum(result_block * result_block, axis=(0, 1, 2))
@@ -109,30 +127,36 @@
         .astype(jnp.bfloat16)
         .reshape(point_count, own_width)
     )
-    summed_own = lax.psum(own_squares, "grid")
-    squares_all = lax.all_gather(summed_own, "orb", axis=0, tiled=True)
-    scale_all = 1.0 / jnp.sqrt(squares_all / point_total + EPSILON)
-    scale_own = lax.dynamic_slice_in_dim(scale_all, lax.axis_index("orb") * own_width, own_width)
+    orbitals_all = lax.all_gather(rounded_orbitals, "orb", axis=1, tiled=True)
+    total_width = orbitals_all.shape[1]
+    rows = total_width // grid_size
+    hamiltonian_part = contract_points(orbitals_all, rounded_image)
+    margin_part = contract_points(orbitals_all, rounded_orbitals)
+    wide = orbitals_all.astype(jnp.float32)
+    column_squares = jnp.sum(wide * wide, axis=0)
+    body = jnp.concatenate(
+        [
+            hamiltonian_part.reshape(grid_size, rows, own_width),
+            margin_part.reshape(grid_size, rows, own_width),
+        ],
+        axis=2,
+    )
+    tail = jnp.concatenate(
+        [
+            column_squares.reshape(grid_size, rows),
+            jnp.broadcast_to(own_squares[None, :], (grid_size, own_width)),
+            jnp.zeros((grid_size, own_width - rows), jnp.float32),
+        ],
+        axis=1,
+    )
+    slots = jnp.concatenate([body, tail[:, None, :]], axis=1)
+    combined = reduce_scatter_grid(slots)
+    scale_own = 1.0 / jnp.sqrt(combined[rows, rows : rows + own_width] / point_total + EPSILON)
+    column_scale = 1.0 / jnp.sqrt(combined[rows, :rows] / point_total + EPSILON)
     filtered = result_block * scale_own
-    orbitals_all, images_all = (
-        lax.all_gather(rounded_orbitals, "orb", axis=1, tiled=True),
-        lax.all_gather(rounded_image, "orb", axis=1, tiled=True),
-    )
-    hamiltonian_part = contract_points(images_all, rounded_orbitals)
-    margin_part = contract_points(orbitals_all, rounded_orbitals)
-    combined = lax.psum_scatter(
-        jnp.concatenate([hamiltonian_part, margin_part], axis=1),
-        "grid",
-        scatter_dimension=0,
-        tiled=True,
-    )
-    column_count = combined.shape[0]
-    column_scale = lax.dynamic_slice_in_dim(
-        scale_all, lax.axis_index("grid") * column_count, column_count
-    )
     pair_scale = scale_own[:, None] * column_scale[None, :] / point_total
-    hamiltonian_block = combined[:, :own_width].T * pair_scale
-    margin_block = combined[:, own_width:].T * pair_scale
+    hamiltonian_block = combined[:rows, :own_width].T * pair_scale
+    margin_block = combined[:rows, own_width:].T * pair_scale
     return (filtered, hamiltonian_block, margin_block)
 
 

time: 413 us -> 182 us (0.44)
  waiting for transfers between devices: 217 us -> 79.7 us
  blocking collectives: 125 us -> 0 us
  starting transfers between devices: 30.2 us -> 57.7 us
  other arithmetic: 6.55 us -> 11 us
    unnamed x4 -> x1, waiting for transfers between devices: 148 us -> 0.02 us
    psum x1 -> x0, blocking collectives: 108 us -> none  [on_device(): summed_own = lax.psum(own_squares, 'grid')]
    ppermute x10 -> x16, starting transfers between devices: 30.1 us -> 57.6 us  [the longest x6 24.2 us: reduce_scatter_grid(): buf = keep + lax.ppermute(send, 'grid', pairs)]
    ppermute x10 -> x16, waiting for transfers between devices: 20.4 us -> 45.9 us  [the longest x6 24.3 us: reduce_scatter_grid(): buf = keep + lax.ppermute(send, 'grid', pairs)]
    all_gather x1 -> x0, blocking collectives: 16.9 us -> none  [on_device(): squares_all = lax.all_gather(summed_own, 'orb', axis=0, tiled=True)]
    all_gather x2 -> x1, waiting for transfers between devices: 47.9 us -> 33.8 us  [on_device(): orbitals_all = lax.all_gather(rounded_orbitals, 'orb', axis=1, tiled=True)]
  transfers between devices with their start and end apart: 13 -> 17, of which waited for: 6 -> 12; matrix products, arithmetic and copies ran while one was open for 4% -> 7% of each run, Pallas kernels for 0% -> 0%
where the time goes in v1:
time: 182 us; the launch traced here: 181 us
  waiting for transfers between devices  79.7 us (44%)
  starting transfers between devices  57.7 us (32%)
  between operations  14.6 us (8%)
  matrix products  11.8 us (6%)
  other arithmetic  11 us (6%)
  local copies, waits for them, and re-layouts  6.16 us (3%)
    all_gather x1, waiting for transfers between devices, on_device(): orbitals_all = lax.all_gather(rounded_orbitals, 'orb', axis=1, tiled=True)  33.8 us
    ppermute x6, waiting for transfers between devices, reduce_scatter_grid(): buf = keep + lax.ppermute(send, 'grid', pairs)  24.3 us
    ppermute x6, starting transfers between devices, reduce_scatter_grid(): buf = keep + lax.ppermute(send, 'grid', pairs)  24.2 us
    ppermute x5, starting transfers between devices, halo_layers(): after = lax.ppermute(initial, 'grid', down).astype(shard.dtype)  22.3 us
    ppermute x5, waiting for transfers between devices, halo_layers(): before = lax.ppermute(last, 'grid', up).astype(shard.dtype)  19.8 us
    ppermute x5, starting transfers between devices, halo_layers(): before = lax.ppermute(last, 'grid', up).astype(shard.dtype)  11 us
    dot_general x5, matrix products, apply_hamiltonian(): jnp.einsum('pq,zqo->zpo', plane, flat, precision=lax.Precision.HIGHEST, p...  10.4 us
  transfers between devices with their start and end apart: 17, of which 12 were waited for; matrix products, arithmetic and copies ran while one was open for 7% of the time, Pallas kernels for 0%

profile of v1, /device:TPU:6, one launch (start us, length us, event | category | flops | bytes accessed | tf_op | source)
XLA Modules:
  0.0 181.0 jit_solution(14058231074587495252)
XLA Ops:
  8.3 10.7 %collective-permute-start = (bf16[4,16,16,128]{3,2,1,0:T(8,128)(2,1)S(1)}, bf16[4,16,16,128]{3,2,1,0:T(8,128)(2,1)S(1)}, u32[]{:S(2)}, u32[]{:S(2)}) collective-permute-start(bf16[4,16,16,128]{3,2,1,0:T(8,128)(2,1)S(1)} %convert_element_type.233), channel_id=1, source_target_pairs={{8,0},{16,8},{24,16},{32,24},{40,32},{48,40},{56,48},{64,56},{72,6... | collective-permute-start | bytes 786440 | tf_op jit(solution)/shard_map/ppermute | solution.py:24
  19.0 1.9 %collective-permute-start.1 = (bf16[4,16,16,128]{3,2,1,0:T(8,128)(2,1)S(1)}, bf16[4,16,16,128]{3,2,1,0:T(8,128)(2,1)S(1)}, u32[]{:S(2)}, u32[]{:S(2)}) collective-permute-start(bf16[4,16,16,128]{3,2,1,0:T(8,128)(2,1)S(1)} %convert_element_type.233), channel_id=1, source_target_pairs={{0,8},{8,16},{16,24},{24,32},{32,40},{40,48},{48,56},{56,64},{64,7... | collective-permute-start | bytes 786440 | tf_op jit(solution)/shard_map/ppermute | solution.py:23
  21.7 2.7 %fusion.102 = f32[256,4,128]{2,0,1:T(8,128)S(1)} fusion(f32[4,256,128]{2,1,0:T(8,128)} %bitcast.96, s32[256]{0:T(256)S(1)} %get-tuple-element.22, s32[256]{0:T(256)S(1)} %get-tuple-element.23), kind=kOutput, calls=%fused_computation.176 | convolution fusion | flops 408944640 | bytes 1050624 | tf_op jit(solution)/shard_map/pq,zqo->zpo/dot_general | solution.py:59
  24.5 4.3 %collective-permute-done.1 = bf16[4,16,16,128]{3,2,1,0:T(8,128)(2,1)S(1)} collective-permute-done((bf16[4,16,16,128]{3,2,1,0:T(8,128)(2,1)S(1)}, bf16[4,16,16,128]{3,2,1,0:T(8,128)(2,1)S(1)}, u32[]{:S(2)}, u32[]{:S(2)}) %collective-permute-start.1) | collective-permute-done | bytes 262176 | tf_op jit(solution)/shard_map/ppermute | solution.py:23
  29.2 1.9 %collective-permute-start.2 = (bf16[4,16,16,128]{3,2,1,0:T(8,128)(2,1)S(1)}, bf16[4,16,16,128]{3,2,1,0:T(8,128)(2,1)S(1)}, u32[]{:S(2)}, u32[]{:S(2)}) collective-permute-start(bf16[4,16,16,128]{3,2,1,0:T(8,128)(2,1)S(1)} %get-tuple-element.9), channel_id=1, source_target_pairs={{8,0},{16,8},{24,16},{32,24},{40,32},{48,40},{56,48},{64,56},{72,6... | collective-permute-start | bytes 786440 | tf_op jit(solution)/shard_map/ppermute | solution.py:24
  31.1 2.4 %collective-permute-start.3 = (bf16[4,16,16,128]{3,2,1,0:T(8,128)(2,1)S(1)}, bf16[4,16,16,128]{3,2,1,0:T(8,128)(2,1)S(1)}, u32[]{:S(2)}, u32[]{:S(2)}) collective-permute-start(bf16[4,16,16,128]{3,2,1,0:T(8,128)(2,1)S(1)} %get-tuple-element.9), channel_id=1, source_target_pairs={{0,8},{8,16},{16,24},{24,32},{32,40},{40,48},{48,56},{56,64},{64,7... | collective-permute-start | bytes 786440 | tf_op jit(solution)/shard_map/ppermute | solution.py:23
  33.6 1.9 %convolution_bitcast_fusion.3 = f32[4,256,128]{1,2,0:T(8,128)S(1)} fusion(f32[4,256,128]{2,1,0:T(8,128)S(1)} %bitcast.101, s32[256]{0:T(256)S(1)} %get-tuple-element.22, s32[256]{0:T(256)S(1)} %get-tuple-element.23), kind=kOutput, calls=%fused_computation.44 | convolution fusion | flops 408944640 | bytes 1050624 | tf_op jit(solution)/shard_map/pq,zqo->zpo/dot_general | solution.py:59
  35.8 5.1 %collective-permute-done.3 = bf16[4,16,16,128]{3,2,1,0:T(8,128)(2,1)S(1)} collective-permute-done((bf16[4,16,16,128]{3,2,1,0:T(8,128)(2,1)S(1)}, bf16[4,16,16,128]{3,2,1,0:T(8,128)(2,1)S(1)}, u32[]{:S(2)}, u32[]{:S(2)}) %collective-permute-start.3) | collective-permute-done | bytes 262176 | tf_op jit(solution)/shard_map/ppermute | solution.py:23
  41.4 1.9 %collective-permute-start.4 = (bf16[4,16,16,128]{3,2,1,0:T(8,128)(2,1)S(1)}, bf16[4,16,16,128]{3,2,1,0:T(8,128)(2,1)S(1)}, u32[]{:S(2)}, u32[]{:S(2)}) collective-permute-start(bf16[4,16,16,128]{3,2,1,0:T(8,128)(2,1)S(1)} %get-tuple-element.7), channel_id=1, source_target_pairs={{8,0},{16,8},{24,16},{32,24},{40,32},{48,40},{56,48},{64,56},{72,6... | collective-permute-start | bytes 786440 | tf_op jit(solution)/shard_map/ppermute | solution.py:24
  43.3 2.4 %collective-permute-start.5 = (bf16[4,16,16,128]{3,2,1,0:T(8,128)(2,1)S(1)}, bf16[4,16,16,128]{3,2,1,0:T(8,128)(2,1)S(1)}, u32[]{:S(2)}, u32[]{:S(2)}) collective-permute-start(bf16[4,16,16,128]{3,2,1,0:T(8,128)(2,1)S(1)} %get-tuple-element.7), channel_id=1, source_target_pairs={{0,8},{8,16},{16,24},{24,32},{32,40},{40,48},{48,56},{56,64},{64,7... | collective-permute-start | bytes 786440 | tf_op jit(solution)/shard_map/ppermute | solution.py:23
  45.8 1.9 %convolution_bitcast_fusion.2 = f32[4,256,128]{1,2,0:T(8,128)S(1)} fusion(f32[4,256,128]{2,1,0:T(8,128)S(1)} %bitcast.97, s32[256]{0:T(256)S(1)} %get-tuple-element.22, s32[256]{0:T(256)S(1)} %get-tuple-element.23), kind=kOutput, calls=%fused_computation.43 | convolution fusion | flops 408944640 | bytes 1050624 | tf_op jit(solution)/shard_map/pq,zqo->zpo/dot_general | solution.py:59
  47.9 5.2 %collective-permute-done.5 = bf16[4,16,16,128]{3,2,1,0:T(8,128)(2,1)S(1)} collective-permute-done((bf16[4,16,16,128]{3,2,1,0:T(8,128)(2,1)S(1)}, bf16[4,16,16,128]{3,2,1,0:T(8,128)(2,1)S(1)}, u32[]{:S(2)}, u32[]{:S(2)}) %collective-permute-start.5) | collective-permute-done | bytes 262176 | tf_op jit(solution)/shard_map/ppermute | solution.py:23
  53.6 1.9 %collective-permute-start.6 = (bf16[4,16,16,128]{3,2,1,0:T(8,128)(2,1)S(1)}, bf16[4,16,16,128]{3,2,1,0:T(8,128)(2,1)S(1)}, u32[]{:S(2)}, u32[]{:S(2)}) collective-permute-start(bf16[4,16,16,128]{3,2,1,0:T(8,128)(2,1)S(1)} %get-tuple-element.5), channel_id=1, source_target_pairs={{8,0},{16,8},{24,16},{32,24},{40,32},{48,40},{56,48},{64,56},{72,6... | collective-permute-start | bytes 786440 | tf_op jit(solution)/shard_map/ppermute | solution.py:24
  55.5 2.4 %collective-permute-start.7 = (bf16[4,16,16,128]{3,2,1,0:T(8,128)(2,1)S(1)}, bf16[4,16,16,128]{3,2,1,0:T(8,128)(2,1)S(1)}, u32[]{:S(2)}, u32[]{:S(2)}) collective-permute-start(bf16[4,16,16,128]{3,2,1,0:T(8,128)(2,1)S(1)} %get-tuple-element.5), channel_id=1, source_target_pairs={{0,8},{8,16},{16,24},{24,32},{32,40},{40,48},{48,56},{56,64},{64,7... | collective-permute-start | bytes 786440 | tf_op jit(solution)/shard_map/ppermute | solution.py:23
  58.0 1.9 %convolution_bitcast_fusion.1 = f32[4,256,128]{1,2,0:T(8,128)S(1)} fusion(f32[4,256,128]{2,1,0:T(8,128)S(1)} %bitcast.106, s32[256]{0:T(256)S(1)} %get-tuple-element.22, s32[256]{0:T(256)S(1)} %get-tuple-element.23), kind=kOutput, calls=%fused_computation.42 | convolution fusion | flops 408944640 | bytes 1050624 | tf_op jit(solution)/shard_map/pq,zqo->zpo/dot_general | solution.py:59
  60.1 5.2 %collective-permute-done.7 = bf16[4,16,16,128]{3,2,1,0:T(8,128)(2,1)S(1)} collective-permute-done((bf16[4,16,16,128]{3,2,1,0:T(8,128)(2,1)S(1)}, bf16[4,16,16,128]{3,2,1,0:T(8,128)(2,1)S(1)}, u32[]{:S(2)}, u32[]{:S(2)}) %collective-permute-start.7) | collective-permute-done | bytes 262176 | tf_op jit(solution)/shard_map/ppermute | solution.py:23
  68.6 5.9 %collective-permute-start.8 = (bf16[4,16,16,128]{3,2,1,0:T(8,128)(2,1)}, bf16[4,16,16,128]{3,2,1,0:T(8,128)(2,1)S(1)}, u32[]{:S(2)}, u32[]{:S(2)}) collective-permute-start(bf16[4,16,16,128]{3,2,1,0:T(8,128)(2,1)} %convert_element_type.261), channel_id=1, source_target_pairs={{8,0},{16,8},{24,16},{32,24},{40,32},{48,40},{56,48},{64,56},{72,6... | collective-permute-start | bytes 786440 | tf_op jit(solution)/shard_map/ppermute | solution.py:24
  74.5 1.9 %convolution_bitcast_fusion = f32[4,256,128]{1,2,0:T(8,128)S(1)} fusion(f32[4,256,128]{2,1,0:T(8,128)S(1)} %bitcast.95, s32[256]{0:T(256)S(1)} %get-tuple-element.22, s32[256]{0:T(256)S(1)} %get-tuple-element.23), kind=kOutput, calls=%fused_computation.41 | convolution fusion | flops 408944640 | bytes 1050624 | tf_op jit(solution)/shard_map/pq,zqo->zpo/dot_general | solution.py:59
  78.9 33.8 %all-gather.2.cloned.1.call-done = bf16[1024,1024]{1,0:T(8,128)(2,1)} async-done(((bf16[1024,128]{1,0:T(8,128)(2,1)}), bf16[1024,1024]{1,0:T(8,128)(2,1)}) %all-gather.2.cloned.1.call-update) | async-done | bytes 2097168 | tf_op jit(solution)/shard_map/all_gather | solution.py:130
  112.7 2.1 %multiply_reduce_fusion = f32[1024]{0:T(1024)S(1)} fusion(bf16[1024,1024]{1,0:T(8,128)(2,1)} %all-gather.2.cloned.1.call-done), kind=kLoop, calls=%fused_computation | loop fusion | flops 3144704 | bytes 2101248 | tf_op jit(solution)/shard_map/reduce_sum | solution.py:136
  114.9 2.9 %copy.191 = bf16[1024,1024]{1,0:T(8,128)(2,1)S(1)} copy(bf16[1024,1024]{0,1:T(8,128)(2,1)} %bitcast.94) | data formatting | bytes 4194304 | tf_op jit(solution)/shard_map/dot_general | solution.py:93
  124.2 2.1 %collective-permute-done.10 = f32[2,2,2,2,2,17,256]{6,4,5,3,2,1,0:T(2,128)S(1)} collective-permute-done((f32[2,2,2,2,2,17,256]{6,4,5,3,2,1,0:T(2,128)}, f32[2,2,2,2,2,17,256]{6,4,5,3,2,1,0:T(2,128)S(1)}, u32[]{:S(2)}, u32[]{:S(2)}) %collective-permute-start.10) | collective-permute-done | bytes 557088 | tf_op jit(solution)/shard_map/ppermute | solution.py:112
  127.0 3.6 %collective-permute-start.11 = (f32[2,2,2,2,17,256]{5,3,4,2,1,0:T(2,128)S(1)}, f32[2,2,2,2,17,256]{5,3,4,2,1,0:T(2,128)S(1)}, u32[]{:S(2)}, u32[]{:S(2)}) collective-permute-start(f32[2,2,2,2,17,256]{5,3,4,2,1,0:T(2,128)S(1)} %select_bitcast_fusion.1), channel_id=1, source_target_pairs={{0,16},{8,24},{16,0},{24,8},{32,48},{40,56},{48,32},{56,40},{64,80... | collective-permute-start | bytes 835592 | tf_op jit(solution)/shard_map/ppermute | solution.py:112
  130.6 7.0 %collective-permute-done.11 = f32[2,2,2,2,17,256]{5,3,4,2,1,0:T(2,128)S(1)} collective-permute-done((f32[2,2,2,2,17,256]{5,3,4,2,1,0:T(2,128)S(1)}, f32[2,2,2,2,17,256]{5,3,4,2,1,0:T(2,128)S(1)}, u32[]{:S(2)}, u32[]{:S(2)}) %collective-permute-start.11) | collective-permute-done | bytes 278560 | tf_op jit(solution)/shard_map/ppermute | solution.py:112
  138.1 4.6 %collective-permute-start.12 = (f32[2,2,2,17,256]{4,2,3,1,0:T(2,128)S(1)}, f32[2,2,2,17,256]{4,2,3,1,0:T(2,128)S(1)}, u32[]{:S(2)}, u32[]{:S(2)}) collective-permute-start(f32[2,2,2,17,256]{4,2,3,1,0:T(2,128)S(1)} %bitcast.109), channel_id=1, source_target_pairs={{0,32},{8,40},{16,48},{24,56},{32,0},{40,8},{48,16},{56,24},{64,96... | collective-permute-start | bytes 417800 | tf_op jit(solution)/shard_map/ppermute | solution.py:112
  142.7 6.1 %collective-permute-done.12 = f32[2,2,2,17,256]{4,2,3,1,0:T(2,128)S(1)} collective-permute-done((f32[2,2,2,17,256]{4,2,3,1,0:T(2,128)S(1)}, f32[2,2,2,17,256]{4,2,3,1,0:T(2,128)S(1)}, u32[]{:S(2)}, u32[]{:S(2)}) %collective-permute-start.12) | collective-permute-done | bytes 139296 | tf_op jit(solution)/shard_map/ppermute | solution.py:112
  149.1 7.9 %collective-permute-start.13 = (f32[2,2,17,256]{3,1,2,0:T(2,128)S(1)}, f32[2,2,17,256]{3,1,2,0:T(2,128)S(1)}, u32[]{:S(2)}, u32[]{:S(2)}) collective-permute-start(f32[2,2,17,256]{3,1,2,0:T(2,128)S(1)} %bitcast.110), channel_id=1, source_target_pairs={{0,64},{8,72},{16,80},{24,88},{32,96},{40,104},{48,112},{56,120},{... | collective-permute-start | bytes 208904 | tf_op jit(solution)/shard_map/ppermute | solution.py:112
  157.0 2.3 %collective-permute-done.13 = f32[2,2,17,256]{3,1,2,0:T(2,128)S(1)} collective-permute-done((f32[2,2,17,256]{3,1,2,0:T(2,128)S(1)}, f32[2,2,17,256]{3,1,2,0:T(2,128)S(1)}, u32[]{:S(2)}, u32[]{:S(2)}) %collective-permute-start.13) | collective-permute-done | bytes 69664 | tf_op jit(solution)/shard_map/ppermute | solution.py:112
  159.4 2.8 %collective-permute-start.14 = (f32[2,17,256]{2,0,1:T(2,128)S(1)}, f32[2,17,256]{2,0,1:T(2,128)S(1)}, u32[]{:S(2)}, u32[]{:S(2)}) collective-permute-start(f32[2,17,256]{2,0,1:T(2,128)S(1)} %bitcast.111), channel_id=1, source_target_pairs={{0,128},{8,136},{16,144},{24,152},{32,160},{40,168},{48,176},{56,1... | collective-permute-start | bytes 104456 | tf_op jit(solution)/shard_map/ppermute | solution.py:112
  162.2 3.1 %collective-permute-done.14 = f32[2,17,256]{2,0,1:T(2,128)S(1)} collective-permute-done((f32[2,17,256]{2,0,1:T(2,128)S(1)}, f32[2,17,256]{2,0,1:T(2,128)S(1)}, u32[]{:S(2)}, u32[]{:S(2)}) %collective-permute-start.14) | collective-permute-done | bytes 34848 | tf_op jit(solution)/shard_map/ppermute | solution.py:112
  165.3 3.4 %collective-permute-start.15 = (f32[17,256]{1,0:T(8,128)S(1)}, f32[17,256]{1,0:T(8,128)S(1)}, u32[]{:S(2)}, u32[]{:S(2)}) collective-permute-start(f32[17,256]{1,0:T(8,128)S(1)} %bitcast.112), channel_id=1, source_target_pairs={{0,256},{8,264},{16,272},{24,280},{32,288},{40,296},{48,304},{56,3... | collective-permute-start | bytes 52232 | tf_op jit(solution)/shard_map/ppermute | solution.py:112
  168.8 3.8 %collective-permute-done.15 = f32[17,256]{1,0:T(8,128)S(1)} collective-permute-done((f32[17,256]{1,0:T(8,128)S(1)}, f32[17,256]{1,0:T(8,128)S(1)}, u32[]{:S(2)}, u32[]{:S(2)}) %collective-permute-start.15) | collective-permute-done | bytes 17440 | tf_op jit(solution)/shard_map/ppermute | solution.py:112
  (71 shorter events, 19.2 us)
Async XLA Ops:
  7.2 105.6 %all-gather.2.cloned.1.call-start = ((), (), s32[]{:S(2)}) async-start(), calls=%async_computation | async-start | bytes 2359296 | tf_op jit(solution)/shard_map/all_gather | solution.py:130
  8.3 16.1 %collective-permute-start = (bf16[4,16,16,128]{3,2,1,0:T(8,128)(2,1)S(1)}, bf16[4,16,16,128]{3,2,1,0:T(8,128)(2,1)S(1)}, u32[]{:S(2)}, u32[]{:S(2)}) collective-permute-start(bf16[4,16,16,128]{3,2,1,0:T(8,128)(2,1)S(1)} %convert_element_type.233), channel_id=1, source_target_pairs={{8,0},{16,8},{24,16},{32,24},{40,32},{48,40},{56,48},{64,56},{72,6... | collective-permute-start | bytes 786440 | tf_op jit(solution)/shard_map/ppermute | solution.py:24
  19.0 9.8 %collective-permute-start.1 = (bf16[4,16,16,128]{3,2,1,0:T(8,128)(2,1)S(1)}, bf16[4,16,16,128]{3,2,1,0:T(8,128)(2,1)S(1)}, u32[]{:S(2)}, u32[]{:S(2)}) collective-permute-start(bf16[4,16,16,128]{3,2,1,0:T(8,128)(2,1)S(1)} %convert_element_type.233), channel_id=1, source_target_pairs={{0,8},{8,16},{16,24},{24,32},{32,40},{40,48},{48,56},{56,64},{64,7... | collective-permute-start | bytes 786440 | tf_op jit(solution)/shard_map/ppermute | solution.py:23
  21.7 7.1 %copy-start = (f32[4,16,16,128]{3,2,1,0:T(8,128)S(1)}, f32[4,16,16,128]{3,2,1,0:T(8,128)}, u32[]{:S(2)}) copy-start(f32[4,16,16,128]{3,2,1,0:T(8,128)} %param.2) | copy-start | bytes 1572868
  21.7 7.2 %copy-start.2 = (f32[4,16,16]{2,1,0:T(8,128)S(1)}, f32[4,16,16]{2,1,0:T(8,128)}, u32[]{:S(2)}) copy-start(f32[4,16,16]{2,1,0:T(8,128)} %param.3) | copy-start | bytes 12292
  29.2 6.5 %collective-permute-start.2 = (bf16[4,16,16,128]{3,2,1,0:T(8,128)(2,1)S(1)}, bf16[4,16,16,128]{3,2,1,0:T(8,128)(2,1)S(1)}, u32[]{:S(2)}, u32[]{:S(2)}) collective-permute-start(bf16[4,16,16,128]{3,2,1,0:T(8,128)(2,1)S(1)} %get-tuple-element.9), channel_id=1, source_target_pairs={{8,0},{16,8},{24,16},{32,24},{40,32},{48,40},{56,48},{64,56},{72,6... | collective-permute-start | bytes 786440 | tf_op jit(solution)/shard_map/ppermute | solution.py:24
  31.1 9.8 %collective-permute-start.3 = (bf16[4,16,16,128]{3,2,1,0:T(8,128)(2,1)S(1)}, bf16[4,16,16,128]{3,2,1,0:T(8,128)(2,1)S(1)}, u32[]{:S(2)}, u32[]{:S(2)}) collective-permute-start(bf16[4,16,16,128]{3,2,1,0:T(8,128)(2,1)S(1)} %get-tuple-element.9), channel_id=1, source_target_pairs={{0,8},{8,16},{16,24},{24,32},{32,40},{40,48},{48,56},{56,64},{64,7... | collective-permute-start | bytes 786440 | tf_op jit(solution)/shard_map/ppermute | solution.py:23
  41.4 6.5 %collective-permute-start.4 = (bf16[4,16,16,128]{3,2,1,0:T(8,128)(2,1)S(1)}, bf16[4,16,16,128]{3,2,1,0:T(8,128)(2,1)S(1)}, u32[]{:S(2)}, u32[]{:S(2)}) collective-permute-start(bf16[4,16,16,128]{3,2,1,0:T(8,128)(2,1)S(1)} %get-tuple-element.7), channel_id=1, source_target_pairs={{8,0},{16,8},{24,16},{32,24},{40,32},{48,40},{56,48},{64,56},{72,6... | collective-permute-start | bytes 786440 | tf_op jit(solution)/shard_map/ppermute | solution.py:24
  43.3 9.8 %collective-permute-start.5 = (bf16[4,16,16,128]{3,2,1,0:T(8,128)(2,1)S(1)}, bf16[4,16,16,128]{3,2,1,0:T(8,128)(2,1)S(1)}, u32[]{:S(2)}, u32[]{:S(2)}) collective-permute-start(bf16[4,16,16,128]{3,2,1,0:T(8,128)(2,1)S(1)} %get-tuple-element.7), channel_id=1, source_target_pairs={{0,8},{8,16},{16,24},{24,32},{32,40},{40,48},{48,56},{56,64},{64,7... | collective-permute-start | bytes 786440 | tf_op jit(solution)/shard_map/ppermute | solution.py:23
  53.6 6.5 %collective-permute-start.6 = (bf16[4,16,16,128]{3,2,1,0:T(8,128)(2,1)S(1)}, bf16[4,16,16,128]{3,2,1,0:T(8,128)(2,1)S(1)}, u32[]{:S(2)}, u32[]{:S(2)}) collective-permute-start(bf16[4,16,16,128]{3,2,1,0:T(8,128)(2,1)S(1)} %get-tuple-element.5), channel_id=1, source_target_pairs={{8,0},{16,8},{24,16},{32,24},{40,32},{48,40},{56,48},{64,56},{72,6... | collective-permute-start | bytes 786440 | tf_op jit(solution)/shard_map/ppermute | solution.py:24
  55.5 9.8 %collective-permute-start.7 = (bf16[4,16,16,128]{3,2,1,0:T(8,128)(2,1)S(1)}, bf16[4,16,16,128]{3,2,1,0:T(8,128)(2,1)S(1)}, u32[]{:S(2)}, u32[]{:S(2)}) collective-permute-start(bf16[4,16,16,128]{3,2,1,0:T(8,128)(2,1)S(1)} %get-tuple-element.5), channel_id=1, source_target_pairs={{0,8},{8,16},{16,24},{24,32},{32,40},{40,48},{48,56},{56,64},{64,7... | collective-permute-start | bytes 786440 | tf_op jit(solution)/shard_map/ppermute | solution.py:23
  66.7 10.1 %collective-permute-start.9 = (bf16[4,16,16,128]{3,2,1,0:T(8,128)(2,1)}, bf16[4,16,16,128]{3,2,1,0:T(8,128)(2,1)S(1)}, u32[]{:S(2)}, u32[]{:S(2)}) collective-permute-start(bf16[4,16,16,128]{3,2,1,0:T(8,128)(2,1)} %convert_element_type.261), channel_id=1, source_target_pairs={{0,8},{8,16},{16,24},{24,32},{32,40},{40,48},{48,56},{56,64},{64,7... | collective-permute-start | bytes 786440 | tf_op jit(solution)/shard_map/ppermute | solution.py:23
  68.6 9.9 %collective-permute-start.8 = (bf16[4,16,16,128]{3,2,1,0:T(8,128)(2,1)}, bf16[4,16,16,128]{3,2,1,0:T(8,128)(2,1)S(1)}, u32[]{:S(2)}, u32[]{:S(2)}) collective-permute-start(bf16[4,16,16,128]{3,2,1,0:T(8,128)(2,1)} %convert_element_type.261), channel_id=1, source_target_pairs={{8,0},{16,8},{24,16},{32,24},{40,32},{48,40},{56,48},{64,56},{72,6... | collective-permute-start | bytes 786440 | tf_op jit(solution)/shard_map/ppermute | solution.py:24
  114.9 2.9 %copy-start.1 = (bf16[4,16,16,128]{3,2,1,0:T(8,128)(2,1)S(1)}, bf16[4,16,16,128]{3,2,1,0:T(8,128)(2,1)}, u32[]{:S(2)}) copy-start(bf16[4,16,16,128]{3,2,1,0:T(8,128)(2,1)} %convert_element_type.261) | copy-start | bytes 786436
  122.3 4.0 %collective-permute-start.10 = (f32[2,2,2,2,2,17,256]{6,4,5,3,2,1,0:T(2,128)}, f32[2,2,2,2,2,17,256]{6,4,5,3,2,1,0:T(2,128)S(1)}, u32[]{:S(2)}, u32[]{:S(2)}) collective-permute-start(f32[2,2,2,2,2,17,256]{6,4,5,3,2,1,0:T(2,128)} %copy.196), channel_id=1, source_target_pairs={{0,8},{8,0},{16,24},{24,16},{32,40},{40,32},{48,56},{56,48},{64,72... | collective-permute-start | bytes 1671176 | tf_op jit(solution)/shard_map/ppermute | solution.py:112
  127.0 10.6 %collective-permute-start.11 = (f32[2,2,2,2,17,256]{5,3,4,2,1,0:T(2,128)S(1)}, f32[2,2,2,2,17,256]{5,3,4,2,1,0:T(2,128)S(1)}, u32[]{:S(2)}, u32[]{:S(2)}) collective-permute-start(f32[2,2,2,2,17,256]{5,3,4,2,1,0:T(2,128)S(1)} %select_bitcast_fusion.1), channel_id=1, source_target_pairs={{0,16},{8,24},{16,0},{24,8},{32,48},{40,56},{48,32},{56,40},{64,80... | collective-permute-start | bytes 835592 | tf_op jit(solution)/shard_map/ppermute | solution.py:112
  138.1 10.7 %collective-permute-start.12 = (f32[2,2,2,17,256]{4,2,3,1,0:T(2,128)S(1)}, f32[2,2,2,17,256]{4,2,3,1,0:T(2,128)S(1)}, u32[]{:S(2)}, u32[]{:S(2)}) collective-permute-start(f32[2,2,2,17,256]{4,2,3,1,0:T(2,128)S(1)} %bitcast.109), channel_id=1, source_target_pairs={{0,32},{8,40},{16,48},{24,56},{32,0},{40,8},{48,16},{56,24},{64,96... | collective-permute-start | bytes 417800 | tf_op jit(solution)/shard_map/ppermute | solution.py:112
  149.1 10.2 %collective-permute-start.13 = (f32[2,2,17,256]{3,1,2,0:T(2,128)S(1)}, f32[2,2,17,256]{3,1,2,0:T(2,128)S(1)}, u32[]{:S(2)}, u32[]{:S(2)}) collective-permute-start(f32[2,2,17,256]{3,1,2,0:T(2,128)S(1)} %bitcast.110), channel_id=1, source_target_pairs={{0,64},{8,72},{16,80},{24,88},{32,96},{40,104},{48,112},{56,120},{... | collective-permute-start | bytes 208904 | tf_op jit(solution)/shard_map/ppermute | solution.py:112
  159.4 5.8 %collective-permute-start.14 = (f32[2,17,256]{2,0,1:T(2,128)S(1)}, f32[2,17,256]{2,0,1:T(2,128)S(1)}, u32[]{:S(2)}, u32[]{:S(2)}) collective-permute-start(f32[2,17,256]{2,0,1:T(2,128)S(1)} %bitcast.111), channel_id=1, source_target_pairs={{0,128},{8,136},{16,144},{24,152},{32,160},{40,168},{48,176},{56,1... | collective-permute-start | bytes 104456 | tf_op jit(solution)/shard_map/ppermute | solution.py:112
  165.3 7.2 %collective-permute-start.15 = (f32[17,256]{1,0:T(8,128)S(1)}, f32[17,256]{1,0:T(8,128)S(1)}, u32[]{:S(2)}, u32[]{:S(2)}) collective-permute-start(f32[17,256]{1,0:T(8,128)S(1)} %bitcast.112), channel_id=1, source_target_pairs={{0,256},{8,264},{16,272},{24,280},{32,288},{40,296},{48,304},{56,3... | collective-permute-start | bytes 52232 | tf_op jit(solution)/shard_map/ppermute | solution.py:112
Sparse Core Ops, SparseCore 0:
  66.7 45.9 all-gather.1

commit v2 on v1

--- a/solution.py
+++ b/solution.py
@@ -96,21 +96,23 @@
 
 
 def reduce_scatter_grid(slots):
-    size = slots.shape[0]
-    bits = size.bit_length() - 1
-    me = lax.axis_index("grid")
-    rest = slots.shape[1:]
-    buf = slots.reshape((2,) * bits + rest)
-    for bit in range(bits):
-        axis = bits - 1 - bit
-        mine = (me >> bit) & 1
-        low = lax.index_in_dim(buf, 0, axis=axis, keepdims=False)
-        high = lax.index_in_dim(buf, 1, axis=axis, keepdims=False)
-        keep = jnp.where(mine == 1, high, low)
-        send = jnp.where(mine == 1, low, high)
-        pairs = [(i, i ^ (1 << bit)) for i in range(size)]
-        buf = keep + lax.ppermute(send, "grid", pairs)
-    return buf
+    received = lax.all_to_all(slots, "grid", 0, 0, tiled=True)
+    return jnp.sum(received, axis=0)
+
+
+def gather_ring(block):
+    size = lax.axis_size("orb")
+    right = [(i, (i + 1) % size) for i in range(size)]
+    left = [(i, (i - 1) % size) for i in range(size)]
+    ahead = {0: block}
+    from_left, from_right = block, block
+    for step in range(1, size // 2 + 1):
+        from_left = lax.ppermute(from_left, "orb", right)
+        ahead[size - step] = from_left
+        if step <= (size - 1) // 2:
+            from_right = lax.ppermute(from_right, "orb", left)
+            ahead[step] = from_right
+    return jnp.concatenate([ahead[k] for k in range(size)], axis=1)
 
 
 def on_device(orbitals, potential):
@@ -127,7 +129,7 @@
         .astype(jnp.bfloat16)
         .reshape(point_count, own_width)
     )
-    orbitals_all = lax.all_gather(rounded_orbitals, "orb", axis=1, tiled=True)
+    orbitals_all = gather_ring(rounded_orbitals)
     total_width = orbitals_all.shape[1]
     rows = total_width // grid_size
     hamiltonian_part = contract_points(orbitals_all, rounded_image)
@@ -150,6 +152,7 @@
         axis=1,
     )
     slots = jnp.concatenate([body, tail[:, None, :]], axis=1)
+    slots = jnp.roll(slots, lax.axis_index("orb") * (grid_size * own_width // total_width), axis=0)
     combined = reduce_scatter_grid(slots)
     scale_own = 1.0 / jnp.sqrt(combined[rows, rows : rows + own_width] / point_total + EPSILON)
     column_scale = 1.0 / jnp.sqrt(combined[rows, :rows] / point_total + EPSILON)

time: 182 us -> 166 us (0.912)
  the two profiles are of different devices: /device:TPU:6 before, /device:TPU:1 now
where the time goes in v2:
time: 166 us; the launch traced here: 165 us
  blocking collectives  58.8 us (35%)
  starting transfers between devices  54.8 us (33%)
  waiting for transfers between devices  18.6 us (11%)
  matrix products  11.8 us (7%)
  other arithmetic  10.6 us (6%)
  local copies, waits for them, and re-layouts  9.3 us (6%)
    all_to_all x1, blocking collectives, reduce_scatter_grid(): received = lax.all_to_all(slots, 'grid', 0, 0, tiled=True)  58.8 us
    ppermute x5, starting transfers between devices, halo_layers(): before = lax.ppermute(last, 'grid', up).astype(shard.dtype)  19.1 us
    ppermute x5, starting transfers between devices, halo_layers(): after = lax.ppermute(initial, 'grid', down).astype(shard.dtype)  16.9 us
    ppermute x4, waiting for transfers between devices, gather_ring(): from_left = lax.ppermute(from_left, 'orb', right)  15 us
    dot_general x5, matrix products, apply_hamiltonian(): jnp.einsum('pq,zqo->zpo', plane, flat, precision=lax.Precision.HIGHEST, p...  10.4 us
    ppermute x4, starting transfers between devices, gather_ring(): from_left = lax.ppermute(from_left, 'orb', right)  9.72 us
    ppermute x3, starting transfers between devices, gather_ring(): from_right = lax.ppermute(from_right, 'orb', left)  9 us
    unnamed x15, local copies, waits for them, and re-layouts  4.38 us
  transfers between devices with their start and end apart: 17, of which 6 were waited for; matrix products, arithmetic and copies ran while one was open for 11% of the time, Pallas kernels for 0%

profile of v2, /device:TPU:1, one launch (start us, length us, event | category | flops | bytes accessed | tf_op | source)
XLA Modules:
  0.0 165.1 jit_solution(3148656462981606062)
XLA Ops:
  0.6 1.1 convert_element_type.233
  1.7 8.7 %collective-permute-start = (bf16[4,16,16,128]{3,2,1,0:T(8,128)(2,1)S(1)}, bf16[4,16,16,128]{3,2,1,0:T(8,128)(2,1)S(1)}, u32[]{:S(2)}, u32[]{:S(2)}) collective-permute-start(bf16[4,16,16,128]{3,2,1,0:T(8,128)(2,1)S(1)} %convert_element_type.233), channel_id=1, source_target_pairs={{8,0},{16,8},{24,16},{32,24},{40,32},{48,40},{56,48},{64,56},{72,6... | collective-permute-start | bytes 786440 | tf_op jit(solution)/shard_map/ppermute | solution.py:24
  10.5 1.9 %collective-permute-start.1 = (bf16[4,16,16,128]{3,2,1,0:T(8,128)(2,1)S(1)}, bf16[4,16,16,128]{3,2,1,0:T(8,128)(2,1)S(1)}, u32[]{:S(2)}, u32[]{:S(2)}) collective-permute-start(bf16[4,16,16,128]{3,2,1,0:T(8,128)(2,1)S(1)} %convert_element_type.233), channel_id=1, source_target_pairs={{0,8},{8,16},{16,24},{24,32},{32,40},{40,48},{48,56},{56,64},{64,7... | collective-permute-start | bytes 786440 | tf_op jit(solution)/shard_map/ppermute | solution.py:23
  13.2 2.7 %fusion.107 = f32[256,4,128]{2,0,1:T(8,128)S(1)} fusion(f32[4,256,128]{2,1,0:T(8,128)} %bitcast.64, s32[256]{0:T(256)S(1)} %get-tuple-element.13, s32[256]{0:T(256)S(1)} %get-tuple-element.14), kind=kOutput, calls=%fused_computation.179 | convolution fusion | flops 408944640 | bytes 1050624 | tf_op jit(solution)/shard_map/pq,zqo->zpo/dot_general | solution.py:59
  16.4 2.4 %collective-permute-start.2 = (bf16[4,16,16,128]{3,2,1,0:T(8,128)(2,1)S(1)}, bf16[4,16,16,128]{3,2,1,0:T(8,128)(2,1)S(1)}, u32[]{:S(2)}, u32[]{:S(2)}) collective-permute-start(bf16[4,16,16,128]{3,2,1,0:T(8,128)(2,1)S(1)} %get-tuple-element.9), channel_id=1, source_target_pairs={{8,0},{16,8},{24,16},{32,24},{40,32},{48,40},{56,48},{64,56},{72,6... | collective-permute-start | bytes 786440 | tf_op jit(solution)/shard_map/ppermute | solution.py:24
  18.9 3.6 %collective-permute-start.3 = (bf16[4,16,16,128]{3,2,1,0:T(8,128)(2,1)S(1)}, bf16[4,16,16,128]{3,2,1,0:T(8,128)(2,1)S(1)}, u32[]{:S(2)}, u32[]{:S(2)}) collective-permute-start(bf16[4,16,16,128]{3,2,1,0:T(8,128)(2,1)S(1)} %get-tuple-element.9), channel_id=1, source_target_pairs={{0,8},{8,16},{16,24},{24,32},{32,40},{40,48},{48,56},{56,64},{64,7... | collective-permute-start | bytes 786440 | tf_op jit(solution)/shard_map/ppermute | solution.py:23
  22.5 1.9 %convolution_bitcast_fusion.3 = f32[4,256,128]{1,2,0:T(8,128)S(1)} fusion(f32[4,256,128]{2,1,0:T(8,128)S(1)} %bitcast.70, s32[256]{0:T(256)S(1)} %get-tuple-element.13, s32[256]{0:T(256)S(1)} %get-tuple-element.14), kind=kOutput, calls=%fused_computation.55 | convolution fusion | flops 408944640 | bytes 1050624 | tf_op jit(solution)/shard_map/pq,zqo->zpo/dot_general | solution.py:59
  24.7 1.1 collective-permute-done.3
  26.2 1.9 %collective-permute-start.4 = (bf16[4,16,16,128]{3,2,1,0:T(8,128)(2,1)S(1)}, bf16[4,16,16,128]{3,2,1,0:T(8,128)(2,1)S(1)}, u32[]{:S(2)}, u32[]{:S(2)}) collective-permute-start(bf16[4,16,16,128]{3,2,1,0:T(8,128)(2,1)S(1)} %get-tuple-element.7), channel_id=1, source_target_pairs={{8,0},{16,8},{24,16},{32,24},{40,32},{48,40},{56,48},{64,56},{72,6... | collective-permute-start | bytes 786440 | tf_op jit(solution)/shard_map/ppermute | solution.py:24
  28.2 4.4 %collective-permute-start.5 = (bf16[4,16,16,128]{3,2,1,0:T(8,128)(2,1)S(1)}, bf16[4,16,16,128]{3,2,1,0:T(8,128)(2,1)S(1)}, u32[]{:S(2)}, u32[]{:S(2)}) collective-permute-start(bf16[4,16,16,128]{3,2,1,0:T(8,128)(2,1)S(1)} %get-tuple-element.7), channel_id=1, source_target_pairs={{0,8},{8,16},{16,24},{24,32},{32,40},{40,48},{48,56},{56,64},{64,7... | collective-permute-start | bytes 786440 | tf_op jit(solution)/shard_map/ppermute | solution.py:23
  32.6 1.9 %convolution_bitcast_fusion.2 = f32[4,256,128]{1,2,0:T(8,128)S(1)} fusion(f32[4,256,128]{2,1,0:T(8,128)S(1)} %bitcast.65, s32[256]{0:T(256)S(1)} %get-tuple-element.13, s32[256]{0:T(256)S(1)} %get-tuple-element.14), kind=kOutput, calls=%fused_computation.54 | convolution fusion | flops 408944640 | bytes 1050624 | tf_op jit(solution)/shard_map/pq,zqo->zpo/dot_general | solution.py:59
  34.8 1.1 collective-permute-done.5
  35.9 1.1 fusion.200
  37.0 1.9 %collective-permute-start.6 = (bf16[4,16,16,128]{3,2,1,0:T(8,128)(2,1)}, bf16[4,16,16,128]{3,2,1,0:T(8,128)(2,1)S(1)}, u32[]{:S(2)}, u32[]{:S(2)}) collective-permute-start(bf16[4,16,16,128]{3,2,1,0:T(8,128)(2,1)} %get-tuple-element.5), channel_id=1, source_target_pairs={{8,0},{16,8},{24,16},{32,24},{40,32},{48,40},{56,48},{64,56},{72,6... | collective-permute-start | bytes 786440 | tf_op jit(solution)/shard_map/ppermute | solution.py:24
  38.9 4.4 %collective-permute-start.7 = (bf16[4,16,16,128]{3,2,1,0:T(8,128)(2,1)}, bf16[4,16,16,128]{3,2,1,0:T(8,128)(2,1)S(1)}, u32[]{:S(2)}, u32[]{:S(2)}) collective-permute-start(bf16[4,16,16,128]{3,2,1,0:T(8,128)(2,1)} %get-tuple-element.5), channel_id=1, source_target_pairs={{0,8},{8,16},{16,24},{24,32},{32,40},{40,48},{48,56},{56,64},{64,7... | collective-permute-start | bytes 786440 | tf_op jit(solution)/shard_map/ppermute | solution.py:23
  43.3 1.9 %convolution_bitcast_fusion.1 = f32[4,256,128]{1,2,0:T(8,128)S(1)} fusion(f32[4,256,128]{2,1,0:T(8,128)S(1)} %bitcast.75, s32[256]{0:T(256)S(1)} %get-tuple-element.13, s32[256]{0:T(256)S(1)} %get-tuple-element.14), kind=kOutput, calls=%fused_computation.53 | convolution fusion | flops 408944640 | bytes 1050624 | tf_op jit(solution)/shard_map/pq,zqo->zpo/dot_general | solution.py:59
  45.7 1.2 collective-permute-done.7
  47.5 1.9 %collective-permute-start.8 = (bf16[1024,128]{1,0:T(8,128)(2,1)S(1)}, bf16[1024,128]{1,0:T(8,128)(2,1)}, u32[]{:S(2)}, u32[]{:S(2)}) collective-permute-start(bf16[1024,128]{1,0:T(8,128)(2,1)S(1)} %bitcast.66), channel_id=1, source_target_pairs={{0,7},{1,0},{2,1},{3,2},{4,3},{5,4},{6,5},{7,6},{8,15},{9,8},{10,9... | collective-permute-start | bytes 786440 | tf_op jit(solution)/shard_map/ppermute | solution.py:113
  49.4 3.4 %collective-permute-start.11 = (bf16[1024,128]{1,0:T(8,128)(2,1)S(1)}, bf16[1024,128]{1,0:T(8,128)(2,1)}, u32[]{:S(2)}, u32[]{:S(2)}) collective-permute-start(bf16[1024,128]{1,0:T(8,128)(2,1)S(1)} %bitcast.67), channel_id=1, source_target_pairs={{0,1},{1,2},{2,3},{3,4},{4,5},{5,6},{6,7},{7,0},{8,9},{9,10},{10,1... | collective-permute-start | bytes 786440 | tf_op jit(solution)/shard_map/ppermute | solution.py:110
  52.9 1.9 %collective-permute-start.15 = (bf16[4,16,16,128]{3,2,1,0:T(8,128)(2,1)S(1)}, bf16[4,16,16,128]{3,2,1,0:T(8,128)(2,1)}, u32[]{:S(2)}, u32[]{:S(2)}) collective-permute-start(bf16[4,16,16,128]{3,2,1,0:T(8,128)(2,1)S(1)} %convert_element_type.261), channel_id=1, source_target_pairs={{8,0},{16,8},{24,16},{32,24},{40,32},{48,40},{56,48},{64,56},{72,6... | collective-permute-start | bytes 786440 | tf_op jit(solution)/shard_map/ppermute | solution.py:24
  54.8 4.8 %collective-permute-start.16 = (bf16[4,16,16,128]{3,2,1,0:T(8,128)(2,1)S(1)}, bf16[4,16,16,128]{3,2,1,0:T(8,128)(2,1)}, u32[]{:S(2)}, u32[]{:S(2)}) collective-permute-start(bf16[4,16,16,128]{3,2,1,0:T(8,128)(2,1)S(1)} %convert_element_type.261), channel_id=1, source_target_pairs={{0,8},{8,16},{16,24},{24,32},{32,40},{40,48},{48,56},{56,64},{64,7... | collective-permute-start | bytes 786440 | tf_op jit(solution)/shard_map/ppermute | solution.py:23
  59.7 2.9 %collective-permute-start.9 = (bf16[1024,128]{1,0:T(8,128)(2,1)}, bf16[1024,128]{1,0:T(8,128)(2,1)}, u32[]{:S(2)}, u32[]{:S(2)}) collective-permute-start(bf16[1024,128]{1,0:T(8,128)(2,1)} %collective-permute-done.8), channel_id=1, source_target_pairs={{0,7},{1,0},{2,1},{3,2},{4,3},{5,4},{6,5},{7,6},{8,15},{9,8},{10,9... | collective-permute-start | bytes 786440 | tf_op jit(solution)/shard_map/ppermute | solution.py:113
  62.7 2.5 %collective-permute-start.12 = (bf16[1024,128]{1,0:T(8,128)(2,1)}, bf16[1024,128]{1,0:T(8,128)(2,1)}, u32[]{:S(2)}, u32[]{:S(2)}) collective-permute-start(bf16[1024,128]{1,0:T(8,128)(2,1)} %collective-permute-done.11), channel_id=1, source_target_pairs={{0,1},{1,2},{2,3},{3,4},{4,5},{5,6},{6,7},{7,0},{8,9},{9,10},{10,1... | collective-permute-start | bytes 786440 | tf_op jit(solution)/shard_map/ppermute | solution.py:110
  65.2 1.9 %convolution_bitcast_fusion = f32[4,256,128]{1,2,0:T(8,128)S(1)} fusion(f32[4,256,128]{2,1,0:T(8,128)S(1)} %bitcast.63, s32[256]{0:T(256)S(1)} %get-tuple-element.13, s32[256]{0:T(256)S(1)} %get-tuple-element.14), kind=kOutput, calls=%fused_computation.52 | convolution fusion | flops 408944640 | bytes 1050624 | tf_op jit(solution)/shard_map/pq,zqo->zpo/dot_general | solution.py:59
  69.4 4.1 %collective-permute-start.10 = (bf16[1024,128]{1,0:T(8,128)(2,1)}, bf16[1024,128]{1,0:T(8,128)(2,1)S(1)}, u32[]{:S(2)}, u32[]{:S(2)}) collective-permute-start(bf16[1024,128]{1,0:T(8,128)(2,1)} %collective-permute-done.9), channel_id=1, source_target_pairs={{0,7},{1,0},{2,1},{3,2},{4,3},{5,4},{6,5},{7,6},{8,15},{9,8},{10,9... | collective-permute-start | bytes 786440 | tf_op jit(solution)/shard_map/ppermute | solution.py:113
  73.6 1.9 %collective-permute-start.13 = (bf16[1024,128]{1,0:T(8,128)(2,1)}, bf16[1024,128]{1,0:T(8,128)(2,1)S(1)}, u32[]{:S(2)}, u32[]{:S(2)}) collective-permute-start(bf16[1024,128]{1,0:T(8,128)(2,1)} %collective-permute-done.12), channel_id=1, source_target_pairs={{0,1},{1,2},{2,3},{3,4},{4,5},{5,6},{6,7},{7,0},{8,9},{9,10},{10,1... | collective-permute-start | bytes 786440 | tf_op jit(solution)/shard_map/ppermute | solution.py:110
  75.5 1.0 fusion.14
  76.6 8.6 %collective-permute-done.13 = bf16[1024,128]{1,0:T(8,128)(2,1)S(1)} collective-permute-done((bf16[1024,128]{1,0:T(8,128)(2,1)}, bf16[1024,128]{1,0:T(8,128)(2,1)S(1)}, u32[]{:S(2)}, u32[]{:S(2)}) %collective-permute-start.13) | collective-permute-done | bytes 262176 | tf_op jit(solution)/shard_map/ppermute | solution.py:110
  85.2 1.9 %collective-permute-start.14 = (bf16[1024,128]{1,0:T(8,128)(2,1)S(1)}, bf16[1024,128]{1,0:T(8,128)(2,1)S(1)}, u32[]{:S(2)}, u32[]{:S(2)}) collective-permute-start(bf16[1024,128]{1,0:T(8,128)(2,1)S(1)} %collective-permute-done.13), channel_id=1, source_target_pairs={{0,1},{1,2},{2,3},{3,4},{4,5},{5,6},{6,7},{7,0},{8,9},{9,10},{10,1... | collective-permute-start | bytes 786440 | tf_op jit(solution)/shard_map/ppermute | solution.py:110
  89.3 6.4 %collective-permute-done.14 = bf16[1024,128]{1,0:T(8,128)(2,1)S(1)} collective-permute-done((bf16[1024,128]{1,0:T(8,128)(2,1)S(1)}, bf16[1024,128]{1,0:T(8,128)(2,1)S(1)}, u32[]{:S(2)}, u32[]{:S(2)}) %collective-permute-start.14) | collective-permute-done | bytes 262176 | tf_op jit(solution)/shard_map/ppermute | solution.py:110
  99.3 2.9 %copy.20 = bf16[1024,1024]{1,0:T(8,128)(2,1)S(1)} copy(bf16[1024,1024]{0,1:T(8,128)(2,1)} %bitcast.62) | data formatting | bytes 4194304 | tf_op jit(solution)/shard_map/dot_general | solution.py:93
  104.5 58.8 %all_to_all.5 = f32[64,17,256]{2,1,0:T(8,128)S(1)} all-to-all(f32[64,17,256]{2,1,0:T(8,128)S(1)} %fusion.2), channel_id=1, replica_groups=mesh['grid'=64,'orb'=8] {'grid'}, dimensions={0} | all-to-all | bytes 2228224 | tf_op jit(solution)/shard_map/all_to_all | solution.py:99
  (64 shorter events, 15.4 us)
Async XLA Ops:
  1.7 14.2 %collective-permute-start = (bf16[4,16,16,128]{3,2,1,0:T(8,128)(2,1)S(1)}, bf16[4,16,16,128]{3,2,1,0:T(8,128)(2,1)S(1)}, u32[]{:S(2)}, u32[]{:S(2)}) collective-permute-start(bf16[4,16,16,128]{3,2,1,0:T(8,128)(2,1)S(1)} %convert_element_type.233), channel_id=1, source_target_pairs={{8,0},{16,8},{24,16},{32,24},{40,32},{48,40},{56,48},{64,56},{72,6... | collective-permute-start | bytes 786440 | tf_op jit(solution)/shard_map/ppermute | solution.py:24
  10.5 5.5 %collective-permute-start.1 = (bf16[4,16,16,128]{3,2,1,0:T(8,128)(2,1)S(1)}, bf16[4,16,16,128]{3,2,1,0:T(8,128)(2,1)S(1)}, u32[]{:S(2)}, u32[]{:S(2)}) collective-permute-start(bf16[4,16,16,128]{3,2,1,0:T(8,128)(2,1)S(1)} %convert_element_type.233), channel_id=1, source_target_pairs={{0,8},{8,16},{16,24},{24,32},{32,40},{40,48},{48,56},{56,64},{64,7... | collective-permute-start | bytes 786440 | tf_op jit(solution)/shard_map/ppermute | solution.py:23
  13.2 2.9 %copy-start.1 = (f32[4,16,16,128]{3,2,1,0:T(8,128)S(1)}, f32[4,16,16,128]{3,2,1,0:T(8,128)}, u32[]{:S(2)}) copy-start(f32[4,16,16,128]{3,2,1,0:T(8,128)} %param.2) | copy-start | bytes 1572868
  13.2 2.9 %copy-start.3 = (f32[4,16,16]{2,1,0:T(8,128)S(1)}, f32[4,16,16]{2,1,0:T(8,128)}, u32[]{:S(2)}) copy-start(f32[4,16,16]{2,1,0:T(8,128)} %param.3) | copy-start | bytes 12292
  16.4 8.2 %collective-permute-start.2 = (bf16[4,16,16,128]{3,2,1,0:T(8,128)(2,1)S(1)}, bf16[4,16,16,128]{3,2,1,0:T(8,128)(2,1)S(1)}, u32[]{:S(2)}, u32[]{:S(2)}) collective-permute-start(bf16[4,16,16,128]{3,2,1,0:T(8,128)(2,1)S(1)} %get-tuple-element.9), channel_id=1, source_target_pairs={{8,0},{16,8},{24,16},{32,24},{40,32},{48,40},{56,48},{64,56},{72,6... | collective-permute-start | bytes 786440 | tf_op jit(solution)/shard_map/ppermute | solution.py:24
  18.9 6.9 %collective-permute-start.3 = (bf16[4,16,16,128]{3,2,1,0:T(8,128)(2,1)S(1)}, bf16[4,16,16,128]{3,2,1,0:T(8,128)(2,1)S(1)}, u32[]{:S(2)}, u32[]{:S(2)}) collective-permute-start(bf16[4,16,16,128]{3,2,1,0:T(8,128)(2,1)S(1)} %get-tuple-element.9), channel_id=1, source_target_pairs={{0,8},{8,16},{16,24},{24,32},{32,40},{40,48},{48,56},{56,64},{64,7... | collective-permute-start | bytes 786440 | tf_op jit(solution)/shard_map/ppermute | solution.py:23
  26.2 8.5 %collective-permute-start.4 = (bf16[4,16,16,128]{3,2,1,0:T(8,128)(2,1)S(1)}, bf16[4,16,16,128]{3,2,1,0:T(8,128)(2,1)S(1)}, u32[]{:S(2)}, u32[]{:S(2)}) collective-permute-start(bf16[4,16,16,128]{3,2,1,0:T(8,128)(2,1)S(1)} %get-tuple-element.7), channel_id=1, source_target_pairs={{8,0},{16,8},{24,16},{32,24},{40,32},{48,40},{56,48},{64,56},{72,6... | collective-permute-start | bytes 786440 | tf_op jit(solution)/shard_map/ppermute | solution.py:24
  28.2 7.7 %collective-permute-start.5 = (bf16[4,16,16,128]{3,2,1,0:T(8,128)(2,1)S(1)}, bf16[4,16,16,128]{3,2,1,0:T(8,128)(2,1)S(1)}, u32[]{:S(2)}, u32[]{:S(2)}) collective-permute-start(bf16[4,16,16,128]{3,2,1,0:T(8,128)(2,1)S(1)} %get-tuple-element.7), channel_id=1, source_target_pairs={{0,8},{8,16},{16,24},{24,32},{32,40},{40,48},{48,56},{56,64},{64,7... | collective-permute-start | bytes 786440 | tf_op jit(solution)/shard_map/ppermute | solution.py:23
  37.0 8.6 %collective-permute-start.6 = (bf16[4,16,16,128]{3,2,1,0:T(8,128)(2,1)}, bf16[4,16,16,128]{3,2,1,0:T(8,128)(2,1)S(1)}, u32[]{:S(2)}, u32[]{:S(2)}) collective-permute-start(bf16[4,16,16,128]{3,2,1,0:T(8,128)(2,1)} %get-tuple-element.5), channel_id=1, source_target_pairs={{8,0},{16,8},{24,16},{32,24},{40,32},{48,40},{56,48},{64,56},{72,6... | collective-permute-start | bytes 786440 | tf_op jit(solution)/shard_map/ppermute | solution.py:24
  38.9 8.0 %collective-permute-start.7 = (bf16[4,16,16,128]{3,2,1,0:T(8,128)(2,1)}, bf16[4,16,16,128]{3,2,1,0:T(8,128)(2,1)S(1)}, u32[]{:S(2)}, u32[]{:S(2)}) collective-permute-start(bf16[4,16,16,128]{3,2,1,0:T(8,128)(2,1)} %get-tuple-element.5), channel_id=1, source_target_pairs={{0,8},{8,16},{16,24},{24,32},{32,40},{40,48},{48,56},{56,64},{64,7... | collective-permute-start | bytes 786440 | tf_op jit(solution)/shard_map/ppermute | solution.py:23
  47.5 12.3 %collective-permute-start.8 = (bf16[1024,128]{1,0:T(8,128)(2,1)S(1)}, bf16[1024,128]{1,0:T(8,128)(2,1)}, u32[]{:S(2)}, u32[]{:S(2)}) collective-permute-start(bf16[1024,128]{1,0:T(8,128)(2,1)S(1)} %bitcast.66), channel_id=1, source_target_pairs={{0,7},{1,0},{2,1},{3,2},{4,3},{5,4},{6,5},{7,6},{8,15},{9,8},{10,9... | collective-permute-start | bytes 786440 | tf_op jit(solution)/shard_map/ppermute | solution.py:113
  49.4 13.3 %collective-permute-start.11 = (bf16[1024,128]{1,0:T(8,128)(2,1)S(1)}, bf16[1024,128]{1,0:T(8,128)(2,1)}, u32[]{:S(2)}, u32[]{:S(2)}) collective-permute-start(bf16[1024,128]{1,0:T(8,128)(2,1)S(1)} %bitcast.67), channel_id=1, source_target_pairs={{0,1},{1,2},{2,3},{3,4},{4,5},{5,6},{6,7},{7,0},{8,9},{9,10},{10,1... | collective-permute-start | bytes 786440 | tf_op jit(solution)/shard_map/ppermute | solution.py:110
  52.9 14.5 %collective-permute-start.15 = (bf16[4,16,16,128]{3,2,1,0:T(8,128)(2,1)S(1)}, bf16[4,16,16,128]{3,2,1,0:T(8,128)(2,1)}, u32[]{:S(2)}, u32[]{:S(2)}) collective-permute-start(bf16[4,16,16,128]{3,2,1,0:T(8,128)(2,1)S(1)} %convert_element_type.261), channel_id=1, source_target_pairs={{8,0},{16,8},{24,16},{32,24},{40,32},{48,40},{56,48},{64,56},{72,6... | collective-permute-start | bytes 786440 | tf_op jit(solution)/shard_map/ppermute | solution.py:24
  54.8 13.6 %collective-permute-start.16 = (bf16[4,16,16,128]{3,2,1,0:T(8,128)(2,1)S(1)}, bf16[4,16,16,128]{3,2,1,0:T(8,128)(2,1)}, u32[]{:S(2)}, u32[]{:S(2)}) collective-permute-start(bf16[4,16,16,128]{3,2,1,0:T(8,128)(2,1)S(1)} %convert_element_type.261), channel_id=1, source_target_pairs={{0,8},{8,16},{16,24},{24,32},{32,40},{40,48},{48,56},{56,64},{64,7... | collective-permute-start | bytes 786440 | tf_op jit(solution)/shard_map/ppermute | solution.py:23
  59.7 9.7 %collective-permute-start.9 = (bf16[1024,128]{1,0:T(8,128)(2,1)}, bf16[1024,128]{1,0:T(8,128)(2,1)}, u32[]{:S(2)}, u32[]{:S(2)}) collective-permute-start(bf16[1024,128]{1,0:T(8,128)(2,1)} %collective-permute-done.8), channel_id=1, source_target_pairs={{0,7},{1,0},{2,1},{3,2},{4,3},{5,4},{6,5},{7,6},{8,15},{9,8},{10,9... | collective-permute-start | bytes 786440 | tf_op jit(solution)/shard_map/ppermute | solution.py:113
  62.7 10.9 %collective-permute-start.12 = (bf16[1024,128]{1,0:T(8,128)(2,1)}, bf16[1024,128]{1,0:T(8,128)(2,1)}, u32[]{:S(2)}, u32[]{:S(2)}) collective-permute-start(bf16[1024,128]{1,0:T(8,128)(2,1)} %collective-permute-done.11), channel_id=1, source_target_pairs={{0,1},{1,2},{2,3},{3,4},{4,5},{5,6},{6,7},{7,0},{8,9},{9,10},{10,1... | collective-permute-start | bytes 786440 | tf_op jit(solution)/shard_map/ppermute | solution.py:110
  69.4 19.7 %collective-permute-start.10 = (bf16[1024,128]{1,0:T(8,128)(2,1)}, bf16[1024,128]{1,0:T(8,128)(2,1)S(1)}, u32[]{:S(2)}, u32[]{:S(2)}) collective-permute-start(bf16[1024,128]{1,0:T(8,128)(2,1)} %collective-permute-done.9), channel_id=1, source_target_pairs={{0,7},{1,0},{2,1},{3,2},{4,3},{5,4},{6,5},{7,6},{8,15},{9,8},{10,9... | collective-permute-start | bytes 786440 | tf_op jit(solution)/shard_map/ppermute | solution.py:113
  73.6 11.6 %collective-permute-start.13 = (bf16[1024,128]{1,0:T(8,128)(2,1)}, bf16[1024,128]{1,0:T(8,128)(2,1)S(1)}, u32[]{:S(2)}, u32[]{:S(2)}) collective-permute-start(bf16[1024,128]{1,0:T(8,128)(2,1)} %collective-permute-done.12), channel_id=1, source_target_pairs={{0,1},{1,2},{2,3},{3,4},{4,5},{5,6},{6,7},{7,0},{8,9},{9,10},{10,1... | collective-permute-start | bytes 786440 | tf_op jit(solution)/shard_map/ppermute | solution.py:110
  85.2 10.5 %collective-permute-start.14 = (bf16[1024,128]{1,0:T(8,128)(2,1)S(1)}, bf16[1024,128]{1,0:T(8,128)(2,1)S(1)}, u32[]{:S(2)}, u32[]{:S(2)}) collective-permute-start(bf16[1024,128]{1,0:T(8,128)(2,1)S(1)} %collective-permute-done.13), channel_id=1, source_target_pairs={{0,1},{1,2},{2,3},{3,4},{4,5},{5,6},{6,7},{7,0},{8,9},{9,10},{10,1... | collective-permute-start | bytes 786440 | tf_op jit(solution)/shard_map/ppermute | solution.py:110
  97.9 1.3 copy-start
  102.1 1.0 copy-start.2

commit v3 on v2

--- a/solution.py
+++ b/solution.py
@@ -95,9 +95,31 @@
     )
 
 
+def halving_order(bits):
+    order = [0, 1, 4, 2, 5, 3]
+    if bits != 6:
+        order = list(range(bits))
+    return order
+
+
 def reduce_scatter_grid(slots):
-    received = lax.all_to_all(slots, "grid", 0, 0, tiled=True)
-    return jnp.sum(received, axis=0)
+    size = slots.shape[0]
+    bits = size.bit_length() - 1
+    me = lax.axis_index("grid")
+    rest = slots.shape[1:]
+    buf = slots.reshape((2,) * bits + rest)
+    remaining = list(range(bits - 1, -1, -1))
+    for bit in halving_order(bits):
+        axis = remaining.index(bit)
+        remaining.remove(bit)
+        mine = (me >> bit) & 1
+        low = lax.index_in_dim(buf, 0, axis=axis, keepdims=False)
+        high = lax.index_in_dim(buf, 1, axis=axis, keepdims=False)
+        keep = jnp.where(mine == 1, high, low)
+        send = jnp.where(mine == 1, low, high)
+        pairs = [(i, i ^ (1 << bit)) for i in range(size)]
+        buf = keep + lax.ppermute(send, "grid", pairs)
+    return buf
 
 
 def gather_ring(block):

time: 166 us -> 171 us (1.030)
  the two profiles are of different devices: /device:TPU:1 before, /device:TPU:6 now
where the time goes in v3:
time: 171 us; the launch traced here: 170 us
  starting transfers between devices  66.6 us (39%)
  waiting for transfers between devices  66 us (39%)
  other arithmetic  13.3 us (8%)
  matrix products  11.8 us (7%)
  local copies, waits for them, and re-layouts  10.8 us (6%)
    ppermute x6, waiting for transfers between devices, reduce_scatter_grid(): buf = keep + lax.ppermute(send, 'grid', pairs)  33 us
    ppermute x5, waiting for transfers between devices, halo_layers(): before = lax.ppermute(last, 'grid', up).astype(shard.dtype)  20.1 us
    ppermute x5, starting transfers between devices, halo_layers(): after = lax.ppermute(initial, 'grid', down).astype(shard.dtype)  18.3 us
    ppermute x3, starting transfers between devices, gather_ring(): from_right = lax.ppermute(from_right, 'orb', left)  15.8 us
    ppermute x6, starting transfers between devices, reduce_scatter_grid(): buf = keep + lax.ppermute(send, 'grid', pairs)  13.1 us
    ppermute x4, waiting for transfers between devices, gather_ring(): from_left = lax.ppermute(from_left, 'orb', right)  13 us
    ppermute x5, starting transfers between devices, halo_layers(): before = lax.ppermute(last, 'grid', up).astype(shard.dtype)  11.5 us
    dot_general x5, matrix products, apply_hamiltonian(): jnp.einsum('pq,zqo->zpo', plane, flat, precision=lax.Precision.HIGHEST, p...  10.4 us
  transfers between devices with their start and end apart: 23, of which 12 were waited for; matrix products, arithmetic and copies ran while one was open for 10% of the time, Pallas kernels for 0%

profile of v3, /device:TPU:6, one launch (start us, length us, event | category | flops | bytes accessed | tf_op | source)
XLA Modules:
  0.0 169.9 jit_solution(13734154900441660788)
XLA Ops:
  1.7 10.7 %collective-permute-start = (bf16[4,16,16,128]{3,2,1,0:T(8,128)(2,1)S(1)}, bf16[4,16,16,128]{3,2,1,0:T(8,128)(2,1)S(1)}, u32[]{:S(2)}, u32[]{:S(2)}) collective-permute-start(bf16[4,16,16,128]{3,2,1,0:T(8,128)(2,1)S(1)} %convert_element_type.233), channel_id=1, source_target_pairs={{8,0},{16,8},{24,16},{32,24},{40,32},{48,40},{56,48},{64,56},{72,6... | collective-permute-start | bytes 786440 | tf_op jit(solution)/shard_map/ppermute | solution.py:24
  12.4 1.9 %collective-permute-start.1 = (bf16[4,16,16,128]{3,2,1,0:T(8,128)(2,1)S(1)}, bf16[4,16,16,128]{3,2,1,0:T(8,128)(2,1)S(1)}, u32[]{:S(2)}, u32[]{:S(2)}) collective-permute-start(bf16[4,16,16,128]{3,2,1,0:T(8,128)(2,1)S(1)} %convert_element_type.233), channel_id=1, source_target_pairs={{0,8},{8,16},{16,24},{24,32},{32,40},{40,48},{48,56},{56,64},{64,7... | collective-permute-start | bytes 786440 | tf_op jit(solution)/shard_map/ppermute | solution.py:23
  15.1 2.7 %fusion.111 = f32[256,4,128]{2,0,1:T(8,128)S(1)} fusion(f32[4,256,128]{2,1,0:T(8,128)} %bitcast.134, s32[256]{0:T(256)S(1)} %get-tuple-element.24, s32[256]{0:T(256)S(1)} %get-tuple-element.25), kind=kOutput, calls=%fused_computation.190 | convolution fusion | flops 408944640 | bytes 1050624 | tf_op jit(solution)/shard_map/pq,zqo->zpo/dot_general | solution.py:59
  17.9 4.3 %collective-permute-done.1 = bf16[4,16,16,128]{3,2,1,0:T(8,128)(2,1)S(1)} collective-permute-done((bf16[4,16,16,128]{3,2,1,0:T(8,128)(2,1)S(1)}, bf16[4,16,16,128]{3,2,1,0:T(8,128)(2,1)S(1)}, u32[]{:S(2)}, u32[]{:S(2)}) %collective-permute-start.1) | collective-permute-done | bytes 262176 | tf_op jit(solution)/shard_map/ppermute | solution.py:23
  22.6 1.9 %collective-permute-start.2 = (bf16[4,16,16,128]{3,2,1,0:T(8,128)(2,1)S(1)}, bf16[4,16,16,128]{3,2,1,0:T(8,128)(2,1)S(1)}, u32[]{:S(2)}, u32[]{:S(2)}) collective-permute-start(bf16[4,16,16,128]{3,2,1,0:T(8,128)(2,1)S(1)} %get-tuple-element.9), channel_id=1, source_target_pairs={{8,0},{16,8},{24,16},{32,24},{40,32},{48,40},{56,48},{64,56},{72,6... | collective-permute-start | bytes 786440 | tf_op jit(solution)/shard_map/ppermute | solution.py:24
  24.6 2.4 %collective-permute-start.3 = (bf16[4,16,16,128]{3,2,1,0:T(8,128)(2,1)S(1)}, bf16[4,16,16,128]{3,2,1,0:T(8,128)(2,1)S(1)}, u32[]{:S(2)}, u32[]{:S(2)}) collective-permute-start(bf16[4,16,16,128]{3,2,1,0:T(8,128)(2,1)S(1)} %get-tuple-element.9), channel_id=1, source_target_pairs={{0,8},{8,16},{16,24},{24,32},{32,40},{40,48},{48,56},{56,64},{64,7... | collective-permute-start | bytes 786440 | tf_op jit(solution)/shard_map/ppermute | solution.py:23
  27.0 1.9 %convolution_bitcast_fusion.3 = f32[4,256,128]{1,2,0:T(8,128)S(1)} fusion(f32[4,256,128]{2,1,0:T(8,128)S(1)} %bitcast.140, s32[256]{0:T(256)S(1)} %get-tuple-element.24, s32[256]{0:T(256)S(1)} %get-tuple-element.25), kind=kOutput, calls=%fused_computation.55 | convolution fusion | flops 408944640 | bytes 1050624 | tf_op jit(solution)/shard_map/pq,zqo->zpo/dot_general | solution.py:59
  29.2 5.1 %collective-permute-done.3 = bf16[4,16,16,128]{3,2,1,0:T(8,128)(2,1)S(1)} collective-permute-done((bf16[4,16,16,128]{3,2,1,0:T(8,128)(2,1)S(1)}, bf16[4,16,16,128]{3,2,1,0:T(8,128)(2,1)S(1)}, u32[]{:S(2)}, u32[]{:S(2)}) %collective-permute-start.3) | collective-permute-done | bytes 262176 | tf_op jit(solution)/shard_map/ppermute | solution.py:23
  36.8 2.4 %collective-permute-start.5 = (bf16[4,16,16,128]{3,2,1,0:T(8,128)(2,1)S(1)}, bf16[4,16,16,128]{3,2,1,0:T(8,128)(2,1)S(1)}, u32[]{:S(2)}, u32[]{:S(2)}) collective-permute-start(bf16[4,16,16,128]{3,2,1,0:T(8,128)(2,1)S(1)} %get-tuple-element.7), channel_id=1, source_target_pairs={{0,8},{8,16},{16,24},{24,32},{32,40},{40,48},{48,56},{56,64},{64,7... | collective-permute-start | bytes 786440 | tf_op jit(solution)/shard_map/ppermute | solution.py:23
  39.2 1.9 %convolution_bitcast_fusion.2 = f32[4,256,128]{1,2,0:T(8,128)S(1)} fusion(f32[4,256,128]{2,1,0:T(8,128)S(1)} %bitcast.135, s32[256]{0:T(256)S(1)} %get-tuple-element.24, s32[256]{0:T(256)S(1)} %get-tuple-element.25), kind=kOutput, calls=%fused_computation.54 | convolution fusion | flops 408944640 | bytes 1050624 | tf_op jit(solution)/shard_map/pq,zqo->zpo/dot_general | solution.py:59
  41.4 5.2 %collective-permute-done.5 = bf16[4,16,16,128]{3,2,1,0:T(8,128)(2,1)S(1)} collective-permute-done((bf16[4,16,16,128]{3,2,1,0:T(8,128)(2,1)S(1)}, bf16[4,16,16,128]{3,2,1,0:T(8,128)(2,1)S(1)}, u32[]{:S(2)}, u32[]{:S(2)}) %collective-permute-start.5) | collective-permute-done | bytes 262176 | tf_op jit(solution)/shard_map/ppermute | solution.py:23
  49.6 2.4 %collective-permute-start.7 = (bf16[4,16,16,128]{3,2,1,0:T(8,128)(2,1)}, bf16[4,16,16,128]{3,2,1,0:T(8,128)(2,1)S(1)}, u32[]{:S(2)}, u32[]{:S(2)}) collective-permute-start(bf16[4,16,16,128]{3,2,1,0:T(8,128)(2,1)} %get-tuple-element.5), channel_id=1, source_target_pairs={{0,8},{8,16},{16,24},{24,32},{32,40},{40,48},{48,56},{56,64},{64,7... | collective-permute-start | bytes 786440 | tf_op jit(solution)/shard_map/ppermute | solution.py:23
  52.1 1.9 %convolution_bitcast_fusion.1 = f32[4,256,128]{1,2,0:T(8,128)S(1)} fusion(f32[4,256,128]{2,1,0:T(8,128)S(1)} %bitcast.145, s32[256]{0:T(256)S(1)} %get-tuple-element.24, s32[256]{0:T(256)S(1)} %get-tuple-element.25), kind=kOutput, calls=%fused_computation.53 | convolution fusion | flops 408944640 | bytes 1050624 | tf_op jit(solution)/shard_map/pq,zqo->zpo/dot_general | solution.py:59
  54.2 5.4 %collective-permute-done.7 = bf16[4,16,16,128]{3,2,1,0:T(8,128)(2,1)S(1)} collective-permute-done((bf16[4,16,16,128]{3,2,1,0:T(8,128)(2,1)}, bf16[4,16,16,128]{3,2,1,0:T(8,128)(2,1)S(1)}, u32[]{:S(2)}, u32[]{:S(2)}) %collective-permute-start.7) | collective-permute-done | bytes 262176 | tf_op jit(solution)/shard_map/ppermute | solution.py:23
  60.2 5.4 %collective-permute-start.8 = (bf16[1024,128]{1,0:T(8,128)(2,1)S(1)}, bf16[1024,128]{1,0:T(8,128)(2,1)}, u32[]{:S(2)}, u32[]{:S(2)}) collective-permute-start(bf16[1024,128]{1,0:T(8,128)(2,1)S(1)} %bitcast.136), channel_id=1, source_target_pairs={{0,7},{1,0},{2,1},{3,2},{4,3},{5,4},{6,5},{7,6},{8,15},{9,8},{10,9... | collective-permute-start | bytes 786440 | tf_op jit(solution)/shard_map/ppermute | solution.py:135
  65.6 1.9 %collective-permute-start.11 = (bf16[1024,128]{1,0:T(8,128)(2,1)S(1)}, bf16[1024,128]{1,0:T(8,128)(2,1)}, u32[]{:S(2)}, u32[]{:S(2)}) collective-permute-start(bf16[1024,128]{1,0:T(8,128)(2,1)S(1)} %bitcast.137), channel_id=1, source_target_pairs={{0,1},{1,2},{2,3},{3,4},{4,5},{5,6},{6,7},{7,0},{8,9},{9,10},{10,1... | collective-permute-start | bytes 786440 | tf_op jit(solution)/shard_map/ppermute | solution.py:132
  69.5 2.4 %collective-permute-start.16 = (bf16[4,16,16,128]{3,2,1,0:T(8,128)(2,1)S(1)}, bf16[4,16,16,128]{3,2,1,0:T(8,128)(2,1)}, u32[]{:S(2)}, u32[]{:S(2)}) collective-permute-start(bf16[4,16,16,128]{3,2,1,0:T(8,128)(2,1)S(1)} %convert_element_type.261), channel_id=1, source_target_pairs={{0,8},{8,16},{16,24},{24,32},{32,40},{40,48},{48,56},{56,64},{64,7... | collective-permute-start | bytes 786440 | tf_op jit(solution)/shard_map/ppermute | solution.py:23
  72.0 5.1 %collective-permute-start.9 = (bf16[1024,128]{1,0:T(8,128)(2,1)}, bf16[1024,128]{1,0:T(8,128)(2,1)}, u32[]{:S(2)}, u32[]{:S(2)}) collective-permute-start(bf16[1024,128]{1,0:T(8,128)(2,1)} %collective-permute-done.8), channel_id=1, source_target_pairs={{0,7},{1,0},{2,1},{3,2},{4,3},{5,4},{6,5},{7,6},{8,15},{9,8},{10,9... | collective-permute-start | bytes 786440 | tf_op jit(solution)/shard_map/ppermute | solution.py:135
  77.2 2.1 %collective-permute-start.12 = (bf16[1024,128]{1,0:T(8,128)(2,1)}, bf16[1024,128]{1,0:T(8,128)(2,1)}, u32[]{:S(2)}, u32[]{:S(2)}) collective-permute-start(bf16[1024,128]{1,0:T(8,128)(2,1)} %collective-permute-done.11), channel_id=1, source_target_pairs={{0,1},{1,2},{2,3},{3,4},{4,5},{5,6},{6,7},{7,0},{8,9},{9,10},{10,1... | collective-permute-start | bytes 786440 | tf_op jit(solution)/shard_map/ppermute | solution.py:132
  79.3 1.9 %convolution_bitcast_fusion = f32[4,256,128]{1,2,0:T(8,128)S(1)} fusion(f32[4,256,128]{2,1,0:T(8,128)S(1)} %bitcast.132, s32[256]{0:T(256)S(1)} %get-tuple-element.24, s32[256]{0:T(256)S(1)} %get-tuple-element.25), kind=kOutput, calls=%fused_computation.52 | convolution fusion | flops 408944640 | bytes 1050624 | tf_op jit(solution)/shard_map/pq,zqo->zpo/dot_general | solution.py:59
  83.5 5.3 %collective-permute-start.10 = (bf16[1024,128]{1,0:T(8,128)(2,1)}, bf16[1024,128]{1,0:T(8,128)(2,1)S(1)}, u32[]{:S(2)}, u32[]{:S(2)}) collective-permute-start(bf16[1024,128]{1,0:T(8,128)(2,1)} %collective-permute-done.9), channel_id=1, source_target_pairs={{0,7},{1,0},{2,1},{3,2},{4,3},{5,4},{6,5},{7,6},{8,15},{9,8},{10,9... | collective-permute-start | bytes 786440 | tf_op jit(solution)/shard_map/ppermute | solution.py:135
  91.8 7.6 %collective-permute-done.13 = bf16[1024,128]{1,0:T(8,128)(2,1)S(1)} collective-permute-done((bf16[1024,128]{1,0:T(8,128)(2,1)}, bf16[1024,128]{1,0:T(8,128)(2,1)S(1)}, u32[]{:S(2)}, u32[]{:S(2)}) %collective-permute-start.13) | collective-permute-done | bytes 262176 | tf_op jit(solution)/shard_map/ppermute | solution.py:132
  103.5 5.4 %collective-permute-done.14 = bf16[1024,128]{1,0:T(8,128)(2,1)S(1)} collective-permute-done((bf16[1024,128]{1,0:T(8,128)(2,1)S(1)}, bf16[1024,128]{1,0:T(8,128)(2,1)S(1)}, u32[]{:S(2)}, u32[]{:S(2)}) %collective-permute-start.14) | collective-permute-done | bytes 262176 | tf_op jit(solution)/shard_map/ppermute | solution.py:132
  112.4 2.9 %copy.20 = bf16[1024,1024]{1,0:T(8,128)(2,1)S(1)} copy(bf16[1024,1024]{0,1:T(8,128)(2,1)} %bitcast.131) | data formatting | bytes 4194304 | tf_op jit(solution)/shard_map/dot_general | solution.py:93
  121.8 2.1 %collective-permute-done.17 = f32[2,2,2,2,2,17,256]{6,4,3,2,1,0,5:T(2,128)S(1)} collective-permute-done((f32[2,2,2,2,2,17,256]{6,4,3,2,1,0,5:T(2,128)}, f32[2,2,2,2,2,17,256]{6,4,3,2,1,0,5:T(2,128)S(1)}, u32[]{:S(2)}, u32[]{:S(2)}) %collective-permute-start.17) | collective-permute-done | bytes 557088 | tf_op jit(solution)/shard_map/ppermute | solution.py:121
  127.2 8.7 %collective-permute-done.18 = f32[2,2,2,2,17,256]{5,3,2,1,0,4:T(2,128)S(1)} collective-permute-done((f32[2,2,2,2,17,256]{5,3,2,1,0,4:T(2,128)S(1)}, f32[2,2,2,2,17,256]{5,3,2,1,0,4:T(2,128)S(1)}, u32[]{:S(2)}, u32[]{:S(2)}) %collective-permute-start.18) | collective-permute-done | bytes 278560 | tf_op jit(solution)/shard_map/ppermute | solution.py:121
  136.2 2.4 %collective-permute-start.19 = (f32[2,2,2,17,256]{4,2,1,0,3:T(2,128)S(1)}, f32[2,2,2,17,256]{4,2,1,0,3:T(2,128)S(1)}, u32[]{:S(2)}, u32[]{:S(2)}) collective-permute-start(f32[2,2,2,17,256]{4,2,1,0,3:T(2,128)S(1)} %fusion.118), channel_id=1, source_target_pairs={{0,128},{8,136},{16,144},{24,152},{32,160},{40,168},{48,176},{56,1... | collective-permute-start | bytes 417800 | tf_op jit(solution)/shard_map/ppermute | solution.py:121
  138.7 4.5 %collective-permute-done.19 = f32[2,2,2,17,256]{4,2,1,0,3:T(2,128)S(1)} collective-permute-done((f32[2,2,2,17,256]{4,2,1,0,3:T(2,128)S(1)}, f32[2,2,2,17,256]{4,2,1,0,3:T(2,128)S(1)}, u32[]{:S(2)}, u32[]{:S(2)}) %collective-permute-start.19) | collective-permute-done | bytes 139296 | tf_op jit(solution)/shard_map/ppermute | solution.py:121
  145.4 5.7 %collective-permute-done.20 = f32[2,2,17,256]{3,1,0,2:T(2,128)S(1)} collective-permute-done((f32[2,2,17,256]{3,1,0,2:T(2,128)S(1)}, f32[2,2,17,256]{3,1,0,2:T(2,128)S(1)}, u32[]{:S(2)}, u32[]{:S(2)}) %collective-permute-start.20) | collective-permute-done | bytes 69664 | tf_op jit(solution)/shard_map/ppermute | solution.py:121
  151.3 3.0 %collective-permute-start.21 = (f32[2,17,256]{2,0,1:T(2,128)S(1)}, f32[2,17,256]{2,0,1:T(2,128)S(1)}, u32[]{:S(2)}, u32[]{:S(2)}) collective-permute-start(f32[2,17,256]{2,0,1:T(2,128)S(1)} %fusion.128), channel_id=1, source_target_pairs={{0,256},{8,264},{16,272},{24,280},{32,288},{40,296},{48,304},{56,3... | collective-permute-start | bytes 104456 | tf_op jit(solution)/shard_map/ppermute | solution.py:121
  154.3 4.3 %collective-permute-done.21 = f32[2,17,256]{2,0,1:T(2,128)S(1)} collective-permute-done((f32[2,17,256]{2,0,1:T(2,128)S(1)}, f32[2,17,256]{2,0,1:T(2,128)S(1)}, u32[]{:S(2)}, u32[]{:S(2)}) %collective-permute-start.21) | collective-permute-done | bytes 34848 | tf_op jit(solution)/shard_map/ppermute | solution.py:121
  160.6 7.7 %collective-permute-done.22 = f32[17,256]{1,0:T(8,128)S(1)} collective-permute-done((f32[17,256]{1,0:T(8,128)S(1)}, f32[17,256]{1,0:T(8,128)S(1)}, u32[]{:S(2)}, u32[]{:S(2)}) %collective-permute-start.22) | collective-permute-done | bytes 17440 | tf_op jit(solution)/shard_map/ppermute | solution.py:121
  (91 shorter events, 39.9 us)
Async XLA Ops:
  1.7 16.1 %collective-permute-start = (bf16[4,16,16,128]{3,2,1,0:T(8,128)(2,1)S(1)}, bf16[4,16,16,128]{3,2,1,0:T(8,128)(2,1)S(1)}, u32[]{:S(2)}, u32[]{:S(2)}) collective-permute-start(bf16[4,16,16,128]{3,2,1,0:T(8,128)(2,1)S(1)} %convert_element_type.233), channel_id=1, source_target_pairs={{8,0},{16,8},{24,16},{32,24},{40,32},{48,40},{56,48},{64,56},{72,6... | collective-permute-start | bytes 786440 | tf_op jit(solution)/shard_map/ppermute | solution.py:24
  12.4 9.8 %collective-permute-start.1 = (bf16[4,16,16,128]{3,2,1,0:T(8,128)(2,1)S(1)}, bf16[4,16,16,128]{3,2,1,0:T(8,128)(2,1)S(1)}, u32[]{:S(2)}, u32[]{:S(2)}) collective-permute-start(bf16[4,16,16,128]{3,2,1,0:T(8,128)(2,1)S(1)} %convert_element_type.233), channel_id=1, source_target_pairs={{0,8},{8,16},{16,24},{24,32},{32,40},{40,48},{48,56},{56,64},{64,7... | collective-permute-start | bytes 786440 | tf_op jit(solution)/shard_map/ppermute | solution.py:23
  15.1 7.1 %copy-start.1 = (f32[4,16,16,128]{3,2,1,0:T(8,128)S(1)}, f32[4,16,16,128]{3,2,1,0:T(8,128)}, u32[]{:S(2)}) copy-start(f32[4,16,16,128]{3,2,1,0:T(8,128)} %param.2) | copy-start | bytes 1572868
  15.1 7.2 %copy-start.3 = (f32[4,16,16]{2,1,0:T(8,128)S(1)}, f32[4,16,16]{2,1,0:T(8,128)}, u32[]{:S(2)}) copy-start(f32[4,16,16]{2,1,0:T(8,128)} %param.3) | copy-start | bytes 12292
  22.6 6.5 %collective-permute-start.2 = (bf16[4,16,16,128]{3,2,1,0:T(8,128)(2,1)S(1)}, bf16[4,16,16,128]{3,2,1,0:T(8,128)(2,1)S(1)}, u32[]{:S(2)}, u32[]{:S(2)}) collective-permute-start(bf16[4,16,16,128]{3,2,1,0:T(8,128)(2,1)S(1)} %get-tuple-element.9), channel_id=1, source_target_pairs={{8,0},{16,8},{24,16},{32,24},{40,32},{48,40},{56,48},{64,56},{72,6... | collective-permute-start | bytes 786440 | tf_op jit(solution)/shard_map/ppermute | solution.py:24
  24.6 9.8 %collective-permute-start.3 = (bf16[4,16,16,128]{3,2,1,0:T(8,128)(2,1)S(1)}, bf16[4,16,16,128]{3,2,1,0:T(8,128)(2,1)S(1)}, u32[]{:S(2)}, u32[]{:S(2)}) collective-permute-start(bf16[4,16,16,128]{3,2,1,0:T(8,128)(2,1)S(1)} %get-tuple-element.9), channel_id=1, source_target_pairs={{0,8},{8,16},{16,24},{24,32},{32,40},{40,48},{48,56},{56,64},{64,7... | collective-permute-start | bytes 786440 | tf_op jit(solution)/shard_map/ppermute | solution.py:23
  34.8 6.5 %collective-permute-start.4 = (bf16[4,16,16,128]{3,2,1,0:T(8,128)(2,1)S(1)}, bf16[4,16,16,128]{3,2,1,0:T(8,128)(2,1)S(1)}, u32[]{:S(2)}, u32[]{:S(2)}) collective-permute-start(bf16[4,16,16,128]{3,2,1,0:T(8,128)(2,1)S(1)} %get-tuple-element.7), channel_id=1, source_target_pairs={{8,0},{16,8},{24,16},{32,24},{40,32},{48,40},{56,48},{64,56},{72,6... | collective-permute-start | bytes 786440 | tf_op jit(solution)/shard_map/ppermute | solution.py:24
  36.8 9.8 %collective-permute-start.5 = (bf16[4,16,16,128]{3,2,1,0:T(8,128)(2,1)S(1)}, bf16[4,16,16,128]{3,2,1,0:T(8,128)(2,1)S(1)}, u32[]{:S(2)}, u32[]{:S(2)}) collective-permute-start(bf16[4,16,16,128]{3,2,1,0:T(8,128)(2,1)S(1)} %get-tuple-element.7), channel_id=1, source_target_pairs={{0,8},{8,16},{16,24},{24,32},{32,40},{40,48},{48,56},{56,64},{64,7... | collective-permute-start | bytes 786440 | tf_op jit(solution)/shard_map/ppermute | solution.py:23
  47.7 6.5 %collective-permute-start.6 = (bf16[4,16,16,128]{3,2,1,0:T(8,128)(2,1)}, bf16[4,16,16,128]{3,2,1,0:T(8,128)(2,1)S(1)}, u32[]{:S(2)}, u32[]{:S(2)}) collective-permute-start(bf16[4,16,16,128]{3,2,1,0:T(8,128)(2,1)} %get-tuple-element.5), channel_id=1, source_target_pairs={{8,0},{16,8},{24,16},{32,24},{40,32},{48,40},{56,48},{64,56},{72,6... | collective-permute-start | bytes 786440 | tf_op jit(solution)/shard_map/ppermute | solution.py:24
  49.6 10.0 %collective-permute-start.7 = (bf16[4,16,16,128]{3,2,1,0:T(8,128)(2,1)}, bf16[4,16,16,128]{3,2,1,0:T(8,128)(2,1)S(1)}, u32[]{:S(2)}, u32[]{:S(2)}) collective-permute-start(bf16[4,16,16,128]{3,2,1,0:T(8,128)(2,1)} %get-tuple-element.5), channel_id=1, source_target_pairs={{0,8},{8,16},{16,24},{24,32},{32,40},{40,48},{48,56},{56,64},{64,7... | collective-permute-start | bytes 786440 | tf_op jit(solution)/shard_map/ppermute | solution.py:23
  60.2 11.8 %collective-permute-start.8 = (bf16[1024,128]{1,0:T(8,128)(2,1)S(1)}, bf16[1024,128]{1,0:T(8,128)(2,1)}, u32[]{:S(2)}, u32[]{:S(2)}) collective-permute-start(bf16[1024,128]{1,0:T(8,128)(2,1)S(1)} %bitcast.136), channel_id=1, source_target_pairs={{0,7},{1,0},{2,1},{3,2},{4,3},{5,4},{6,5},{7,6},{8,15},{9,8},{10,9... | collective-permute-start | bytes 786440 | tf_op jit(solution)/shard_map/ppermute | solution.py:135
  65.6 11.6 %collective-permute-start.11 = (bf16[1024,128]{1,0:T(8,128)(2,1)S(1)}, bf16[1024,128]{1,0:T(8,128)(2,1)}, u32[]{:S(2)}, u32[]{:S(2)}) collective-permute-start(bf16[1024,128]{1,0:T(8,128)(2,1)S(1)} %bitcast.137), channel_id=1, source_target_pairs={{0,1},{1,2},{2,3},{3,4},{4,5},{5,6},{6,7},{7,0},{8,9},{9,10},{10,1... | collective-permute-start | bytes 786440 | tf_op jit(solution)/shard_map/ppermute | solution.py:132
  67.6 13.9 %collective-permute-start.15 = (bf16[4,16,16,128]{3,2,1,0:T(8,128)(2,1)S(1)}, bf16[4,16,16,128]{3,2,1,0:T(8,128)(2,1)}, u32[]{:S(2)}, u32[]{:S(2)}) collective-permute-start(bf16[4,16,16,128]{3,2,1,0:T(8,128)(2,1)S(1)} %convert_element_type.261), channel_id=1, source_target_pairs={{8,0},{16,8},{24,16},{32,24},{40,32},{48,40},{56,48},{64,56},{72,6... | collective-permute-start | bytes 786440 | tf_op jit(solution)/shard_map/ppermute | solution.py:24
  69.5 13.0 %collective-permute-start.16 = (bf16[4,16,16,128]{3,2,1,0:T(8,128)(2,1)S(1)}, bf16[4,16,16,128]{3,2,1,0:T(8,128)(2,1)}, u32[]{:S(2)}, u32[]{:S(2)}) collective-permute-start(bf16[4,16,16,128]{3,2,1,0:T(8,128)(2,1)S(1)} %convert_element_type.261), channel_id=1, source_target_pairs={{0,8},{8,16},{16,24},{24,32},{32,40},{40,48},{48,56},{56,64},{64,7... | collective-permute-start | bytes 786440 | tf_op jit(solution)/shard_map/ppermute | solution.py:23
  72.0 11.5 %collective-permute-start.9 = (bf16[1024,128]{1,0:T(8,128)(2,1)}, bf16[1024,128]{1,0:T(8,128)(2,1)}, u32[]{:S(2)}, u32[]{:S(2)}) collective-permute-start(bf16[1024,128]{1,0:T(8,128)(2,1)} %collective-permute-done.8), channel_id=1, source_target_pairs={{0,7},{1,0},{2,1},{3,2},{4,3},{5,4},{6,5},{7,6},{8,15},{9,8},{10,9... | collective-permute-start | bytes 786440 | tf_op jit(solution)/shard_map/ppermute | solution.py:135
  77.2 11.6 %collective-permute-start.12 = (bf16[1024,128]{1,0:T(8,128)(2,1)}, bf16[1024,128]{1,0:T(8,128)(2,1)}, u32[]{:S(2)}, u32[]{:S(2)}) collective-permute-start(bf16[1024,128]{1,0:T(8,128)(2,1)} %collective-permute-done.11), channel_id=1, source_target_pairs={{0,1},{1,2},{2,3},{3,4},{4,5},{5,6},{6,7},{7,0},{8,9},{9,10},{10,1... | collective-permute-start | bytes 786440 | tf_op jit(solution)/shard_map/ppermute | solution.py:132
  83.5 19.9 %collective-permute-start.10 = (bf16[1024,128]{1,0:T(8,128)(2,1)}, bf16[1024,128]{1,0:T(8,128)(2,1)S(1)}, u32[]{:S(2)}, u32[]{:S(2)}) collective-permute-start(bf16[1024,128]{1,0:T(8,128)(2,1)} %collective-permute-done.9), channel_id=1, source_target_pairs={{0,7},{1,0},{2,1},{3,2},{4,3},{5,4},{6,5},{7,6},{8,15},{9,8},{10,9... | collective-permute-start | bytes 786440 | tf_op jit(solution)/shard_map/ppermute | solution.py:135
  88.8 10.6 %collective-permute-start.13 = (bf16[1024,128]{1,0:T(8,128)(2,1)}, bf16[1024,128]{1,0:T(8,128)(2,1)S(1)}, u32[]{:S(2)}, u32[]{:S(2)}) collective-permute-start(bf16[1024,128]{1,0:T(8,128)(2,1)} %collective-permute-done.12), channel_id=1, source_target_pairs={{0,1},{1,2},{2,3},{3,4},{4,5},{5,6},{6,7},{7,0},{8,9},{9,10},{10,1... | collective-permute-start | bytes 786440 | tf_op jit(solution)/shard_map/ppermute | solution.py:132
  99.3 9.5 %collective-permute-start.14 = (bf16[1024,128]{1,0:T(8,128)(2,1)S(1)}, bf16[1024,128]{1,0:T(8,128)(2,1)S(1)}, u32[]{:S(2)}, u32[]{:S(2)}) collective-permute-start(bf16[1024,128]{1,0:T(8,128)(2,1)S(1)} %collective-permute-done.13), channel_id=1, source_target_pairs={{0,1},{1,2},{2,3},{3,4},{4,5},{5,6},{6,7},{7,0},{8,9},{9,10},{10,1... | collective-permute-start | bytes 786440 | tf_op jit(solution)/shard_map/ppermute | solution.py:132
  111.1 1.4 copy-start
  115.3 1.0 copy-start.2
  119.9 4.0 %collective-permute-start.17 = (f32[2,2,2,2,2,17,256]{6,4,3,2,1,0,5:T(2,128)}, f32[2,2,2,2,2,17,256]{6,4,3,2,1,0,5:T(2,128)S(1)}, u32[]{:S(2)}, u32[]{:S(2)}) collective-permute-start(f32[2,2,2,2,2,17,256]{6,4,3,2,1,0,5:T(2,128)} %bitcast.125), channel_id=1, source_target_pairs={{0,8},{8,0},{16,24},{24,16},{32,40},{40,32},{48,56},{56,48},{64,72... | collective-permute-start | bytes 1671176 | tf_op jit(solution)/shard_map/ppermute | solution.py:121
  125.3 10.6 %collective-permute-start.18 = (f32[2,2,2,2,17,256]{5,3,2,1,0,4:T(2,128)S(1)}, f32[2,2,2,2,17,256]{5,3,2,1,0,4:T(2,128)S(1)}, u32[]{:S(2)}, u32[]{:S(2)}) collective-permute-start(f32[2,2,2,2,17,256]{5,3,2,1,0,4:T(2,128)S(1)} %bitcast.148), channel_id=1, source_target_pairs={{0,16},{8,24},{16,0},{24,8},{32,48},{40,56},{48,32},{56,40},{64,80... | collective-permute-start | bytes 835592 | tf_op jit(solution)/shard_map/ppermute | solution.py:121
  136.2 6.9 %collective-permute-start.19 = (f32[2,2,2,17,256]{4,2,1,0,3:T(2,128)S(1)}, f32[2,2,2,17,256]{4,2,1,0,3:T(2,128)S(1)}, u32[]{:S(2)}, u32[]{:S(2)}) collective-permute-start(f32[2,2,2,17,256]{4,2,1,0,3:T(2,128)S(1)} %fusion.118), channel_id=1, source_target_pairs={{0,128},{8,136},{16,144},{24,152},{32,160},{40,168},{48,176},{56,1... | collective-permute-start | bytes 417800 | tf_op jit(solution)/shard_map/ppermute | solution.py:121
  143.5 7.7 %collective-permute-start.20 = (f32[2,2,17,256]{3,1,0,2:T(2,128)S(1)}, f32[2,2,17,256]{3,1,0,2:T(2,128)S(1)}, u32[]{:S(2)}, u32[]{:S(2)}) collective-permute-start(f32[2,2,17,256]{3,1,0,2:T(2,128)S(1)} %bitcast.149), channel_id=1, source_target_pairs={{0,32},{8,40},{16,48},{24,56},{32,0},{40,8},{48,16},{56,24},{64,96... | collective-permute-start | bytes 208904 | tf_op jit(solution)/shard_map/ppermute | solution.py:121
  151.3 7.3 %collective-permute-start.21 = (f32[2,17,256]{2,0,1:T(2,128)S(1)}, f32[2,17,256]{2,0,1:T(2,128)S(1)}, u32[]{:S(2)}, u32[]{:S(2)}) collective-permute-start(f32[2,17,256]{2,0,1:T(2,128)S(1)} %fusion.128), channel_id=1, source_target_pairs={{0,256},{8,264},{16,272},{24,280},{32,288},{40,296},{48,304},{56,3... | collective-permute-start | bytes 104456 | tf_op jit(solution)/shard_map/ppermute | solution.py:121
  158.7 9.6 %collective-permute-start.22 = (f32[17,256]{1,0:T(8,128)S(1)}, f32[17,256]{1,0:T(8,128)S(1)}, u32[]{:S(2)}, u32[]{:S(2)}) collective-permute-start(f32[17,256]{1,0:T(8,128)S(1)} %bitcast.150), channel_id=1, source_target_pairs={{0,64},{8,72},{16,80},{24,88},{32,96},{40,104},{48,112},{56,120},{... | collective-permute-start | bytes 52232 | tf_op jit(solution)/shard_map/ppermute | solution.py:121

commit v4 on v2

--- a/solution.py
+++ b/solution.py
@@ -1,9 +1,10 @@
 import jax
 import jax.numpy as jnp
 from jax import lax
-from jax.sharding import PartitionSpec as P
+from jax.sharding import Mesh, PartitionSpec as P
 
 DEGREE = 4
+GRID = ("chip", "core")
 
 
 STENCIL = (-205.0 / 72.0, 8.0 / 5.0, -1.0 / 5.0, 8.0 / 315.0, -1.0 / 560.0)
@@ -14,14 +15,14 @@
 
 
 def halo_layers(shard, width):
-    size = lax.axis_size("grid")
+    size = lax.axis_size(GRID)
     length = shard.shape[0]
     up = [(i, i + 1) for i in range(size - 1)]
     down = [(j, i) for i, j in up]
     last = lax.slice_in_dim(shard, length - width, length, axis=0).astype(jnp.bfloat16)
     initial = lax.slice_in_dim(shard, 0, width, axis=0).astype(jnp.bfloat16)
-    before = lax.ppermute(last, "grid", up).astype(shard.dtype)
-    after = lax.ppermute(initial, "grid", down).astype(shard.dtype)
+    before = lax.ppermute(last, GRID, up).astype(shard.dtype)
+    after = lax.ppermute(initial, GRID, down).astype(shard.dtype)
     return jnp.concatenate([before, shard, after], axis=0)
 
 
@@ -96,7 +97,14 @@
 
 
 def reduce_scatter_grid(slots):
-    received = lax.all_to_all(slots, "grid", 0, 0, tiled=True)
+    pairs = lax.axis_size("core")
+    mine = lax.axis_index("core")
+    split = slots.reshape((slots.shape[0] // pairs, pairs) + slots.shape[1:])
+    low, high = split[:, 0], split[:, 1]
+    keep = jnp.where(mine == 1, high, low)
+    send = jnp.where(mine == 1, low, high)
+    chip_part = keep + lax.ppermute(send, "core", [(0, 1), (1, 0)])
+    received = lax.all_to_all(chip_part, "chip", 0, 0, tiled=True)
     return jnp.sum(received, axis=0)
 
 
@@ -118,7 +126,7 @@
 def on_device(orbitals, potential):
     own_width = orbitals.shape[3]
     point_count = orbitals.shape[0] * orbitals.shape[1] * orbitals.shape[2]
-    grid_size = lax.axis_size("grid")
+    grid_size = lax.axis_size(GRID)
     point_total = float(point_count * grid_size)
     plane = plane_matrix(orbitals.shape[1], orbitals.shape[2])
     result_block = chebyshev(orbitals, potential, plane)
@@ -164,11 +172,13 @@
 
 
 def solution(mesh):
-    placed = (P("grid", None, None, "orb"), P("grid", None, None))
+    grid_size, orb_size = mesh.devices.shape
+    split_mesh = Mesh(mesh.devices.reshape(grid_size // 2, 2, orb_size), ("chip", "core", "orb"))
+    placed = (P(GRID, None, None, "orb"), P(GRID, None, None))
     return jax.shard_map(
         on_device,
-        mesh=mesh,
+        mesh=split_mesh,
         in_specs=placed,
-        out_specs=(P("grid", None, None, "orb"), P("orb", "grid"), P("orb", "grid")),
+        out_specs=(P(GRID, None, None, "orb"), P("orb", GRID), P("orb", GRID)),
         check_vma=False,
     )

time: 166 us -> 153 us (0.922)
  the two profiles are of different devices: /device:TPU:1 before, /device:TPU:6 now
where the time goes in v4:
time: 153 us; the launch traced here: 150 us
  starting transfers between devices  55.4 us (36%)
  waiting for transfers between devices  35 us (23%)
  blocking collectives  25.1 us (16%)
  other arithmetic  11.8 us (8%)
  matrix products  11.8 us (8%)
  local copies, waits for them, and re-layouts  9.8 us (6%)
    all_to_all x1, blocking collectives, reduce_scatter_grid(): received = lax.all_to_all(chip_part, 'chip', 0, 0, tiled=True)  25.1 us
    ppermute x5, waiting for transfers between devices, halo_layers(): before = lax.ppermute(last, GRID, up).astype(shard.dtype)  20.1 us
    ppermute x5, starting transfers between devices, halo_layers(): after = lax.ppermute(initial, GRID, down).astype(shard.dtype)  18.3 us
    ppermute x3, starting transfers between devices, gather_ring(): from_right = lax.ppermute(from_right, 'orb', left)  15.8 us
    ppermute x4, waiting for transfers between devices, gather_ring(): from_left = lax.ppermute(from_left, 'orb', right)  13 us
    ppermute x5, starting transfers between devices, halo_layers(): before = lax.ppermute(last, GRID, up).astype(shard.dtype)  11.5 us
    dot_general x5, matrix products, apply_hamiltonian(): jnp.einsum('pq,zqo->zpo', plane, flat, precision=lax.Precision.HIGHEST, p...  10.4 us
    ppermute x4, starting transfers between devices, gather_ring(): from_left = lax.ppermute(from_left, 'orb', right)  7.85 us
  transfers between devices with their start and end apart: 18, of which 7 were waited for; matrix products, arithmetic and copies ran while one was open for 12% of the time, Pallas kernels for 0%

profile of v4, /device:TPU:6, one launch (start us, length us, event | category | flops | bytes accessed | tf_op | source)
XLA Modules:
  0.0 150.1 jit_solution(9722870247545308777)
XLA Ops:
  1.7 10.7 %collective-permute-start = (bf16[4,16,16,128]{3,2,1,0:T(8,128)(2,1)S(1)}, bf16[4,16,16,128]{3,2,1,0:T(8,128)(2,1)S(1)}, u32[]{:S(2)}, u32[]{:S(2)}) collective-permute-start(bf16[4,16,16,128]{3,2,1,0:T(8,128)(2,1)S(1)} %convert_element_type.233), channel_id=1, source_target_pairs={{8,0},{16,8},{24,16},{32,24},{40,32},{48,40},{56,48},{64,56},{72,6... | collective-permute-start | bytes 786440 | tf_op jit(solution)/shard_map/ppermute | solution.py:25
  12.4 1.9 %collective-permute-start.1 = (bf16[4,16,16,128]{3,2,1,0:T(8,128)(2,1)S(1)}, bf16[4,16,16,128]{3,2,1,0:T(8,128)(2,1)S(1)}, u32[]{:S(2)}, u32[]{:S(2)}) collective-permute-start(bf16[4,16,16,128]{3,2,1,0:T(8,128)(2,1)S(1)} %convert_element_type.233), channel_id=1, source_target_pairs={{0,8},{8,16},{16,24},{24,32},{32,40},{40,48},{48,56},{56,64},{64,7... | collective-permute-start | bytes 786440 | tf_op jit(solution)/shard_map/ppermute | solution.py:24
  15.1 2.7 %fusion.109 = f32[256,4,128]{2,0,1:T(8,128)S(1)} fusion(f32[4,256,128]{2,1,0:T(8,128)} %bitcast.73, s32[256]{0:T(256)S(1)} %get-tuple-element.15, s32[256]{0:T(256)S(1)} %get-tuple-element.16), kind=kOutput, calls=%fused_computation.184 | convolution fusion | flops 408944640 | bytes 1050624 | tf_op jit(solution)/shard_map/pq,zqo->zpo/dot_general | solution.py:60
  17.9 4.3 %collective-permute-done.1 = bf16[4,16,16,128]{3,2,1,0:T(8,128)(2,1)S(1)} collective-permute-done((bf16[4,16,16,128]{3,2,1,0:T(8,128)(2,1)S(1)}, bf16[4,16,16,128]{3,2,1,0:T(8,128)(2,1)S(1)}, u32[]{:S(2)}, u32[]{:S(2)}) %collective-permute-start.1) | collective-permute-done | bytes 262176 | tf_op jit(solution)/shard_map/ppermute | solution.py:24
  22.6 1.9 %collective-permute-start.2 = (bf16[4,16,16,128]{3,2,1,0:T(8,128)(2,1)S(1)}, bf16[4,16,16,128]{3,2,1,0:T(8,128)(2,1)S(1)}, u32[]{:S(2)}, u32[]{:S(2)}) collective-permute-start(bf16[4,16,16,128]{3,2,1,0:T(8,128)(2,1)S(1)} %get-tuple-element.9), channel_id=1, source_target_pairs={{8,0},{16,8},{24,16},{32,24},{40,32},{48,40},{56,48},{64,56},{72,6... | collective-permute-start | bytes 786440 | tf_op jit(solution)/shard_map/ppermute | solution.py:25
  24.6 2.4 %collective-permute-start.3 = (bf16[4,16,16,128]{3,2,1,0:T(8,128)(2,1)S(1)}, bf16[4,16,16,128]{3,2,1,0:T(8,128)(2,1)S(1)}, u32[]{:S(2)}, u32[]{:S(2)}) collective-permute-start(bf16[4,16,16,128]{3,2,1,0:T(8,128)(2,1)S(1)} %get-tuple-element.9), channel_id=1, source_target_pairs={{0,8},{8,16},{16,24},{24,32},{32,40},{40,48},{48,56},{56,64},{64,7... | collective-permute-start | bytes 786440 | tf_op jit(solution)/shard_map/ppermute | solution.py:24
  27.0 1.9 %convolution_bitcast_fusion.3 = f32[4,256,128]{1,2,0:T(8,128)S(1)} fusion(f32[4,256,128]{2,1,0:T(8,128)S(1)} %bitcast.79, s32[256]{0:T(256)S(1)} %get-tuple-element.15, s32[256]{0:T(256)S(1)} %get-tuple-element.16), kind=kOutput, calls=%fused_computation.55 | convolution fusion | flops 408944640 | bytes 1050624 | tf_op jit(solution)/shard_map/pq,zqo->zpo/dot_general | solution.py:60
  29.2 5.1 %collective-permute-done.3 = bf16[4,16,16,128]{3,2,1,0:T(8,128)(2,1)S(1)} collective-permute-done((bf16[4,16,16,128]{3,2,1,0:T(8,128)(2,1)S(1)}, bf16[4,16,16,128]{3,2,1,0:T(8,128)(2,1)S(1)}, u32[]{:S(2)}, u32[]{:S(2)}) %collective-permute-start.3) | collective-permute-done | bytes 262176 | tf_op jit(solution)/shard_map/ppermute | solution.py:24
  34.8 1.9 %collective-permute-start.4 = (bf16[4,16,16,128]{3,2,1,0:T(8,128)(2,1)S(1)}, bf16[4,16,16,128]{3,2,1,0:T(8,128)(2,1)S(1)}, u32[]{:S(2)}, u32[]{:S(2)}) collective-permute-start(bf16[4,16,16,128]{3,2,1,0:T(8,128)(2,1)S(1)} %get-tuple-element.7), channel_id=1, source_target_pairs={{8,0},{16,8},{24,16},{32,24},{40,32},{48,40},{56,48},{64,56},{72,6... | collective-permute-start | bytes 786440 | tf_op jit(solution)/shard_map/ppermute | solution.py:25
  36.8 2.4 %collective-permute-start.5 = (bf16[4,16,16,128]{3,2,1,0:T(8,128)(2,1)S(1)}, bf16[4,16,16,128]{3,2,1,0:T(8,128)(2,1)S(1)}, u32[]{:S(2)}, u32[]{:S(2)}) collective-permute-start(bf16[4,16,16,128]{3,2,1,0:T(8,128)(2,1)S(1)} %get-tuple-element.7), channel_id=1, source_target_pairs={{0,8},{8,16},{16,24},{24,32},{32,40},{40,48},{48,56},{56,64},{64,7... | collective-permute-start | bytes 786440 | tf_op jit(solution)/shard_map/ppermute | solution.py:24
  39.2 1.9 %convolution_bitcast_fusion.2 = f32[4,256,128]{1,2,0:T(8,128)S(1)} fusion(f32[4,256,128]{2,1,0:T(8,128)S(1)} %bitcast.74, s32[256]{0:T(256)S(1)} %get-tuple-element.15, s32[256]{0:T(256)S(1)} %get-tuple-element.16), kind=kOutput, calls=%fused_computation.54 | convolution fusion | flops 408944640 | bytes 1050624 | tf_op jit(solution)/shard_map/pq,zqo->zpo/dot_general | solution.py:60
  41.4 5.2 %collective-permute-done.5 = bf16[4,16,16,128]{3,2,1,0:T(8,128)(2,1)S(1)} collective-permute-done((bf16[4,16,16,128]{3,2,1,0:T(8,128)(2,1)S(1)}, bf16[4,16,16,128]{3,2,1,0:T(8,128)(2,1)S(1)}, u32[]{:S(2)}, u32[]{:S(2)}) %collective-permute-start.5) | collective-permute-done | bytes 262176 | tf_op jit(solution)/shard_map/ppermute | solution.py:24
  47.7 1.9 %collective-permute-start.6 = (bf16[4,16,16,128]{3,2,1,0:T(8,128)(2,1)}, bf16[4,16,16,128]{3,2,1,0:T(8,128)(2,1)S(1)}, u32[]{:S(2)}, u32[]{:S(2)}) collective-permute-start(bf16[4,16,16,128]{3,2,1,0:T(8,128)(2,1)} %get-tuple-element.5), channel_id=1, source_target_pairs={{8,0},{16,8},{24,16},{32,24},{40,32},{48,40},{56,48},{64,56},{72,6... | collective-permute-start | bytes 786440 | tf_op jit(solution)/shard_map/ppermute | solution.py:25
  49.6 2.4 %collective-permute-start.7 = (bf16[4,16,16,128]{3,2,1,0:T(8,128)(2,1)}, bf16[4,16,16,128]{3,2,1,0:T(8,128)(2,1)S(1)}, u32[]{:S(2)}, u32[]{:S(2)}) collective-permute-start(bf16[4,16,16,128]{3,2,1,0:T(8,128)(2,1)} %get-tuple-element.5), channel_id=1, source_target_pairs={{0,8},{8,16},{16,24},{24,32},{32,40},{40,48},{48,56},{56,64},{64,7... | collective-permute-start | bytes 786440 | tf_op jit(solution)/shard_map/ppermute | solution.py:24
  52.1 1.9 %convolution_bitcast_fusion.1 = f32[4,256,128]{1,2,0:T(8,128)S(1)} fusion(f32[4,256,128]{2,1,0:T(8,128)S(1)} %bitcast.84, s32[256]{0:T(256)S(1)} %get-tuple-element.15, s32[256]{0:T(256)S(1)} %get-tuple-element.16), kind=kOutput, calls=%fused_computation.53 | convolution fusion | flops 408944640 | bytes 1050624 | tf_op jit(solution)/shard_map/pq,zqo->zpo/dot_general | solution.py:60
  54.2 5.4 %collective-permute-done.7 = bf16[4,16,16,128]{3,2,1,0:T(8,128)(2,1)S(1)} collective-permute-done((bf16[4,16,16,128]{3,2,1,0:T(8,128)(2,1)}, bf16[4,16,16,128]{3,2,1,0:T(8,128)(2,1)S(1)}, u32[]{:S(2)}, u32[]{:S(2)}) %collective-permute-start.7) | collective-permute-done | bytes 262176 | tf_op jit(solution)/shard_map/ppermute | solution.py:24
  60.2 5.4 %collective-permute-start.8 = (bf16[1024,128]{1,0:T(8,128)(2,1)S(1)}, bf16[1024,128]{1,0:T(8,128)(2,1)}, u32[]{:S(2)}, u32[]{:S(2)}) collective-permute-start(bf16[1024,128]{1,0:T(8,128)(2,1)S(1)} %bitcast.75), channel_id=1, source_target_pairs={{0,7},{1,0},{2,1},{3,2},{4,3},{5,4},{6,5},{7,6},{8,15},{9,8},{10,9... | collective-permute-start | bytes 786440 | tf_op jit(solution)/shard_map/ppermute | solution.py:121
  65.6 1.9 %collective-permute-start.11 = (bf16[1024,128]{1,0:T(8,128)(2,1)S(1)}, bf16[1024,128]{1,0:T(8,128)(2,1)}, u32[]{:S(2)}, u32[]{:S(2)}) collective-permute-start(bf16[1024,128]{1,0:T(8,128)(2,1)S(1)} %bitcast.76), channel_id=1, source_target_pairs={{0,1},{1,2},{2,3},{3,4},{4,5},{5,6},{6,7},{7,0},{8,9},{9,10},{10,1... | collective-permute-start | bytes 786440 | tf_op jit(solution)/shard_map/ppermute | solution.py:118
  67.6 1.9 %collective-permute-start.15 = (bf16[4,16,16,128]{3,2,1,0:T(8,128)(2,1)S(1)}, bf16[4,16,16,128]{3,2,1,0:T(8,128)(2,1)}, u32[]{:S(2)}, u32[]{:S(2)}) collective-permute-start(bf16[4,16,16,128]{3,2,1,0:T(8,128)(2,1)S(1)} %convert_element_type.261), channel_id=1, source_target_pairs={{8,0},{16,8},{24,16},{32,24},{40,32},{48,40},{56,48},{64,56},{72,6... | collective-permute-start | bytes 786440 | tf_op jit(solution)/shard_map/ppermute | solution.py:25
  69.5 2.4 %collective-permute-start.16 = (bf16[4,16,16,128]{3,2,1,0:T(8,128)(2,1)S(1)}, bf16[4,16,16,128]{3,2,1,0:T(8,128)(2,1)}, u32[]{:S(2)}, u32[]{:S(2)}) collective-permute-start(bf16[4,16,16,128]{3,2,1,0:T(8,128)(2,1)S(1)} %convert_element_type.261), channel_id=1, source_target_pairs={{0,8},{8,16},{16,24},{24,32},{32,40},{40,48},{48,56},{56,64},{64,7... | collective-permute-start | bytes 786440 | tf_op jit(solution)/shard_map/ppermute | solution.py:24
  72.0 5.1 %collective-permute-start.9 = (bf16[1024,128]{1,0:T(8,128)(2,1)}, bf16[1024,128]{1,0:T(8,128)(2,1)}, u32[]{:S(2)}, u32[]{:S(2)}) collective-permute-start(bf16[1024,128]{1,0:T(8,128)(2,1)} %collective-permute-done.8), channel_id=1, source_target_pairs={{0,7},{1,0},{2,1},{3,2},{4,3},{5,4},{6,5},{7,6},{8,15},{9,8},{10,9... | collective-permute-start | bytes 786440 | tf_op jit(solution)/shard_map/ppermute | solution.py:121
  77.2 2.1 %collective-permute-start.12 = (bf16[1024,128]{1,0:T(8,128)(2,1)}, bf16[1024,128]{1,0:T(8,128)(2,1)}, u32[]{:S(2)}, u32[]{:S(2)}) collective-permute-start(bf16[1024,128]{1,0:T(8,128)(2,1)} %collective-permute-done.11), channel_id=1, source_target_pairs={{0,1},{1,2},{2,3},{3,4},{4,5},{5,6},{6,7},{7,0},{8,9},{9,10},{10,1... | collective-permute-start | bytes 786440 | tf_op jit(solution)/shard_map/ppermute | solution.py:118
  79.3 1.9 %convolution_bitcast_fusion = f32[4,256,128]{1,2,0:T(8,128)S(1)} fusion(f32[4,256,128]{2,1,0:T(8,128)S(1)} %bitcast.71, s32[256]{0:T(256)S(1)} %get-tuple-element.15, s32[256]{0:T(256)S(1)} %get-tuple-element.16), kind=kOutput, calls=%fused_computation.52 | convolution fusion | flops 408944640 | bytes 1050624 | tf_op jit(solution)/shard_map/pq,zqo->zpo/dot_general | solution.py:60
  83.5 5.3 %collective-permute-start.10 = (bf16[1024,128]{1,0:T(8,128)(2,1)}, bf16[1024,128]{1,0:T(8,128)(2,1)S(1)}, u32[]{:S(2)}, u32[]{:S(2)}) collective-permute-start(bf16[1024,128]{1,0:T(8,128)(2,1)} %collective-permute-done.9), channel_id=1, source_target_pairs={{0,7},{1,0},{2,1},{3,2},{4,3},{5,4},{6,5},{7,6},{8,15},{9,8},{10,9... | collective-permute-start | bytes 786440 | tf_op jit(solution)/shard_map/ppermute | solution.py:121
  88.8 1.9 %collective-permute-start.13 = (bf16[1024,128]{1,0:T(8,128)(2,1)}, bf16[1024,128]{1,0:T(8,128)(2,1)S(1)}, u32[]{:S(2)}, u32[]{:S(2)}) collective-permute-start(bf16[1024,128]{1,0:T(8,128)(2,1)} %collective-permute-done.12), channel_id=1, source_target_pairs={{0,1},{1,2},{2,3},{3,4},{4,5},{5,6},{6,7},{7,0},{8,9},{9,10},{10,1... | collective-permute-start | bytes 786440 | tf_op jit(solution)/shard_map/ppermute | solution.py:118
  91.8 7.6 %collective-permute-done.13 = bf16[1024,128]{1,0:T(8,128)(2,1)S(1)} collective-permute-done((bf16[1024,128]{1,0:T(8,128)(2,1)}, bf16[1024,128]{1,0:T(8,128)(2,1)S(1)}, u32[]{:S(2)}, u32[]{:S(2)}) %collective-permute-start.13) | collective-permute-done | bytes 262176 | tf_op jit(solution)/shard_map/ppermute | solution.py:118
  99.3 1.9 %collective-permute-start.14 = (bf16[1024,128]{1,0:T(8,128)(2,1)S(1)}, bf16[1024,128]{1,0:T(8,128)(2,1)S(1)}, u32[]{:S(2)}, u32[]{:S(2)}) collective-permute-start(bf16[1024,128]{1,0:T(8,128)(2,1)S(1)} %collective-permute-done.13), channel_id=1, source_target_pairs={{0,1},{1,2},{2,3},{3,4},{4,5},{5,6},{6,7},{7,0},{8,9},{9,10},{10,1... | collective-permute-start | bytes 786440 | tf_op jit(solution)/shard_map/ppermute | solution.py:118
  103.5 5.4 %collective-permute-done.14 = bf16[1024,128]{1,0:T(8,128)(2,1)S(1)} collective-permute-done((bf16[1024,128]{1,0:T(8,128)(2,1)S(1)}, bf16[1024,128]{1,0:T(8,128)(2,1)S(1)}, u32[]{:S(2)}, u32[]{:S(2)}) %collective-permute-start.14) | collective-permute-done | bytes 262176 | tf_op jit(solution)/shard_map/ppermute | solution.py:118
  112.4 2.9 %copy.37 = bf16[1024,1024]{1,0:T(8,128)(2,1)S(1)} copy(bf16[1024,1024]{0,1:T(8,128)(2,1)} %bitcast.70) | data formatting | bytes 4194304 | tf_op jit(solution)/shard_map/dot_general | solution.py:94
  118.8 1.9 %collective-permute-start.17 = (f32[32,17,256]{2,0,1:T(8,128)S(1)}, f32[32,17,256]{2,0,1:T(8,128)S(1)}, u32[]{:S(2)}, u32[]{:S(2)}) collective-permute-start(f32[32,17,256]{2,0,1:T(8,128)S(1)} %bitcast.86), channel_id=1, source_target_pairs={{0,8},{8,0},{1,9},{9,1},{2,10},{10,2},{3,11},{11,3},{4,12},{12,4},... | collective-permute-start | bytes 1671176 | tf_op jit(solution)/shard_map/ppermute | solution.py:106
  120.7 1.9 %collective-permute-done.17 = f32[32,17,256]{2,0,1:T(8,128)S(1)} collective-permute-done((f32[32,17,256]{2,0,1:T(8,128)S(1)}, f32[32,17,256]{2,0,1:T(8,128)S(1)}, u32[]{:S(2)}, u32[]{:S(2)}) %collective-permute-start.17) | collective-permute-done | bytes 557088 | tf_op jit(solution)/shard_map/ppermute | solution.py:106
  123.4 25.1 %all_to_all.5 = f32[32,17,256]{2,1,0:T(8,128)S(1)} all-to-all(f32[32,17,256]{2,1,0:T(8,128)S(1)} %copy.45), channel_id=1, replica_groups=mesh['chip'=32,'core'=2,'orb'=8] {'chip'}, dimensions={0} | all-to-all | bytes 1114112 | tf_op jit(solution)/shard_map/all_to_all | solution.py:107
  (71 shorter events, 20.2 us)
Async XLA Ops:
  1.7 16.1 %collective-permute-start = (bf16[4,16,16,128]{3,2,1,0:T(8,128)(2,1)S(1)}, bf16[4,16,16,128]{3,2,1,0:T(8,128)(2,1)S(1)}, u32[]{:S(2)}, u32[]{:S(2)}) collective-permute-start(bf16[4,16,16,128]{3,2,1,0:T(8,128)(2,1)S(1)} %convert_element_type.233), channel_id=1, source_target_pairs={{8,0},{16,8},{24,16},{32,24},{40,32},{48,40},{56,48},{64,56},{72,6... | collective-permute-start | bytes 786440 | tf_op jit(solution)/shard_map/ppermute | solution.py:25
  12.4 9.8 %collective-permute-start.1 = (bf16[4,16,16,128]{3,2,1,0:T(8,128)(2,1)S(1)}, bf16[4,16,16,128]{3,2,1,0:T(8,128)(2,1)S(1)}, u32[]{:S(2)}, u32[]{:S(2)}) collective-permute-start(bf16[4,16,16,128]{3,2,1,0:T(8,128)(2,1)S(1)} %convert_element_type.233), channel_id=1, source_target_pairs={{0,8},{8,16},{16,24},{24,32},{32,40},{40,48},{48,56},{56,64},{64,7... | collective-permute-start | bytes 786440 | tf_op jit(solution)/shard_map/ppermute | solution.py:24
  15.1 7.1 %copy-start.1 = (f32[4,16,16,128]{3,2,1,0:T(8,128)S(1)}, f32[4,16,16,128]{3,2,1,0:T(8,128)}, u32[]{:S(2)}) copy-start(f32[4,16,16,128]{3,2,1,0:T(8,128)} %param.2) | copy-start | bytes 1572868
  15.1 7.2 %copy-start.3 = (f32[4,16,16]{2,1,0:T(8,128)S(1)}, f32[4,16,16]{2,1,0:T(8,128)}, u32[]{:S(2)}) copy-start(f32[4,16,16]{2,1,0:T(8,128)} %param.3) | copy-start | bytes 12292
  22.6 6.5 %collective-permute-start.2 = (bf16[4,16,16,128]{3,2,1,0:T(8,128)(2,1)S(1)}, bf16[4,16,16,128]{3,2,1,0:T(8,128)(2,1)S(1)}, u32[]{:S(2)}, u32[]{:S(2)}) collective-permute-start(bf16[4,16,16,128]{3,2,1,0:T(8,128)(2,1)S(1)} %get-tuple-element.9), channel_id=1, source_target_pairs={{8,0},{16,8},{24,16},{32,24},{40,32},{48,40},{56,48},{64,56},{72,6... | collective-permute-start | bytes 786440 | tf_op jit(solution)/shard_map/ppermute | solution.py:25
  24.6 9.8 %collective-permute-start.3 = (bf16[4,16,16,128]{3,2,1,0:T(8,128)(2,1)S(1)}, bf16[4,16,16,128]{3,2,1,0:T(8,128)(2,1)S(1)}, u32[]{:S(2)}, u32[]{:S(2)}) collective-permute-start(bf16[4,16,16,128]{3,2,1,0:T(8,128)(2,1)S(1)} %get-tuple-element.9), channel_id=1, source_target_pairs={{0,8},{8,16},{16,24},{24,32},{32,40},{40,48},{48,56},{56,64},{64,7... | collective-permute-start | bytes 786440 | tf_op jit(solution)/shard_map/ppermute | solution.py:24
  34.8 6.5 %collective-permute-start.4 = (bf16[4,16,16,128]{3,2,1,0:T(8,128)(2,1)S(1)}, bf16[4,16,16,128]{3,2,1,0:T(8,128)(2,1)S(1)}, u32[]{:S(2)}, u32[]{:S(2)}) collective-permute-start(bf16[4,16,16,128]{3,2,1,0:T(8,128)(2,1)S(1)} %get-tuple-element.7), channel_id=1, source_target_pairs={{8,0},{16,8},{24,16},{32,24},{40,32},{48,40},{56,48},{64,56},{72,6... | collective-permute-start | bytes 786440 | tf_op jit(solution)/shard_map/ppermute | solution.py:25
  36.8 9.8 %collective-permute-start.5 = (bf16[4,16,16,128]{3,2,1,0:T(8,128)(2,1)S(1)}, bf16[4,16,16,128]{3,2,1,0:T(8,128)(2,1)S(1)}, u32[]{:S(2)}, u32[]{:S(2)}) collective-permute-start(bf16[4,16,16,128]{3,2,1,0:T(8,128)(2,1)S(1)} %get-tuple-element.7), channel_id=1, source_target_pairs={{0,8},{8,16},{16,24},{24,32},{32,40},{40,48},{48,56},{56,64},{64,7... | collective-permute-start | bytes 786440 | tf_op jit(solution)/shard_map/ppermute | solution.py:24
  47.7 6.5 %collective-permute-start.6 = (bf16[4,16,16,128]{3,2,1,0:T(8,128)(2,1)}, bf16[4,16,16,128]{3,2,1,0:T(8,128)(2,1)S(1)}, u32[]{:S(2)}, u32[]{:S(2)}) collective-permute-start(bf16[4,16,16,128]{3,2,1,0:T(8,128)(2,1)} %get-tuple-element.5), channel_id=1, source_target_pairs={{8,0},{16,8},{24,16},{32,24},{40,32},{48,40},{56,48},{64,56},{72,6... | collective-permute-start | bytes 786440 | tf_op jit(solution)/shard_map/ppermute | solution.py:25
  49.6 10.0 %collective-permute-start.7 = (bf16[4,16,16,128]{3,2,1,0:T(8,128)(2,1)}, bf16[4,16,16,128]{3,2,1,0:T(8,128)(2,1)S(1)}, u32[]{:S(2)}, u32[]{:S(2)}) collective-permute-start(bf16[4,16,16,128]{3,2,1,0:T(8,128)(2,1)} %get-tuple-element.5), channel_id=1, source_target_pairs={{0,8},{8,16},{16,24},{24,32},{32,40},{40,48},{48,56},{56,64},{64,7... | collective-permute-start | bytes 786440 | tf_op jit(solution)/shard_map/ppermute | solution.py:24
  60.2 11.8 %collective-permute-start.8 = (bf16[1024,128]{1,0:T(8,128)(2,1)S(1)}, bf16[1024,128]{1,0:T(8,128)(2,1)}, u32[]{:S(2)}, u32[]{:S(2)}) collective-permute-start(bf16[1024,128]{1,0:T(8,128)(2,1)S(1)} %bitcast.75), channel_id=1, source_target_pairs={{0,7},{1,0},{2,1},{3,2},{4,3},{5,4},{6,5},{7,6},{8,15},{9,8},{10,9... | collective-permute-start | bytes 786440 | tf_op jit(solution)/shard_map/ppermute | solution.py:121
  65.6 11.6 %collective-permute-start.11 = (bf16[1024,128]{1,0:T(8,128)(2,1)S(1)}, bf16[1024,128]{1,0:T(8,128)(2,1)}, u32[]{:S(2)}, u32[]{:S(2)}) collective-permute-start(bf16[1024,128]{1,0:T(8,128)(2,1)S(1)} %bitcast.76), channel_id=1, source_target_pairs={{0,1},{1,2},{2,3},{3,4},{4,5},{5,6},{6,7},{7,0},{8,9},{9,10},{10,1... | collective-permute-start | bytes 786440 | tf_op jit(solution)/shard_map/ppermute | solution.py:118
  67.6 13.9 %collective-permute-start.15 = (bf16[4,16,16,128]{3,2,1,0:T(8,128)(2,1)S(1)}, bf16[4,16,16,128]{3,2,1,0:T(8,128)(2,1)}, u32[]{:S(2)}, u32[]{:S(2)}) collective-permute-start(bf16[4,16,16,128]{3,2,1,0:T(8,128)(2,1)S(1)} %convert_element_type.261), channel_id=1, source_target_pairs={{8,0},{16,8},{24,16},{32,24},{40,32},{48,40},{56,48},{64,56},{72,6... | collective-permute-start | bytes 786440 | tf_op jit(solution)/shard_map/ppermute | solution.py:25
  69.5 13.0 %collective-permute-start.16 = (bf16[4,16,16,128]{3,2,1,0:T(8,128)(2,1)S(1)}, bf16[4,16,16,128]{3,2,1,0:T(8,128)(2,1)}, u32[]{:S(2)}, u32[]{:S(2)}) collective-permute-start(bf16[4,16,16,128]{3,2,1,0:T(8,128)(2,1)S(1)} %convert_element_type.261), channel_id=1, source_target_pairs={{0,8},{8,16},{16,24},{24,32},{32,40},{40,48},{48,56},{56,64},{64,7... | collective-permute-start | bytes 786440 | tf_op jit(solution)/shard_map/ppermute | solution.py:24
  72.0 11.5 %collective-permute-start.9 = (bf16[1024,128]{1,0:T(8,128)(2,1)}, bf16[1024,128]{1,0:T(8,128)(2,1)}, u32[]{:S(2)}, u32[]{:S(2)}) collective-permute-start(bf16[1024,128]{1,0:T(8,128)(2,1)} %collective-permute-done.8), channel_id=1, source_target_pairs={{0,7},{1,0},{2,1},{3,2},{4,3},{5,4},{6,5},{7,6},{8,15},{9,8},{10,9... | collective-permute-start | bytes 786440 | tf_op jit(solution)/shard_map/ppermute | solution.py:121
  77.2 11.6 %collective-permute-start.12 = (bf16[1024,128]{1,0:T(8,128)(2,1)}, bf16[1024,128]{1,0:T(8,128)(2,1)}, u32[]{:S(2)}, u32[]{:S(2)}) collective-permute-start(bf16[1024,128]{1,0:T(8,128)(2,1)} %collective-permute-done.11), channel_id=1, source_target_pairs={{0,1},{1,2},{2,3},{3,4},{4,5},{5,6},{6,7},{7,0},{8,9},{9,10},{10,1... | collective-permute-start | bytes 786440 | tf_op jit(solution)/shard_map/ppermute | solution.py:118
  83.5 19.9 %collective-permute-start.10 = (bf16[1024,128]{1,0:T(8,128)(2,1)}, bf16[1024,128]{1,0:T(8,128)(2,1)S(1)}, u32[]{:S(2)}, u32[]{:S(2)}) collective-permute-start(bf16[1024,128]{1,0:T(8,128)(2,1)} %collective-permute-done.9), channel_id=1, source_target_pairs={{0,7},{1,0},{2,1},{3,2},{4,3},{5,4},{6,5},{7,6},{8,15},{9,8},{10,9... | collective-permute-start | bytes 786440 | tf_op jit(solution)/shard_map/ppermute | solution.py:121
  88.8 10.6 %collective-permute-start.13 = (bf16[1024,128]{1,0:T(8,128)(2,1)}, bf16[1024,128]{1,0:T(8,128)(2,1)S(1)}, u32[]{:S(2)}, u32[]{:S(2)}) collective-permute-start(bf16[1024,128]{1,0:T(8,128)(2,1)} %collective-permute-done.12), channel_id=1, source_target_pairs={{0,1},{1,2},{2,3},{3,4},{4,5},{5,6},{6,7},{7,0},{8,9},{9,10},{10,1... | collective-permute-start | bytes 786440 | tf_op jit(solution)/shard_map/ppermute | solution.py:118
  99.3 9.5 %collective-permute-start.14 = (bf16[1024,128]{1,0:T(8,128)(2,1)S(1)}, bf16[1024,128]{1,0:T(8,128)(2,1)S(1)}, u32[]{:S(2)}, u32[]{:S(2)}) collective-permute-start(bf16[1024,128]{1,0:T(8,128)(2,1)S(1)} %collective-permute-done.13), channel_id=1, source_target_pairs={{0,1},{1,2},{2,3},{3,4},{4,5},{5,6},{6,7},{7,0},{8,9},{9,10},{10,1... | collective-permute-start | bytes 786440 | tf_op jit(solution)/shard_map/ppermute | solution.py:118
  111.1 1.3 copy-start
  115.3 1.0 copy-start.2
  118.8 3.9 %collective-permute-start.17 = (f32[32,17,256]{2,0,1:T(8,128)S(1)}, f32[32,17,256]{2,0,1:T(8,128)S(1)}, u32[]{:S(2)}, u32[]{:S(2)}) collective-permute-start(f32[32,17,256]{2,0,1:T(8,128)S(1)} %bitcast.86), channel_id=1, source_target_pairs={{0,8},{8,0},{1,9},{9,1},{2,10},{10,2},{3,11},{11,3},{4,12},{12,4},... | collective-permute-start | bytes 1671176 | tf_op jit(solution)/shard_map/ppermute | solution.py:106

commit v5 on v4

--- a/solution.py
+++ b/solution.py
@@ -4,7 +4,7 @@
 from jax.sharding import Mesh, PartitionSpec as P
 
 DEGREE = 4
-GRID = ("chip", "core")
+GRID = ("x", "z", "core")
 
 
 STENCIL = (-205.0 / 72.0, 8.0 / 5.0, -1.0 / 5.0, 8.0 / 315.0, -1.0 / 560.0)
@@ -104,8 +104,9 @@
     keep = jnp.where(mine == 1, high, low)
     send = jnp.where(mine == 1, low, high)
     chip_part = keep + lax.ppermute(send, "core", [(0, 1), (1, 0)])
-    received = lax.all_to_all(chip_part, "chip", 0, 0, tiled=True)
-    return jnp.sum(received, axis=0)
+    chip_part = chip_part.reshape((lax.axis_size("x"), lax.axis_size("z")) + slots.shape[1:])
+    row_part = jnp.sum(lax.all_to_all(chip_part, "x", 0, 0, tiled=True), axis=0)
+    return jnp.sum(lax.all_to_all(row_part, "z", 0, 0, tiled=True), axis=0)
 
 
 def gather_ring(block):
@@ -120,7 +121,7 @@
         if step <= (size - 1) // 2:
             from_right = lax.ppermute(from_right, "orb", left)
             ahead[step] = from_right
-    return jnp.concatenate([ahead[k] for k in range(size)], axis=1)
+    return [ahead[k] for k in range(size)]
 
 
 def on_device(orbitals, potential):
@@ -137,13 +138,18 @@
         .astype(jnp.bfloat16)
         .reshape(point_count, own_width)
     )
-    orbitals_all = gather_ring(rounded_orbitals)
-    total_width = orbitals_all.shape[1]
+    blocks = gather_ring(rounded_orbitals)
+    total_width = own_width * len(blocks)
     rows = total_width // grid_size
-    hamiltonian_part = contract_points(orbitals_all, rounded_image)
-    margin_part = contract_points(orbitals_all, rounded_orbitals)
-    wide = orbitals_all.astype(jnp.float32)
-    column_squares = jnp.sum(wide * wide, axis=0)
+    hamiltonian_part = jnp.concatenate(
+        [contract_points(block, rounded_image) for block in blocks], axis=0
+    )
+    margin_part = jnp.concatenate(
+        [contract_points(block, rounded_orbitals) for block in blocks], axis=0
+    )
+    column_squares = jnp.concatenate(
+        [jnp.sum(jnp.square(block.astype(jnp.float32)), axis=0) for block in blocks], axis=0
+    )
     body = jnp.concatenate(
         [
             hamiltonian_part.reshape(grid_size, rows, own_width),
@@ -173,7 +179,10 @@
 
 def solution(mesh):
     grid_size, orb_size = mesh.devices.shape
-    split_mesh = Mesh(mesh.devices.reshape(grid_size // 2, 2, orb_size), ("chip", "core", "orb"))
+    z_size = min(8, grid_size // 2)
+    split_mesh = Mesh(
+        mesh.devices.reshape(grid_size // (2 * z_size), z_size, 2, orb_size), ("x", "z", "core", "orb")
+    )
     placed = (P(GRID, None, None, "orb"), P(GRID, None, None))
     return jax.shard_map(
         on_device,

time: 153 us -> 153 us (level)
  local copies, waits for them, and re-layouts: 9.8 us -> 4.54 us
  starting transfers between devices: 55.4 us -> 59.1 us
  waiting for transfers between devices: 35 us -> 37.9 us
  matrix products: 11.8 us -> 14.6 us
  other arithmetic: 11.8 us -> 9.02 us
    ppermute x5, starting transfers between devices: 18.3 us -> 22.6 us  [halo_layers(): after = lax.ppermute(initial, GRID, down).astype(shard.dtype)]
    unnamed x16 -> x14, local copies, waits for them, and re-layouts: 4.42 us -> 0.86 us
    dot_general x1 -> x0, local copies, waits for them, and re-layouts: 2.85 us -> none  [contract_points(): lax.dot_general(left_side, right_side, (((0,), (0,)), ((), ())), preferre...]
    dot_general x2 -> x16, matrix products: 1.4 us -> 4.25 us  [contract_points(): lax.dot_general(left_side, right_side, (((0,), (0,)), ((), ())), preferre...]
    ppermute x3, waiting for transfers between devices: 0.01 us -> 2.09 us  [gather_ring(): from_right = lax.ppermute(from_right, 'orb', left)]
    reshape x1 -> x4, local copies, waits for them, and re-layouts: 0.07 us -> 2.08 us  [the longest x1 1.21 us: on_device(): hamiltonian_part.reshape(grid_size, rows, own_width)]
    all_to_all x1 -> x2, blocking collectives: 25.1 us -> 24.7 us  [the longest x1 12.4 us: reduce_scatter_grid(): row_part = jnp.sum(lax.all_to_all(chip_part, 'x', 0, 0, tiled=True), axis=0)]
  transfers between devices with their start and end apart: 18 -> 18, of which waited for: 7 -> 9; matrix products, arithmetic and copies ran while one was open for 12% -> 11% of each run, Pallas kernels for 0% -> 0%
where the time goes in v5:
time: 153 us; the launch traced here: 151 us
  starting transfers between devices  59.1 us (39%)
  waiting for transfers between devices  37.9 us (25%)
  blocking collectives  24.7 us (16%)
  matrix products  14.6 us (10%)
  other arithmetic  9.02 us (6%)
  local copies, waits for them, and re-layouts  4.54 us (3%)
    ppermute x5, starting transfers between devices, halo_layers(): after = lax.ppermute(initial, GRID, down).astype(shard.dtype)  22.6 us
    ppermute x5, waiting for transfers between devices, halo_layers(): before = lax.ppermute(last, GRID, up).astype(shard.dtype)  20.3 us
    ppermute x3, starting transfers between devices, gather_ring(): from_right = lax.ppermute(from_right, 'orb', left)  16.1 us
    ppermute x4, waiting for transfers between devices, gather_ring(): from_left = lax.ppermute(from_left, 'orb', right)  13.6 us
    all_to_all x1, blocking collectives, reduce_scatter_grid(): row_part = jnp.sum(lax.all_to_all(chip_part, 'x', 0, 0, tiled=True), axis=0)  12.4 us
    all_to_all x1, blocking collectives, reduce_scatter_grid(): return jnp.sum(lax.all_to_all(row_part, 'z', 0, 0, tiled=True), axis=0)  12.3 us
    ppermute x5, starting transfers between devices, halo_layers(): before = lax.ppermute(last, GRID, up).astype(shard.dtype)  10.6 us
    dot_general x5, matrix products, apply_hamiltonian(): jnp.einsum('pq,zqo->zpo', plane, flat, precision=lax.Precision.HIGHEST, p...  10.4 us
  transfers between devices with their start and end apart: 18, of which 9 were waited for; matrix products, arithmetic and copies ran while one was open for 11% of the time, Pallas kernels for 0%

profile of v5, /device:TPU:6, one launch (start us, length us, event | category | flops | bytes accessed | tf_op | source)
XLA Modules:
  0.0 151.2 jit_solution(14075371616929427996)
XLA Ops:
  1.7 10.7 %collective-permute-start = (bf16[4,16,16,128]{3,2,1,0:T(8,128)(2,1)S(1)}, bf16[4,16,16,128]{3,2,1,0:T(8,128)(2,1)S(1)}, u32[]{:S(2)}, u32[]{:S(2)}) collective-permute-start(bf16[4,16,16,128]{3,2,1,0:T(8,128)(2,1)S(1)} %convert_element_type.255), channel_id=1, source_target_pairs={{8,0},{16,8},{24,16},{32,24},{40,32},{48,40},{56,48},{64,56},{72,6... | collective-permute-start | bytes 786440 | tf_op jit(solution)/shard_map/ppermute | solution.py:25
  12.4 1.9 %collective-permute-start.1 = (bf16[4,16,16,128]{3,2,1,0:T(8,128)(2,1)S(1)}, bf16[4,16,16,128]{3,2,1,0:T(8,128)(2,1)S(1)}, u32[]{:S(2)}, u32[]{:S(2)}) collective-permute-start(bf16[4,16,16,128]{3,2,1,0:T(8,128)(2,1)S(1)} %convert_element_type.255), channel_id=1, source_target_pairs={{0,8},{8,16},{16,24},{24,32},{32,40},{40,48},{48,56},{56,64},{64,7... | collective-permute-start | bytes 786440 | tf_op jit(solution)/shard_map/ppermute | solution.py:24
  15.2 2.7 %fusion.112 = f32[256,4,128]{2,0,1:T(8,128)S(1)} fusion(f32[4,256,128]{2,1,0:T(8,128)} %bitcast.128, s32[256]{0:T(256)S(1)} %get-tuple-element.18, s32[256]{0:T(256)S(1)} %get-tuple-element.19), kind=kOutput, calls=%fused_computation.210 | convolution fusion | flops 408944640 | bytes 1050624 | tf_op jit(solution)/shard_map/pq,zqo->zpo/dot_general | solution.py:60
  17.9 4.3 %collective-permute-done.1 = bf16[4,16,16,128]{3,2,1,0:T(8,128)(2,1)S(1)} collective-permute-done((bf16[4,16,16,128]{3,2,1,0:T(8,128)(2,1)S(1)}, bf16[4,16,16,128]{3,2,1,0:T(8,128)(2,1)S(1)}, u32[]{:S(2)}, u32[]{:S(2)}) %collective-permute-start.1) | collective-permute-done | bytes 262176 | tf_op jit(solution)/shard_map/ppermute | solution.py:24
  22.6 2.4 %collective-permute-start.2 = (bf16[4,16,16,128]{3,2,1,0:T(8,128)(2,1)S(1)}, bf16[4,16,16,128]{3,2,1,0:T(8,128)(2,1)S(1)}, u32[]{:S(2)}, u32[]{:S(2)}) collective-permute-start(bf16[4,16,16,128]{3,2,1,0:T(8,128)(2,1)S(1)} %get-tuple-element.11), channel_id=1, source_target_pairs={{8,0},{16,8},{24,16},{32,24},{40,32},{48,40},{56,48},{64,56},{72,6... | collective-permute-start | bytes 786440 | tf_op jit(solution)/shard_map/ppermute | solution.py:25
  25.0 1.9 %collective-permute-start.3 = (bf16[4,16,16,128]{3,2,1,0:T(8,128)(2,1)S(1)}, bf16[4,16,16,128]{3,2,1,0:T(8,128)(2,1)S(1)}, u32[]{:S(2)}, u32[]{:S(2)}) collective-permute-start(bf16[4,16,16,128]{3,2,1,0:T(8,128)(2,1)S(1)} %get-tuple-element.11), channel_id=1, source_target_pairs={{0,8},{8,16},{16,24},{24,32},{32,40},{40,48},{48,56},{56,64},{64,7... | collective-permute-start | bytes 786440 | tf_op jit(solution)/shard_map/ppermute | solution.py:24
  27.0 1.9 %convolution_bitcast_fusion.3 = f32[4,256,128]{1,2,0:T(8,128)S(1)} fusion(f32[4,256,128]{2,1,0:T(8,128)S(1)} %bitcast.130, s32[256]{0:T(256)S(1)} %get-tuple-element.18, s32[256]{0:T(256)S(1)} %get-tuple-element.19), kind=kOutput, calls=%fused_computation.49 | convolution fusion | flops 408944640 | bytes 1050624 | tf_op jit(solution)/shard_map/pq,zqo->zpo/dot_general | solution.py:60
  29.2 5.6 %collective-permute-done.3 = bf16[4,16,16,128]{3,2,1,0:T(8,128)(2,1)S(1)} collective-permute-done((bf16[4,16,16,128]{3,2,1,0:T(8,128)(2,1)S(1)}, bf16[4,16,16,128]{3,2,1,0:T(8,128)(2,1)S(1)}, u32[]{:S(2)}, u32[]{:S(2)}) %collective-permute-start.3) | collective-permute-done | bytes 262176 | tf_op jit(solution)/shard_map/ppermute | solution.py:24
  35.3 1.9 %collective-permute-start.4 = (bf16[4,16,16,128]{3,2,1,0:T(8,128)(2,1)S(1)}, bf16[4,16,16,128]{3,2,1,0:T(8,128)(2,1)S(1)}, u32[]{:S(2)}, u32[]{:S(2)}) collective-permute-start(bf16[4,16,16,128]{3,2,1,0:T(8,128)(2,1)S(1)} %get-tuple-element.9), channel_id=1, source_target_pairs={{8,0},{16,8},{24,16},{32,24},{40,32},{48,40},{56,48},{64,56},{72,6... | collective-permute-start | bytes 786440 | tf_op jit(solution)/shard_map/ppermute | solution.py:25
  37.2 2.4 %collective-permute-start.5 = (bf16[4,16,16,128]{3,2,1,0:T(8,128)(2,1)S(1)}, bf16[4,16,16,128]{3,2,1,0:T(8,128)(2,1)S(1)}, u32[]{:S(2)}, u32[]{:S(2)}) collective-permute-start(bf16[4,16,16,128]{3,2,1,0:T(8,128)(2,1)S(1)} %get-tuple-element.9), channel_id=1, source_target_pairs={{0,8},{8,16},{16,24},{24,32},{32,40},{40,48},{48,56},{56,64},{64,7... | collective-permute-start | bytes 786440 | tf_op jit(solution)/shard_map/ppermute | solution.py:24
  39.7 1.9 %convolution_bitcast_fusion.2 = f32[4,256,128]{1,2,0:T(8,128)S(1)} fusion(f32[4,256,128]{2,1,0:T(8,128)S(1)} %bitcast.129, s32[256]{0:T(256)S(1)} %get-tuple-element.18, s32[256]{0:T(256)S(1)} %get-tuple-element.19), kind=kOutput, calls=%fused_computation.48 | convolution fusion | flops 408944640 | bytes 1050624 | tf_op jit(solution)/shard_map/pq,zqo->zpo/dot_general | solution.py:60
  41.8 5.2 %collective-permute-done.5 = bf16[4,16,16,128]{3,2,1,0:T(8,128)(2,1)S(1)} collective-permute-done((bf16[4,16,16,128]{3,2,1,0:T(8,128)(2,1)S(1)}, bf16[4,16,16,128]{3,2,1,0:T(8,128)(2,1)S(1)}, u32[]{:S(2)}, u32[]{:S(2)}) %collective-permute-start.5) | collective-permute-done | bytes 262176 | tf_op jit(solution)/shard_map/ppermute | solution.py:24
  47.5 1.9 %collective-permute-start.6 = (bf16[4,16,16,128]{3,2,1,0:T(8,128)(2,1)S(1)}, bf16[4,16,16,128]{3,2,1,0:T(8,128)(2,1)S(1)}, u32[]{:S(2)}, u32[]{:S(2)}) collective-permute-start(bf16[4,16,16,128]{3,2,1,0:T(8,128)(2,1)S(1)} %get-tuple-element.7), channel_id=1, source_target_pairs={{8,0},{16,8},{24,16},{32,24},{40,32},{48,40},{56,48},{64,56},{72,6... | collective-permute-start | bytes 786440 | tf_op jit(solution)/shard_map/ppermute | solution.py:25
  49.4 2.4 %collective-permute-start.7 = (bf16[4,16,16,128]{3,2,1,0:T(8,128)(2,1)S(1)}, bf16[4,16,16,128]{3,2,1,0:T(8,128)(2,1)S(1)}, u32[]{:S(2)}, u32[]{:S(2)}) collective-permute-start(bf16[4,16,16,128]{3,2,1,0:T(8,128)(2,1)S(1)} %get-tuple-element.7), channel_id=1, source_target_pairs={{0,8},{8,16},{16,24},{24,32},{32,40},{40,48},{48,56},{56,64},{64,7... | collective-permute-start | bytes 786440 | tf_op jit(solution)/shard_map/ppermute | solution.py:24
  51.8 1.9 %convolution_bitcast_fusion.1 = f32[4,256,128]{1,2,0:T(8,128)S(1)} fusion(f32[4,256,128]{2,1,0:T(8,128)S(1)} %bitcast.135, s32[256]{0:T(256)S(1)} %get-tuple-element.18, s32[256]{0:T(256)S(1)} %get-tuple-element.19), kind=kOutput, calls=%fused_computation.47 | convolution fusion | flops 408944640 | bytes 1050624 | tf_op jit(solution)/shard_map/pq,zqo->zpo/dot_general | solution.py:60
  54.0 5.2 %collective-permute-done.7 = bf16[4,16,16,128]{3,2,1,0:T(8,128)(2,1)S(1)} collective-permute-done((bf16[4,16,16,128]{3,2,1,0:T(8,128)(2,1)S(1)}, bf16[4,16,16,128]{3,2,1,0:T(8,128)(2,1)S(1)}, u32[]{:S(2)}, u32[]{:S(2)}) %collective-permute-start.7) | collective-permute-done | bytes 262176 | tf_op jit(solution)/shard_map/ppermute | solution.py:24
  59.9 1.9 %collective-permute-start.9 = (bf16[4,16,16,128]{3,2,1,0:T(8,128)(2,1)S(1)}, bf16[4,16,16,128]{3,2,1,0:T(8,128)(2,1)S(1)}, u32[]{:S(2)}, u32[]{:S(2)}) collective-permute-start(bf16[4,16,16,128]{3,2,1,0:T(8,128)(2,1)S(1)} %get-tuple-element.6), channel_id=1, source_target_pairs={{0,8},{8,16},{16,24},{24,32},{32,40},{40,48},{48,56},{56,64},{64,7... | collective-permute-start | bytes 786440 | tf_op jit(solution)/shard_map/ppermute | solution.py:24
  61.8 5.8 %collective-permute-start.8 = (bf16[4,16,16,128]{3,2,1,0:T(8,128)(2,1)S(1)}, bf16[4,16,16,128]{3,2,1,0:T(8,128)(2,1)S(1)}, u32[]{:S(2)}, u32[]{:S(2)}) collective-permute-start(bf16[4,16,16,128]{3,2,1,0:T(8,128)(2,1)S(1)} %get-tuple-element.6), channel_id=1, source_target_pairs={{8,0},{16,8},{24,16},{32,24},{40,32},{48,40},{56,48},{64,56},{72,6... | collective-permute-start | bytes 786440 | tf_op jit(solution)/shard_map/ppermute | solution.py:25
  67.6 5.4 %collective-permute-start.10 = (bf16[1024,128]{1,0:T(8,128)(2,1)S(1)}, bf16[1024,128]{1,0:T(8,128)(2,1)S(1)}, u32[]{:S(2)}, u32[]{:S(2)}) collective-permute-start(bf16[1024,128]{1,0:T(8,128)(2,1)S(1)} %bitcast.118), channel_id=1, source_target_pairs={{0,7},{1,0},{2,1},{3,2},{4,3},{5,4},{6,5},{7,6},{8,15},{9,8},{10,9... | collective-permute-start | bytes 786440 | tf_op jit(solution)/shard_map/ppermute | solution.py:122
  72.9 2.1 %collective-permute-start.13 = (bf16[1024,128]{1,0:T(8,128)(2,1)S(1)}, bf16[1024,128]{1,0:T(8,128)(2,1)S(1)}, u32[]{:S(2)}, u32[]{:S(2)}) collective-permute-start(bf16[1024,128]{1,0:T(8,128)(2,1)S(1)} %bitcast.119), channel_id=1, source_target_pairs={{0,1},{1,2},{2,3},{3,4},{4,5},{5,6},{6,7},{7,0},{8,9},{9,10},{10,1... | collective-permute-start | bytes 786440 | tf_op jit(solution)/shard_map/ppermute | solution.py:119
  75.1 1.9 %convolution_bitcast_fusion = f32[4,256,128]{1,2,0:T(8,128)S(1)} fusion(f32[4,256,128]{2,1,0:T(8,128)S(1)} %bitcast.127, s32[256]{0:T(256)S(1)} %get-tuple-element.18, s32[256]{0:T(256)S(1)} %get-tuple-element.19), kind=kOutput, calls=%fused_computation.46 | convolution fusion | flops 408944640 | bytes 1050624 | tf_op jit(solution)/shard_map/pq,zqo->zpo/dot_general | solution.py:60
  78.6 5.1 %collective-permute-start.11 = (bf16[1024,128]{1,0:T(8,128)(2,1)S(1)}, bf16[1024,128]{1,0:T(8,128)(2,1)S(1)}, u32[]{:S(2)}, u32[]{:S(2)}) collective-permute-start(bf16[1024,128]{1,0:T(8,128)(2,1)S(1)} %collective-permute-done.10), channel_id=1, source_target_pairs={{0,7},{1,0},{2,1},{3,2},{4,3},{5,4},{6,5},{7,6},{8,15},{9,8},{10,9... | collective-permute-start | bytes 786440 | tf_op jit(solution)/shard_map/ppermute | solution.py:122
  84.2 1.9 %collective-permute-start.14 = (bf16[1024,128]{1,0:T(8,128)(2,1)S(1)}, bf16[1024,128]{1,0:T(8,128)(2,1)S(1)}, u32[]{:S(2)}, u32[]{:S(2)}) collective-permute-start(bf16[1024,128]{1,0:T(8,128)(2,1)S(1)} %collective-permute-done.13), channel_id=1, source_target_pairs={{0,1},{1,2},{2,3},{3,4},{4,5},{5,6},{6,7},{7,0},{8,9},{9,10},{10,1... | collective-permute-start | bytes 786440 | tf_op jit(solution)/shard_map/ppermute | solution.py:119
  87.6 5.6 %collective-permute-start.12 = (bf16[1024,128]{1,0:T(8,128)(2,1)S(1)}, bf16[1024,128]{1,0:T(8,128)(2,1)S(1)}, u32[]{:S(2)}, u32[]{:S(2)}) collective-permute-start(bf16[1024,128]{1,0:T(8,128)(2,1)S(1)} %collective-permute-done.11), channel_id=1, source_target_pairs={{0,7},{1,0},{2,1},{3,2},{4,3},{5,4},{6,5},{7,6},{8,15},{9,8},{10,9... | collective-permute-start | bytes 786440 | tf_op jit(solution)/shard_map/ppermute | solution.py:122
  93.9 1.9 %collective-permute-start.15 = (bf16[1024,128]{1,0:T(8,128)(2,1)S(1)}, bf16[1024,128]{1,0:T(8,128)(2,1)S(1)}, u32[]{:S(2)}, u32[]{:S(2)}) collective-permute-start(bf16[1024,128]{1,0:T(8,128)(2,1)S(1)} %collective-permute-done.14), channel_id=1, source_target_pairs={{0,1},{1,2},{2,3},{3,4},{4,5},{5,6},{6,7},{7,0},{8,9},{9,10},{10,1... | collective-permute-start | bytes 786440 | tf_op jit(solution)/shard_map/ppermute | solution.py:119
  97.3 6.9 %collective-permute-done.15 = bf16[1024,128]{1,0:T(8,128)(2,1)S(1)} collective-permute-done((bf16[1024,128]{1,0:T(8,128)(2,1)S(1)}, bf16[1024,128]{1,0:T(8,128)(2,1)S(1)}, u32[]{:S(2)}, u32[]{:S(2)}) %collective-permute-start.15) | collective-permute-done | bytes 262176 | tf_op jit(solution)/shard_map/ppermute | solution.py:119
  104.1 1.9 %collective-permute-start.16 = (bf16[1024,128]{1,0:T(8,128)(2,1)S(1)}, bf16[1024,128]{1,0:T(8,128)(2,1)S(1)}, u32[]{:S(2)}, u32[]{:S(2)}) collective-permute-start(bf16[1024,128]{1,0:T(8,128)(2,1)S(1)} %collective-permute-done.15), channel_id=1, source_target_pairs={{0,1},{1,2},{2,3},{3,4},{4,5},{5,6},{6,7},{7,0},{8,9},{9,10},{10,1... | collective-permute-start | bytes 786440 | tf_op jit(solution)/shard_map/ppermute | solution.py:119
  106.9 6.8 %collective-permute-done.16 = bf16[1024,128]{1,0:T(8,128)(2,1)S(1)} collective-permute-done((bf16[1024,128]{1,0:T(8,128)(2,1)S(1)}, bf16[1024,128]{1,0:T(8,128)(2,1)S(1)}, u32[]{:S(2)}, u32[]{:S(2)}) %collective-permute-start.16) | collective-permute-done | bytes 262176 | tf_op jit(solution)/shard_map/ppermute | solution.py:119
  120.7 1.9 %collective-permute-start.17 = (f32[32,17,256]{2,0,1:T(8,128)S(1)}, f32[32,17,256]{2,0,1:T(8,128)S(1)}, u32[]{:S(2)}, u32[]{:S(2)}) collective-permute-start(f32[32,17,256]{2,0,1:T(8,128)S(1)} %bitcast.136), channel_id=1, source_target_pairs={{0,8},{8,0},{1,9},{9,1},{2,10},{10,2},{3,11},{11,3},{4,12},{12,4},... | collective-permute-start | bytes 1671176 | tf_op jit(solution)/shard_map/ppermute | solution.py:106
  122.6 1.9 %collective-permute-done.17 = f32[32,17,256]{2,0,1:T(8,128)S(1)} collective-permute-done((f32[32,17,256]{2,0,1:T(8,128)S(1)}, f32[32,17,256]{2,0,1:T(8,128)S(1)}, u32[]{:S(2)}, u32[]{:S(2)}) %collective-permute-start.17) | collective-permute-done | bytes 557088 | tf_op jit(solution)/shard_map/ppermute | solution.py:106
  124.7 12.4 %all_to_all.10 = f32[4,8,17,256]{3,1,2,0:T(8,128)S(1)} all-to-all(f32[4,8,17,256]{3,1,2,0:T(8,128)S(1)} %copy.95), channel_id=1, replica_groups=mesh['x'=4,'z'=8,'core'=2,'orb'=8] {'x'}, dimensions={0} | all-to-all | bytes 1114112 | tf_op jit(solution)/shard_map/all_to_all | solution.py:108
  137.2 12.3 %all_to_all.11 = f32[8,17,256]{2,1,0:T(8,128)S(1)} all-to-all(f32[8,17,256]{2,1,0:T(8,128)S(1)} %copy.97), channel_id=1, replica_groups=mesh['x'=4,'z'=8,'core'=2,'orb'=8] {'z'}, dimensions={0} | all-to-all | bytes 278528 | tf_op jit(solution)/shard_map/all_to_all | solution.py:109
  (99 shorter events, 19.9 us)
Async XLA Ops:
  1.7 16.1 %collective-permute-start = (bf16[4,16,16,128]{3,2,1,0:T(8,128)(2,1)S(1)}, bf16[4,16,16,128]{3,2,1,0:T(8,128)(2,1)S(1)}, u32[]{:S(2)}, u32[]{:S(2)}) collective-permute-start(bf16[4,16,16,128]{3,2,1,0:T(8,128)(2,1)S(1)} %convert_element_type.255), channel_id=1, source_target_pairs={{8,0},{16,8},{24,16},{32,24},{40,32},{48,40},{56,48},{64,56},{72,6... | collective-permute-start | bytes 786440 | tf_op jit(solution)/shard_map/ppermute | solution.py:25
  12.4 9.8 %collective-permute-start.1 = (bf16[4,16,16,128]{3,2,1,0:T(8,128)(2,1)S(1)}, bf16[4,16,16,128]{3,2,1,0:T(8,128)(2,1)S(1)}, u32[]{:S(2)}, u32[]{:S(2)}) collective-permute-start(bf16[4,16,16,128]{3,2,1,0:T(8,128)(2,1)S(1)} %convert_element_type.255), channel_id=1, source_target_pairs={{0,8},{8,16},{16,24},{24,32},{32,40},{40,48},{48,56},{56,64},{64,7... | collective-permute-start | bytes 786440 | tf_op jit(solution)/shard_map/ppermute | solution.py:24
  17.8 4.4 %copy-start = (f32[4,16,16,128]{3,2,1,0:T(8,128)S(1)}, f32[4,16,16,128]{3,2,1,0:T(8,128)}, u32[]{:S(2)}) copy-start(f32[4,16,16,128]{3,2,1,0:T(8,128)} %param.2) | copy-start | bytes 1572868
  17.8 4.4 %copy-start.1 = (f32[4,16,16]{2,1,0:T(8,128)S(1)}, f32[4,16,16]{2,1,0:T(8,128)}, u32[]{:S(2)}) copy-start(f32[4,16,16]{2,1,0:T(8,128)} %param.3) | copy-start | bytes 12292
  22.6 6.5 %collective-permute-start.2 = (bf16[4,16,16,128]{3,2,1,0:T(8,128)(2,1)S(1)}, bf16[4,16,16,128]{3,2,1,0:T(8,128)(2,1)S(1)}, u32[]{:S(2)}, u32[]{:S(2)}) collective-permute-start(bf16[4,16,16,128]{3,2,1,0:T(8,128)(2,1)S(1)} %get-tuple-element.11), channel_id=1, source_target_pairs={{8,0},{16,8},{24,16},{32,24},{40,32},{48,40},{56,48},{64,56},{72,6... | collective-permute-start | bytes 786440 | tf_op jit(solution)/shard_map/ppermute | solution.py:25
  25.0 9.8 %collective-permute-start.3 = (bf16[4,16,16,128]{3,2,1,0:T(8,128)(2,1)S(1)}, bf16[4,16,16,128]{3,2,1,0:T(8,128)(2,1)S(1)}, u32[]{:S(2)}, u32[]{:S(2)}) collective-permute-start(bf16[4,16,16,128]{3,2,1,0:T(8,128)(2,1)S(1)} %get-tuple-element.11), channel_id=1, source_target_pairs={{0,8},{8,16},{16,24},{24,32},{32,40},{40,48},{48,56},{56,64},{64,7... | collective-permute-start | bytes 786440 | tf_op jit(solution)/shard_map/ppermute | solution.py:24
  35.3 6.5 %collective-permute-start.4 = (bf16[4,16,16,128]{3,2,1,0:T(8,128)(2,1)S(1)}, bf16[4,16,16,128]{3,2,1,0:T(8,128)(2,1)S(1)}, u32[]{:S(2)}, u32[]{:S(2)}) collective-permute-start(bf16[4,16,16,128]{3,2,1,0:T(8,128)(2,1)S(1)} %get-tuple-element.9), channel_id=1, source_target_pairs={{8,0},{16,8},{24,16},{32,24},{40,32},{48,40},{56,48},{64,56},{72,6... | collective-permute-start | bytes 786440 | tf_op jit(solution)/shard_map/ppermute | solution.py:25
  37.2 9.8 %collective-permute-start.5 = (bf16[4,16,16,128]{3,2,1,0:T(8,128)(2,1)S(1)}, bf16[4,16,16,128]{3,2,1,0:T(8,128)(2,1)S(1)}, u32[]{:S(2)}, u32[]{:S(2)}) collective-permute-start(bf16[4,16,16,128]{3,2,1,0:T(8,128)(2,1)S(1)} %get-tuple-element.9), channel_id=1, source_target_pairs={{0,8},{8,16},{16,24},{24,32},{32,40},{40,48},{48,56},{56,64},{64,7... | collective-permute-start | bytes 786440 | tf_op jit(solution)/shard_map/ppermute | solution.py:24
  47.5 6.5 %collective-permute-start.6 = (bf16[4,16,16,128]{3,2,1,0:T(8,128)(2,1)S(1)}, bf16[4,16,16,128]{3,2,1,0:T(8,128)(2,1)S(1)}, u32[]{:S(2)}, u32[]{:S(2)}) collective-permute-start(bf16[4,16,16,128]{3,2,1,0:T(8,128)(2,1)S(1)} %get-tuple-element.7), channel_id=1, source_target_pairs={{8,0},{16,8},{24,16},{32,24},{40,32},{48,40},{56,48},{64,56},{72,6... | collective-permute-start | bytes 786440 | tf_op jit(solution)/shard_map/ppermute | solution.py:25
  49.4 9.8 %collective-permute-start.7 = (bf16[4,16,16,128]{3,2,1,0:T(8,128)(2,1)S(1)}, bf16[4,16,16,128]{3,2,1,0:T(8,128)(2,1)S(1)}, u32[]{:S(2)}, u32[]{:S(2)}) collective-permute-start(bf16[4,16,16,128]{3,2,1,0:T(8,128)(2,1)S(1)} %get-tuple-element.7), channel_id=1, source_target_pairs={{0,8},{8,16},{16,24},{24,32},{32,40},{40,48},{48,56},{56,64},{64,7... | collective-permute-start | bytes 786440 | tf_op jit(solution)/shard_map/ppermute | solution.py:24
  59.9 17.7 %collective-permute-start.9 = (bf16[4,16,16,128]{3,2,1,0:T(8,128)(2,1)S(1)}, bf16[4,16,16,128]{3,2,1,0:T(8,128)(2,1)S(1)}, u32[]{:S(2)}, u32[]{:S(2)}) collective-permute-start(bf16[4,16,16,128]{3,2,1,0:T(8,128)(2,1)S(1)} %get-tuple-element.6), channel_id=1, source_target_pairs={{0,8},{8,16},{16,24},{24,32},{32,40},{40,48},{48,56},{56,64},{64,7... | collective-permute-start | bytes 786440 | tf_op jit(solution)/shard_map/ppermute | solution.py:24
  61.8 15.9 %collective-permute-start.8 = (bf16[4,16,16,128]{3,2,1,0:T(8,128)(2,1)S(1)}, bf16[4,16,16,128]{3,2,1,0:T(8,128)(2,1)S(1)}, u32[]{:S(2)}, u32[]{:S(2)}) collective-permute-start(bf16[4,16,16,128]{3,2,1,0:T(8,128)(2,1)S(1)} %get-tuple-element.6), channel_id=1, source_target_pairs={{8,0},{16,8},{24,16},{32,24},{40,32},{48,40},{56,48},{64,56},{72,6... | collective-permute-start | bytes 786440 | tf_op jit(solution)/shard_map/ppermute | solution.py:25
  67.6 10.8 %collective-permute-start.10 = (bf16[1024,128]{1,0:T(8,128)(2,1)S(1)}, bf16[1024,128]{1,0:T(8,128)(2,1)S(1)}, u32[]{:S(2)}, u32[]{:S(2)}) collective-permute-start(bf16[1024,128]{1,0:T(8,128)(2,1)S(1)} %bitcast.118), channel_id=1, source_target_pairs={{0,7},{1,0},{2,1},{3,2},{4,3},{5,4},{6,5},{7,6},{8,15},{9,8},{10,9... | collective-permute-start | bytes 786440 | tf_op jit(solution)/shard_map/ppermute | solution.py:122
  72.9 11.1 %collective-permute-start.13 = (bf16[1024,128]{1,0:T(8,128)(2,1)S(1)}, bf16[1024,128]{1,0:T(8,128)(2,1)S(1)}, u32[]{:S(2)}, u32[]{:S(2)}) collective-permute-start(bf16[1024,128]{1,0:T(8,128)(2,1)S(1)} %bitcast.119), channel_id=1, source_target_pairs={{0,1},{1,2},{2,3},{3,4},{4,5},{5,6},{6,7},{7,0},{8,9},{9,10},{10,1... | collective-permute-start | bytes 786440 | tf_op jit(solution)/shard_map/ppermute | solution.py:119
  78.6 9.0 %collective-permute-start.11 = (bf16[1024,128]{1,0:T(8,128)(2,1)S(1)}, bf16[1024,128]{1,0:T(8,128)(2,1)S(1)}, u32[]{:S(2)}, u32[]{:S(2)}) collective-permute-start(bf16[1024,128]{1,0:T(8,128)(2,1)S(1)} %collective-permute-done.10), channel_id=1, source_target_pairs={{0,7},{1,0},{2,1},{3,2},{4,3},{5,4},{6,5},{7,6},{8,15},{9,8},{10,9... | collective-permute-start | bytes 786440 | tf_op jit(solution)/shard_map/ppermute | solution.py:122
  84.2 9.7 %collective-permute-start.14 = (bf16[1024,128]{1,0:T(8,128)(2,1)S(1)}, bf16[1024,128]{1,0:T(8,128)(2,1)S(1)}, u32[]{:S(2)}, u32[]{:S(2)}) collective-permute-start(bf16[1024,128]{1,0:T(8,128)(2,1)S(1)} %collective-permute-done.13), channel_id=1, source_target_pairs={{0,1},{1,2},{2,3},{3,4},{4,5},{5,6},{6,7},{7,0},{8,9},{9,10},{10,1... | collective-permute-start | bytes 786440 | tf_op jit(solution)/shard_map/ppermute | solution.py:119
  87.6 9.5 %collective-permute-start.12 = (bf16[1024,128]{1,0:T(8,128)(2,1)S(1)}, bf16[1024,128]{1,0:T(8,128)(2,1)S(1)}, u32[]{:S(2)}, u32[]{:S(2)}) collective-permute-start(bf16[1024,128]{1,0:T(8,128)(2,1)S(1)} %collective-permute-done.11), channel_id=1, source_target_pairs={{0,7},{1,0},{2,1},{3,2},{4,3},{5,4},{6,5},{7,6},{8,15},{9,8},{10,9... | collective-permute-start | bytes 786440 | tf_op jit(solution)/shard_map/ppermute | solution.py:122
  93.9 10.3 %collective-permute-start.15 = (bf16[1024,128]{1,0:T(8,128)(2,1)S(1)}, bf16[1024,128]{1,0:T(8,128)(2,1)S(1)}, u32[]{:S(2)}, u32[]{:S(2)}) collective-permute-start(bf16[1024,128]{1,0:T(8,128)(2,1)S(1)} %collective-permute-done.14), channel_id=1, source_target_pairs={{0,1},{1,2},{2,3},{3,4},{4,5},{5,6},{6,7},{7,0},{8,9},{9,10},{10,1... | collective-permute-start | bytes 786440 | tf_op jit(solution)/shard_map/ppermute | solution.py:119
  104.1 9.5 %collective-permute-start.16 = (bf16[1024,128]{1,0:T(8,128)(2,1)S(1)}, bf16[1024,128]{1,0:T(8,128)(2,1)S(1)}, u32[]{:S(2)}, u32[]{:S(2)}) collective-permute-start(bf16[1024,128]{1,0:T(8,128)(2,1)S(1)} %collective-permute-done.15), channel_id=1, source_target_pairs={{0,1},{1,2},{2,3},{3,4},{4,5},{5,6},{6,7},{7,0},{8,9},{9,10},{10,1... | collective-permute-start | bytes 786440 | tf_op jit(solution)/shard_map/ppermute | solution.py:119
  114.7 0.8 copy-start.2
  120.7 3.9 %collective-permute-start.17 = (f32[32,17,256]{2,0,1:T(8,128)S(1)}, f32[32,17,256]{2,0,1:T(8,128)S(1)}, u32[]{:S(2)}, u32[]{:S(2)}) collective-permute-start(f32[32,17,256]{2,0,1:T(8,128)S(1)} %bitcast.136), channel_id=1, source_target_pairs={{0,8},{8,0},{1,9},{9,1},{2,10},{10,2},{3,11},{11,3},{4,12},{12,4},... | collective-permute-start | bytes 1671176 | tf_op jit(solution)/shard_map/ppermute | solution.py:106

commit v6 on v5

--- a/solution.py
+++ b/solution.py
@@ -61,7 +61,7 @@
         "pq,zqo->zpo",
         plane,
         flat,
-        precision=lax.Precision.HIGHEST,
+        precision=lax.Precision.HIGH,
         preferred_element_type=jnp.float32,
     )
     laplacian = laplacian + in_plane.reshape(current.shape)
@@ -104,9 +104,29 @@
     keep = jnp.where(mine == 1, high, low)
     send = jnp.where(mine == 1, low, high)
     chip_part = keep + lax.ppermute(send, "core", [(0, 1), (1, 0)])
-    chip_part = chip_part.reshape((lax.axis_size("x"), lax.axis_size("z")) + slots.shape[1:])
-    row_part = jnp.sum(lax.all_to_all(chip_part, "x", 0, 0, tiled=True), axis=0)
-    return jnp.sum(lax.all_to_all(row_part, "z", 0, 0, tiled=True), axis=0)
+    received = lax.all_to_all(chip_part, ("x", "z"), 0, 0, tiled=True)
+    return jnp.sum(received, axis=0)
+
+
+def shifted(value, shift):
+    size = lax.axis_size("orb")
+    return lax.ppermute(value, "orb", [(i, (i + shift) % size) for i in range(size)])
+
+
+def gather_blocks(block):
+    if lax.axis_size("orb") != 8:
+        return gather_ring(block)
+    ahead = {0: block}
+    for step in (1, 2):
+        ahead[-step] = shifted(block, step)
+        ahead[step] = shifted(block, -step)
+    half = block.shape[0] // 2
+    ahead[3] = shifted(ahead[2], -1)
+    ahead[-3] = shifted(ahead[-2], 1)
+    ahead[4] = jnp.concatenate(
+        [shifted(ahead[2][:half], -2), shifted(ahead[-2][half:], 2)], axis=0
+    )
+    return [ahead[k] if k <= 4 else ahead[k - 8] for k in range(8)]
 
 
 def gather_ring(block):
@@ -138,7 +158,7 @@
         .astype(jnp.bfloat16)
         .reshape(point_count, own_width)
     )
-    blocks = gather_ring(rounded_orbitals)
+    blocks = gather_blocks(rounded_orbitals)
     total_width = own_width * len(blocks)
     rows = total_width // grid_size
     hamiltonian_part = jnp.concatenate(

time: 153 us -> 158 us (1.033)
  waiting for transfers between devices: 37.9 us -> 29.3 us
  starting transfers between devices: 59.1 us -> 63.6 us
  matrix products: 14.6 us -> 18.7 us
  local copies, waits for them, and re-layouts: 4.54 us -> 8.2 us
    ppermute x7 -> x8, waiting for transfers between devices: 15.7 us -> 5.94 us  [shifted(): lax.ppermute(value, 'orb', [(i, (i + shift) % size) for i in range(size)])]
    dot_general x16, matrix products: 4.25 us -> 9.34 us  [contract_points(): lax.dot_general(left_side, right_side, (((0,), (0,)), ((), ())), preferre...]
    ppermute x7 -> x8, starting transfers between devices: 23.9 us -> 28.4 us  [shifted(): lax.ppermute(value, 'orb', [(i, (i + shift) % size) for i in range(size)])]
    all_to_all x2 -> x1, blocking collectives: 24.7 us -> 25.1 us  [reduce_scatter_grid(): received = lax.all_to_all(chip_part, ('x', 'z'), 0, 0, tiled=True)]
  transfers between devices with their start and end apart: 18 -> 19, of which waited for: 9 -> 8; matrix products, arithmetic and copies ran while one was open for 11% -> 14% of each run, Pallas kernels for 0% -> 0%
where the time goes in v6:
time: 158 us; the launch traced here: 155 us
  starting transfers between devices  63.6 us (40%)
  waiting for transfers between devices  29.3 us (19%)
  blocking collectives  25.1 us (16%)
  matrix products  18.7 us (12%)
  other arithmetic  9.03 us (6%)
  local copies, waits for them, and re-layouts  8.2 us (5%)
    ppermute x8, starting transfers between devices, shifted(): lax.ppermute(value, 'orb', [(i, (i + shift) % size) for i in range(size)])  28.4 us
    all_to_all x1, blocking collectives, reduce_scatter_grid(): received = lax.all_to_all(chip_part, ('x', 'z'), 0, 0, tiled=True)  25.1 us
    ppermute x5, starting transfers between devices, halo_layers(): after = lax.ppermute(initial, GRID, down).astype(shard.dtype)  22.4 us
    ppermute x5, waiting for transfers between devices, halo_layers(): before = lax.ppermute(last, GRID, up).astype(shard.dtype)  21.4 us
    ppermute x5, starting transfers between devices, halo_layers(): before = lax.ppermute(last, GRID, up).astype(shard.dtype)  10.8 us
    dot_general x5, matrix products, apply_hamiltonian(): jnp.einsum('pq,zqo->zpo', plane, flat, precision=lax.Precision.HIGH, pref...  9.36 us
    dot_general x16, matrix products, contract_points(): lax.dot_general(left_side, right_side, (((0,), (0,)), ((), ())), preferre...  9.34 us
    ppermute x8, waiting for transfers between devices, shifted(): lax.ppermute(value, 'orb', [(i, (i + shift) % size) for i in range(size)])  5.94 us
  transfers between devices with their start and end apart: 19, of which 8 were waited for; matrix products, arithmetic and copies ran while one was open for 14% of the time, Pallas kernels for 0%

profile of v6, /device:TPU:6, one launch (start us, length us, event | category | flops | bytes accessed | tf_op | source)
XLA Modules:
  0.0 155.1 jit_solution(15541090492731428269)
XLA Ops:
  1.7 10.7 %collective-permute-start = (bf16[4,16,16,128]{3,2,1,0:T(8,128)(2,1)S(1)}, bf16[4,16,16,128]{3,2,1,0:T(8,128)(2,1)S(1)}, u32[]{:S(2)}, u32[]{:S(2)}) collective-permute-start(bf16[4,16,16,128]{3,2,1,0:T(8,128)(2,1)S(1)} %convert_element_type.255), channel_id=1, source_target_pairs={{8,0},{16,8},{24,16},{32,24},{40,32},{48,40},{56,48},{64,56},{72,6... | collective-permute-start | bytes 786440 | tf_op jit(solution)/shard_map/ppermute | solution.py:25
  12.4 1.9 %collective-permute-start.1 = (bf16[4,16,16,128]{3,2,1,0:T(8,128)(2,1)S(1)}, bf16[4,16,16,128]{3,2,1,0:T(8,128)(2,1)S(1)}, u32[]{:S(2)}, u32[]{:S(2)}) collective-permute-start(bf16[4,16,16,128]{3,2,1,0:T(8,128)(2,1)S(1)} %convert_element_type.255), channel_id=1, source_target_pairs={{0,8},{8,16},{16,24},{24,32},{32,40},{40,48},{48,56},{56,64},{64,7... | collective-permute-start | bytes 786440 | tf_op jit(solution)/shard_map/ppermute | solution.py:24
  15.2 2.4 %fusion.111 = f32[256,4,128]{2,0,1:T(8,128)S(1)} fusion(f32[4,256,128]{2,1,0:T(8,128)} %bitcast.126, s32[256]{0:T(256)S(1)} %get-tuple-element.18, s32[256]{0:T(256)S(1)} %get-tuple-element.19), kind=kOutput, calls=%fused_computation.209 | convolution fusion | flops 207618048 | bytes 1050624 | tf_op jit(solution)/shard_map/pq,zqo->zpo/dot_general | solution.py:60
  17.6 4.5 %collective-permute-done.1 = bf16[4,16,16,128]{3,2,1,0:T(8,128)(2,1)S(1)} collective-permute-done((bf16[4,16,16,128]{3,2,1,0:T(8,128)(2,1)S(1)}, bf16[4,16,16,128]{3,2,1,0:T(8,128)(2,1)S(1)}, u32[]{:S(2)}, u32[]{:S(2)}) %collective-permute-start.1) | collective-permute-done | bytes 262176 | tf_op jit(solution)/shard_map/ppermute | solution.py:24
  22.6 2.1 %collective-permute-start.2 = (bf16[4,16,16,128]{3,2,1,0:T(8,128)(2,1)S(1)}, bf16[4,16,16,128]{3,2,1,0:T(8,128)(2,1)S(1)}, u32[]{:S(2)}, u32[]{:S(2)}) collective-permute-start(bf16[4,16,16,128]{3,2,1,0:T(8,128)(2,1)S(1)} %get-tuple-element.11), channel_id=1, source_target_pairs={{8,0},{16,8},{24,16},{32,24},{40,32},{48,40},{56,48},{64,56},{72,6... | collective-permute-start | bytes 786440 | tf_op jit(solution)/shard_map/ppermute | solution.py:25
  24.8 2.2 %collective-permute-start.3 = (bf16[4,16,16,128]{3,2,1,0:T(8,128)(2,1)S(1)}, bf16[4,16,16,128]{3,2,1,0:T(8,128)(2,1)S(1)}, u32[]{:S(2)}, u32[]{:S(2)}) collective-permute-start(bf16[4,16,16,128]{3,2,1,0:T(8,128)(2,1)S(1)} %get-tuple-element.11), channel_id=1, source_target_pairs={{0,8},{8,16},{16,24},{24,32},{32,40},{40,48},{48,56},{56,64},{64,7... | collective-permute-start | bytes 786440 | tf_op jit(solution)/shard_map/ppermute | solution.py:24
  27.0 1.5 convolution_bitcast_fusion.3
  28.8 5.7 %collective-permute-done.3 = bf16[4,16,16,128]{3,2,1,0:T(8,128)(2,1)S(1)} collective-permute-done((bf16[4,16,16,128]{3,2,1,0:T(8,128)(2,1)S(1)}, bf16[4,16,16,128]{3,2,1,0:T(8,128)(2,1)S(1)}, u32[]{:S(2)}, u32[]{:S(2)}) %collective-permute-start.3) | collective-permute-done | bytes 262176 | tf_op jit(solution)/shard_map/ppermute | solution.py:24
  35.0 1.9 %collective-permute-start.4 = (bf16[4,16,16,128]{3,2,1,0:T(8,128)(2,1)S(1)}, bf16[4,16,16,128]{3,2,1,0:T(8,128)(2,1)S(1)}, u32[]{:S(2)}, u32[]{:S(2)}) collective-permute-start(bf16[4,16,16,128]{3,2,1,0:T(8,128)(2,1)S(1)} %get-tuple-element.9), channel_id=1, source_target_pairs={{8,0},{16,8},{24,16},{32,24},{40,32},{48,40},{56,48},{64,56},{72,6... | collective-permute-start | bytes 786440 | tf_op jit(solution)/shard_map/ppermute | solution.py:25
  37.0 2.4 %collective-permute-start.5 = (bf16[4,16,16,128]{3,2,1,0:T(8,128)(2,1)S(1)}, bf16[4,16,16,128]{3,2,1,0:T(8,128)(2,1)S(1)}, u32[]{:S(2)}, u32[]{:S(2)}) collective-permute-start(bf16[4,16,16,128]{3,2,1,0:T(8,128)(2,1)S(1)} %get-tuple-element.9), channel_id=1, source_target_pairs={{0,8},{8,16},{16,24},{24,32},{32,40},{40,48},{48,56},{56,64},{64,7... | collective-permute-start | bytes 786440 | tf_op jit(solution)/shard_map/ppermute | solution.py:24
  39.4 1.5 convolution_bitcast_fusion.2
  41.2 5.6 %collective-permute-done.5 = bf16[4,16,16,128]{3,2,1,0:T(8,128)(2,1)S(1)} collective-permute-done((bf16[4,16,16,128]{3,2,1,0:T(8,128)(2,1)S(1)}, bf16[4,16,16,128]{3,2,1,0:T(8,128)(2,1)S(1)}, u32[]{:S(2)}, u32[]{:S(2)}) %collective-permute-start.5) | collective-permute-done | bytes 262176 | tf_op jit(solution)/shard_map/ppermute | solution.py:24
  47.2 1.9 %collective-permute-start.6 = (bf16[4,16,16,128]{3,2,1,0:T(8,128)(2,1)S(1)}, bf16[4,16,16,128]{3,2,1,0:T(8,128)(2,1)S(1)}, u32[]{:S(2)}, u32[]{:S(2)}) collective-permute-start(bf16[4,16,16,128]{3,2,1,0:T(8,128)(2,1)S(1)} %get-tuple-element.7), channel_id=1, source_target_pairs={{8,0},{16,8},{24,16},{32,24},{40,32},{48,40},{56,48},{64,56},{72,6... | collective-permute-start | bytes 786440 | tf_op jit(solution)/shard_map/ppermute | solution.py:25
  49.2 2.4 %collective-permute-start.7 = (bf16[4,16,16,128]{3,2,1,0:T(8,128)(2,1)S(1)}, bf16[4,16,16,128]{3,2,1,0:T(8,128)(2,1)S(1)}, u32[]{:S(2)}, u32[]{:S(2)}) collective-permute-start(bf16[4,16,16,128]{3,2,1,0:T(8,128)(2,1)S(1)} %get-tuple-element.7), channel_id=1, source_target_pairs={{0,8},{8,16},{16,24},{24,32},{32,40},{40,48},{48,56},{56,64},{64,7... | collective-permute-start | bytes 786440 | tf_op jit(solution)/shard_map/ppermute | solution.py:24
  51.6 1.5 convolution_bitcast_fusion.1
  53.4 5.6 %collective-permute-done.7 = bf16[4,16,16,128]{3,2,1,0:T(8,128)(2,1)S(1)} collective-permute-done((bf16[4,16,16,128]{3,2,1,0:T(8,128)(2,1)S(1)}, bf16[4,16,16,128]{3,2,1,0:T(8,128)(2,1)S(1)}, u32[]{:S(2)}, u32[]{:S(2)}) %collective-permute-start.7) | collective-permute-done | bytes 262176 | tf_op jit(solution)/shard_map/ppermute | solution.py:24
  59.6 1.9 %collective-permute-start.9 = (bf16[4,16,16,128]{3,2,1,0:T(8,128)(2,1)S(1)}, bf16[4,16,16,128]{3,2,1,0:T(8,128)(2,1)S(1)}, u32[]{:S(2)}, u32[]{:S(2)}) collective-permute-start(bf16[4,16,16,128]{3,2,1,0:T(8,128)(2,1)S(1)} %get-tuple-element.6), channel_id=1, source_target_pairs={{0,8},{8,16},{16,24},{24,32},{32,40},{40,48},{48,56},{56,64},{64,7... | collective-permute-start | bytes 786440 | tf_op jit(solution)/shard_map/ppermute | solution.py:24
  61.5 5.8 %collective-permute-start.8 = (bf16[4,16,16,128]{3,2,1,0:T(8,128)(2,1)S(1)}, bf16[4,16,16,128]{3,2,1,0:T(8,128)(2,1)S(1)}, u32[]{:S(2)}, u32[]{:S(2)}) collective-permute-start(bf16[4,16,16,128]{3,2,1,0:T(8,128)(2,1)S(1)} %get-tuple-element.6), channel_id=1, source_target_pairs={{8,0},{16,8},{24,16},{32,24},{40,32},{48,40},{56,48},{64,56},{72,6... | collective-permute-start | bytes 786440 | tf_op jit(solution)/shard_map/ppermute | solution.py:25
  67.3 5.4 %collective-permute-start.10 = (bf16[1024,128]{1,0:T(8,128)(2,1)S(1)}, bf16[1024,128]{1,0:T(8,128)(2,1)S(1)}, u32[]{:S(2)}, u32[]{:S(2)}) collective-permute-start(bf16[1024,128]{1,0:T(8,128)(2,1)S(1)} %bitcast.114), channel_id=1, source_target_pairs={{0,7},{1,0},{2,1},{3,2},{4,3},{5,4},{6,5},{7,6},{8,15},{9,8},{10,9... | collective-permute-start | bytes 786440 | tf_op jit(solution)/shard_map/ppermute | solution.py:113
  72.7 4.0 %collective-permute-start.11 = (bf16[1024,128]{1,0:T(8,128)(2,1)S(1)}, bf16[1024,128]{1,0:T(8,128)(2,1)S(1)}, u32[]{:S(2)}, u32[]{:S(2)}) collective-permute-start(bf16[1024,128]{1,0:T(8,128)(2,1)S(1)} %bitcast.115), channel_id=1, source_target_pairs={{0,6},{1,7},{2,0},{3,1},{4,2},{5,3},{6,4},{7,5},{8,14},{9,15},{10,... | collective-permute-start | bytes 786440 | tf_op jit(solution)/shard_map/ppermute | solution.py:113
  76.7 2.7 %collective-permute-start.14 = (bf16[1024,128]{1,0:T(8,128)(2,1)S(1)}, bf16[1024,128]{1,0:T(8,128)(2,1)S(1)}, u32[]{:S(2)}, u32[]{:S(2)}) collective-permute-start(bf16[1024,128]{1,0:T(8,128)(2,1)S(1)} %bitcast.116), channel_id=1, source_target_pairs={{0,2},{1,3},{2,4},{3,5},{4,6},{5,7},{6,0},{7,1},{8,10},{9,11},{10,... | collective-permute-start | bytes 786440 | tf_op jit(solution)/shard_map/ppermute | solution.py:113
  79.4 2.3 %convolution_bitcast_fusion = f32[4,256,128]{1,2,0:T(8,128)} fusion(f32[4,256,128]{2,1,0:T(8,128)S(1)} %bitcast.125, s32[256]{0:T(256)S(1)} %get-tuple-element.18, s32[256]{0:T(256)S(1)} %get-tuple-element.19), kind=kOutput, calls=%fused_computation.46 | convolution fusion | flops 207618048 | bytes 1050624 | tf_op jit(solution)/shard_map/pq,zqo->zpo/dot_general | solution.py:60
  83.4 3.9 %collective-permute-done.11 = bf16[1024,128]{1,0:T(8,128)(2,1)S(1)} collective-permute-done((bf16[1024,128]{1,0:T(8,128)(2,1)S(1)}, bf16[1024,128]{1,0:T(8,128)(2,1)S(1)}, u32[]{:S(2)}, u32[]{:S(2)}) %collective-permute-start.11) | collective-permute-done | bytes 262176 | tf_op jit(solution)/shard_map/ppermute | solution.py:113
  87.3 1.9 %collective-permute-start.17 = (bf16[1024,128]{1,0:T(8,128)(2,1)S(1)}, bf16[1024,128]{1,0:T(8,128)(2,1)S(1)}, u32[]{:S(2)}, u32[]{:S(2)}) collective-permute-start(bf16[1024,128]{1,0:T(8,128)(2,1)S(1)} %bitcast.117), channel_id=1, source_target_pairs={{0,1},{1,2},{2,3},{3,4},{4,5},{5,6},{6,7},{7,0},{8,9},{9,10},{10,1... | collective-permute-start | bytes 786440 | tf_op jit(solution)/shard_map/ppermute | solution.py:113
  90.7 5.8 %collective-permute-start.13 = (bf16[512,128]{1,0:T(8,128)(2,1)}, bf16[512,128]{1,0:T(8,128)(2,1)}, u32[]{:S(2)}, u32[]{:S(2)}) collective-permute-start(bf16[512,128]{1,0:T(8,128)(2,1)} %slice.222), channel_id=1, source_target_pairs={{0,6},{1,7},{2,0},{3,1},{4,2},{5,3},{6,4},{7,5},{8,14},{9,15},{10,... | collective-permute-start | bytes 393224 | tf_op jit(solution)/shard_map/ppermute | solution.py:113
  97.2 1.9 %collective-permute-start.15 = (bf16[512,128]{1,0:T(8,128)(2,1)}, bf16[512,128]{1,0:T(8,128)(2,1)}, u32[]{:S(2)}, u32[]{:S(2)}) collective-permute-start(bf16[512,128]{1,0:T(8,128)(2,1)} %slice.223), channel_id=1, source_target_pairs={{0,2},{1,3},{2,4},{3,5},{4,6},{5,7},{6,0},{7,1},{8,10},{9,11},{10,... | collective-permute-start | bytes 393224 | tf_op jit(solution)/shard_map/ppermute | solution.py:113
  101.4 4.7 %collective-permute-start.12 = (bf16[1024,128]{1,0:T(8,128)(2,1)S(1)}, bf16[1024,128]{1,0:T(8,128)(2,1)S(1)}, u32[]{:S(2)}, u32[]{:S(2)}) collective-permute-start(bf16[1024,128]{1,0:T(8,128)(2,1)S(1)} %collective-permute-done.11), channel_id=1, source_target_pairs={{0,7},{1,0},{2,1},{3,2},{4,3},{5,4},{6,5},{7,6},{8,15},{9,8},{10,9... | collective-permute-start | bytes 786440 | tf_op jit(solution)/shard_map/ppermute | solution.py:113
  106.1 1.9 %collective-permute-start.16 = (bf16[1024,128]{1,0:T(8,128)(2,1)S(1)}, bf16[1024,128]{1,0:T(8,128)(2,1)S(1)}, u32[]{:S(2)}, u32[]{:S(2)}) collective-permute-start(bf16[1024,128]{1,0:T(8,128)(2,1)S(1)} %collective-permute-done.14), channel_id=1, source_target_pairs={{0,1},{1,2},{2,3},{3,4},{4,5},{5,6},{6,7},{7,0},{8,9},{9,10},{10,1... | collective-permute-start | bytes 786440 | tf_op jit(solution)/shard_map/ppermute | solution.py:113
  122.6 1.3 fusion.209
  124.0 1.9 %collective-permute-start.18 = (f32[32,17,256]{2,0,1:T(8,128)S(1)}, f32[32,17,256]{2,0,1:T(8,128)S(1)}, u32[]{:S(2)}, u32[]{:S(2)}) collective-permute-start(f32[32,17,256]{2,0,1:T(8,128)S(1)} %bitcast.134), channel_id=1, source_target_pairs={{0,8},{8,0},{1,9},{9,1},{2,10},{10,2},{3,11},{11,3},{4,12},{12,4},... | collective-permute-start | bytes 1671176 | tf_op jit(solution)/shard_map/ppermute | solution.py:106
  125.9 1.9 %collective-permute-done.18 = f32[32,17,256]{2,0,1:T(8,128)S(1)} collective-permute-done((f32[32,17,256]{2,0,1:T(8,128)S(1)}, f32[32,17,256]{2,0,1:T(8,128)S(1)}, u32[]{:S(2)}, u32[]{:S(2)}) %collective-permute-start.18) | collective-permute-done | bytes 557088 | tf_op jit(solution)/shard_map/ppermute | solution.py:106
  128.4 25.1 %all_to_all.5 = f32[32,17,256]{2,1,0:T(8,128)S(1)} all-to-all(f32[32,17,256]{2,1,0:T(8,128)S(1)} %copy.68), channel_id=1, replica_groups=mesh['x'=4,'z'=8,'core'=2,'orb'=8] {'x','z'}, dimensions={0} | all-to-all | bytes 1114112 | tf_op jit(solution)/shard_map/all_to_all | solution.py:107
  (104 shorter events, 27.3 us)
Async XLA Ops:
  1.7 15.9 %collective-permute-start = (bf16[4,16,16,128]{3,2,1,0:T(8,128)(2,1)S(1)}, bf16[4,16,16,128]{3,2,1,0:T(8,128)(2,1)S(1)}, u32[]{:S(2)}, u32[]{:S(2)}) collective-permute-start(bf16[4,16,16,128]{3,2,1,0:T(8,128)(2,1)S(1)} %convert_element_type.255), channel_id=1, source_target_pairs={{8,0},{16,8},{24,16},{32,24},{40,32},{48,40},{56,48},{64,56},{72,6... | collective-permute-start | bytes 786440 | tf_op jit(solution)/shard_map/ppermute | solution.py:25
  12.4 9.8 %collective-permute-start.1 = (bf16[4,16,16,128]{3,2,1,0:T(8,128)(2,1)S(1)}, bf16[4,16,16,128]{3,2,1,0:T(8,128)(2,1)S(1)}, u32[]{:S(2)}, u32[]{:S(2)}) collective-permute-start(bf16[4,16,16,128]{3,2,1,0:T(8,128)(2,1)S(1)} %convert_element_type.255), channel_id=1, source_target_pairs={{0,8},{8,16},{16,24},{24,32},{32,40},{40,48},{48,56},{56,64},{64,7... | collective-permute-start | bytes 786440 | tf_op jit(solution)/shard_map/ppermute | solution.py:24
  17.6 4.7 %copy-start = (f32[4,16,16,128]{3,2,1,0:T(8,128)S(1)}, f32[4,16,16,128]{3,2,1,0:T(8,128)}, u32[]{:S(2)}) copy-start(f32[4,16,16,128]{3,2,1,0:T(8,128)} %param.2) | copy-start | bytes 1572868
  17.6 4.7 %copy-start.1 = (f32[4,16,16]{2,1,0:T(8,128)S(1)}, f32[4,16,16]{2,1,0:T(8,128)}, u32[]{:S(2)}) copy-start(f32[4,16,16]{2,1,0:T(8,128)} %param.3) | copy-start | bytes 12292
  22.6 6.1 %collective-permute-start.2 = (bf16[4,16,16,128]{3,2,1,0:T(8,128)(2,1)S(1)}, bf16[4,16,16,128]{3,2,1,0:T(8,128)(2,1)S(1)}, u32[]{:S(2)}, u32[]{:S(2)}) collective-permute-start(bf16[4,16,16,128]{3,2,1,0:T(8,128)(2,1)S(1)} %get-tuple-element.11), channel_id=1, source_target_pairs={{8,0},{16,8},{24,16},{32,24},{40,32},{48,40},{56,48},{64,56},{72,6... | collective-permute-start | bytes 786440 | tf_op jit(solution)/shard_map/ppermute | solution.py:25
  24.8 9.8 %collective-permute-start.3 = (bf16[4,16,16,128]{3,2,1,0:T(8,128)(2,1)S(1)}, bf16[4,16,16,128]{3,2,1,0:T(8,128)(2,1)S(1)}, u32[]{:S(2)}, u32[]{:S(2)}) collective-permute-start(bf16[4,16,16,128]{3,2,1,0:T(8,128)(2,1)S(1)} %get-tuple-element.11), channel_id=1, source_target_pairs={{0,8},{8,16},{16,24},{24,32},{32,40},{40,48},{48,56},{56,64},{64,7... | collective-permute-start | bytes 786440 | tf_op jit(solution)/shard_map/ppermute | solution.py:24
  35.0 6.1 %collective-permute-start.4 = (bf16[4,16,16,128]{3,2,1,0:T(8,128)(2,1)S(1)}, bf16[4,16,16,128]{3,2,1,0:T(8,128)(2,1)S(1)}, u32[]{:S(2)}, u32[]{:S(2)}) collective-permute-start(bf16[4,16,16,128]{3,2,1,0:T(8,128)(2,1)S(1)} %get-tuple-element.9), channel_id=1, source_target_pairs={{8,0},{16,8},{24,16},{32,24},{40,32},{48,40},{56,48},{64,56},{72,6... | collective-permute-start | bytes 786440 | tf_op jit(solution)/shard_map/ppermute | solution.py:25
  37.0 9.8 %collective-permute-start.5 = (bf16[4,16,16,128]{3,2,1,0:T(8,128)(2,1)S(1)}, bf16[4,16,16,128]{3,2,1,0:T(8,128)(2,1)S(1)}, u32[]{:S(2)}, u32[]{:S(2)}) collective-permute-start(bf16[4,16,16,128]{3,2,1,0:T(8,128)(2,1)S(1)} %get-tuple-element.9), channel_id=1, source_target_pairs={{0,8},{8,16},{16,24},{24,32},{32,40},{40,48},{48,56},{56,64},{64,7... | collective-permute-start | bytes 786440 | tf_op jit(solution)/shard_map/ppermute | solution.py:24
  47.2 6.1 %collective-permute-start.6 = (bf16[4,16,16,128]{3,2,1,0:T(8,128)(2,1)S(1)}, bf16[4,16,16,128]{3,2,1,0:T(8,128)(2,1)S(1)}, u32[]{:S(2)}, u32[]{:S(2)}) collective-permute-start(bf16[4,16,16,128]{3,2,1,0:T(8,128)(2,1)S(1)} %get-tuple-element.7), channel_id=1, source_target_pairs={{8,0},{16,8},{24,16},{32,24},{40,32},{48,40},{56,48},{64,56},{72,6... | collective-permute-start | bytes 786440 | tf_op jit(solution)/shard_map/ppermute | solution.py:25
  49.2 9.8 %collective-permute-start.7 = (bf16[4,16,16,128]{3,2,1,0:T(8,128)(2,1)S(1)}, bf16[4,16,16,128]{3,2,1,0:T(8,128)(2,1)S(1)}, u32[]{:S(2)}, u32[]{:S(2)}) collective-permute-start(bf16[4,16,16,128]{3,2,1,0:T(8,128)(2,1)S(1)} %get-tuple-element.7), channel_id=1, source_target_pairs={{0,8},{8,16},{16,24},{24,32},{32,40},{40,48},{48,56},{56,64},{64,7... | collective-permute-start | bytes 786440 | tf_op jit(solution)/shard_map/ppermute | solution.py:24
  59.6 37.6 %collective-permute-start.9 = (bf16[4,16,16,128]{3,2,1,0:T(8,128)(2,1)S(1)}, bf16[4,16,16,128]{3,2,1,0:T(8,128)(2,1)S(1)}, u32[]{:S(2)}, u32[]{:S(2)}) collective-permute-start(bf16[4,16,16,128]{3,2,1,0:T(8,128)(2,1)S(1)} %get-tuple-element.6), channel_id=1, source_target_pairs={{0,8},{8,16},{16,24},{24,32},{32,40},{40,48},{48,56},{56,64},{64,7... | collective-permute-start | bytes 786440 | tf_op jit(solution)/shard_map/ppermute | solution.py:24
  61.5 37.9 %collective-permute-start.8 = (bf16[4,16,16,128]{3,2,1,0:T(8,128)(2,1)S(1)}, bf16[4,16,16,128]{3,2,1,0:T(8,128)(2,1)S(1)}, u32[]{:S(2)}, u32[]{:S(2)}) collective-permute-start(bf16[4,16,16,128]{3,2,1,0:T(8,128)(2,1)S(1)} %get-tuple-element.6), channel_id=1, source_target_pairs={{8,0},{16,8},{24,16},{32,24},{40,32},{48,40},{56,48},{64,56},{72,6... | collective-permute-start | bytes 786440 | tf_op jit(solution)/shard_map/ppermute | solution.py:25
  67.3 32.5 %collective-permute-start.10 = (bf16[1024,128]{1,0:T(8,128)(2,1)S(1)}, bf16[1024,128]{1,0:T(8,128)(2,1)S(1)}, u32[]{:S(2)}, u32[]{:S(2)}) collective-permute-start(bf16[1024,128]{1,0:T(8,128)(2,1)S(1)} %bitcast.114), channel_id=1, source_target_pairs={{0,7},{1,0},{2,1},{3,2},{4,3},{5,4},{6,5},{7,6},{8,15},{9,8},{10,9... | collective-permute-start | bytes 786440 | tf_op jit(solution)/shard_map/ppermute | solution.py:113
  72.7 14.6 %collective-permute-start.11 = (bf16[1024,128]{1,0:T(8,128)(2,1)S(1)}, bf16[1024,128]{1,0:T(8,128)(2,1)S(1)}, u32[]{:S(2)}, u32[]{:S(2)}) collective-permute-start(bf16[1024,128]{1,0:T(8,128)(2,1)S(1)} %bitcast.115), channel_id=1, source_target_pairs={{0,6},{1,7},{2,0},{3,1},{4,2},{5,3},{6,4},{7,5},{8,14},{9,15},{10,... | collective-permute-start | bytes 786440 | tf_op jit(solution)/shard_map/ppermute | solution.py:113
  76.7 13.9 %collective-permute-start.14 = (bf16[1024,128]{1,0:T(8,128)(2,1)S(1)}, bf16[1024,128]{1,0:T(8,128)(2,1)S(1)}, u32[]{:S(2)}, u32[]{:S(2)}) collective-permute-start(bf16[1024,128]{1,0:T(8,128)(2,1)S(1)} %bitcast.116), channel_id=1, source_target_pairs={{0,2},{1,3},{2,4},{3,5},{4,6},{5,7},{6,0},{7,1},{8,10},{9,11},{10,... | collective-permute-start | bytes 786440 | tf_op jit(solution)/shard_map/ppermute | solution.py:113
  87.3 13.8 %collective-permute-start.17 = (bf16[1024,128]{1,0:T(8,128)(2,1)S(1)}, bf16[1024,128]{1,0:T(8,128)(2,1)S(1)}, u32[]{:S(2)}, u32[]{:S(2)}) collective-permute-start(bf16[1024,128]{1,0:T(8,128)(2,1)S(1)} %bitcast.117), channel_id=1, source_target_pairs={{0,1},{1,2},{2,3},{3,4},{4,5},{5,6},{6,7},{7,0},{8,9},{9,10},{10,1... | collective-permute-start | bytes 786440 | tf_op jit(solution)/shard_map/ppermute | solution.py:113
  90.7 19.7 %collective-permute-start.13 = (bf16[512,128]{1,0:T(8,128)(2,1)}, bf16[512,128]{1,0:T(8,128)(2,1)}, u32[]{:S(2)}, u32[]{:S(2)}) collective-permute-start(bf16[512,128]{1,0:T(8,128)(2,1)} %slice.222), channel_id=1, source_target_pairs={{0,6},{1,7},{2,0},{3,1},{4,2},{5,3},{6,4},{7,5},{8,14},{9,15},{10,... | collective-permute-start | bytes 393224 | tf_op jit(solution)/shard_map/ppermute | solution.py:113
  97.2 14.2 %collective-permute-start.15 = (bf16[512,128]{1,0:T(8,128)(2,1)}, bf16[512,128]{1,0:T(8,128)(2,1)}, u32[]{:S(2)}, u32[]{:S(2)}) collective-permute-start(bf16[512,128]{1,0:T(8,128)(2,1)} %slice.223), channel_id=1, source_target_pairs={{0,2},{1,3},{2,4},{3,5},{4,6},{5,7},{6,0},{7,1},{8,10},{9,11},{10,... | collective-permute-start | bytes 393224 | tf_op jit(solution)/shard_map/ppermute | solution.py:113
  101.4 11.1 %collective-permute-start.12 = (bf16[1024,128]{1,0:T(8,128)(2,1)S(1)}, bf16[1024,128]{1,0:T(8,128)(2,1)S(1)}, u32[]{:S(2)}, u32[]{:S(2)}) collective-permute-start(bf16[1024,128]{1,0:T(8,128)(2,1)S(1)} %collective-permute-done.11), channel_id=1, source_target_pairs={{0,7},{1,0},{2,1},{3,2},{4,3},{5,4},{6,5},{7,6},{8,15},{9,8},{10,9... | collective-permute-start | bytes 786440 | tf_op jit(solution)/shard_map/ppermute | solution.py:113
  106.1 9.5 %collective-permute-start.16 = (bf16[1024,128]{1,0:T(8,128)(2,1)S(1)}, bf16[1024,128]{1,0:T(8,128)(2,1)S(1)}, u32[]{:S(2)}, u32[]{:S(2)}) collective-permute-start(bf16[1024,128]{1,0:T(8,128)(2,1)S(1)} %collective-permute-done.14), channel_id=1, source_target_pairs={{0,1},{1,2},{2,3},{3,4},{4,5},{5,6},{6,7},{7,0},{8,9},{9,10},{10,1... | collective-permute-start | bytes 786440 | tf_op jit(solution)/shard_map/ppermute | solution.py:113
  108.6 4.8 %copy-start.2 = (f32[1024,128]{1,0:T(8,128)}, f32[1024,128]{1,0:T(8,128)S(1)}, u32[]{:S(2)}) copy-start(f32[1024,128]{1,0:T(8,128)S(1)} %convolution_dynamic-update-slice_fusion.5) | copy-start | bytes 1572868
  116.5 3.0 %copy-start.3 = (f32[1024,128]{1,0:T(8,128)S(1)}, f32[1024,128]{1,0:T(8,128)}, u32[]{:S(2)}) copy-start(f32[1024,128]{1,0:T(8,128)} %copy-done.2) | copy-start | bytes 1572868
  124.0 3.9 %collective-permute-start.18 = (f32[32,17,256]{2,0,1:T(8,128)S(1)}, f32[32,17,256]{2,0,1:T(8,128)S(1)}, u32[]{:S(2)}, u32[]{:S(2)}) collective-permute-start(f32[32,17,256]{2,0,1:T(8,128)S(1)} %bitcast.134), channel_id=1, source_target_pairs={{0,8},{8,0},{1,9},{9,1},{2,10},{10,2},{3,11},{11,3},{4,12},{12,4},... | collective-permute-start | bytes 1671176 | tf_op jit(solution)/shard_map/ppermute | solution.py:106

commit v7 on v5

--- a/solution.py
+++ b/solution.py
@@ -61,7 +61,7 @@
         "pq,zqo->zpo",
         plane,
         flat,
-        precision=lax.Precision.HIGHEST,
+        precision=lax.Precision.HIGH,
         preferred_element_type=jnp.float32,
     )
     laplacian = laplacian + in_plane.reshape(current.shape)

time: 153 us -> 152 us (level)
  matrix products: 14.6 us -> 12.8 us
    dot_general x5, matrix products: 10.4 us -> 8.56 us  [apply_hamiltonian(): jnp.einsum('pq,zqo->zpo', plane, flat, precision=lax.Precision.HIGH, pref...]
  transfers between devices with their start and end apart: 18 -> 18, of which waited for: 9 -> 9; matrix products, arithmetic and copies ran while one was open for 11% -> 10% of each run, Pallas kernels for 0% -> 0%
where the time goes in v7:
time: 152 us; the launch traced here: 151 us
  starting transfers between devices  59.1 us (39%)
  waiting for transfers between devices  39.1 us (26%)
  blocking collectives  24.7 us (16%)
  matrix products  12.8 us (8%)
  other arithmetic  9.02 us (6%)
  local copies, waits for them, and re-layouts  4.54 us (3%)
    ppermute x5, starting transfers between devices, halo_layers(): after = lax.ppermute(initial, GRID, down).astype(shard.dtype)  22.4 us
    ppermute x5, waiting for transfers between devices, halo_layers(): before = lax.ppermute(last, GRID, up).astype(shard.dtype)  21.4 us
    ppermute x3, starting transfers between devices, gather_ring(): from_right = lax.ppermute(from_right, 'orb', left)  16.1 us
    ppermute x4, waiting for transfers between devices, gather_ring(): from_left = lax.ppermute(from_left, 'orb', right)  13.6 us
    all_to_all x1, blocking collectives, reduce_scatter_grid(): row_part = jnp.sum(lax.all_to_all(chip_part, 'x', 0, 0, tiled=True), axis=0)  12.4 us
    all_to_all x1, blocking collectives, reduce_scatter_grid(): return jnp.sum(lax.all_to_all(row_part, 'z', 0, 0, tiled=True), axis=0)  12.3 us
    ppermute x5, starting transfers between devices, halo_layers(): before = lax.ppermute(last, GRID, up).astype(shard.dtype)  10.8 us
    dot_general x5, matrix products, apply_hamiltonian(): jnp.einsum('pq,zqo->zpo', plane, flat, precision=lax.Precision.HIGH, pref...  8.56 us
  transfers between devices with their start and end apart: 18, of which 9 were waited for; matrix products, arithmetic and copies ran while one was open for 10% of the time, Pallas kernels for 0%

profile of v7, /device:TPU:6, one launch (start us, length us, event | category | flops | bytes accessed | tf_op | source)
XLA Modules:
  0.0 150.5 jit_solution(11903997277485378412)
XLA Ops:
  1.7 10.7 %collective-permute-start = (bf16[4,16,16,128]{3,2,1,0:T(8,128)(2,1)S(1)}, bf16[4,16,16,128]{3,2,1,0:T(8,128)(2,1)S(1)}, u32[]{:S(2)}, u32[]{:S(2)}) collective-permute-start(bf16[4,16,16,128]{3,2,1,0:T(8,128)(2,1)S(1)} %convert_element_type.255), channel_id=1, source_target_pairs={{8,0},{16,8},{24,16},{32,24},{40,32},{48,40},{56,48},{64,56},{72,6... | collective-permute-start | bytes 786440 | tf_op jit(solution)/shard_map/ppermute | solution.py:25
  12.4 1.9 %collective-permute-start.1 = (bf16[4,16,16,128]{3,2,1,0:T(8,128)(2,1)S(1)}, bf16[4,16,16,128]{3,2,1,0:T(8,128)(2,1)S(1)}, u32[]{:S(2)}, u32[]{:S(2)}) collective-permute-start(bf16[4,16,16,128]{3,2,1,0:T(8,128)(2,1)S(1)} %convert_element_type.255), channel_id=1, source_target_pairs={{0,8},{8,16},{16,24},{24,32},{32,40},{40,48},{48,56},{56,64},{64,7... | collective-permute-start | bytes 786440 | tf_op jit(solution)/shard_map/ppermute | solution.py:24
  15.2 2.4 %fusion.112 = f32[256,4,128]{2,0,1:T(8,128)S(1)} fusion(f32[4,256,128]{2,1,0:T(8,128)} %bitcast.128, s32[256]{0:T(256)S(1)} %get-tuple-element.18, s32[256]{0:T(256)S(1)} %get-tuple-element.19), kind=kOutput, calls=%fused_computation.210 | convolution fusion | flops 207618048 | bytes 1050624 | tf_op jit(solution)/shard_map/pq,zqo->zpo/dot_general | solution.py:60
  17.6 4.5 %collective-permute-done.1 = bf16[4,16,16,128]{3,2,1,0:T(8,128)(2,1)S(1)} collective-permute-done((bf16[4,16,16,128]{3,2,1,0:T(8,128)(2,1)S(1)}, bf16[4,16,16,128]{3,2,1,0:T(8,128)(2,1)S(1)}, u32[]{:S(2)}, u32[]{:S(2)}) %collective-permute-start.1) | collective-permute-done | bytes 262176 | tf_op jit(solution)/shard_map/ppermute | solution.py:24
  22.6 2.1 %collective-permute-start.2 = (bf16[4,16,16,128]{3,2,1,0:T(8,128)(2,1)S(1)}, bf16[4,16,16,128]{3,2,1,0:T(8,128)(2,1)S(1)}, u32[]{:S(2)}, u32[]{:S(2)}) collective-permute-start(bf16[4,16,16,128]{3,2,1,0:T(8,128)(2,1)S(1)} %get-tuple-element.11), channel_id=1, source_target_pairs={{8,0},{16,8},{24,16},{32,24},{40,32},{48,40},{56,48},{64,56},{72,6... | collective-permute-start | bytes 786440 | tf_op jit(solution)/shard_map/ppermute | solution.py:25
  24.8 2.2 %collective-permute-start.3 = (bf16[4,16,16,128]{3,2,1,0:T(8,128)(2,1)S(1)}, bf16[4,16,16,128]{3,2,1,0:T(8,128)(2,1)S(1)}, u32[]{:S(2)}, u32[]{:S(2)}) collective-permute-start(bf16[4,16,16,128]{3,2,1,0:T(8,128)(2,1)S(1)} %get-tuple-element.11), channel_id=1, source_target_pairs={{0,8},{8,16},{16,24},{24,32},{32,40},{40,48},{48,56},{56,64},{64,7... | collective-permute-start | bytes 786440 | tf_op jit(solution)/shard_map/ppermute | solution.py:24
  27.0 1.5 %convolution_bitcast_fusion.3 = f32[4,256,128]{1,2,0:T(8,128)S(1)} fusion(f32[4,256,128]{2,1,0:T(8,128)S(1)} %bitcast.130, s32[256]{0:T(256)S(1)} %get-tuple-element.18, s32[256]{0:T(256)S(1)} %get-tuple-element.19), kind=kOutput, calls=%fused_computation.49 | convolution fusion | flops 207618048 | bytes 1050624 | tf_op jit(solution)/shard_map/pq,zqo->zpo/dot_general | solution.py:60
  28.8 5.7 %collective-permute-done.3 = bf16[4,16,16,128]{3,2,1,0:T(8,128)(2,1)S(1)} collective-permute-done((bf16[4,16,16,128]{3,2,1,0:T(8,128)(2,1)S(1)}, bf16[4,16,16,128]{3,2,1,0:T(8,128)(2,1)S(1)}, u32[]{:S(2)}, u32[]{:S(2)}) %collective-permute-start.3) | collective-permute-done | bytes 262176 | tf_op jit(solution)/shard_map/ppermute | solution.py:24
  35.0 1.9 %collective-permute-start.4 = (bf16[4,16,16,128]{3,2,1,0:T(8,128)(2,1)S(1)}, bf16[4,16,16,128]{3,2,1,0:T(8,128)(2,1)S(1)}, u32[]{:S(2)}, u32[]{:S(2)}) collective-permute-start(bf16[4,16,16,128]{3,2,1,0:T(8,128)(2,1)S(1)} %get-tuple-element.9), channel_id=1, source_target_pairs={{8,0},{16,8},{24,16},{32,24},{40,32},{48,40},{56,48},{64,56},{72,6... | collective-permute-start | bytes 786440 | tf_op jit(solution)/shard_map/ppermute | solution.py:25
  37.0 2.4 %collective-permute-start.5 = (bf16[4,16,16,128]{3,2,1,0:T(8,128)(2,1)S(1)}, bf16[4,16,16,128]{3,2,1,0:T(8,128)(2,1)S(1)}, u32[]{:S(2)}, u32[]{:S(2)}) collective-permute-start(bf16[4,16,16,128]{3,2,1,0:T(8,128)(2,1)S(1)} %get-tuple-element.9), channel_id=1, source_target_pairs={{0,8},{8,16},{16,24},{24,32},{32,40},{40,48},{48,56},{56,64},{64,7... | collective-permute-start | bytes 786440 | tf_op jit(solution)/shard_map/ppermute | solution.py:24
  39.4 1.5 %convolution_bitcast_fusion.2 = f32[4,256,128]{1,2,0:T(8,128)S(1)} fusion(f32[4,256,128]{2,1,0:T(8,128)S(1)} %bitcast.129, s32[256]{0:T(256)S(1)} %get-tuple-element.18, s32[256]{0:T(256)S(1)} %get-tuple-element.19), kind=kOutput, calls=%fused_computation.48 | convolution fusion | flops 207618048 | bytes 1050624 | tf_op jit(solution)/shard_map/pq,zqo->zpo/dot_general | solution.py:60
  41.2 5.6 %collective-permute-done.5 = bf16[4,16,16,128]{3,2,1,0:T(8,128)(2,1)S(1)} collective-permute-done((bf16[4,16,16,128]{3,2,1,0:T(8,128)(2,1)S(1)}, bf16[4,16,16,128]{3,2,1,0:T(8,128)(2,1)S(1)}, u32[]{:S(2)}, u32[]{:S(2)}) %collective-permute-start.5) | collective-permute-done | bytes 262176 | tf_op jit(solution)/shard_map/ppermute | solution.py:24
  47.2 1.9 %collective-permute-start.6 = (bf16[4,16,16,128]{3,2,1,0:T(8,128)(2,1)S(1)}, bf16[4,16,16,128]{3,2,1,0:T(8,128)(2,1)S(1)}, u32[]{:S(2)}, u32[]{:S(2)}) collective-permute-start(bf16[4,16,16,128]{3,2,1,0:T(8,128)(2,1)S(1)} %get-tuple-element.7), channel_id=1, source_target_pairs={{8,0},{16,8},{24,16},{32,24},{40,32},{48,40},{56,48},{64,56},{72,6... | collective-permute-start | bytes 786440 | tf_op jit(solution)/shard_map/ppermute | solution.py:25
  49.2 2.4 %collective-permute-start.7 = (bf16[4,16,16,128]{3,2,1,0:T(8,128)(2,1)S(1)}, bf16[4,16,16,128]{3,2,1,0:T(8,128)(2,1)S(1)}, u32[]{:S(2)}, u32[]{:S(2)}) collective-permute-start(bf16[4,16,16,128]{3,2,1,0:T(8,128)(2,1)S(1)} %get-tuple-element.7), channel_id=1, source_target_pairs={{0,8},{8,16},{16,24},{24,32},{32,40},{40,48},{48,56},{56,64},{64,7... | collective-permute-start | bytes 786440 | tf_op jit(solution)/shard_map/ppermute | solution.py:24
  51.6 1.5 %convolution_bitcast_fusion.1 = f32[4,256,128]{1,2,0:T(8,128)S(1)} fusion(f32[4,256,128]{2,1,0:T(8,128)S(1)} %bitcast.135, s32[256]{0:T(256)S(1)} %get-tuple-element.18, s32[256]{0:T(256)S(1)} %get-tuple-element.19), kind=kOutput, calls=%fused_computation.47 | convolution fusion | flops 207618048 | bytes 1050624 | tf_op jit(solution)/shard_map/pq,zqo->zpo/dot_general | solution.py:60
  53.4 5.6 %collective-permute-done.7 = bf16[4,16,16,128]{3,2,1,0:T(8,128)(2,1)S(1)} collective-permute-done((bf16[4,16,16,128]{3,2,1,0:T(8,128)(2,1)S(1)}, bf16[4,16,16,128]{3,2,1,0:T(8,128)(2,1)S(1)}, u32[]{:S(2)}, u32[]{:S(2)}) %collective-permute-start.7) | collective-permute-done | bytes 262176 | tf_op jit(solution)/shard_map/ppermute | solution.py:24
  59.6 1.9 %collective-permute-start.9 = (bf16[4,16,16,128]{3,2,1,0:T(8,128)(2,1)S(1)}, bf16[4,16,16,128]{3,2,1,0:T(8,128)(2,1)S(1)}, u32[]{:S(2)}, u32[]{:S(2)}) collective-permute-start(bf16[4,16,16,128]{3,2,1,0:T(8,128)(2,1)S(1)} %get-tuple-element.6), channel_id=1, source_target_pairs={{0,8},{8,16},{16,24},{24,32},{32,40},{40,48},{48,56},{56,64},{64,7... | collective-permute-start | bytes 786440 | tf_op jit(solution)/shard_map/ppermute | solution.py:24
  61.5 5.8 %collective-permute-start.8 = (bf16[4,16,16,128]{3,2,1,0:T(8,128)(2,1)S(1)}, bf16[4,16,16,128]{3,2,1,0:T(8,128)(2,1)S(1)}, u32[]{:S(2)}, u32[]{:S(2)}) collective-permute-start(bf16[4,16,16,128]{3,2,1,0:T(8,128)(2,1)S(1)} %get-tuple-element.6), channel_id=1, source_target_pairs={{8,0},{16,8},{24,16},{32,24},{40,32},{48,40},{56,48},{64,56},{72,6... | collective-permute-start | bytes 786440 | tf_op jit(solution)/shard_map/ppermute | solution.py:25
  67.3 5.4 %collective-permute-start.10 = (bf16[1024,128]{1,0:T(8,128)(2,1)S(1)}, bf16[1024,128]{1,0:T(8,128)(2,1)S(1)}, u32[]{:S(2)}, u32[]{:S(2)}) collective-permute-start(bf16[1024,128]{1,0:T(8,128)(2,1)S(1)} %bitcast.118), channel_id=1, source_target_pairs={{0,7},{1,0},{2,1},{3,2},{4,3},{5,4},{6,5},{7,6},{8,15},{9,8},{10,9... | collective-permute-start | bytes 786440 | tf_op jit(solution)/shard_map/ppermute | solution.py:122
  72.7 2.1 %collective-permute-start.13 = (bf16[1024,128]{1,0:T(8,128)(2,1)S(1)}, bf16[1024,128]{1,0:T(8,128)(2,1)S(1)}, u32[]{:S(2)}, u32[]{:S(2)}) collective-permute-start(bf16[1024,128]{1,0:T(8,128)(2,1)S(1)} %bitcast.119), channel_id=1, source_target_pairs={{0,1},{1,2},{2,3},{3,4},{4,5},{5,6},{6,7},{7,0},{8,9},{9,10},{10,1... | collective-permute-start | bytes 786440 | tf_op jit(solution)/shard_map/ppermute | solution.py:119
  74.8 1.5 %convolution_bitcast_fusion = f32[4,256,128]{1,2,0:T(8,128)S(1)} fusion(f32[4,256,128]{2,1,0:T(8,128)S(1)} %bitcast.127, s32[256]{0:T(256)S(1)} %get-tuple-element.18, s32[256]{0:T(256)S(1)} %get-tuple-element.19), kind=kOutput, calls=%fused_computation.46 | convolution fusion | flops 207618048 | bytes 1050624 | tf_op jit(solution)/shard_map/pq,zqo->zpo/dot_general | solution.py:60
  77.9 5.1 %collective-permute-start.11 = (bf16[1024,128]{1,0:T(8,128)(2,1)S(1)}, bf16[1024,128]{1,0:T(8,128)(2,1)S(1)}, u32[]{:S(2)}, u32[]{:S(2)}) collective-permute-start(bf16[1024,128]{1,0:T(8,128)(2,1)S(1)} %collective-permute-done.10), channel_id=1, source_target_pairs={{0,7},{1,0},{2,1},{3,2},{4,3},{5,4},{6,5},{7,6},{8,15},{9,8},{10,9... | collective-permute-start | bytes 786440 | tf_op jit(solution)/shard_map/ppermute | solution.py:122
  83.6 1.9 %collective-permute-start.14 = (bf16[1024,128]{1,0:T(8,128)(2,1)S(1)}, bf16[1024,128]{1,0:T(8,128)(2,1)S(1)}, u32[]{:S(2)}, u32[]{:S(2)}) collective-permute-start(bf16[1024,128]{1,0:T(8,128)(2,1)S(1)} %collective-permute-done.13), channel_id=1, source_target_pairs={{0,1},{1,2},{2,3},{3,4},{4,5},{5,6},{6,7},{7,0},{8,9},{9,10},{10,1... | collective-permute-start | bytes 786440 | tf_op jit(solution)/shard_map/ppermute | solution.py:119
  86.9 5.6 %collective-permute-start.12 = (bf16[1024,128]{1,0:T(8,128)(2,1)S(1)}, bf16[1024,128]{1,0:T(8,128)(2,1)S(1)}, u32[]{:S(2)}, u32[]{:S(2)}) collective-permute-start(bf16[1024,128]{1,0:T(8,128)(2,1)S(1)} %collective-permute-done.11), channel_id=1, source_target_pairs={{0,7},{1,0},{2,1},{3,2},{4,3},{5,4},{6,5},{7,6},{8,15},{9,8},{10,9... | collective-permute-start | bytes 786440 | tf_op jit(solution)/shard_map/ppermute | solution.py:122
  93.2 1.9 %collective-permute-start.15 = (bf16[1024,128]{1,0:T(8,128)(2,1)S(1)}, bf16[1024,128]{1,0:T(8,128)(2,1)S(1)}, u32[]{:S(2)}, u32[]{:S(2)}) collective-permute-start(bf16[1024,128]{1,0:T(8,128)(2,1)S(1)} %collective-permute-done.14), channel_id=1, source_target_pairs={{0,1},{1,2},{2,3},{3,4},{4,5},{5,6},{6,7},{7,0},{8,9},{9,10},{10,1... | collective-permute-start | bytes 786440 | tf_op jit(solution)/shard_map/ppermute | solution.py:119
  96.6 6.9 %collective-permute-done.15 = bf16[1024,128]{1,0:T(8,128)(2,1)S(1)} collective-permute-done((bf16[1024,128]{1,0:T(8,128)(2,1)S(1)}, bf16[1024,128]{1,0:T(8,128)(2,1)S(1)}, u32[]{:S(2)}, u32[]{:S(2)}) %collective-permute-start.15) | collective-permute-done | bytes 262176 | tf_op jit(solution)/shard_map/ppermute | solution.py:119
  103.5 1.9 %collective-permute-start.16 = (bf16[1024,128]{1,0:T(8,128)(2,1)S(1)}, bf16[1024,128]{1,0:T(8,128)(2,1)S(1)}, u32[]{:S(2)}, u32[]{:S(2)}) collective-permute-start(bf16[1024,128]{1,0:T(8,128)(2,1)S(1)} %collective-permute-done.15), channel_id=1, source_target_pairs={{0,1},{1,2},{2,3},{3,4},{4,5},{5,6},{6,7},{7,0},{8,9},{9,10},{10,1... | collective-permute-start | bytes 786440 | tf_op jit(solution)/shard_map/ppermute | solution.py:119
  106.2 6.8 %collective-permute-done.16 = bf16[1024,128]{1,0:T(8,128)(2,1)S(1)} collective-permute-done((bf16[1024,128]{1,0:T(8,128)(2,1)S(1)}, bf16[1024,128]{1,0:T(8,128)(2,1)S(1)}, u32[]{:S(2)}, u32[]{:S(2)}) %collective-permute-start.16) | collective-permute-done | bytes 262176 | tf_op jit(solution)/shard_map/ppermute | solution.py:119
  120.0 1.9 %collective-permute-start.17 = (f32[32,17,256]{2,0,1:T(8,128)S(1)}, f32[32,17,256]{2,0,1:T(8,128)S(1)}, u32[]{:S(2)}, u32[]{:S(2)}) collective-permute-start(f32[32,17,256]{2,0,1:T(8,128)S(1)} %bitcast.136), channel_id=1, source_target_pairs={{0,8},{8,0},{1,9},{9,1},{2,10},{10,2},{3,11},{11,3},{4,12},{12,4},... | collective-permute-start | bytes 1671176 | tf_op jit(solution)/shard_map/ppermute | solution.py:106
  121.9 1.9 %collective-permute-done.17 = f32[32,17,256]{2,0,1:T(8,128)S(1)} collective-permute-done((f32[32,17,256]{2,0,1:T(8,128)S(1)}, f32[32,17,256]{2,0,1:T(8,128)S(1)}, u32[]{:S(2)}, u32[]{:S(2)}) %collective-permute-start.17) | collective-permute-done | bytes 557088 | tf_op jit(solution)/shard_map/ppermute | solution.py:106
  124.1 12.4 %all_to_all.10 = f32[4,8,17,256]{3,1,2,0:T(8,128)S(1)} all-to-all(f32[4,8,17,256]{3,1,2,0:T(8,128)S(1)} %copy.95), channel_id=1, replica_groups=mesh['x'=4,'z'=8,'core'=2,'orb'=8] {'x'}, dimensions={0} | all-to-all | bytes 1114112 | tf_op jit(solution)/shard_map/all_to_all | solution.py:108
  136.6 12.3 %all_to_all.11 = f32[8,17,256]{2,1,0:T(8,128)S(1)} all-to-all(f32[8,17,256]{2,1,0:T(8,128)S(1)} %copy.97), channel_id=1, replica_groups=mesh['x'=4,'z'=8,'core'=2,'orb'=8] {'z'}, dimensions={0} | all-to-all | bytes 278528 | tf_op jit(solution)/shard_map/all_to_all | solution.py:109
  (99 shorter events, 19.9 us)
Async XLA Ops:
  1.7 15.9 %collective-permute-start = (bf16[4,16,16,128]{3,2,1,0:T(8,128)(2,1)S(1)}, bf16[4,16,16,128]{3,2,1,0:T(8,128)(2,1)S(1)}, u32[]{:S(2)}, u32[]{:S(2)}) collective-permute-start(bf16[4,16,16,128]{3,2,1,0:T(8,128)(2,1)S(1)} %convert_element_type.255), channel_id=1, source_target_pairs={{8,0},{16,8},{24,16},{32,24},{40,32},{48,40},{56,48},{64,56},{72,6... | collective-permute-start | bytes 786440 | tf_op jit(solution)/shard_map/ppermute | solution.py:25
  12.4 9.8 %collective-permute-start.1 = (bf16[4,16,16,128]{3,2,1,0:T(8,128)(2,1)S(1)}, bf16[4,16,16,128]{3,2,1,0:T(8,128)(2,1)S(1)}, u32[]{:S(2)}, u32[]{:S(2)}) collective-permute-start(bf16[4,16,16,128]{3,2,1,0:T(8,128)(2,1)S(1)} %convert_element_type.255), channel_id=1, source_target_pairs={{0,8},{8,16},{16,24},{24,32},{32,40},{40,48},{48,56},{56,64},{64,7... | collective-permute-start | bytes 786440 | tf_op jit(solution)/shard_map/ppermute | solution.py:24
  17.6 4.7 %copy-start = (f32[4,16,16,128]{3,2,1,0:T(8,128)S(1)}, f32[4,16,16,128]{3,2,1,0:T(8,128)}, u32[]{:S(2)}) copy-start(f32[4,16,16,128]{3,2,1,0:T(8,128)} %param.2) | copy-start | bytes 1572868
  17.6 4.7 %copy-start.1 = (f32[4,16,16]{2,1,0:T(8,128)S(1)}, f32[4,16,16]{2,1,0:T(8,128)}, u32[]{:S(2)}) copy-start(f32[4,16,16]{2,1,0:T(8,128)} %param.3) | copy-start | bytes 12292
  22.6 6.2 %collective-permute-start.2 = (bf16[4,16,16,128]{3,2,1,0:T(8,128)(2,1)S(1)}, bf16[4,16,16,128]{3,2,1,0:T(8,128)(2,1)S(1)}, u32[]{:S(2)}, u32[]{:S(2)}) collective-permute-start(bf16[4,16,16,128]{3,2,1,0:T(8,128)(2,1)S(1)} %get-tuple-element.11), channel_id=1, source_target_pairs={{8,0},{16,8},{24,16},{32,24},{40,32},{48,40},{56,48},{64,56},{72,6... | collective-permute-start | bytes 786440 | tf_op jit(solution)/shard_map/ppermute | solution.py:25
  24.8 9.8 %collective-permute-start.3 = (bf16[4,16,16,128]{3,2,1,0:T(8,128)(2,1)S(1)}, bf16[4,16,16,128]{3,2,1,0:T(8,128)(2,1)S(1)}, u32[]{:S(2)}, u32[]{:S(2)}) collective-permute-start(bf16[4,16,16,128]{3,2,1,0:T(8,128)(2,1)S(1)} %get-tuple-element.11), channel_id=1, source_target_pairs={{0,8},{8,16},{16,24},{24,32},{32,40},{40,48},{48,56},{56,64},{64,7... | collective-permute-start | bytes 786440 | tf_op jit(solution)/shard_map/ppermute | solution.py:24
  35.0 6.1 %collective-permute-start.4 = (bf16[4,16,16,128]{3,2,1,0:T(8,128)(2,1)S(1)}, bf16[4,16,16,128]{3,2,1,0:T(8,128)(2,1)S(1)}, u32[]{:S(2)}, u32[]{:S(2)}) collective-permute-start(bf16[4,16,16,128]{3,2,1,0:T(8,128)(2,1)S(1)} %get-tuple-element.9), channel_id=1, source_target_pairs={{8,0},{16,8},{24,16},{32,24},{40,32},{48,40},{56,48},{64,56},{72,6... | collective-permute-start | bytes 786440 | tf_op jit(solution)/shard_map/ppermute | solution.py:25
  37.0 9.8 %collective-permute-start.5 = (bf16[4,16,16,128]{3,2,1,0:T(8,128)(2,1)S(1)}, bf16[4,16,16,128]{3,2,1,0:T(8,128)(2,1)S(1)}, u32[]{:S(2)}, u32[]{:S(2)}) collective-permute-start(bf16[4,16,16,128]{3,2,1,0:T(8,128)(2,1)S(1)} %get-tuple-element.9), channel_id=1, source_target_pairs={{0,8},{8,16},{16,24},{24,32},{32,40},{40,48},{48,56},{56,64},{64,7... | collective-permute-start | bytes 786440 | tf_op jit(solution)/shard_map/ppermute | solution.py:24
  47.2 6.1 %collective-permute-start.6 = (bf16[4,16,16,128]{3,2,1,0:T(8,128)(2,1)S(1)}, bf16[4,16,16,128]{3,2,1,0:T(8,128)(2,1)S(1)}, u32[]{:S(2)}, u32[]{:S(2)}) collective-permute-start(bf16[4,16,16,128]{3,2,1,0:T(8,128)(2,1)S(1)} %get-tuple-element.7), channel_id=1, source_target_pairs={{8,0},{16,8},{24,16},{32,24},{40,32},{48,40},{56,48},{64,56},{72,6... | collective-permute-start | bytes 786440 | tf_op jit(solution)/shard_map/ppermute | solution.py:25
  49.2 9.8 %collective-permute-start.7 = (bf16[4,16,16,128]{3,2,1,0:T(8,128)(2,1)S(1)}, bf16[4,16,16,128]{3,2,1,0:T(8,128)(2,1)S(1)}, u32[]{:S(2)}, u32[]{:S(2)}) collective-permute-start(bf16[4,16,16,128]{3,2,1,0:T(8,128)(2,1)S(1)} %get-tuple-element.7), channel_id=1, source_target_pairs={{0,8},{8,16},{16,24},{24,32},{32,40},{40,48},{48,56},{56,64},{64,7... | collective-permute-start | bytes 786440 | tf_op jit(solution)/shard_map/ppermute | solution.py:24
  59.6 17.4 %collective-permute-start.9 = (bf16[4,16,16,128]{3,2,1,0:T(8,128)(2,1)S(1)}, bf16[4,16,16,128]{3,2,1,0:T(8,128)(2,1)S(1)}, u32[]{:S(2)}, u32[]{:S(2)}) collective-permute-start(bf16[4,16,16,128]{3,2,1,0:T(8,128)(2,1)S(1)} %get-tuple-element.6), channel_id=1, source_target_pairs={{0,8},{8,16},{16,24},{24,32},{32,40},{40,48},{48,56},{56,64},{64,7... | collective-permute-start | bytes 786440 | tf_op jit(solution)/shard_map/ppermute | solution.py:24
  61.5 15.5 %collective-permute-start.8 = (bf16[4,16,16,128]{3,2,1,0:T(8,128)(2,1)S(1)}, bf16[4,16,16,128]{3,2,1,0:T(8,128)(2,1)S(1)}, u32[]{:S(2)}, u32[]{:S(2)}) collective-permute-start(bf16[4,16,16,128]{3,2,1,0:T(8,128)(2,1)S(1)} %get-tuple-element.6), channel_id=1, source_target_pairs={{8,0},{16,8},{24,16},{32,24},{40,32},{48,40},{56,48},{64,56},{72,6... | collective-permute-start | bytes 786440 | tf_op jit(solution)/shard_map/ppermute | solution.py:25
  67.3 10.4 %collective-permute-start.10 = (bf16[1024,128]{1,0:T(8,128)(2,1)S(1)}, bf16[1024,128]{1,0:T(8,128)(2,1)S(1)}, u32[]{:S(2)}, u32[]{:S(2)}) collective-permute-start(bf16[1024,128]{1,0:T(8,128)(2,1)S(1)} %bitcast.118), channel_id=1, source_target_pairs={{0,7},{1,0},{2,1},{3,2},{4,3},{5,4},{6,5},{7,6},{8,15},{9,8},{10,9... | collective-permute-start | bytes 786440 | tf_op jit(solution)/shard_map/ppermute | solution.py:122
  72.7 10.7 %collective-permute-start.13 = (bf16[1024,128]{1,0:T(8,128)(2,1)S(1)}, bf16[1024,128]{1,0:T(8,128)(2,1)S(1)}, u32[]{:S(2)}, u32[]{:S(2)}) collective-permute-start(bf16[1024,128]{1,0:T(8,128)(2,1)S(1)} %bitcast.119), channel_id=1, source_target_pairs={{0,1},{1,2},{2,3},{3,4},{4,5},{5,6},{6,7},{7,0},{8,9},{9,10},{10,1... | collective-permute-start | bytes 786440 | tf_op jit(solution)/shard_map/ppermute | solution.py:119
  77.9 9.0 %collective-permute-start.11 = (bf16[1024,128]{1,0:T(8,128)(2,1)S(1)}, bf16[1024,128]{1,0:T(8,128)(2,1)S(1)}, u32[]{:S(2)}, u32[]{:S(2)}) collective-permute-start(bf16[1024,128]{1,0:T(8,128)(2,1)S(1)} %collective-permute-done.10), channel_id=1, source_target_pairs={{0,7},{1,0},{2,1},{3,2},{4,3},{5,4},{6,5},{7,6},{8,15},{9,8},{10,9... | collective-permute-start | bytes 786440 | tf_op jit(solution)/shard_map/ppermute | solution.py:122
  83.6 9.7 %collective-permute-start.14 = (bf16[1024,128]{1,0:T(8,128)(2,1)S(1)}, bf16[1024,128]{1,0:T(8,128)(2,1)S(1)}, u32[]{:S(2)}, u32[]{:S(2)}) collective-permute-start(bf16[1024,128]{1,0:T(8,128)(2,1)S(1)} %collective-permute-done.13), channel_id=1, source_target_pairs={{0,1},{1,2},{2,3},{3,4},{4,5},{5,6},{6,7},{7,0},{8,9},{9,10},{10,1... | collective-permute-start | bytes 786440 | tf_op jit(solution)/shard_map/ppermute | solution.py:119
  86.9 9.5 %collective-permute-start.12 = (bf16[1024,128]{1,0:T(8,128)(2,1)S(1)}, bf16[1024,128]{1,0:T(8,128)(2,1)S(1)}, u32[]{:S(2)}, u32[]{:S(2)}) collective-permute-start(bf16[1024,128]{1,0:T(8,128)(2,1)S(1)} %collective-permute-done.11), channel_id=1, source_target_pairs={{0,7},{1,0},{2,1},{3,2},{4,3},{5,4},{6,5},{7,6},{8,15},{9,8},{10,9... | collective-permute-start | bytes 786440 | tf_op jit(solution)/shard_map/ppermute | solution.py:122
  93.2 10.3 %collective-permute-start.15 = (bf16[1024,128]{1,0:T(8,128)(2,1)S(1)}, bf16[1024,128]{1,0:T(8,128)(2,1)S(1)}, u32[]{:S(2)}, u32[]{:S(2)}) collective-permute-start(bf16[1024,128]{1,0:T(8,128)(2,1)S(1)} %collective-permute-done.14), channel_id=1, source_target_pairs={{0,1},{1,2},{2,3},{3,4},{4,5},{5,6},{6,7},{7,0},{8,9},{9,10},{10,1... | collective-permute-start | bytes 786440 | tf_op jit(solution)/shard_map/ppermute | solution.py:119
  103.5 9.5 %collective-permute-start.16 = (bf16[1024,128]{1,0:T(8,128)(2,1)S(1)}, bf16[1024,128]{1,0:T(8,128)(2,1)S(1)}, u32[]{:S(2)}, u32[]{:S(2)}) collective-permute-start(bf16[1024,128]{1,0:T(8,128)(2,1)S(1)} %collective-permute-done.15), channel_id=1, source_target_pairs={{0,1},{1,2},{2,3},{3,4},{4,5},{5,6},{6,7},{7,0},{8,9},{9,10},{10,1... | collective-permute-start | bytes 786440 | tf_op jit(solution)/shard_map/ppermute | solution.py:119
  114.1 0.8 copy-start.2
  120.0 3.9 %collective-permute-start.17 = (f32[32,17,256]{2,0,1:T(8,128)S(1)}, f32[32,17,256]{2,0,1:T(8,128)S(1)}, u32[]{:S(2)}, u32[]{:S(2)}) collective-permute-start(f32[32,17,256]{2,0,1:T(8,128)S(1)} %bitcast.136), channel_id=1, source_target_pairs={{0,8},{8,0},{1,9},{9,1},{2,10},{10,2},{3,11},{11,3},{4,12},{12,4},... | collective-permute-start | bytes 1671176 | tf_op jit(solution)/shard_map/ppermute | solution.py:106

commit v8 on v7

--- a/solution.py
+++ b/solution.py
@@ -4,7 +4,7 @@
 from jax.sharding import Mesh, PartitionSpec as P
 
 DEGREE = 4
-GRID = ("x", "z", "core")
+GRID = ("x1", "x0", "z", "core")
 
 
 STENCIL = (-205.0 / 72.0, 8.0 / 5.0, -1.0 / 5.0, 8.0 / 315.0, -1.0 / 560.0)
@@ -104,9 +104,19 @@
     keep = jnp.where(mine == 1, high, low)
     send = jnp.where(mine == 1, low, high)
     chip_part = keep + lax.ppermute(send, "core", [(0, 1), (1, 0)])
-    chip_part = chip_part.reshape((lax.axis_size("x"), lax.axis_size("z")) + slots.shape[1:])
-    row_part = jnp.sum(lax.all_to_all(chip_part, "x", 0, 0, tiled=True), axis=0)
-    return jnp.sum(lax.all_to_all(row_part, "z", 0, 0, tiled=True), axis=0)
+    halves = chip_part.reshape(
+        (lax.axis_size("x1"), lax.axis_size("x0"), lax.axis_size("z")) + slots.shape[1:]
+    )
+    if lax.axis_size("x0") == 2:
+        side = lax.axis_index("x0")
+        low, high = halves[:, 0], halves[:, 1]
+        keep = jnp.where(side == 1, high, low)
+        send = jnp.where(side == 1, low, high)
+        halves = keep + lax.ppermute(send, "x0", [(0, 1), (1, 0)])
+    else:
+        halves = halves[:, 0]
+    received = lax.all_to_all(halves.reshape((-1,) + slots.shape[1:]), ("x1", "z"), 0, 0, tiled=True)
+    return jnp.sum(received, axis=0)
 
 
 def gather_ring(block):
@@ -180,8 +190,11 @@
 def solution(mesh):
     grid_size, orb_size = mesh.devices.shape
     z_size = min(8, grid_size // 2)
+    x_size = grid_size // (2 * z_size)
+    x_low = 2 if x_size % 2 == 0 else 1
     split_mesh = Mesh(
-        mesh.devices.reshape(grid_size // (2 * z_size), z_size, 2, orb_size), ("x", "z", "core", "orb")
+        mesh.devices.reshape(x_size // x_low, x_low, z_size, 2, orb_size),
+        ("x1", "x0", "z", "core", "orb"),
     )
     placed = (P(GRID, None, None, "orb"), P(GRID, None, None))
     return jax.shard_map(

time: 152 us -> 154 us (1.013)
  blocking collectives: 24.7 us -> 15.9 us
  waiting for transfers between devices: 39.1 us -> 47.2 us
  starting transfers between devices: 59.1 us -> 61.5 us
    all_to_all x2 -> x1, blocking collectives: 24.7 us -> 15.9 us  [reduce_scatter_grid(): lax.all_to_all(halves.reshape((-1,) + slots.shape[1:]), ('x1', 'z'), 0, 0...]
    ppermute x0 -> x1, waiting for transfers between devices: none -> 8.14 us  [reduce_scatter_grid(): halves = keep + lax.ppermute(send, 'x0', [(0, 1), (1, 0)])]
    ppermute x0 -> x1, starting transfers between devices: none -> 2.44 us  [reduce_scatter_grid(): halves = keep + lax.ppermute(send, 'x0', [(0, 1), (1, 0)])]
  transfers between devices with their start and end apart: 18 -> 19, of which waited for: 9 -> 10; matrix products, arithmetic and copies ran while one was open for 10% -> 9% of each run, Pallas kernels for 0% -> 0%
where the time goes in v8:
time: 154 us; the launch traced here: 152 us
  starting transfers between devices  61.5 us (40%)
  waiting for transfers between devices  47.2 us (31%)
  blocking collectives  15.9 us (10%)
  matrix products  12.8 us (8%)
  other arithmetic  9.03 us (6%)
  local copies, waits for them, and re-layouts  4.62 us (3%)
    ppermute x5, starting transfers between devices, halo_layers(): after = lax.ppermute(initial, GRID, down).astype(shard.dtype)  22.4 us
    ppermute x5, waiting for transfers between devices, halo_layers(): before = lax.ppermute(last, GRID, up).astype(shard.dtype)  21.4 us
    ppermute x3, starting transfers between devices, gather_ring(): from_right = lax.ppermute(from_right, 'orb', left)  16.1 us
    all_to_all x1, blocking collectives, reduce_scatter_grid(): lax.all_to_all(halves.reshape((-1,) + slots.shape[1:]), ('x1', 'z'), 0, 0...  15.9 us
    ppermute x4, waiting for transfers between devices, gather_ring(): from_left = lax.ppermute(from_left, 'orb', right)  13.6 us
    ppermute x5, starting transfers between devices, halo_layers(): before = lax.ppermute(last, GRID, up).astype(shard.dtype)  10.8 us
    dot_general x5, matrix products, apply_hamiltonian(): jnp.einsum('pq,zqo->zpo', plane, flat, precision=lax.Precision.HIGH, pref...  8.56 us
    ppermute x1, waiting for transfers between devices, reduce_scatter_grid(): halves = keep + lax.ppermute(send, 'x0', [(0, 1), (1, 0)])  8.14 us
  transfers between devices with their start and end apart: 19, of which 10 were waited for; matrix products, arithmetic and copies ran while one was open for 9% of the time, Pallas kernels for 0%

profile of v8, /device:TPU:6, one launch (start us, length us, event | category | flops | bytes accessed | tf_op | source)
XLA Modules:
  0.0 152.4 jit_solution(17256816372065126975)
XLA Ops:
  1.7 10.7 %collective-permute-start = (bf16[4,16,16,128]{3,2,1,0:T(8,128)(2,1)S(1)}, bf16[4,16,16,128]{3,2,1,0:T(8,128)(2,1)S(1)}, u32[]{:S(2)}, u32[]{:S(2)}) collective-permute-start(bf16[4,16,16,128]{3,2,1,0:T(8,128)(2,1)S(1)} %convert_element_type.255), channel_id=1, source_target_pairs={{8,0},{16,8},{24,16},{32,24},{40,32},{48,40},{56,48},{64,56},{72,6... | collective-permute-start | bytes 786440 | tf_op jit(solution)/shard_map/ppermute | solution.py:25
  12.4 1.9 %collective-permute-start.1 = (bf16[4,16,16,128]{3,2,1,0:T(8,128)(2,1)S(1)}, bf16[4,16,16,128]{3,2,1,0:T(8,128)(2,1)S(1)}, u32[]{:S(2)}, u32[]{:S(2)}) collective-permute-start(bf16[4,16,16,128]{3,2,1,0:T(8,128)(2,1)S(1)} %convert_element_type.255), channel_id=1, source_target_pairs={{0,8},{8,16},{16,24},{24,32},{32,40},{40,48},{48,56},{56,64},{64,7... | collective-permute-start | bytes 786440 | tf_op jit(solution)/shard_map/ppermute | solution.py:24
  15.2 2.4 %fusion.114 = f32[256,4,128]{2,0,1:T(8,128)S(1)} fusion(f32[4,256,128]{2,1,0:T(8,128)} %bitcast.151, s32[256]{0:T(256)S(1)} %get-tuple-element.18, s32[256]{0:T(256)S(1)} %get-tuple-element.19), kind=kOutput, calls=%fused_computation.214 | convolution fusion | flops 207618048 | bytes 1050624 | tf_op jit(solution)/shard_map/pq,zqo->zpo/dot_general | solution.py:60
  17.6 4.5 %collective-permute-done.1 = bf16[4,16,16,128]{3,2,1,0:T(8,128)(2,1)S(1)} collective-permute-done((bf16[4,16,16,128]{3,2,1,0:T(8,128)(2,1)S(1)}, bf16[4,16,16,128]{3,2,1,0:T(8,128)(2,1)S(1)}, u32[]{:S(2)}, u32[]{:S(2)}) %collective-permute-start.1) | collective-permute-done | bytes 262176 | tf_op jit(solution)/shard_map/ppermute | solution.py:24
  22.6 2.1 %collective-permute-start.2 = (bf16[4,16,16,128]{3,2,1,0:T(8,128)(2,1)S(1)}, bf16[4,16,16,128]{3,2,1,0:T(8,128)(2,1)S(1)}, u32[]{:S(2)}, u32[]{:S(2)}) collective-permute-start(bf16[4,16,16,128]{3,2,1,0:T(8,128)(2,1)S(1)} %get-tuple-element.11), channel_id=1, source_target_pairs={{8,0},{16,8},{24,16},{32,24},{40,32},{48,40},{56,48},{64,56},{72,6... | collective-permute-start | bytes 786440 | tf_op jit(solution)/shard_map/ppermute | solution.py:25
  24.8 2.2 %collective-permute-start.3 = (bf16[4,16,16,128]{3,2,1,0:T(8,128)(2,1)S(1)}, bf16[4,16,16,128]{3,2,1,0:T(8,128)(2,1)S(1)}, u32[]{:S(2)}, u32[]{:S(2)}) collective-permute-start(bf16[4,16,16,128]{3,2,1,0:T(8,128)(2,1)S(1)} %get-tuple-element.11), channel_id=1, source_target_pairs={{0,8},{8,16},{16,24},{24,32},{32,40},{40,48},{48,56},{56,64},{64,7... | collective-permute-start | bytes 786440 | tf_op jit(solution)/shard_map/ppermute | solution.py:24
  27.0 1.5 %convolution_bitcast_fusion.3 = f32[4,256,128]{1,2,0:T(8,128)S(1)} fusion(f32[4,256,128]{2,1,0:T(8,128)S(1)} %bitcast.153, s32[256]{0:T(256)S(1)} %get-tuple-element.18, s32[256]{0:T(256)S(1)} %get-tuple-element.19), kind=kOutput, calls=%fused_computation.49 | convolution fusion | flops 207618048 | bytes 1050624 | tf_op jit(solution)/shard_map/pq,zqo->zpo/dot_general | solution.py:60
  28.8 5.7 %collective-permute-done.3 = bf16[4,16,16,128]{3,2,1,0:T(8,128)(2,1)S(1)} collective-permute-done((bf16[4,16,16,128]{3,2,1,0:T(8,128)(2,1)S(1)}, bf16[4,16,16,128]{3,2,1,0:T(8,128)(2,1)S(1)}, u32[]{:S(2)}, u32[]{:S(2)}) %collective-permute-start.3) | collective-permute-done | bytes 262176 | tf_op jit(solution)/shard_map/ppermute | solution.py:24
  35.0 1.9 %collective-permute-start.4 = (bf16[4,16,16,128]{3,2,1,0:T(8,128)(2,1)S(1)}, bf16[4,16,16,128]{3,2,1,0:T(8,128)(2,1)S(1)}, u32[]{:S(2)}, u32[]{:S(2)}) collective-permute-start(bf16[4,16,16,128]{3,2,1,0:T(8,128)(2,1)S(1)} %get-tuple-element.9), channel_id=1, source_target_pairs={{8,0},{16,8},{24,16},{32,24},{40,32},{48,40},{56,48},{64,56},{72,6... | collective-permute-start | bytes 786440 | tf_op jit(solution)/shard_map/ppermute | solution.py:25
  37.0 2.4 %collective-permute-start.5 = (bf16[4,16,16,128]{3,2,1,0:T(8,128)(2,1)S(1)}, bf16[4,16,16,128]{3,2,1,0:T(8,128)(2,1)S(1)}, u32[]{:S(2)}, u32[]{:S(2)}) collective-permute-start(bf16[4,16,16,128]{3,2,1,0:T(8,128)(2,1)S(1)} %get-tuple-element.9), channel_id=1, source_target_pairs={{0,8},{8,16},{16,24},{24,32},{32,40},{40,48},{48,56},{56,64},{64,7... | collective-permute-start | bytes 786440 | tf_op jit(solution)/shard_map/ppermute | solution.py:24
  39.4 1.5 %convolution_bitcast_fusion.2 = f32[4,256,128]{1,2,0:T(8,128)S(1)} fusion(f32[4,256,128]{2,1,0:T(8,128)S(1)} %bitcast.152, s32[256]{0:T(256)S(1)} %get-tuple-element.18, s32[256]{0:T(256)S(1)} %get-tuple-element.19), kind=kOutput, calls=%fused_computation.48 | convolution fusion | flops 207618048 | bytes 1050624 | tf_op jit(solution)/shard_map/pq,zqo->zpo/dot_general | solution.py:60
  41.2 5.6 %collective-permute-done.5 = bf16[4,16,16,128]{3,2,1,0:T(8,128)(2,1)S(1)} collective-permute-done((bf16[4,16,16,128]{3,2,1,0:T(8,128)(2,1)S(1)}, bf16[4,16,16,128]{3,2,1,0:T(8,128)(2,1)S(1)}, u32[]{:S(2)}, u32[]{:S(2)}) %collective-permute-start.5) | collective-permute-done | bytes 262176 | tf_op jit(solution)/shard_map/ppermute | solution.py:24
  47.2 1.9 %collective-permute-start.6 = (bf16[4,16,16,128]{3,2,1,0:T(8,128)(2,1)S(1)}, bf16[4,16,16,128]{3,2,1,0:T(8,128)(2,1)S(1)}, u32[]{:S(2)}, u32[]{:S(2)}) collective-permute-start(bf16[4,16,16,128]{3,2,1,0:T(8,128)(2,1)S(1)} %get-tuple-element.7), channel_id=1, source_target_pairs={{8,0},{16,8},{24,16},{32,24},{40,32},{48,40},{56,48},{64,56},{72,6... | collective-permute-start | bytes 786440 | tf_op jit(solution)/shard_map/ppermute | solution.py:25
  49.2 2.4 %collective-permute-start.7 = (bf16[4,16,16,128]{3,2,1,0:T(8,128)(2,1)S(1)}, bf16[4,16,16,128]{3,2,1,0:T(8,128)(2,1)S(1)}, u32[]{:S(2)}, u32[]{:S(2)}) collective-permute-start(bf16[4,16,16,128]{3,2,1,0:T(8,128)(2,1)S(1)} %get-tuple-element.7), channel_id=1, source_target_pairs={{0,8},{8,16},{16,24},{24,32},{32,40},{40,48},{48,56},{56,64},{64,7... | collective-permute-start | bytes 786440 | tf_op jit(solution)/shard_map/ppermute | solution.py:24
  51.6 1.5 %convolution_bitcast_fusion.1 = f32[4,256,128]{1,2,0:T(8,128)S(1)} fusion(f32[4,256,128]{2,1,0:T(8,128)S(1)} %bitcast.158, s32[256]{0:T(256)S(1)} %get-tuple-element.18, s32[256]{0:T(256)S(1)} %get-tuple-element.19), kind=kOutput, calls=%fused_computation.47 | convolution fusion | flops 207618048 | bytes 1050624 | tf_op jit(solution)/shard_map/pq,zqo->zpo/dot_general | solution.py:60
  53.4 5.6 %collective-permute-done.7 = bf16[4,16,16,128]{3,2,1,0:T(8,128)(2,1)S(1)} collective-permute-done((bf16[4,16,16,128]{3,2,1,0:T(8,128)(2,1)S(1)}, bf16[4,16,16,128]{3,2,1,0:T(8,128)(2,1)S(1)}, u32[]{:S(2)}, u32[]{:S(2)}) %collective-permute-start.7) | collective-permute-done | bytes 262176 | tf_op jit(solution)/shard_map/ppermute | solution.py:24
  59.6 1.9 %collective-permute-start.9 = (bf16[4,16,16,128]{3,2,1,0:T(8,128)(2,1)S(1)}, bf16[4,16,16,128]{3,2,1,0:T(8,128)(2,1)S(1)}, u32[]{:S(2)}, u32[]{:S(2)}) collective-permute-start(bf16[4,16,16,128]{3,2,1,0:T(8,128)(2,1)S(1)} %get-tuple-element.6), channel_id=1, source_target_pairs={{0,8},{8,16},{16,24},{24,32},{32,40},{40,48},{48,56},{56,64},{64,7... | collective-permute-start | bytes 786440 | tf_op jit(solution)/shard_map/ppermute | solution.py:24
  61.5 5.8 %collective-permute-start.8 = (bf16[4,16,16,128]{3,2,1,0:T(8,128)(2,1)S(1)}, bf16[4,16,16,128]{3,2,1,0:T(8,128)(2,1)S(1)}, u32[]{:S(2)}, u32[]{:S(2)}) collective-permute-start(bf16[4,16,16,128]{3,2,1,0:T(8,128)(2,1)S(1)} %get-tuple-element.6), channel_id=1, source_target_pairs={{8,0},{16,8},{24,16},{32,24},{40,32},{48,40},{56,48},{64,56},{72,6... | collective-permute-start | bytes 786440 | tf_op jit(solution)/shard_map/ppermute | solution.py:25
  67.3 5.4 %collective-permute-start.10 = (bf16[1024,128]{1,0:T(8,128)(2,1)S(1)}, bf16[1024,128]{1,0:T(8,128)(2,1)S(1)}, u32[]{:S(2)}, u32[]{:S(2)}) collective-permute-start(bf16[1024,128]{1,0:T(8,128)(2,1)S(1)} %bitcast.139), channel_id=1, source_target_pairs={{0,7},{1,0},{2,1},{3,2},{4,3},{5,4},{6,5},{7,6},{8,15},{9,8},{10,9... | collective-permute-start | bytes 786440 | tf_op jit(solution)/shard_map/ppermute | solution.py:132
  72.7 2.1 %collective-permute-start.13 = (bf16[1024,128]{1,0:T(8,128)(2,1)S(1)}, bf16[1024,128]{1,0:T(8,128)(2,1)S(1)}, u32[]{:S(2)}, u32[]{:S(2)}) collective-permute-start(bf16[1024,128]{1,0:T(8,128)(2,1)S(1)} %bitcast.140), channel_id=1, source_target_pairs={{0,1},{1,2},{2,3},{3,4},{4,5},{5,6},{6,7},{7,0},{8,9},{9,10},{10,1... | collective-permute-start | bytes 786440 | tf_op jit(solution)/shard_map/ppermute | solution.py:129
  77.9 5.1 %collective-permute-start.11 = (bf16[1024,128]{1,0:T(8,128)(2,1)S(1)}, bf16[1024,128]{1,0:T(8,128)(2,1)S(1)}, u32[]{:S(2)}, u32[]{:S(2)}) collective-permute-start(bf16[1024,128]{1,0:T(8,128)(2,1)S(1)} %collective-permute-done.10), channel_id=1, source_target_pairs={{0,7},{1,0},{2,1},{3,2},{4,3},{5,4},{6,5},{7,6},{8,15},{9,8},{10,9... | collective-permute-start | bytes 786440 | tf_op jit(solution)/shard_map/ppermute | solution.py:132
  83.6 1.9 %collective-permute-start.14 = (bf16[1024,128]{1,0:T(8,128)(2,1)S(1)}, bf16[1024,128]{1,0:T(8,128)(2,1)S(1)}, u32[]{:S(2)}, u32[]{:S(2)}) collective-permute-start(bf16[1024,128]{1,0:T(8,128)(2,1)S(1)} %collective-permute-done.13), channel_id=1, source_target_pairs={{0,1},{1,2},{2,3},{3,4},{4,5},{5,6},{6,7},{7,0},{8,9},{9,10},{10,1... | collective-permute-start | bytes 786440 | tf_op jit(solution)/shard_map/ppermute | solution.py:129
  86.9 5.6 %collective-permute-start.12 = (bf16[1024,128]{1,0:T(8,128)(2,1)S(1)}, bf16[1024,128]{1,0:T(8,128)(2,1)S(1)}, u32[]{:S(2)}, u32[]{:S(2)}) collective-permute-start(bf16[1024,128]{1,0:T(8,128)(2,1)S(1)} %collective-permute-done.11), channel_id=1, source_target_pairs={{0,7},{1,0},{2,1},{3,2},{4,3},{5,4},{6,5},{7,6},{8,15},{9,8},{10,9... | collective-permute-start | bytes 786440 | tf_op jit(solution)/shard_map/ppermute | solution.py:132
  93.2 1.9 %collective-permute-start.15 = (bf16[1024,128]{1,0:T(8,128)(2,1)S(1)}, bf16[1024,128]{1,0:T(8,128)(2,1)S(1)}, u32[]{:S(2)}, u32[]{:S(2)}) collective-permute-start(bf16[1024,128]{1,0:T(8,128)(2,1)S(1)} %collective-permute-done.14), channel_id=1, source_target_pairs={{0,1},{1,2},{2,3},{3,4},{4,5},{5,6},{6,7},{7,0},{8,9},{9,10},{10,1... | collective-permute-start | bytes 786440 | tf_op jit(solution)/shard_map/ppermute | solution.py:129
  96.6 6.9 %collective-permute-done.15 = bf16[1024,128]{1,0:T(8,128)(2,1)S(1)} collective-permute-done((bf16[1024,128]{1,0:T(8,128)(2,1)S(1)}, bf16[1024,128]{1,0:T(8,128)(2,1)S(1)}, u32[]{:S(2)}, u32[]{:S(2)}) %collective-permute-start.15) | collective-permute-done | bytes 262176 | tf_op jit(solution)/shard_map/ppermute | solution.py:129
  103.5 1.9 %collective-permute-start.16 = (bf16[1024,128]{1,0:T(8,128)(2,1)S(1)}, bf16[1024,128]{1,0:T(8,128)(2,1)S(1)}, u32[]{:S(2)}, u32[]{:S(2)}) collective-permute-start(bf16[1024,128]{1,0:T(8,128)(2,1)S(1)} %collective-permute-done.15), channel_id=1, source_target_pairs={{0,1},{1,2},{2,3},{3,4},{4,5},{5,6},{6,7},{7,0},{8,9},{9,10},{10,1... | collective-permute-start | bytes 786440 | tf_op jit(solution)/shard_map/ppermute | solution.py:129
  106.2 6.8 %collective-permute-done.16 = bf16[1024,128]{1,0:T(8,128)(2,1)S(1)} collective-permute-done((bf16[1024,128]{1,0:T(8,128)(2,1)S(1)}, bf16[1024,128]{1,0:T(8,128)(2,1)S(1)}, u32[]{:S(2)}, u32[]{:S(2)}) %collective-permute-start.16) | collective-permute-done | bytes 262176 | tf_op jit(solution)/shard_map/ppermute | solution.py:129
  120.0 1.9 %collective-permute-start.17 = (f32[32,17,256]{2,0,1:T(8,128)S(1)}, f32[32,17,256]{2,0,1:T(8,128)S(1)}, u32[]{:S(2)}, u32[]{:S(2)}) collective-permute-start(f32[32,17,256]{2,0,1:T(8,128)S(1)} %bitcast.159), channel_id=1, source_target_pairs={{0,8},{8,0},{1,9},{9,1},{2,10},{10,2},{3,11},{11,3},{4,12},{12,4},... | collective-permute-start | bytes 1671176 | tf_op jit(solution)/shard_map/ppermute | solution.py:106
  122.0 1.9 %collective-permute-done.17 = f32[32,17,256]{2,0,1:T(8,128)S(1)} collective-permute-done((f32[32,17,256]{2,0,1:T(8,128)S(1)}, f32[32,17,256]{2,0,1:T(8,128)S(1)}, u32[]{:S(2)}, u32[]{:S(2)}) %collective-permute-start.17) | collective-permute-done | bytes 557088 | tf_op jit(solution)/shard_map/ppermute | solution.py:106
  124.0 2.4 %collective-permute-start.18 = (f32[2,8,17,256]{3,1,0,2:T(8,128)S(1)}, f32[2,8,17,256]{3,1,0,2:T(8,128)S(1)}, u32[]{:S(2)}, u32[]{:S(2)}) collective-permute-start(f32[2,8,17,256]{3,1,0,2:T(8,128)S(1)} %select_bitcast_fusion), channel_id=1, source_target_pairs={{0,128},{128,0},{1,129},{129,1},{2,130},{130,2},{3,131},{131,3},{4... | collective-permute-start | bytes 835592 | tf_op jit(solution)/shard_map/ppermute | solution.py:115
  126.5 8.1 %collective-permute-done.18 = f32[2,8,17,256]{3,1,0,2:T(8,128)S(1)} collective-permute-done((f32[2,8,17,256]{3,1,0,2:T(8,128)S(1)}, f32[2,8,17,256]{3,1,0,2:T(8,128)S(1)}, u32[]{:S(2)}, u32[]{:S(2)}) %collective-permute-start.18) | collective-permute-done | bytes 278560 | tf_op jit(solution)/shard_map/ppermute | solution.py:115
  134.9 15.9 %all_to_all.5 = f32[16,17,256]{2,1,0:T(8,128)S(1)} all-to-all(f32[16,17,256]{2,1,0:T(8,128)S(1)} %copy.83), channel_id=1, replica_groups=mesh['x1'=2,'x0'=2,'z'=8,'core'=2,'orb'=8] {'x1','z'}, dimensions={0} | all-to-all | bytes 557056 | tf_op jit(solution)/shard_map/all_to_all | solution.py:118
  (100 shorter events, 21.6 us)
Async XLA Ops:
  1.7 15.9 %collective-permute-start = (bf16[4,16,16,128]{3,2,1,0:T(8,128)(2,1)S(1)}, bf16[4,16,16,128]{3,2,1,0:T(8,128)(2,1)S(1)}, u32[]{:S(2)}, u32[]{:S(2)}) collective-permute-start(bf16[4,16,16,128]{3,2,1,0:T(8,128)(2,1)S(1)} %convert_element_type.255), channel_id=1, source_target_pairs={{8,0},{16,8},{24,16},{32,24},{40,32},{48,40},{56,48},{64,56},{72,6... | collective-permute-start | bytes 786440 | tf_op jit(solution)/shard_map/ppermute | solution.py:25
  12.4 9.8 %collective-permute-start.1 = (bf16[4,16,16,128]{3,2,1,0:T(8,128)(2,1)S(1)}, bf16[4,16,16,128]{3,2,1,0:T(8,128)(2,1)S(1)}, u32[]{:S(2)}, u32[]{:S(2)}) collective-permute-start(bf16[4,16,16,128]{3,2,1,0:T(8,128)(2,1)S(1)} %convert_element_type.255), channel_id=1, source_target_pairs={{0,8},{8,16},{16,24},{24,32},{32,40},{40,48},{48,56},{56,64},{64,7... | collective-permute-start | bytes 786440 | tf_op jit(solution)/shard_map/ppermute | solution.py:24
  17.6 4.7 %copy-start = (f32[4,16,16,128]{3,2,1,0:T(8,128)S(1)}, f32[4,16,16,128]{3,2,1,0:T(8,128)}, u32[]{:S(2)}) copy-start(f32[4,16,16,128]{3,2,1,0:T(8,128)} %param.2) | copy-start | bytes 1572868
  17.6 4.7 %copy-start.1 = (f32[4,16,16]{2,1,0:T(8,128)S(1)}, f32[4,16,16]{2,1,0:T(8,128)}, u32[]{:S(2)}) copy-start(f32[4,16,16]{2,1,0:T(8,128)} %param.3) | copy-start | bytes 12292
  22.6 6.2 %collective-permute-start.2 = (bf16[4,16,16,128]{3,2,1,0:T(8,128)(2,1)S(1)}, bf16[4,16,16,128]{3,2,1,0:T(8,128)(2,1)S(1)}, u32[]{:S(2)}, u32[]{:S(2)}) collective-permute-start(bf16[4,16,16,128]{3,2,1,0:T(8,128)(2,1)S(1)} %get-tuple-element.11), channel_id=1, source_target_pairs={{8,0},{16,8},{24,16},{32,24},{40,32},{48,40},{56,48},{64,56},{72,6... | collective-permute-start | bytes 786440 | tf_op jit(solution)/shard_map/ppermute | solution.py:25
  24.8 9.8 %collective-permute-start.3 = (bf16[4,16,16,128]{3,2,1,0:T(8,128)(2,1)S(1)}, bf16[4,16,16,128]{3,2,1,0:T(8,128)(2,1)S(1)}, u32[]{:S(2)}, u32[]{:S(2)}) collective-permute-start(bf16[4,16,16,128]{3,2,1,0:T(8,128)(2,1)S(1)} %get-tuple-element.11), channel_id=1, source_target_pairs={{0,8},{8,16},{16,24},{24,32},{32,40},{40,48},{48,56},{56,64},{64,7... | collective-permute-start | bytes 786440 | tf_op jit(solution)/shard_map/ppermute | solution.py:24
  35.0 6.1 %collective-permute-start.4 = (bf16[4,16,16,128]{3,2,1,0:T(8,128)(2,1)S(1)}, bf16[4,16,16,128]{3,2,1,0:T(8,128)(2,1)S(1)}, u32[]{:S(2)}, u32[]{:S(2)}) collective-permute-start(bf16[4,16,16,128]{3,2,1,0:T(8,128)(2,1)S(1)} %get-tuple-element.9), channel_id=1, source_target_pairs={{8,0},{16,8},{24,16},{32,24},{40,32},{48,40},{56,48},{64,56},{72,6... | collective-permute-start | bytes 786440 | tf_op jit(solution)/shard_map/ppermute | solution.py:25
  37.0 9.8 %collective-permute-start.5 = (bf16[4,16,16,128]{3,2,1,0:T(8,128)(2,1)S(1)}, bf16[4,16,16,128]{3,2,1,0:T(8,128)(2,1)S(1)}, u32[]{:S(2)}, u32[]{:S(2)}) collective-permute-start(bf16[4,16,16,128]{3,2,1,0:T(8,128)(2,1)S(1)} %get-tuple-element.9), channel_id=1, source_target_pairs={{0,8},{8,16},{16,24},{24,32},{32,40},{40,48},{48,56},{56,64},{64,7... | collective-permute-start | bytes 786440 | tf_op jit(solution)/shard_map/ppermute | solution.py:24
  47.2 6.1 %collective-permute-start.6 = (bf16[4,16,16,128]{3,2,1,0:T(8,128)(2,1)S(1)}, bf16[4,16,16,128]{3,2,1,0:T(8,128)(2,1)S(1)}, u32[]{:S(2)}, u32[]{:S(2)}) collective-permute-start(bf16[4,16,16,128]{3,2,1,0:T(8,128)(2,1)S(1)} %get-tuple-element.7), channel_id=1, source_target_pairs={{8,0},{16,8},{24,16},{32,24},{40,32},{48,40},{56,48},{64,56},{72,6... | collective-permute-start | bytes 786440 | tf_op jit(solution)/shard_map/ppermute | solution.py:25
  49.2 9.8 %collective-permute-start.7 = (bf16[4,16,16,128]{3,2,1,0:T(8,128)(2,1)S(1)}, bf16[4,16,16,128]{3,2,1,0:T(8,128)(2,1)S(1)}, u32[]{:S(2)}, u32[]{:S(2)}) collective-permute-start(bf16[4,16,16,128]{3,2,1,0:T(8,128)(2,1)S(1)} %get-tuple-element.7), channel_id=1, source_target_pairs={{0,8},{8,16},{16,24},{24,32},{32,40},{40,48},{48,56},{56,64},{64,7... | collective-permute-start | bytes 786440 | tf_op jit(solution)/shard_map/ppermute | solution.py:24
  59.6 17.4 %collective-permute-start.9 = (bf16[4,16,16,128]{3,2,1,0:T(8,128)(2,1)S(1)}, bf16[4,16,16,128]{3,2,1,0:T(8,128)(2,1)S(1)}, u32[]{:S(2)}, u32[]{:S(2)}) collective-permute-start(bf16[4,16,16,128]{3,2,1,0:T(8,128)(2,1)S(1)} %get-tuple-element.6), channel_id=1, source_target_pairs={{0,8},{8,16},{16,24},{24,32},{32,40},{40,48},{48,56},{56,64},{64,7... | collective-permute-start | bytes 786440 | tf_op jit(solution)/shard_map/ppermute | solution.py:24
  61.5 15.5 %collective-permute-start.8 = (bf16[4,16,16,128]{3,2,1,0:T(8,128)(2,1)S(1)}, bf16[4,16,16,128]{3,2,1,0:T(8,128)(2,1)S(1)}, u32[]{:S(2)}, u32[]{:S(2)}) collective-permute-start(bf16[4,16,16,128]{3,2,1,0:T(8,128)(2,1)S(1)} %get-tuple-element.6), channel_id=1, source_target_pairs={{8,0},{16,8},{24,16},{32,24},{40,32},{48,40},{56,48},{64,56},{72,6... | collective-permute-start | bytes 786440 | tf_op jit(solution)/shard_map/ppermute | solution.py:25
  67.3 10.4 %collective-permute-start.10 = (bf16[1024,128]{1,0:T(8,128)(2,1)S(1)}, bf16[1024,128]{1,0:T(8,128)(2,1)S(1)}, u32[]{:S(2)}, u32[]{:S(2)}) collective-permute-start(bf16[1024,128]{1,0:T(8,128)(2,1)S(1)} %bitcast.139), channel_id=1, source_target_pairs={{0,7},{1,0},{2,1},{3,2},{4,3},{5,4},{6,5},{7,6},{8,15},{9,8},{10,9... | collective-permute-start | bytes 786440 | tf_op jit(solution)/shard_map/ppermute | solution.py:132
  72.7 10.7 %collective-permute-start.13 = (bf16[1024,128]{1,0:T(8,128)(2,1)S(1)}, bf16[1024,128]{1,0:T(8,128)(2,1)S(1)}, u32[]{:S(2)}, u32[]{:S(2)}) collective-permute-start(bf16[1024,128]{1,0:T(8,128)(2,1)S(1)} %bitcast.140), channel_id=1, source_target_pairs={{0,1},{1,2},{2,3},{3,4},{4,5},{5,6},{6,7},{7,0},{8,9},{9,10},{10,1... | collective-permute-start | bytes 786440 | tf_op jit(solution)/shard_map/ppermute | solution.py:129
  77.9 9.0 %collective-permute-start.11 = (bf16[1024,128]{1,0:T(8,128)(2,1)S(1)}, bf16[1024,128]{1,0:T(8,128)(2,1)S(1)}, u32[]{:S(2)}, u32[]{:S(2)}) collective-permute-start(bf16[1024,128]{1,0:T(8,128)(2,1)S(1)} %collective-permute-done.10), channel_id=1, source_target_pairs={{0,7},{1,0},{2,1},{3,2},{4,3},{5,4},{6,5},{7,6},{8,15},{9,8},{10,9... | collective-permute-start | bytes 786440 | tf_op jit(solution)/shard_map/ppermute | solution.py:132
  83.6 9.7 %collective-permute-start.14 = (bf16[1024,128]{1,0:T(8,128)(2,1)S(1)}, bf16[1024,128]{1,0:T(8,128)(2,1)S(1)}, u32[]{:S(2)}, u32[]{:S(2)}) collective-permute-start(bf16[1024,128]{1,0:T(8,128)(2,1)S(1)} %collective-permute-done.13), channel_id=1, source_target_pairs={{0,1},{1,2},{2,3},{3,4},{4,5},{5,6},{6,7},{7,0},{8,9},{9,10},{10,1... | collective-permute-start | bytes 786440 | tf_op jit(solution)/shard_map/ppermute | solution.py:129
  86.9 9.5 %collective-permute-start.12 = (bf16[1024,128]{1,0:T(8,128)(2,1)S(1)}, bf16[1024,128]{1,0:T(8,128)(2,1)S(1)}, u32[]{:S(2)}, u32[]{:S(2)}) collective-permute-start(bf16[1024,128]{1,0:T(8,128)(2,1)S(1)} %collective-permute-done.11), channel_id=1, source_target_pairs={{0,7},{1,0},{2,1},{3,2},{4,3},{5,4},{6,5},{7,6},{8,15},{9,8},{10,9... | collective-permute-start | bytes 786440 | tf_op jit(solution)/shard_map/ppermute | solution.py:132
  93.2 10.3 %collective-permute-start.15 = (bf16[1024,128]{1,0:T(8,128)(2,1)S(1)}, bf16[1024,128]{1,0:T(8,128)(2,1)S(1)}, u32[]{:S(2)}, u32[]{:S(2)}) collective-permute-start(bf16[1024,128]{1,0:T(8,128)(2,1)S(1)} %collective-permute-done.14), channel_id=1, source_target_pairs={{0,1},{1,2},{2,3},{3,4},{4,5},{5,6},{6,7},{7,0},{8,9},{9,10},{10,1... | collective-permute-start | bytes 786440 | tf_op jit(solution)/shard_map/ppermute | solution.py:129
  103.5 9.5 %collective-permute-start.16 = (bf16[1024,128]{1,0:T(8,128)(2,1)S(1)}, bf16[1024,128]{1,0:T(8,128)(2,1)S(1)}, u32[]{:S(2)}, u32[]{:S(2)}) collective-permute-start(bf16[1024,128]{1,0:T(8,128)(2,1)S(1)} %collective-permute-done.15), channel_id=1, source_target_pairs={{0,1},{1,2},{2,3},{3,4},{4,5},{5,6},{6,7},{7,0},{8,9},{9,10},{10,1... | collective-permute-start | bytes 786440 | tf_op jit(solution)/shard_map/ppermute | solution.py:129
  114.1 0.8 copy-start.2
  120.0 3.9 %collective-permute-start.17 = (f32[32,17,256]{2,0,1:T(8,128)S(1)}, f32[32,17,256]{2,0,1:T(8,128)S(1)}, u32[]{:S(2)}, u32[]{:S(2)}) collective-permute-start(f32[32,17,256]{2,0,1:T(8,128)S(1)} %bitcast.159), channel_id=1, source_target_pairs={{0,8},{8,0},{1,9},{9,1},{2,10},{10,2},{3,11},{11,3},{4,12},{12,4},... | collective-permute-start | bytes 1671176 | tf_op jit(solution)/shard_map/ppermute | solution.py:106
  124.0 10.6 %collective-permute-start.18 = (f32[2,8,17,256]{3,1,0,2:T(8,128)S(1)}, f32[2,8,17,256]{3,1,0,2:T(8,128)S(1)}, u32[]{:S(2)}, u32[]{:S(2)}) collective-permute-start(f32[2,8,17,256]{3,1,0,2:T(8,128)S(1)} %select_bitcast_fusion), channel_id=1, source_target_pairs={{0,128},{128,0},{1,129},{129,1},{2,130},{130,2},{3,131},{131,3},{4... | collective-permute-start | bytes 835592 | tf_op jit(solution)/shard_map/ppermute | solution.py:115

commit v9 on v7

--- a/solution.py
+++ b/solution.py
@@ -138,6 +138,7 @@
         .astype(jnp.bfloat16)
         .reshape(point_count, own_width)
     )
+    rounded_orbitals, rounded_image = lax.optimization_barrier((rounded_orbitals, rounded_image))
     blocks = gather_ring(rounded_orbitals)
     total_width = own_width * len(blocks)
     rows = total_width // grid_size

time: 152 us -> 158 us (1.039)
  matrix products: 12.8 us -> 17.9 us
  waiting for transfers between devices: 39.1 us -> 40.7 us
    dot_general x16, matrix products: 4.25 us -> 9.33 us  [contract_points(): lax.dot_general(left_side, right_side, (((0,), (0,)), ((), ())), preferre...]
    ppermute x5, waiting for transfers between devices: 0.01 us -> 1.72 us  [halo_layers(): after = lax.ppermute(initial, GRID, down).astype(shard.dtype)]
  transfers between devices with their start and end apart: 18 -> 18, of which waited for: 9 -> 12; matrix products, arithmetic and copies ran while one was open for 10% -> 11% of each run, Pallas kernels for 0% -> 0%
where the time goes in v9:
time: 158 us; the launch traced here: 156 us
  starting transfers between devices  59.5 us (38%)
  waiting for transfers between devices  40.7 us (26%)
  blocking collectives  24.7 us (16%)
  matrix products  17.9 us (11%)
  other arithmetic  8.73 us (6%)
  local copies, waits for them, and re-layouts  3.74 us (2%)
    ppermute x5, starting transfers between devices, halo_layers(): after = lax.ppermute(initial, GRID, down).astype(shard.dtype)  22.4 us
    ppermute x5, waiting for transfers between devices, halo_layers(): before = lax.ppermute(last, GRID, up).astype(shard.dtype)  21.7 us
    ppermute x3, starting transfers between devices, gather_ring(): from_right = lax.ppermute(from_right, 'orb', left)  16.6 us
    ppermute x4, waiting for transfers between devices, gather_ring(): from_left = lax.ppermute(from_left, 'orb', right)  14.1 us
    all_to_all x1, blocking collectives, reduce_scatter_grid(): row_part = jnp.sum(lax.all_to_all(chip_part, 'x', 0, 0, tiled=True), axis=0)  12.4 us
    all_to_all x1, blocking collectives, reduce_scatter_grid(): return jnp.sum(lax.all_to_all(row_part, 'z', 0, 0, tiled=True), axis=0)  12.3 us
    ppermute x5, starting transfers between devices, halo_layers(): before = lax.ppermute(last, GRID, up).astype(shard.dtype)  10.9 us
    dot_general x16, matrix products, contract_points(): lax.dot_general(left_side, right_side, (((0,), (0,)), ((), ())), preferre...  9.33 us
  transfers between devices with their start and end apart: 18, of which 12 were waited for; matrix products, arithmetic and copies ran while one was open for 11% of the time, Pallas kernels for 0%

profile of v9, /device:TPU:6, one launch (start us, length us, event | category | flops | bytes accessed | tf_op | source)
XLA Modules:
  0.0 156.5 jit_solution(14525080459134685174)
XLA Ops:
  1.7 10.7 %collective-permute-start = (bf16[4,16,16,128]{3,2,1,0:T(8,128)(2,1)S(1)}, bf16[4,16,16,128]{3,2,1,0:T(8,128)(2,1)S(1)}, u32[]{:S(2)}, u32[]{:S(2)}) collective-permute-start(bf16[4,16,16,128]{3,2,1,0:T(8,128)(2,1)S(1)} %convert_element_type.254), channel_id=1, source_target_pairs={{8,0},{16,8},{24,16},{32,24},{40,32},{48,40},{56,48},{64,56},{72,6... | collective-permute-start | bytes 786440 | tf_op jit(solution)/shard_map/ppermute | solution.py:25
  12.4 1.9 %collective-permute-start.1 = (bf16[4,16,16,128]{3,2,1,0:T(8,128)(2,1)S(1)}, bf16[4,16,16,128]{3,2,1,0:T(8,128)(2,1)S(1)}, u32[]{:S(2)}, u32[]{:S(2)}) collective-permute-start(bf16[4,16,16,128]{3,2,1,0:T(8,128)(2,1)S(1)} %convert_element_type.254), channel_id=1, source_target_pairs={{0,8},{8,16},{16,24},{24,32},{32,40},{40,48},{48,56},{56,64},{64,7... | collective-permute-start | bytes 786440 | tf_op jit(solution)/shard_map/ppermute | solution.py:24
  15.2 2.4 %fusion.110 = f32[256,4,128]{2,0,1:T(8,128)S(1)} fusion(f32[4,256,128]{2,1,0:T(8,128)} %bitcast.120, s32[256]{0:T(256)S(1)} %get-tuple-element.20, s32[256]{0:T(256)S(1)} %get-tuple-element.21), kind=kOutput, calls=%fused_computation.208 | convolution fusion | flops 207618048 | bytes 1050624 | tf_op jit(solution)/shard_map/pq,zqo->zpo/dot_general | solution.py:60
  17.6 4.5 %collective-permute-done.1 = bf16[4,16,16,128]{3,2,1,0:T(8,128)(2,1)S(1)} collective-permute-done((bf16[4,16,16,128]{3,2,1,0:T(8,128)(2,1)S(1)}, bf16[4,16,16,128]{3,2,1,0:T(8,128)(2,1)S(1)}, u32[]{:S(2)}, u32[]{:S(2)}) %collective-permute-start.1) | collective-permute-done | bytes 262176 | tf_op jit(solution)/shard_map/ppermute | solution.py:24
  22.6 2.1 %collective-permute-start.2 = (bf16[4,16,16,128]{3,2,1,0:T(8,128)(2,1)S(1)}, bf16[4,16,16,128]{3,2,1,0:T(8,128)(2,1)S(1)}, u32[]{:S(2)}, u32[]{:S(2)}) collective-permute-start(bf16[4,16,16,128]{3,2,1,0:T(8,128)(2,1)S(1)} %get-tuple-element.13), channel_id=1, source_target_pairs={{8,0},{16,8},{24,16},{32,24},{40,32},{48,40},{56,48},{64,56},{72,6... | collective-permute-start | bytes 786440 | tf_op jit(solution)/shard_map/ppermute | solution.py:25
  24.8 2.2 %collective-permute-start.3 = (bf16[4,16,16,128]{3,2,1,0:T(8,128)(2,1)S(1)}, bf16[4,16,16,128]{3,2,1,0:T(8,128)(2,1)S(1)}, u32[]{:S(2)}, u32[]{:S(2)}) collective-permute-start(bf16[4,16,16,128]{3,2,1,0:T(8,128)(2,1)S(1)} %get-tuple-element.13), channel_id=1, source_target_pairs={{0,8},{8,16},{16,24},{24,32},{32,40},{40,48},{48,56},{56,64},{64,7... | collective-permute-start | bytes 786440 | tf_op jit(solution)/shard_map/ppermute | solution.py:24
  27.0 1.5 convolution_bitcast_fusion.3
  28.8 5.7 %collective-permute-done.3 = bf16[4,16,16,128]{3,2,1,0:T(8,128)(2,1)S(1)} collective-permute-done((bf16[4,16,16,128]{3,2,1,0:T(8,128)(2,1)S(1)}, bf16[4,16,16,128]{3,2,1,0:T(8,128)(2,1)S(1)}, u32[]{:S(2)}, u32[]{:S(2)}) %collective-permute-start.3) | collective-permute-done | bytes 262176 | tf_op jit(solution)/shard_map/ppermute | solution.py:24
  35.0 1.9 %collective-permute-start.4 = (bf16[4,16,16,128]{3,2,1,0:T(8,128)(2,1)S(1)}, bf16[4,16,16,128]{3,2,1,0:T(8,128)(2,1)S(1)}, u32[]{:S(2)}, u32[]{:S(2)}) collective-permute-start(bf16[4,16,16,128]{3,2,1,0:T(8,128)(2,1)S(1)} %get-tuple-element.11), channel_id=1, source_target_pairs={{8,0},{16,8},{24,16},{32,24},{40,32},{48,40},{56,48},{64,56},{72,6... | collective-permute-start | bytes 786440 | tf_op jit(solution)/shard_map/ppermute | solution.py:25
  37.0 2.4 %collective-permute-start.5 = (bf16[4,16,16,128]{3,2,1,0:T(8,128)(2,1)S(1)}, bf16[4,16,16,128]{3,2,1,0:T(8,128)(2,1)S(1)}, u32[]{:S(2)}, u32[]{:S(2)}) collective-permute-start(bf16[4,16,16,128]{3,2,1,0:T(8,128)(2,1)S(1)} %get-tuple-element.11), channel_id=1, source_target_pairs={{0,8},{8,16},{16,24},{24,32},{32,40},{40,48},{48,56},{56,64},{64,7... | collective-permute-start | bytes 786440 | tf_op jit(solution)/shard_map/ppermute | solution.py:24
  39.4 1.5 convolution_bitcast_fusion.2
  41.2 5.6 %collective-permute-done.5 = bf16[4,16,16,128]{3,2,1,0:T(8,128)(2,1)S(1)} collective-permute-done((bf16[4,16,16,128]{3,2,1,0:T(8,128)(2,1)S(1)}, bf16[4,16,16,128]{3,2,1,0:T(8,128)(2,1)S(1)}, u32[]{:S(2)}, u32[]{:S(2)}) %collective-permute-start.5) | collective-permute-done | bytes 262176 | tf_op jit(solution)/shard_map/ppermute | solution.py:24
  47.2 1.9 %collective-permute-start.6 = (bf16[4,16,16,128]{3,2,1,0:T(8,128)(2,1)S(1)}, bf16[4,16,16,128]{3,2,1,0:T(8,128)(2,1)S(1)}, u32[]{:S(2)}, u32[]{:S(2)}) collective-permute-start(bf16[4,16,16,128]{3,2,1,0:T(8,128)(2,1)S(1)} %get-tuple-element.9), channel_id=1, source_target_pairs={{8,0},{16,8},{24,16},{32,24},{40,32},{48,40},{56,48},{64,56},{72,6... | collective-permute-start | bytes 786440 | tf_op jit(solution)/shard_map/ppermute | solution.py:25
  49.2 2.4 %collective-permute-start.7 = (bf16[4,16,16,128]{3,2,1,0:T(8,128)(2,1)S(1)}, bf16[4,16,16,128]{3,2,1,0:T(8,128)(2,1)S(1)}, u32[]{:S(2)}, u32[]{:S(2)}) collective-permute-start(bf16[4,16,16,128]{3,2,1,0:T(8,128)(2,1)S(1)} %get-tuple-element.9), channel_id=1, source_target_pairs={{0,8},{8,16},{16,24},{24,32},{32,40},{40,48},{48,56},{56,64},{64,7... | collective-permute-start | bytes 786440 | tf_op jit(solution)/shard_map/ppermute | solution.py:24
  53.4 5.6 %collective-permute-done.7 = bf16[4,16,16,128]{3,2,1,0:T(8,128)(2,1)S(1)} collective-permute-done((bf16[4,16,16,128]{3,2,1,0:T(8,128)(2,1)S(1)}, bf16[4,16,16,128]{3,2,1,0:T(8,128)(2,1)S(1)}, u32[]{:S(2)}, u32[]{:S(2)}) %collective-permute-start.7) | collective-permute-done | bytes 262176 | tf_op jit(solution)/shard_map/ppermute | solution.py:24
  59.5 1.9 %collective-permute-start.9 = (bf16[4,16,16,128]{3,2,1,0:T(8,128)(2,1)S(1)}, bf16[4,16,16,128]{3,2,1,0:T(8,128)(2,1)S(1)}, u32[]{:S(2)}, u32[]{:S(2)}) collective-permute-start(bf16[4,16,16,128]{3,2,1,0:T(8,128)(2,1)S(1)} %convert_element_type.282), channel_id=1, source_target_pairs={{0,8},{8,16},{16,24},{24,32},{32,40},{40,48},{48,56},{56,64},{64,7... | collective-permute-start | bytes 786440 | tf_op jit(solution)/shard_map/ppermute | solution.py:24
  61.4 5.8 %collective-permute-start.8 = (bf16[4,16,16,128]{3,2,1,0:T(8,128)(2,1)S(1)}, bf16[4,16,16,128]{3,2,1,0:T(8,128)(2,1)S(1)}, u32[]{:S(2)}, u32[]{:S(2)}) collective-permute-start(bf16[4,16,16,128]{3,2,1,0:T(8,128)(2,1)S(1)} %convert_element_type.282), channel_id=1, source_target_pairs={{8,0},{16,8},{24,16},{32,24},{40,32},{48,40},{56,48},{64,56},{72,6... | collective-permute-start | bytes 786440 | tf_op jit(solution)/shard_map/ppermute | solution.py:25
  67.2 1.5 convolution_bitcast_fusion
  69.3 1.7 %collective-permute-done.8 = bf16[4,16,16,128]{3,2,1,0:T(8,128)(2,1)S(1)} collective-permute-done((bf16[4,16,16,128]{3,2,1,0:T(8,128)(2,1)S(1)}, bf16[4,16,16,128]{3,2,1,0:T(8,128)(2,1)S(1)}, u32[]{:S(2)}, u32[]{:S(2)}) %collective-permute-start.8) | collective-permute-done | bytes 262176 | tf_op jit(solution)/shard_map/ppermute | solution.py:25
  71.4 5.4 %collective-permute-start.10 = (bf16[1024,128]{1,0:T(8,128)(2,1)S(1)}, bf16[1024,128]{1,0:T(8,128)(2,1)S(1)}, u32[]{:S(2)}, u32[]{:S(2)}) collective-permute-start(bf16[1024,128]{1,0:T(8,128)(2,1)S(1)} %bitcast.99), channel_id=1, source_target_pairs={{0,7},{1,0},{2,1},{3,2},{4,3},{5,4},{6,5},{7,6},{8,15},{9,8},{10,9... | collective-permute-start | bytes 786440 | tf_op jit(solution)/shard_map/ppermute | solution.py:122
  76.8 2.1 %collective-permute-start.13 = (bf16[1024,128]{1,0:T(8,128)(2,1)S(1)}, bf16[1024,128]{1,0:T(8,128)(2,1)S(1)}, u32[]{:S(2)}, u32[]{:S(2)}) collective-permute-start(bf16[1024,128]{1,0:T(8,128)(2,1)S(1)} %bitcast.100), channel_id=1, source_target_pairs={{0,1},{1,2},{2,3},{3,4},{4,5},{5,6},{6,7},{7,0},{8,9},{9,10},{10,1... | collective-permute-start | bytes 786440 | tf_op jit(solution)/shard_map/ppermute | solution.py:119
  80.9 5.6 %collective-permute-start.11 = (bf16[1024,128]{1,0:T(8,128)(2,1)S(1)}, bf16[1024,128]{1,0:T(8,128)(2,1)S(1)}, u32[]{:S(2)}, u32[]{:S(2)}) collective-permute-start(bf16[1024,128]{1,0:T(8,128)(2,1)S(1)} %collective-permute-done.10), channel_id=1, source_target_pairs={{0,7},{1,0},{2,1},{3,2},{4,3},{5,4},{6,5},{7,6},{8,15},{9,8},{10,9... | collective-permute-start | bytes 786440 | tf_op jit(solution)/shard_map/ppermute | solution.py:122
  87.7 1.9 %collective-permute-start.14 = (bf16[1024,128]{1,0:T(8,128)(2,1)S(1)}, bf16[1024,128]{1,0:T(8,128)(2,1)S(1)}, u32[]{:S(2)}, u32[]{:S(2)}) collective-permute-start(bf16[1024,128]{1,0:T(8,128)(2,1)S(1)} %collective-permute-done.13), channel_id=1, source_target_pairs={{0,1},{1,2},{2,3},{3,4},{4,5},{5,6},{6,7},{7,0},{8,9},{9,10},{10,1... | collective-permute-start | bytes 786440 | tf_op jit(solution)/shard_map/ppermute | solution.py:119
  90.4 5.6 %collective-permute-start.12 = (bf16[1024,128]{1,0:T(8,128)(2,1)S(1)}, bf16[1024,128]{1,0:T(8,128)(2,1)S(1)}, u32[]{:S(2)}, u32[]{:S(2)}) collective-permute-start(bf16[1024,128]{1,0:T(8,128)(2,1)S(1)} %collective-permute-done.11), channel_id=1, source_target_pairs={{0,7},{1,0},{2,1},{3,2},{4,3},{5,4},{6,5},{7,6},{8,15},{9,8},{10,9... | collective-permute-start | bytes 786440 | tf_op jit(solution)/shard_map/ppermute | solution.py:122
  97.3 1.9 %collective-permute-start.15 = (bf16[1024,128]{1,0:T(8,128)(2,1)S(1)}, bf16[1024,128]{1,0:T(8,128)(2,1)S(1)}, u32[]{:S(2)}, u32[]{:S(2)}) collective-permute-start(bf16[1024,128]{1,0:T(8,128)(2,1)S(1)} %collective-permute-done.14), channel_id=1, source_target_pairs={{0,1},{1,2},{2,3},{3,4},{4,5},{5,6},{6,7},{7,0},{8,9},{9,10},{10,1... | collective-permute-start | bytes 786440 | tf_op jit(solution)/shard_map/ppermute | solution.py:119
  100.1 8.0 %collective-permute-done.15 = bf16[1024,128]{1,0:T(8,128)(2,1)S(1)} collective-permute-done((bf16[1024,128]{1,0:T(8,128)(2,1)S(1)}, bf16[1024,128]{1,0:T(8,128)(2,1)S(1)}, u32[]{:S(2)}, u32[]{:S(2)}) %collective-permute-start.15) | collective-permute-done | bytes 262176 | tf_op jit(solution)/shard_map/ppermute | solution.py:119
  108.1 1.9 %collective-permute-start.16 = (bf16[1024,128]{1,0:T(8,128)(2,1)S(1)}, bf16[1024,128]{1,0:T(8,128)(2,1)S(1)}, u32[]{:S(2)}, u32[]{:S(2)}) collective-permute-start(bf16[1024,128]{1,0:T(8,128)(2,1)S(1)} %collective-permute-done.15), channel_id=1, source_target_pairs={{0,1},{1,2},{2,3},{3,4},{4,5},{5,6},{6,7},{7,0},{8,9},{9,10},{10,1... | collective-permute-start | bytes 786440 | tf_op jit(solution)/shard_map/ppermute | solution.py:119
  111.4 6.1 %collective-permute-done.16 = bf16[1024,128]{1,0:T(8,128)(2,1)S(1)} collective-permute-done((bf16[1024,128]{1,0:T(8,128)(2,1)S(1)}, bf16[1024,128]{1,0:T(8,128)(2,1)S(1)}, u32[]{:S(2)}, u32[]{:S(2)}) %collective-permute-start.16) | collective-permute-done | bytes 262176 | tf_op jit(solution)/shard_map/ppermute | solution.py:119
  126.0 1.9 %collective-permute-start.17 = (f32[32,17,256]{2,0,1:T(8,128)S(1)}, f32[32,17,256]{2,0,1:T(8,128)S(1)}, u32[]{:S(2)}, u32[]{:S(2)}) collective-permute-start(f32[32,17,256]{2,0,1:T(8,128)S(1)} %bitcast.130), channel_id=1, source_target_pairs={{0,8},{8,0},{1,9},{9,1},{2,10},{10,2},{3,11},{11,3},{4,12},{12,4},... | collective-permute-start | bytes 1671176 | tf_op jit(solution)/shard_map/ppermute | solution.py:106
  128.0 1.9 %collective-permute-done.17 = f32[32,17,256]{2,0,1:T(8,128)S(1)} collective-permute-done((f32[32,17,256]{2,0,1:T(8,128)S(1)}, f32[32,17,256]{2,0,1:T(8,128)S(1)}, u32[]{:S(2)}, u32[]{:S(2)}) %collective-permute-start.17) | collective-permute-done | bytes 557088 | tf_op jit(solution)/shard_map/ppermute | solution.py:106
  130.1 12.4 %all_to_all.10 = f32[4,8,17,256]{3,1,2,0:T(8,128)S(1)} all-to-all(f32[4,8,17,256]{3,1,2,0:T(8,128)S(1)} %copy.95), channel_id=1, replica_groups=mesh['x'=4,'z'=8,'core'=2,'orb'=8] {'x'}, dimensions={0} | all-to-all | bytes 1114112 | tf_op jit(solution)/shard_map/all_to_all | solution.py:108
  142.5 12.3 %all_to_all.11 = f32[8,17,256]{2,1,0:T(8,128)S(1)} all-to-all(f32[8,17,256]{2,1,0:T(8,128)S(1)} %copy.97), channel_id=1, replica_groups=mesh['x'=4,'z'=8,'core'=2,'orb'=8] {'z'}, dimensions={0} | all-to-all | bytes 278528 | tf_op jit(solution)/shard_map/all_to_all | solution.py:109
  (98 shorter events, 24.8 us)
Async XLA Ops:
  1.7 15.9 %collective-permute-start = (bf16[4,16,16,128]{3,2,1,0:T(8,128)(2,1)S(1)}, bf16[4,16,16,128]{3,2,1,0:T(8,128)(2,1)S(1)}, u32[]{:S(2)}, u32[]{:S(2)}) collective-permute-start(bf16[4,16,16,128]{3,2,1,0:T(8,128)(2,1)S(1)} %convert_element_type.254), channel_id=1, source_target_pairs={{8,0},{16,8},{24,16},{32,24},{40,32},{48,40},{56,48},{64,56},{72,6... | collective-permute-start | bytes 786440 | tf_op jit(solution)/shard_map/ppermute | solution.py:25
  12.4 9.8 %collective-permute-start.1 = (bf16[4,16,16,128]{3,2,1,0:T(8,128)(2,1)S(1)}, bf16[4,16,16,128]{3,2,1,0:T(8,128)(2,1)S(1)}, u32[]{:S(2)}, u32[]{:S(2)}) collective-permute-start(bf16[4,16,16,128]{3,2,1,0:T(8,128)(2,1)S(1)} %convert_element_type.254), channel_id=1, source_target_pairs={{0,8},{8,16},{16,24},{24,32},{32,40},{40,48},{48,56},{56,64},{64,7... | collective-permute-start | bytes 786440 | tf_op jit(solution)/shard_map/ppermute | solution.py:24
  17.6 4.7 %copy-start = (f32[4,16,16,128]{3,2,1,0:T(8,128)S(1)}, f32[4,16,16,128]{3,2,1,0:T(8,128)}, u32[]{:S(2)}) copy-start(f32[4,16,16,128]{3,2,1,0:T(8,128)} %param.2) | copy-start | bytes 1572868
  17.6 4.7 %copy-start.1 = (f32[4,16,16]{2,1,0:T(8,128)S(1)}, f32[4,16,16]{2,1,0:T(8,128)}, u32[]{:S(2)}) copy-start(f32[4,16,16]{2,1,0:T(8,128)} %param.3) | copy-start | bytes 12292
  22.6 6.2 %collective-permute-start.2 = (bf16[4,16,16,128]{3,2,1,0:T(8,128)(2,1)S(1)}, bf16[4,16,16,128]{3,2,1,0:T(8,128)(2,1)S(1)}, u32[]{:S(2)}, u32[]{:S(2)}) collective-permute-start(bf16[4,16,16,128]{3,2,1,0:T(8,128)(2,1)S(1)} %get-tuple-element.13), channel_id=1, source_target_pairs={{8,0},{16,8},{24,16},{32,24},{40,32},{48,40},{56,48},{64,56},{72,6... | collective-permute-start | bytes 786440 | tf_op jit(solution)/shard_map/ppermute | solution.py:25
  24.8 9.8 %collective-permute-start.3 = (bf16[4,16,16,128]{3,2,1,0:T(8,128)(2,1)S(1)}, bf16[4,16,16,128]{3,2,1,0:T(8,128)(2,1)S(1)}, u32[]{:S(2)}, u32[]{:S(2)}) collective-permute-start(bf16[4,16,16,128]{3,2,1,0:T(8,128)(2,1)S(1)} %get-tuple-element.13), channel_id=1, source_target_pairs={{0,8},{8,16},{16,24},{24,32},{32,40},{40,48},{48,56},{56,64},{64,7... | collective-permute-start | bytes 786440 | tf_op jit(solution)/shard_map/ppermute | solution.py:24
  35.0 6.1 %collective-permute-start.4 = (bf16[4,16,16,128]{3,2,1,0:T(8,128)(2,1)S(1)}, bf16[4,16,16,128]{3,2,1,0:T(8,128)(2,1)S(1)}, u32[]{:S(2)}, u32[]{:S(2)}) collective-permute-start(bf16[4,16,16,128]{3,2,1,0:T(8,128)(2,1)S(1)} %get-tuple-element.11), channel_id=1, source_target_pairs={{8,0},{16,8},{24,16},{32,24},{40,32},{48,40},{56,48},{64,56},{72,6... | collective-permute-start | bytes 786440 | tf_op jit(solution)/shard_map/ppermute | solution.py:25
  37.0 9.8 %collective-permute-start.5 = (bf16[4,16,16,128]{3,2,1,0:T(8,128)(2,1)S(1)}, bf16[4,16,16,128]{3,2,1,0:T(8,128)(2,1)S(1)}, u32[]{:S(2)}, u32[]{:S(2)}) collective-permute-start(bf16[4,16,16,128]{3,2,1,0:T(8,128)(2,1)S(1)} %get-tuple-element.11), channel_id=1, source_target_pairs={{0,8},{8,16},{16,24},{24,32},{32,40},{40,48},{48,56},{56,64},{64,7... | collective-permute-start | bytes 786440 | tf_op jit(solution)/shard_map/ppermute | solution.py:24
  47.2 6.1 %collective-permute-start.6 = (bf16[4,16,16,128]{3,2,1,0:T(8,128)(2,1)S(1)}, bf16[4,16,16,128]{3,2,1,0:T(8,128)(2,1)S(1)}, u32[]{:S(2)}, u32[]{:S(2)}) collective-permute-start(bf16[4,16,16,128]{3,2,1,0:T(8,128)(2,1)S(1)} %get-tuple-element.9), channel_id=1, source_target_pairs={{8,0},{16,8},{24,16},{32,24},{40,32},{48,40},{56,48},{64,56},{72,6... | collective-permute-start | bytes 786440 | tf_op jit(solution)/shard_map/ppermute | solution.py:25
  49.2 9.8 %collective-permute-start.7 = (bf16[4,16,16,128]{3,2,1,0:T(8,128)(2,1)S(1)}, bf16[4,16,16,128]{3,2,1,0:T(8,128)(2,1)S(1)}, u32[]{:S(2)}, u32[]{:S(2)}) collective-permute-start(bf16[4,16,16,128]{3,2,1,0:T(8,128)(2,1)S(1)} %get-tuple-element.9), channel_id=1, source_target_pairs={{0,8},{8,16},{16,24},{24,32},{32,40},{40,48},{48,56},{56,64},{64,7... | collective-permute-start | bytes 786440 | tf_op jit(solution)/shard_map/ppermute | solution.py:24
  59.5 9.8 %collective-permute-start.9 = (bf16[4,16,16,128]{3,2,1,0:T(8,128)(2,1)S(1)}, bf16[4,16,16,128]{3,2,1,0:T(8,128)(2,1)S(1)}, u32[]{:S(2)}, u32[]{:S(2)}) collective-permute-start(bf16[4,16,16,128]{3,2,1,0:T(8,128)(2,1)S(1)} %convert_element_type.282), channel_id=1, source_target_pairs={{0,8},{8,16},{16,24},{24,32},{32,40},{40,48},{48,56},{56,64},{64,7... | collective-permute-start | bytes 786440 | tf_op jit(solution)/shard_map/ppermute | solution.py:24
  61.4 9.6 %collective-permute-start.8 = (bf16[4,16,16,128]{3,2,1,0:T(8,128)(2,1)S(1)}, bf16[4,16,16,128]{3,2,1,0:T(8,128)(2,1)S(1)}, u32[]{:S(2)}, u32[]{:S(2)}) collective-permute-start(bf16[4,16,16,128]{3,2,1,0:T(8,128)(2,1)S(1)} %convert_element_type.282), channel_id=1, source_target_pairs={{8,0},{16,8},{24,16},{32,24},{40,32},{48,40},{56,48},{64,56},{72,6... | collective-permute-start | bytes 786440 | tf_op jit(solution)/shard_map/ppermute | solution.py:25
  71.4 9.3 %collective-permute-start.10 = (bf16[1024,128]{1,0:T(8,128)(2,1)S(1)}, bf16[1024,128]{1,0:T(8,128)(2,1)S(1)}, u32[]{:S(2)}, u32[]{:S(2)}) collective-permute-start(bf16[1024,128]{1,0:T(8,128)(2,1)S(1)} %bitcast.99), channel_id=1, source_target_pairs={{0,7},{1,0},{2,1},{3,2},{4,3},{5,4},{6,5},{7,6},{8,15},{9,8},{10,9... | collective-permute-start | bytes 786440 | tf_op jit(solution)/shard_map/ppermute | solution.py:122
  76.8 10.6 %collective-permute-start.13 = (bf16[1024,128]{1,0:T(8,128)(2,1)S(1)}, bf16[1024,128]{1,0:T(8,128)(2,1)S(1)}, u32[]{:S(2)}, u32[]{:S(2)}) collective-permute-start(bf16[1024,128]{1,0:T(8,128)(2,1)S(1)} %bitcast.100), channel_id=1, source_target_pairs={{0,1},{1,2},{2,3},{3,4},{4,5},{5,6},{6,7},{7,0},{8,9},{9,10},{10,1... | collective-permute-start | bytes 786440 | tf_op jit(solution)/shard_map/ppermute | solution.py:119
  80.9 9.5 %collective-permute-start.11 = (bf16[1024,128]{1,0:T(8,128)(2,1)S(1)}, bf16[1024,128]{1,0:T(8,128)(2,1)S(1)}, u32[]{:S(2)}, u32[]{:S(2)}) collective-permute-start(bf16[1024,128]{1,0:T(8,128)(2,1)S(1)} %collective-permute-done.10), channel_id=1, source_target_pairs={{0,7},{1,0},{2,1},{3,2},{4,3},{5,4},{6,5},{7,6},{8,15},{9,8},{10,9... | collective-permute-start | bytes 786440 | tf_op jit(solution)/shard_map/ppermute | solution.py:122
  87.7 9.7 %collective-permute-start.14 = (bf16[1024,128]{1,0:T(8,128)(2,1)S(1)}, bf16[1024,128]{1,0:T(8,128)(2,1)S(1)}, u32[]{:S(2)}, u32[]{:S(2)}) collective-permute-start(bf16[1024,128]{1,0:T(8,128)(2,1)S(1)} %collective-permute-done.13), channel_id=1, source_target_pairs={{0,1},{1,2},{2,3},{3,4},{4,5},{5,6},{6,7},{7,0},{8,9},{9,10},{10,1... | collective-permute-start | bytes 786440 | tf_op jit(solution)/shard_map/ppermute | solution.py:119
  90.4 9.5 %collective-permute-start.12 = (bf16[1024,128]{1,0:T(8,128)(2,1)S(1)}, bf16[1024,128]{1,0:T(8,128)(2,1)S(1)}, u32[]{:S(2)}, u32[]{:S(2)}) collective-permute-start(bf16[1024,128]{1,0:T(8,128)(2,1)S(1)} %collective-permute-done.11), channel_id=1, source_target_pairs={{0,7},{1,0},{2,1},{3,2},{4,3},{5,4},{6,5},{7,6},{8,15},{9,8},{10,9... | collective-permute-start | bytes 786440 | tf_op jit(solution)/shard_map/ppermute | solution.py:122
  97.3 10.8 %collective-permute-start.15 = (bf16[1024,128]{1,0:T(8,128)(2,1)S(1)}, bf16[1024,128]{1,0:T(8,128)(2,1)S(1)}, u32[]{:S(2)}, u32[]{:S(2)}) collective-permute-start(bf16[1024,128]{1,0:T(8,128)(2,1)S(1)} %collective-permute-done.14), channel_id=1, source_target_pairs={{0,1},{1,2},{2,3},{3,4},{4,5},{5,6},{6,7},{7,0},{8,9},{9,10},{10,1... | collective-permute-start | bytes 786440 | tf_op jit(solution)/shard_map/ppermute | solution.py:119
  108.1 9.5 %collective-permute-start.16 = (bf16[1024,128]{1,0:T(8,128)(2,1)S(1)}, bf16[1024,128]{1,0:T(8,128)(2,1)S(1)}, u32[]{:S(2)}, u32[]{:S(2)}) collective-permute-start(bf16[1024,128]{1,0:T(8,128)(2,1)S(1)} %collective-permute-done.15), channel_id=1, source_target_pairs={{0,1},{1,2},{2,3},{3,4},{4,5},{5,6},{6,7},{7,0},{8,9},{9,10},{10,1... | collective-permute-start | bytes 786440 | tf_op jit(solution)/shard_map/ppermute | solution.py:119
  126.0 3.9 %collective-permute-start.17 = (f32[32,17,256]{2,0,1:T(8,128)S(1)}, f32[32,17,256]{2,0,1:T(8,128)S(1)}, u32[]{:S(2)}, u32[]{:S(2)}) collective-permute-start(f32[32,17,256]{2,0,1:T(8,128)S(1)} %bitcast.130), channel_id=1, source_target_pairs={{0,8},{8,0},{1,9},{9,1},{2,10},{10,2},{3,11},{11,3},{4,12},{12,4},... | collective-permute-start | bytes 1671176 | tf_op jit(solution)/shard_map/ppermute | solution.py:106

commit v10 on v7

--- a/solution.py
+++ b/solution.py
@@ -115,7 +115,17 @@
     left = [(i, (i - 1) % size) for i in range(size)]
     ahead = {0: block}
     from_left, from_right = block, block
+    half = block.shape[0] // 2
     for step in range(1, size // 2 + 1):
+        if step == size - step and size > 2:
+            ahead[step] = jnp.concatenate(
+                [
+                    lax.ppermute(from_left[:half], "orb", right),
+                    lax.ppermute(from_right[half:], "orb", left),
+                ],
+                axis=0,
+            )
+            continue
         from_left = lax.ppermute(from_left, "orb", right)
         ahead[size - step] = from_left
         if step <= (size - 1) // 2:

time: 152 us -> 151 us (level)
  waiting for transfers between devices: 39.1 us -> 32.1 us
  starting transfers between devices: 59.1 us -> 64.2 us
    ppermute x0 -> x2, starting transfers between devices: none -> 7.04 us  [the longest x1 5.13 us: gather_ring(): lax.ppermute(from_right[half:], 'orb', left)]
    ppermute x4 -> x3, waiting for transfers between devices: 13.6 us -> 7.24 us  [gather_ring(): from_left = lax.ppermute(from_left, 'orb', right)]
    ppermute x4 -> x3, starting transfers between devices: 7.84 us -> 5.93 us  [gather_ring(): from_left = lax.ppermute(from_left, 'orb', right)]
  transfers between devices with their start and end apart: 18 -> 19, of which waited for: 9 -> 10; matrix products, arithmetic and copies ran while one was open for 10% -> 11% of each run, Pallas kernels for 0% -> 0%
where the time goes in v10:
time: 151 us; the launch traced here: 148 us
  starting transfers between devices  64.2 us (43%)
  waiting for transfers between devices  32.1 us (21%)
  blocking collectives  24.7 us (16%)
  matrix products  12.8 us (8%)
  other arithmetic  9.02 us (6%)
  local copies, waits for them, and re-layouts  4.31 us (3%)
    ppermute x5, starting transfers between devices, halo_layers(): after = lax.ppermute(initial, GRID, down).astype(shard.dtype)  22.4 us
    ppermute x5, waiting for transfers between devices, halo_layers(): before = lax.ppermute(last, GRID, up).astype(shard.dtype)  21.4 us
    ppermute x3, starting transfers between devices, gather_ring(): from_right = lax.ppermute(from_right, 'orb', left)  16.1 us
    all_to_all x1, blocking collectives, reduce_scatter_grid(): row_part = jnp.sum(lax.all_to_all(chip_part, 'x', 0, 0, tiled=True), axis=0)  12.4 us
    all_to_all x1, blocking collectives, reduce_scatter_grid(): return jnp.sum(lax.all_to_all(row_part, 'z', 0, 0, tiled=True), axis=0)  12.3 us
    ppermute x5, starting transfers between devices, halo_layers(): before = lax.ppermute(last, GRID, up).astype(shard.dtype)  10.8 us
    dot_general x5, matrix products, apply_hamiltonian(): jnp.einsum('pq,zqo->zpo', plane, flat, precision=lax.Precision.HIGH, pref...  8.56 us
    ppermute x3, waiting for transfers between devices, gather_ring(): from_left = lax.ppermute(from_left, 'orb', right)  7.24 us
  transfers between devices with their start and end apart: 19, of which 10 were waited for; matrix products, arithmetic and copies ran while one was open for 11% of the time, Pallas kernels for 0%

profile of v10, /device:TPU:6, one launch (start us, length us, event | category | flops | bytes accessed | tf_op | source)
XLA Modules:
  0.0 148.5 jit_solution(3311420156998203126)
XLA Ops:
  1.7 10.7 %collective-permute-start = (bf16[4,16,16,128]{3,2,1,0:T(8,128)(2,1)S(1)}, bf16[4,16,16,128]{3,2,1,0:T(8,128)(2,1)S(1)}, u32[]{:S(2)}, u32[]{:S(2)}) collective-permute-start(bf16[4,16,16,128]{3,2,1,0:T(8,128)(2,1)S(1)} %convert_element_type.255), channel_id=1, source_target_pairs={{8,0},{16,8},{24,16},{32,24},{40,32},{48,40},{56,48},{64,56},{72,6... | collective-permute-start | bytes 786440 | tf_op jit(solution)/shard_map/ppermute | solution.py:25
  12.4 1.9 %collective-permute-start.1 = (bf16[4,16,16,128]{3,2,1,0:T(8,128)(2,1)S(1)}, bf16[4,16,16,128]{3,2,1,0:T(8,128)(2,1)S(1)}, u32[]{:S(2)}, u32[]{:S(2)}) collective-permute-start(bf16[4,16,16,128]{3,2,1,0:T(8,128)(2,1)S(1)} %convert_element_type.255), channel_id=1, source_target_pairs={{0,8},{8,16},{16,24},{24,32},{32,40},{40,48},{48,56},{56,64},{64,7... | collective-permute-start | bytes 786440 | tf_op jit(solution)/shard_map/ppermute | solution.py:24
  15.2 2.4 %fusion.112 = f32[256,4,128]{2,0,1:T(8,128)S(1)} fusion(f32[4,256,128]{2,1,0:T(8,128)} %bitcast.128, s32[256]{0:T(256)S(1)} %get-tuple-element.18, s32[256]{0:T(256)S(1)} %get-tuple-element.19), kind=kOutput, calls=%fused_computation.210 | convolution fusion | flops 207618048 | bytes 1050624 | tf_op jit(solution)/shard_map/pq,zqo->zpo/dot_general | solution.py:60
  17.6 4.5 %collective-permute-done.1 = bf16[4,16,16,128]{3,2,1,0:T(8,128)(2,1)S(1)} collective-permute-done((bf16[4,16,16,128]{3,2,1,0:T(8,128)(2,1)S(1)}, bf16[4,16,16,128]{3,2,1,0:T(8,128)(2,1)S(1)}, u32[]{:S(2)}, u32[]{:S(2)}) %collective-permute-start.1) | collective-permute-done | bytes 262176 | tf_op jit(solution)/shard_map/ppermute | solution.py:24
  22.6 2.1 %collective-permute-start.2 = (bf16[4,16,16,128]{3,2,1,0:T(8,128)(2,1)S(1)}, bf16[4,16,16,128]{3,2,1,0:T(8,128)(2,1)S(1)}, u32[]{:S(2)}, u32[]{:S(2)}) collective-permute-start(bf16[4,16,16,128]{3,2,1,0:T(8,128)(2,1)S(1)} %get-tuple-element.11), channel_id=1, source_target_pairs={{8,0},{16,8},{24,16},{32,24},{40,32},{48,40},{56,48},{64,56},{72,6... | collective-permute-start | bytes 786440 | tf_op jit(solution)/shard_map/ppermute | solution.py:25
  24.8 2.2 %collective-permute-start.3 = (bf16[4,16,16,128]{3,2,1,0:T(8,128)(2,1)S(1)}, bf16[4,16,16,128]{3,2,1,0:T(8,128)(2,1)S(1)}, u32[]{:S(2)}, u32[]{:S(2)}) collective-permute-start(bf16[4,16,16,128]{3,2,1,0:T(8,128)(2,1)S(1)} %get-tuple-element.11), channel_id=1, source_target_pairs={{0,8},{8,16},{16,24},{24,32},{32,40},{40,48},{48,56},{56,64},{64,7... | collective-permute-start | bytes 786440 | tf_op jit(solution)/shard_map/ppermute | solution.py:24
  27.0 1.5 %convolution_bitcast_fusion.3 = f32[4,256,128]{1,2,0:T(8,128)S(1)} fusion(f32[4,256,128]{2,1,0:T(8,128)S(1)} %bitcast.130, s32[256]{0:T(256)S(1)} %get-tuple-element.18, s32[256]{0:T(256)S(1)} %get-tuple-element.19), kind=kOutput, calls=%fused_computation.49 | convolution fusion | flops 207618048 | bytes 1050624 | tf_op jit(solution)/shard_map/pq,zqo->zpo/dot_general | solution.py:60
  28.8 5.7 %collective-permute-done.3 = bf16[4,16,16,128]{3,2,1,0:T(8,128)(2,1)S(1)} collective-permute-done((bf16[4,16,16,128]{3,2,1,0:T(8,128)(2,1)S(1)}, bf16[4,16,16,128]{3,2,1,0:T(8,128)(2,1)S(1)}, u32[]{:S(2)}, u32[]{:S(2)}) %collective-permute-start.3) | collective-permute-done | bytes 262176 | tf_op jit(solution)/shard_map/ppermute | solution.py:24
  35.0 1.9 %collective-permute-start.4 = (bf16[4,16,16,128]{3,2,1,0:T(8,128)(2,1)S(1)}, bf16[4,16,16,128]{3,2,1,0:T(8,128)(2,1)S(1)}, u32[]{:S(2)}, u32[]{:S(2)}) collective-permute-start(bf16[4,16,16,128]{3,2,1,0:T(8,128)(2,1)S(1)} %get-tuple-element.9), channel_id=1, source_target_pairs={{8,0},{16,8},{24,16},{32,24},{40,32},{48,40},{56,48},{64,56},{72,6... | collective-permute-start | bytes 786440 | tf_op jit(solution)/shard_map/ppermute | solution.py:25
  37.0 2.4 %collective-permute-start.5 = (bf16[4,16,16,128]{3,2,1,0:T(8,128)(2,1)S(1)}, bf16[4,16,16,128]{3,2,1,0:T(8,128)(2,1)S(1)}, u32[]{:S(2)}, u32[]{:S(2)}) collective-permute-start(bf16[4,16,16,128]{3,2,1,0:T(8,128)(2,1)S(1)} %get-tuple-element.9), channel_id=1, source_target_pairs={{0,8},{8,16},{16,24},{24,32},{32,40},{40,48},{48,56},{56,64},{64,7... | collective-permute-start | bytes 786440 | tf_op jit(solution)/shard_map/ppermute | solution.py:24
  39.4 1.5 %convolution_bitcast_fusion.2 = f32[4,256,128]{1,2,0:T(8,128)S(1)} fusion(f32[4,256,128]{2,1,0:T(8,128)S(1)} %bitcast.129, s32[256]{0:T(256)S(1)} %get-tuple-element.18, s32[256]{0:T(256)S(1)} %get-tuple-element.19), kind=kOutput, calls=%fused_computation.48 | convolution fusion | flops 207618048 | bytes 1050624 | tf_op jit(solution)/shard_map/pq,zqo->zpo/dot_general | solution.py:60
  41.2 5.6 %collective-permute-done.5 = bf16[4,16,16,128]{3,2,1,0:T(8,128)(2,1)S(1)} collective-permute-done((bf16[4,16,16,128]{3,2,1,0:T(8,128)(2,1)S(1)}, bf16[4,16,16,128]{3,2,1,0:T(8,128)(2,1)S(1)}, u32[]{:S(2)}, u32[]{:S(2)}) %collective-permute-start.5) | collective-permute-done | bytes 262176 | tf_op jit(solution)/shard_map/ppermute | solution.py:24
  47.2 1.9 %collective-permute-start.6 = (bf16[4,16,16,128]{3,2,1,0:T(8,128)(2,1)S(1)}, bf16[4,16,16,128]{3,2,1,0:T(8,128)(2,1)S(1)}, u32[]{:S(2)}, u32[]{:S(2)}) collective-permute-start(bf16[4,16,16,128]{3,2,1,0:T(8,128)(2,1)S(1)} %get-tuple-element.7), channel_id=1, source_target_pairs={{8,0},{16,8},{24,16},{32,24},{40,32},{48,40},{56,48},{64,56},{72,6... | collective-permute-start | bytes 786440 | tf_op jit(solution)/shard_map/ppermute | solution.py:25
  49.2 2.4 %collective-permute-start.7 = (bf16[4,16,16,128]{3,2,1,0:T(8,128)(2,1)S(1)}, bf16[4,16,16,128]{3,2,1,0:T(8,128)(2,1)S(1)}, u32[]{:S(2)}, u32[]{:S(2)}) collective-permute-start(bf16[4,16,16,128]{3,2,1,0:T(8,128)(2,1)S(1)} %get-tuple-element.7), channel_id=1, source_target_pairs={{0,8},{8,16},{16,24},{24,32},{32,40},{40,48},{48,56},{56,64},{64,7... | collective-permute-start | bytes 786440 | tf_op jit(solution)/shard_map/ppermute | solution.py:24
  51.6 1.5 %convolution_bitcast_fusion.1 = f32[4,256,128]{1,2,0:T(8,128)S(1)} fusion(f32[4,256,128]{2,1,0:T(8,128)S(1)} %bitcast.135, s32[256]{0:T(256)S(1)} %get-tuple-element.18, s32[256]{0:T(256)S(1)} %get-tuple-element.19), kind=kOutput, calls=%fused_computation.47 | convolution fusion | flops 207618048 | bytes 1050624 | tf_op jit(solution)/shard_map/pq,zqo->zpo/dot_general | solution.py:60
  53.4 5.6 %collective-permute-done.7 = bf16[4,16,16,128]{3,2,1,0:T(8,128)(2,1)S(1)} collective-permute-done((bf16[4,16,16,128]{3,2,1,0:T(8,128)(2,1)S(1)}, bf16[4,16,16,128]{3,2,1,0:T(8,128)(2,1)S(1)}, u32[]{:S(2)}, u32[]{:S(2)}) %collective-permute-start.7) | collective-permute-done | bytes 262176 | tf_op jit(solution)/shard_map/ppermute | solution.py:24
  59.6 1.9 %collective-permute-start.9 = (bf16[4,16,16,128]{3,2,1,0:T(8,128)(2,1)S(1)}, bf16[4,16,16,128]{3,2,1,0:T(8,128)(2,1)S(1)}, u32[]{:S(2)}, u32[]{:S(2)}) collective-permute-start(bf16[4,16,16,128]{3,2,1,0:T(8,128)(2,1)S(1)} %get-tuple-element.6), channel_id=1, source_target_pairs={{0,8},{8,16},{16,24},{24,32},{32,40},{40,48},{48,56},{56,64},{64,7... | collective-permute-start | bytes 786440 | tf_op jit(solution)/shard_map/ppermute | solution.py:24
  61.5 5.8 %collective-permute-start.8 = (bf16[4,16,16,128]{3,2,1,0:T(8,128)(2,1)S(1)}, bf16[4,16,16,128]{3,2,1,0:T(8,128)(2,1)S(1)}, u32[]{:S(2)}, u32[]{:S(2)}) collective-permute-start(bf16[4,16,16,128]{3,2,1,0:T(8,128)(2,1)S(1)} %get-tuple-element.6), channel_id=1, source_target_pairs={{8,0},{16,8},{24,16},{32,24},{40,32},{48,40},{56,48},{64,56},{72,6... | collective-permute-start | bytes 786440 | tf_op jit(solution)/shard_map/ppermute | solution.py:25
  67.3 5.4 %collective-permute-start.10 = (bf16[1024,128]{1,0:T(8,128)(2,1)S(1)}, bf16[1024,128]{1,0:T(8,128)(2,1)S(1)}, u32[]{:S(2)}, u32[]{:S(2)}) collective-permute-start(bf16[1024,128]{1,0:T(8,128)(2,1)S(1)} %bitcast.118), channel_id=1, source_target_pairs={{0,7},{1,0},{2,1},{3,2},{4,3},{5,4},{6,5},{7,6},{8,15},{9,8},{10,9... | collective-permute-start | bytes 786440 | tf_op jit(solution)/shard_map/ppermute | solution.py:132
  72.7 2.1 %collective-permute-start.13 = (bf16[1024,128]{1,0:T(8,128)(2,1)S(1)}, bf16[1024,128]{1,0:T(8,128)(2,1)S(1)}, u32[]{:S(2)}, u32[]{:S(2)}) collective-permute-start(bf16[1024,128]{1,0:T(8,128)(2,1)S(1)} %bitcast.119), channel_id=1, source_target_pairs={{0,1},{1,2},{2,3},{3,4},{4,5},{5,6},{6,7},{7,0},{8,9},{9,10},{10,1... | collective-permute-start | bytes 786440 | tf_op jit(solution)/shard_map/ppermute | solution.py:129
  74.8 1.5 %convolution_bitcast_fusion = f32[4,256,128]{1,2,0:T(8,128)S(1)} fusion(f32[4,256,128]{2,1,0:T(8,128)S(1)} %bitcast.127, s32[256]{0:T(256)S(1)} %get-tuple-element.18, s32[256]{0:T(256)S(1)} %get-tuple-element.19), kind=kOutput, calls=%fused_computation.46 | convolution fusion | flops 207618048 | bytes 1050624 | tf_op jit(solution)/shard_map/pq,zqo->zpo/dot_general | solution.py:60
  77.7 5.1 %collective-permute-start.11 = (bf16[1024,128]{1,0:T(8,128)(2,1)S(1)}, bf16[1024,128]{1,0:T(8,128)(2,1)S(1)}, u32[]{:S(2)}, u32[]{:S(2)}) collective-permute-start(bf16[1024,128]{1,0:T(8,128)(2,1)S(1)} %collective-permute-done.10), channel_id=1, source_target_pairs={{0,7},{1,0},{2,1},{3,2},{4,3},{5,4},{6,5},{7,6},{8,15},{9,8},{10,9... | collective-permute-start | bytes 786440 | tf_op jit(solution)/shard_map/ppermute | solution.py:132
  83.5 1.9 %collective-permute-start.14 = (bf16[1024,128]{1,0:T(8,128)(2,1)S(1)}, bf16[1024,128]{1,0:T(8,128)(2,1)S(1)}, u32[]{:S(2)}, u32[]{:S(2)}) collective-permute-start(bf16[1024,128]{1,0:T(8,128)(2,1)S(1)} %collective-permute-done.13), channel_id=1, source_target_pairs={{0,1},{1,2},{2,3},{3,4},{4,5},{5,6},{6,7},{7,0},{8,9},{9,10},{10,1... | collective-permute-start | bytes 786440 | tf_op jit(solution)/shard_map/ppermute | solution.py:129
  86.9 5.6 %collective-permute-start.12 = (bf16[1024,128]{1,0:T(8,128)(2,1)S(1)}, bf16[1024,128]{1,0:T(8,128)(2,1)S(1)}, u32[]{:S(2)}, u32[]{:S(2)}) collective-permute-start(bf16[1024,128]{1,0:T(8,128)(2,1)S(1)} %collective-permute-done.11), channel_id=1, source_target_pairs={{0,7},{1,0},{2,1},{3,2},{4,3},{5,4},{6,5},{7,6},{8,15},{9,8},{10,9... | collective-permute-start | bytes 786440 | tf_op jit(solution)/shard_map/ppermute | solution.py:132
  93.0 1.9 %collective-permute-start.15 = (bf16[1024,128]{1,0:T(8,128)(2,1)S(1)}, bf16[1024,128]{1,0:T(8,128)(2,1)S(1)}, u32[]{:S(2)}, u32[]{:S(2)}) collective-permute-start(bf16[1024,128]{1,0:T(8,128)(2,1)S(1)} %collective-permute-done.14), channel_id=1, source_target_pairs={{0,1},{1,2},{2,3},{3,4},{4,5},{5,6},{6,7},{7,0},{8,9},{9,10},{10,1... | collective-permute-start | bytes 786440 | tf_op jit(solution)/shard_map/ppermute | solution.py:129
  95.7 6.8 %collective-permute-done.15 = bf16[1024,128]{1,0:T(8,128)(2,1)S(1)} collective-permute-done((bf16[1024,128]{1,0:T(8,128)(2,1)S(1)}, bf16[1024,128]{1,0:T(8,128)(2,1)S(1)}, u32[]{:S(2)}, u32[]{:S(2)}) %collective-permute-start.15) | collective-permute-done | bytes 262176 | tf_op jit(solution)/shard_map/ppermute | solution.py:129
  103.1 1.9 %collective-permute-start.16 = (bf16[512,128]{1,0:T(8,128)(2,1)}, bf16[512,128]{1,0:T(8,128)(2,1)}, u32[]{:S(2)}, u32[]{:S(2)}) collective-permute-start(bf16[512,128]{1,0:T(8,128)(2,1)} %slice.222), channel_id=1, source_target_pairs={{0,1},{1,2},{2,3},{3,4},{4,5},{5,6},{6,7},{7,0},{8,9},{9,10},{10,1... | collective-permute-start | bytes 393224 | tf_op jit(solution)/shard_map/ppermute | solution.py:123
  105.1 5.1 %collective-permute-start.17 = (bf16[512,128]{1,0:T(8,128)(2,1)S(1)}, bf16[512,128]{1,0:T(8,128)(2,1)S(1)}, u32[]{:S(2)}, u32[]{:S(2)}) collective-permute-start(bf16[512,128]{1,0:T(8,128)(2,1)S(1)} %slice.223), channel_id=1, source_target_pairs={{0,7},{1,0},{2,1},{3,2},{4,3},{5,4},{6,5},{7,6},{8,15},{9,8},{10,9... | collective-permute-start | bytes 393224 | tf_op jit(solution)/shard_map/ppermute | solution.py:124
  118.0 1.9 %collective-permute-start.18 = (f32[32,17,256]{2,0,1:T(8,128)S(1)}, f32[32,17,256]{2,0,1:T(8,128)S(1)}, u32[]{:S(2)}, u32[]{:S(2)}) collective-permute-start(f32[32,17,256]{2,0,1:T(8,128)S(1)} %bitcast.136), channel_id=1, source_target_pairs={{0,8},{8,0},{1,9},{9,1},{2,10},{10,2},{3,11},{11,3},{4,12},{12,4},... | collective-permute-start | bytes 1671176 | tf_op jit(solution)/shard_map/ppermute | solution.py:106
  119.9 1.9 %collective-permute-done.18 = f32[32,17,256]{2,0,1:T(8,128)S(1)} collective-permute-done((f32[32,17,256]{2,0,1:T(8,128)S(1)}, f32[32,17,256]{2,0,1:T(8,128)S(1)}, u32[]{:S(2)}, u32[]{:S(2)}) %collective-permute-start.18) | collective-permute-done | bytes 557088 | tf_op jit(solution)/shard_map/ppermute | solution.py:106
  122.1 12.4 %all_to_all.10 = f32[4,8,17,256]{3,1,2,0:T(8,128)S(1)} all-to-all(f32[4,8,17,256]{3,1,2,0:T(8,128)S(1)} %copy.95), channel_id=1, replica_groups=mesh['x'=4,'z'=8,'core'=2,'orb'=8] {'x'}, dimensions={0} | all-to-all | bytes 1114112 | tf_op jit(solution)/shard_map/all_to_all | solution.py:108
  134.5 12.3 %all_to_all.11 = f32[8,17,256]{2,1,0:T(8,128)S(1)} all-to-all(f32[8,17,256]{2,1,0:T(8,128)S(1)} %copy.97), channel_id=1, replica_groups=mesh['x'=4,'z'=8,'core'=2,'orb'=8] {'z'}, dimensions={0} | all-to-all | bytes 278528 | tf_op jit(solution)/shard_map/all_to_all | solution.py:109
  (103 shorter events, 19.6 us)
Async XLA Ops:
  1.7 15.9 %collective-permute-start = (bf16[4,16,16,128]{3,2,1,0:T(8,128)(2,1)S(1)}, bf16[4,16,16,128]{3,2,1,0:T(8,128)(2,1)S(1)}, u32[]{:S(2)}, u32[]{:S(2)}) collective-permute-start(bf16[4,16,16,128]{3,2,1,0:T(8,128)(2,1)S(1)} %convert_element_type.255), channel_id=1, source_target_pairs={{8,0},{16,8},{24,16},{32,24},{40,32},{48,40},{56,48},{64,56},{72,6... | collective-permute-start | bytes 786440 | tf_op jit(solution)/shard_map/ppermute | solution.py:25
  12.4 9.8 %collective-permute-start.1 = (bf16[4,16,16,128]{3,2,1,0:T(8,128)(2,1)S(1)}, bf16[4,16,16,128]{3,2,1,0:T(8,128)(2,1)S(1)}, u32[]{:S(2)}, u32[]{:S(2)}) collective-permute-start(bf16[4,16,16,128]{3,2,1,0:T(8,128)(2,1)S(1)} %convert_element_type.255), channel_id=1, source_target_pairs={{0,8},{8,16},{16,24},{24,32},{32,40},{40,48},{48,56},{56,64},{64,7... | collective-permute-start | bytes 786440 | tf_op jit(solution)/shard_map/ppermute | solution.py:24
  17.6 4.7 %copy-start = (f32[4,16,16,128]{3,2,1,0:T(8,128)S(1)}, f32[4,16,16,128]{3,2,1,0:T(8,128)}, u32[]{:S(2)}) copy-start(f32[4,16,16,128]{3,2,1,0:T(8,128)} %param.2) | copy-start | bytes 1572868
  17.6 4.7 %copy-start.1 = (f32[4,16,16]{2,1,0:T(8,128)S(1)}, f32[4,16,16]{2,1,0:T(8,128)}, u32[]{:S(2)}) copy-start(f32[4,16,16]{2,1,0:T(8,128)} %param.3) | copy-start | bytes 12292
  22.6 6.2 %collective-permute-start.2 = (bf16[4,16,16,128]{3,2,1,0:T(8,128)(2,1)S(1)}, bf16[4,16,16,128]{3,2,1,0:T(8,128)(2,1)S(1)}, u32[]{:S(2)}, u32[]{:S(2)}) collective-permute-start(bf16[4,16,16,128]{3,2,1,0:T(8,128)(2,1)S(1)} %get-tuple-element.11), channel_id=1, source_target_pairs={{8,0},{16,8},{24,16},{32,24},{40,32},{48,40},{56,48},{64,56},{72,6... | collective-permute-start | bytes 786440 | tf_op jit(solution)/shard_map/ppermute | solution.py:25
  24.8 9.8 %collective-permute-start.3 = (bf16[4,16,16,128]{3,2,1,0:T(8,128)(2,1)S(1)}, bf16[4,16,16,128]{3,2,1,0:T(8,128)(2,1)S(1)}, u32[]{:S(2)}, u32[]{:S(2)}) collective-permute-start(bf16[4,16,16,128]{3,2,1,0:T(8,128)(2,1)S(1)} %get-tuple-element.11), channel_id=1, source_target_pairs={{0,8},{8,16},{16,24},{24,32},{32,40},{40,48},{48,56},{56,64},{64,7... | collective-permute-start | bytes 786440 | tf_op jit(solution)/shard_map/ppermute | solution.py:24
  35.0 6.1 %collective-permute-start.4 = (bf16[4,16,16,128]{3,2,1,0:T(8,128)(2,1)S(1)}, bf16[4,16,16,128]{3,2,1,0:T(8,128)(2,1)S(1)}, u32[]{:S(2)}, u32[]{:S(2)}) collective-permute-start(bf16[4,16,16,128]{3,2,1,0:T(8,128)(2,1)S(1)} %get-tuple-element.9), channel_id=1, source_target_pairs={{8,0},{16,8},{24,16},{32,24},{40,32},{48,40},{56,48},{64,56},{72,6... | collective-permute-start | bytes 786440 | tf_op jit(solution)/shard_map/ppermute | solution.py:25
  37.0 9.8 %collective-permute-start.5 = (bf16[4,16,16,128]{3,2,1,0:T(8,128)(2,1)S(1)}, bf16[4,16,16,128]{3,2,1,0:T(8,128)(2,1)S(1)}, u32[]{:S(2)}, u32[]{:S(2)}) collective-permute-start(bf16[4,16,16,128]{3,2,1,0:T(8,128)(2,1)S(1)} %get-tuple-element.9), channel_id=1, source_target_pairs={{0,8},{8,16},{16,24},{24,32},{32,40},{40,48},{48,56},{56,64},{64,7... | collective-permute-start | bytes 786440 | tf_op jit(solution)/shard_map/ppermute | solution.py:24
  47.2 6.1 %collective-permute-start.6 = (bf16[4,16,16,128]{3,2,1,0:T(8,128)(2,1)S(1)}, bf16[4,16,16,128]{3,2,1,0:T(8,128)(2,1)S(1)}, u32[]{:S(2)}, u32[]{:S(2)}) collective-permute-start(bf16[4,16,16,128]{3,2,1,0:T(8,128)(2,1)S(1)} %get-tuple-element.7), channel_id=1, source_target_pairs={{8,0},{16,8},{24,16},{32,24},{40,32},{48,40},{56,48},{64,56},{72,6... | collective-permute-start | bytes 786440 | tf_op jit(solution)/shard_map/ppermute | solution.py:25
  49.2 9.8 %collective-permute-start.7 = (bf16[4,16,16,128]{3,2,1,0:T(8,128)(2,1)S(1)}, bf16[4,16,16,128]{3,2,1,0:T(8,128)(2,1)S(1)}, u32[]{:S(2)}, u32[]{:S(2)}) collective-permute-start(bf16[4,16,16,128]{3,2,1,0:T(8,128)(2,1)S(1)} %get-tuple-element.7), channel_id=1, source_target_pairs={{0,8},{8,16},{16,24},{24,32},{32,40},{40,48},{48,56},{56,64},{64,7... | collective-permute-start | bytes 786440 | tf_op jit(solution)/shard_map/ppermute | solution.py:24
  59.6 17.4 %collective-permute-start.9 = (bf16[4,16,16,128]{3,2,1,0:T(8,128)(2,1)S(1)}, bf16[4,16,16,128]{3,2,1,0:T(8,128)(2,1)S(1)}, u32[]{:S(2)}, u32[]{:S(2)}) collective-permute-start(bf16[4,16,16,128]{3,2,1,0:T(8,128)(2,1)S(1)} %get-tuple-element.6), channel_id=1, source_target_pairs={{0,8},{8,16},{16,24},{24,32},{32,40},{40,48},{48,56},{56,64},{64,7... | collective-permute-start | bytes 786440 | tf_op jit(solution)/shard_map/ppermute | solution.py:24
  61.5 15.5 %collective-permute-start.8 = (bf16[4,16,16,128]{3,2,1,0:T(8,128)(2,1)S(1)}, bf16[4,16,16,128]{3,2,1,0:T(8,128)(2,1)S(1)}, u32[]{:S(2)}, u32[]{:S(2)}) collective-permute-start(bf16[4,16,16,128]{3,2,1,0:T(8,128)(2,1)S(1)} %get-tuple-element.6), channel_id=1, source_target_pairs={{8,0},{16,8},{24,16},{32,24},{40,32},{48,40},{56,48},{64,56},{72,6... | collective-permute-start | bytes 786440 | tf_op jit(solution)/shard_map/ppermute | solution.py:25
  67.3 10.4 %collective-permute-start.10 = (bf16[1024,128]{1,0:T(8,128)(2,1)S(1)}, bf16[1024,128]{1,0:T(8,128)(2,1)S(1)}, u32[]{:S(2)}, u32[]{:S(2)}) collective-permute-start(bf16[1024,128]{1,0:T(8,128)(2,1)S(1)} %bitcast.118), channel_id=1, source_target_pairs={{0,7},{1,0},{2,1},{3,2},{4,3},{5,4},{6,5},{7,6},{8,15},{9,8},{10,9... | collective-permute-start | bytes 786440 | tf_op jit(solution)/shard_map/ppermute | solution.py:132
  72.7 10.9 %collective-permute-start.13 = (bf16[1024,128]{1,0:T(8,128)(2,1)S(1)}, bf16[1024,128]{1,0:T(8,128)(2,1)S(1)}, u32[]{:S(2)}, u32[]{:S(2)}) collective-permute-start(bf16[1024,128]{1,0:T(8,128)(2,1)S(1)} %bitcast.119), channel_id=1, source_target_pairs={{0,1},{1,2},{2,3},{3,4},{4,5},{5,6},{6,7},{7,0},{8,9},{9,10},{10,1... | collective-permute-start | bytes 786440 | tf_op jit(solution)/shard_map/ppermute | solution.py:129
  77.7 9.0 %collective-permute-start.11 = (bf16[1024,128]{1,0:T(8,128)(2,1)S(1)}, bf16[1024,128]{1,0:T(8,128)(2,1)S(1)}, u32[]{:S(2)}, u32[]{:S(2)}) collective-permute-start(bf16[1024,128]{1,0:T(8,128)(2,1)S(1)} %collective-permute-done.10), channel_id=1, source_target_pairs={{0,7},{1,0},{2,1},{3,2},{4,3},{5,4},{6,5},{7,6},{8,15},{9,8},{10,9... | collective-permute-start | bytes 786440 | tf_op jit(solution)/shard_map/ppermute | solution.py:132
  83.5 9.5 %collective-permute-start.14 = (bf16[1024,128]{1,0:T(8,128)(2,1)S(1)}, bf16[1024,128]{1,0:T(8,128)(2,1)S(1)}, u32[]{:S(2)}, u32[]{:S(2)}) collective-permute-start(bf16[1024,128]{1,0:T(8,128)(2,1)S(1)} %collective-permute-done.13), channel_id=1, source_target_pairs={{0,1},{1,2},{2,3},{3,4},{4,5},{5,6},{6,7},{7,0},{8,9},{9,10},{10,1... | collective-permute-start | bytes 786440 | tf_op jit(solution)/shard_map/ppermute | solution.py:129
  86.9 18.1 %collective-permute-start.12 = (bf16[1024,128]{1,0:T(8,128)(2,1)S(1)}, bf16[1024,128]{1,0:T(8,128)(2,1)S(1)}, u32[]{:S(2)}, u32[]{:S(2)}) collective-permute-start(bf16[1024,128]{1,0:T(8,128)(2,1)S(1)} %collective-permute-done.11), channel_id=1, source_target_pairs={{0,7},{1,0},{2,1},{3,2},{4,3},{5,4},{6,5},{7,6},{8,15},{9,8},{10,9... | collective-permute-start | bytes 786440 | tf_op jit(solution)/shard_map/ppermute | solution.py:132
  93.0 9.5 %collective-permute-start.15 = (bf16[1024,128]{1,0:T(8,128)(2,1)S(1)}, bf16[1024,128]{1,0:T(8,128)(2,1)S(1)}, u32[]{:S(2)}, u32[]{:S(2)}) collective-permute-start(bf16[1024,128]{1,0:T(8,128)(2,1)S(1)} %collective-permute-done.14), channel_id=1, source_target_pairs={{0,1},{1,2},{2,3},{3,4},{4,5},{5,6},{6,7},{7,0},{8,9},{9,10},{10,1... | collective-permute-start | bytes 786440 | tf_op jit(solution)/shard_map/ppermute | solution.py:129
  103.1 8.4 %collective-permute-start.16 = (bf16[512,128]{1,0:T(8,128)(2,1)}, bf16[512,128]{1,0:T(8,128)(2,1)}, u32[]{:S(2)}, u32[]{:S(2)}) collective-permute-start(bf16[512,128]{1,0:T(8,128)(2,1)} %slice.222), channel_id=1, source_target_pairs={{0,1},{1,2},{2,3},{3,4},{4,5},{5,6},{6,7},{7,0},{8,9},{9,10},{10,1... | collective-permute-start | bytes 393224 | tf_op jit(solution)/shard_map/ppermute | solution.py:123
  105.1 7.6 %collective-permute-start.17 = (bf16[512,128]{1,0:T(8,128)(2,1)S(1)}, bf16[512,128]{1,0:T(8,128)(2,1)S(1)}, u32[]{:S(2)}, u32[]{:S(2)}) collective-permute-start(bf16[512,128]{1,0:T(8,128)(2,1)S(1)} %slice.223), channel_id=1, source_target_pairs={{0,7},{1,0},{2,1},{3,2},{4,3},{5,4},{6,5},{7,6},{8,15},{9,8},{10,9... | collective-permute-start | bytes 393224 | tf_op jit(solution)/shard_map/ppermute | solution.py:124
  118.0 3.9 %collective-permute-start.18 = (f32[32,17,256]{2,0,1:T(8,128)S(1)}, f32[32,17,256]{2,0,1:T(8,128)S(1)}, u32[]{:S(2)}, u32[]{:S(2)}) collective-permute-start(f32[32,17,256]{2,0,1:T(8,128)S(1)} %bitcast.136), channel_id=1, source_target_pairs={{0,8},{8,0},{1,9},{9,1},{2,10},{10,2},{3,11},{11,3},{4,12},{12,4},... | collective-permute-start | bytes 1671176 | tf_op jit(solution)/shard_map/ppermute | solution.py:106

commit v11 on v10

--- a/solution.py
+++ b/solution.py
@@ -104,9 +104,8 @@
     keep = jnp.where(mine == 1, high, low)
     send = jnp.where(mine == 1, low, high)
     chip_part = keep + lax.ppermute(send, "core", [(0, 1), (1, 0)])
-    chip_part = chip_part.reshape((lax.axis_size("x"), lax.axis_size("z")) + slots.shape[1:])
-    row_part = jnp.sum(lax.all_to_all(chip_part, "x", 0, 0, tiled=True), axis=0)
-    return jnp.sum(lax.all_to_all(row_part, "z", 0, 0, tiled=True), axis=0)
+    received = lax.all_to_all(chip_part, ("x", "z"), 0, 0, tiled=True)
+    return jnp.sum(received, axis=0)
 
 
 def gather_ring(block):

time: 151 us -> 152 us (level)
    all_to_all x2 -> x1, blocking collectives: 24.7 us -> 25.1 us  [reduce_scatter_grid(): received = lax.all_to_all(chip_part, ('x', 'z'), 0, 0, tiled=True)]
where the time goes in v11:
time: 152 us; the launch traced here: 149 us
  starting transfers between devices  64.2 us (42%)
  waiting for transfers between devices  32.1 us (21%)
  blocking collectives  25.1 us (17%)
  matrix products  12.8 us (8%)
  other arithmetic  9.03 us (6%)
  local copies, waits for them, and re-layouts  4.56 us (3%)
    all_to_all x1, blocking collectives, reduce_scatter_grid(): received = lax.all_to_all(chip_part, ('x', 'z'), 0, 0, tiled=True)  25.1 us
    ppermute x5, starting transfers between devices, halo_layers(): after = lax.ppermute(initial, GRID, down).astype(shard.dtype)  22.4 us
    ppermute x5, waiting for transfers between devices, halo_layers(): before = lax.ppermute(last, GRID, up).astype(shard.dtype)  21.4 us
    ppermute x3, starting transfers between devices, gather_ring(): from_right = lax.ppermute(from_right, 'orb', left)  16.1 us
    ppermute x5, starting transfers between devices, halo_layers(): before = lax.ppermute(last, GRID, up).astype(shard.dtype)  10.8 us
    dot_general x5, matrix products, apply_hamiltonian(): jnp.einsum('pq,zqo->zpo', plane, flat, precision=lax.Precision.HIGH, pref...  8.56 us
    ppermute x3, waiting for transfers between devices, gather_ring(): from_left = lax.ppermute(from_left, 'orb', right)  7.24 us
    ppermute x3, starting transfers between devices, gather_ring(): from_left = lax.ppermute(from_left, 'orb', right)  5.93 us
  transfers between devices with their start and end apart: 19, of which 10 were waited for; matrix products, arithmetic and copies ran while one was open for 11% of the time, Pallas kernels for 0%

profile of v11, /device:TPU:6, one launch (start us, length us, event | category | flops | bytes accessed | tf_op | source)
XLA Modules:
  0.0 149.1 jit_solution(990658158630882798)
XLA Ops:
  1.7 10.7 %collective-permute-start = (bf16[4,16,16,128]{3,2,1,0:T(8,128)(2,1)S(1)}, bf16[4,16,16,128]{3,2,1,0:T(8,128)(2,1)S(1)}, u32[]{:S(2)}, u32[]{:S(2)}) collective-permute-start(bf16[4,16,16,128]{3,2,1,0:T(8,128)(2,1)S(1)} %convert_element_type.255), channel_id=1, source_target_pairs={{8,0},{16,8},{24,16},{32,24},{40,32},{48,40},{56,48},{64,56},{72,6... | collective-permute-start | bytes 786440 | tf_op jit(solution)/shard_map/ppermute | solution.py:25
  12.4 1.9 %collective-permute-start.1 = (bf16[4,16,16,128]{3,2,1,0:T(8,128)(2,1)S(1)}, bf16[4,16,16,128]{3,2,1,0:T(8,128)(2,1)S(1)}, u32[]{:S(2)}, u32[]{:S(2)}) collective-permute-start(bf16[4,16,16,128]{3,2,1,0:T(8,128)(2,1)S(1)} %convert_element_type.255), channel_id=1, source_target_pairs={{0,8},{8,16},{16,24},{24,32},{32,40},{40,48},{48,56},{56,64},{64,7... | collective-permute-start | bytes 786440 | tf_op jit(solution)/shard_map/ppermute | solution.py:24
  15.2 2.4 %fusion.111 = f32[256,4,128]{2,0,1:T(8,128)S(1)} fusion(f32[4,256,128]{2,1,0:T(8,128)} %bitcast.124, s32[256]{0:T(256)S(1)} %get-tuple-element.18, s32[256]{0:T(256)S(1)} %get-tuple-element.19), kind=kOutput, calls=%fused_computation.209 | convolution fusion | flops 207618048 | bytes 1050624 | tf_op jit(solution)/shard_map/pq,zqo->zpo/dot_general | solution.py:60
  17.6 4.5 %collective-permute-done.1 = bf16[4,16,16,128]{3,2,1,0:T(8,128)(2,1)S(1)} collective-permute-done((bf16[4,16,16,128]{3,2,1,0:T(8,128)(2,1)S(1)}, bf16[4,16,16,128]{3,2,1,0:T(8,128)(2,1)S(1)}, u32[]{:S(2)}, u32[]{:S(2)}) %collective-permute-start.1) | collective-permute-done | bytes 262176 | tf_op jit(solution)/shard_map/ppermute | solution.py:24
  22.6 2.1 %collective-permute-start.2 = (bf16[4,16,16,128]{3,2,1,0:T(8,128)(2,1)S(1)}, bf16[4,16,16,128]{3,2,1,0:T(8,128)(2,1)S(1)}, u32[]{:S(2)}, u32[]{:S(2)}) collective-permute-start(bf16[4,16,16,128]{3,2,1,0:T(8,128)(2,1)S(1)} %get-tuple-element.11), channel_id=1, source_target_pairs={{8,0},{16,8},{24,16},{32,24},{40,32},{48,40},{56,48},{64,56},{72,6... | collective-permute-start | bytes 786440 | tf_op jit(solution)/shard_map/ppermute | solution.py:25
  24.8 2.2 %collective-permute-start.3 = (bf16[4,16,16,128]{3,2,1,0:T(8,128)(2,1)S(1)}, bf16[4,16,16,128]{3,2,1,0:T(8,128)(2,1)S(1)}, u32[]{:S(2)}, u32[]{:S(2)}) collective-permute-start(bf16[4,16,16,128]{3,2,1,0:T(8,128)(2,1)S(1)} %get-tuple-element.11), channel_id=1, source_target_pairs={{0,8},{8,16},{16,24},{24,32},{32,40},{40,48},{48,56},{56,64},{64,7... | collective-permute-start | bytes 786440 | tf_op jit(solution)/shard_map/ppermute | solution.py:24
  27.0 1.5 %convolution_bitcast_fusion.3 = f32[4,256,128]{1,2,0:T(8,128)S(1)} fusion(f32[4,256,128]{2,1,0:T(8,128)S(1)} %bitcast.126, s32[256]{0:T(256)S(1)} %get-tuple-element.18, s32[256]{0:T(256)S(1)} %get-tuple-element.19), kind=kOutput, calls=%fused_computation.49 | convolution fusion | flops 207618048 | bytes 1050624 | tf_op jit(solution)/shard_map/pq,zqo->zpo/dot_general | solution.py:60
  28.8 5.7 %collective-permute-done.3 = bf16[4,16,16,128]{3,2,1,0:T(8,128)(2,1)S(1)} collective-permute-done((bf16[4,16,16,128]{3,2,1,0:T(8,128)(2,1)S(1)}, bf16[4,16,16,128]{3,2,1,0:T(8,128)(2,1)S(1)}, u32[]{:S(2)}, u32[]{:S(2)}) %collective-permute-start.3) | collective-permute-done | bytes 262176 | tf_op jit(solution)/shard_map/ppermute | solution.py:24
  35.0 1.9 %collective-permute-start.4 = (bf16[4,16,16,128]{3,2,1,0:T(8,128)(2,1)S(1)}, bf16[4,16,16,128]{3,2,1,0:T(8,128)(2,1)S(1)}, u32[]{:S(2)}, u32[]{:S(2)}) collective-permute-start(bf16[4,16,16,128]{3,2,1,0:T(8,128)(2,1)S(1)} %get-tuple-element.9), channel_id=1, source_target_pairs={{8,0},{16,8},{24,16},{32,24},{40,32},{48,40},{56,48},{64,56},{72,6... | collective-permute-start | bytes 786440 | tf_op jit(solution)/shard_map/ppermute | solution.py:25
  37.0 2.4 %collective-permute-start.5 = (bf16[4,16,16,128]{3,2,1,0:T(8,128)(2,1)S(1)}, bf16[4,16,16,128]{3,2,1,0:T(8,128)(2,1)S(1)}, u32[]{:S(2)}, u32[]{:S(2)}) collective-permute-start(bf16[4,16,16,128]{3,2,1,0:T(8,128)(2,1)S(1)} %get-tuple-element.9), channel_id=1, source_target_pairs={{0,8},{8,16},{16,24},{24,32},{32,40},{40,48},{48,56},{56,64},{64,7... | collective-permute-start | bytes 786440 | tf_op jit(solution)/shard_map/ppermute | solution.py:24
  39.4 1.5 %convolution_bitcast_fusion.2 = f32[4,256,128]{1,2,0:T(8,128)S(1)} fusion(f32[4,256,128]{2,1,0:T(8,128)S(1)} %bitcast.125, s32[256]{0:T(256)S(1)} %get-tuple-element.18, s32[256]{0:T(256)S(1)} %get-tuple-element.19), kind=kOutput, calls=%fused_computation.48 | convolution fusion | flops 207618048 | bytes 1050624 | tf_op jit(solution)/shard_map/pq,zqo->zpo/dot_general | solution.py:60
  41.2 5.6 %collective-permute-done.5 = bf16[4,16,16,128]{3,2,1,0:T(8,128)(2,1)S(1)} collective-permute-done((bf16[4,16,16,128]{3,2,1,0:T(8,128)(2,1)S(1)}, bf16[4,16,16,128]{3,2,1,0:T(8,128)(2,1)S(1)}, u32[]{:S(2)}, u32[]{:S(2)}) %collective-permute-start.5) | collective-permute-done | bytes 262176 | tf_op jit(solution)/shard_map/ppermute | solution.py:24
  47.2 1.9 %collective-permute-start.6 = (bf16[4,16,16,128]{3,2,1,0:T(8,128)(2,1)S(1)}, bf16[4,16,16,128]{3,2,1,0:T(8,128)(2,1)S(1)}, u32[]{:S(2)}, u32[]{:S(2)}) collective-permute-start(bf16[4,16,16,128]{3,2,1,0:T(8,128)(2,1)S(1)} %get-tuple-element.7), channel_id=1, source_target_pairs={{8,0},{16,8},{24,16},{32,24},{40,32},{48,40},{56,48},{64,56},{72,6... | collective-permute-start | bytes 786440 | tf_op jit(solution)/shard_map/ppermute | solution.py:25
  49.2 2.4 %collective-permute-start.7 = (bf16[4,16,16,128]{3,2,1,0:T(8,128)(2,1)S(1)}, bf16[4,16,16,128]{3,2,1,0:T(8,128)(2,1)S(1)}, u32[]{:S(2)}, u32[]{:S(2)}) collective-permute-start(bf16[4,16,16,128]{3,2,1,0:T(8,128)(2,1)S(1)} %get-tuple-element.7), channel_id=1, source_target_pairs={{0,8},{8,16},{16,24},{24,32},{32,40},{40,48},{48,56},{56,64},{64,7... | collective-permute-start | bytes 786440 | tf_op jit(solution)/shard_map/ppermute | solution.py:24
  51.6 1.5 %convolution_bitcast_fusion.1 = f32[4,256,128]{1,2,0:T(8,128)S(1)} fusion(f32[4,256,128]{2,1,0:T(8,128)S(1)} %bitcast.131, s32[256]{0:T(256)S(1)} %get-tuple-element.18, s32[256]{0:T(256)S(1)} %get-tuple-element.19), kind=kOutput, calls=%fused_computation.47 | convolution fusion | flops 207618048 | bytes 1050624 | tf_op jit(solution)/shard_map/pq,zqo->zpo/dot_general | solution.py:60
  53.4 5.6 %collective-permute-done.7 = bf16[4,16,16,128]{3,2,1,0:T(8,128)(2,1)S(1)} collective-permute-done((bf16[4,16,16,128]{3,2,1,0:T(8,128)(2,1)S(1)}, bf16[4,16,16,128]{3,2,1,0:T(8,128)(2,1)S(1)}, u32[]{:S(2)}, u32[]{:S(2)}) %collective-permute-start.7) | collective-permute-done | bytes 262176 | tf_op jit(solution)/shard_map/ppermute | solution.py:24
  59.6 1.9 %collective-permute-start.9 = (bf16[4,16,16,128]{3,2,1,0:T(8,128)(2,1)S(1)}, bf16[4,16,16,128]{3,2,1,0:T(8,128)(2,1)S(1)}, u32[]{:S(2)}, u32[]{:S(2)}) collective-permute-start(bf16[4,16,16,128]{3,2,1,0:T(8,128)(2,1)S(1)} %get-tuple-element.6), channel_id=1, source_target_pairs={{0,8},{8,16},{16,24},{24,32},{32,40},{40,48},{48,56},{56,64},{64,7... | collective-permute-start | bytes 786440 | tf_op jit(solution)/shard_map/ppermute | solution.py:24
  61.5 5.8 %collective-permute-start.8 = (bf16[4,16,16,128]{3,2,1,0:T(8,128)(2,1)S(1)}, bf16[4,16,16,128]{3,2,1,0:T(8,128)(2,1)S(1)}, u32[]{:S(2)}, u32[]{:S(2)}) collective-permute-start(bf16[4,16,16,128]{3,2,1,0:T(8,128)(2,1)S(1)} %get-tuple-element.6), channel_id=1, source_target_pairs={{8,0},{16,8},{24,16},{32,24},{40,32},{48,40},{56,48},{64,56},{72,6... | collective-permute-start | bytes 786440 | tf_op jit(solution)/shard_map/ppermute | solution.py:25
  67.3 5.4 %collective-permute-start.10 = (bf16[1024,128]{1,0:T(8,128)(2,1)S(1)}, bf16[1024,128]{1,0:T(8,128)(2,1)S(1)}, u32[]{:S(2)}, u32[]{:S(2)}) collective-permute-start(bf16[1024,128]{1,0:T(8,128)(2,1)S(1)} %bitcast.114), channel_id=1, source_target_pairs={{0,7},{1,0},{2,1},{3,2},{4,3},{5,4},{6,5},{7,6},{8,15},{9,8},{10,9... | collective-permute-start | bytes 786440 | tf_op jit(solution)/shard_map/ppermute | solution.py:131
  72.7 2.1 %collective-permute-start.13 = (bf16[1024,128]{1,0:T(8,128)(2,1)S(1)}, bf16[1024,128]{1,0:T(8,128)(2,1)S(1)}, u32[]{:S(2)}, u32[]{:S(2)}) collective-permute-start(bf16[1024,128]{1,0:T(8,128)(2,1)S(1)} %bitcast.115), channel_id=1, source_target_pairs={{0,1},{1,2},{2,3},{3,4},{4,5},{5,6},{6,7},{7,0},{8,9},{9,10},{10,1... | collective-permute-start | bytes 786440 | tf_op jit(solution)/shard_map/ppermute | solution.py:128
  74.8 1.5 %convolution_bitcast_fusion = f32[4,256,128]{1,2,0:T(8,128)S(1)} fusion(f32[4,256,128]{2,1,0:T(8,128)S(1)} %bitcast.123, s32[256]{0:T(256)S(1)} %get-tuple-element.18, s32[256]{0:T(256)S(1)} %get-tuple-element.19), kind=kOutput, calls=%fused_computation.46 | convolution fusion | flops 207618048 | bytes 1050624 | tf_op jit(solution)/shard_map/pq,zqo->zpo/dot_general | solution.py:60
  77.7 5.1 %collective-permute-start.11 = (bf16[1024,128]{1,0:T(8,128)(2,1)S(1)}, bf16[1024,128]{1,0:T(8,128)(2,1)S(1)}, u32[]{:S(2)}, u32[]{:S(2)}) collective-permute-start(bf16[1024,128]{1,0:T(8,128)(2,1)S(1)} %collective-permute-done.10), channel_id=1, source_target_pairs={{0,7},{1,0},{2,1},{3,2},{4,3},{5,4},{6,5},{7,6},{8,15},{9,8},{10,9... | collective-permute-start | bytes 786440 | tf_op jit(solution)/shard_map/ppermute | solution.py:131
  83.5 1.9 %collective-permute-start.14 = (bf16[1024,128]{1,0:T(8,128)(2,1)S(1)}, bf16[1024,128]{1,0:T(8,128)(2,1)S(1)}, u32[]{:S(2)}, u32[]{:S(2)}) collective-permute-start(bf16[1024,128]{1,0:T(8,128)(2,1)S(1)} %collective-permute-done.13), channel_id=1, source_target_pairs={{0,1},{1,2},{2,3},{3,4},{4,5},{5,6},{6,7},{7,0},{8,9},{9,10},{10,1... | collective-permute-start | bytes 786440 | tf_op jit(solution)/shard_map/ppermute | solution.py:128
  86.9 5.6 %collective-permute-start.12 = (bf16[1024,128]{1,0:T(8,128)(2,1)S(1)}, bf16[1024,128]{1,0:T(8,128)(2,1)S(1)}, u32[]{:S(2)}, u32[]{:S(2)}) collective-permute-start(bf16[1024,128]{1,0:T(8,128)(2,1)S(1)} %collective-permute-done.11), channel_id=1, source_target_pairs={{0,7},{1,0},{2,1},{3,2},{4,3},{5,4},{6,5},{7,6},{8,15},{9,8},{10,9... | collective-permute-start | bytes 786440 | tf_op jit(solution)/shard_map/ppermute | solution.py:131
  93.0 1.9 %collective-permute-start.15 = (bf16[1024,128]{1,0:T(8,128)(2,1)S(1)}, bf16[1024,128]{1,0:T(8,128)(2,1)S(1)}, u32[]{:S(2)}, u32[]{:S(2)}) collective-permute-start(bf16[1024,128]{1,0:T(8,128)(2,1)S(1)} %collective-permute-done.14), channel_id=1, source_target_pairs={{0,1},{1,2},{2,3},{3,4},{4,5},{5,6},{6,7},{7,0},{8,9},{9,10},{10,1... | collective-permute-start | bytes 786440 | tf_op jit(solution)/shard_map/ppermute | solution.py:128
  95.7 6.8 %collective-permute-done.15 = bf16[1024,128]{1,0:T(8,128)(2,1)S(1)} collective-permute-done((bf16[1024,128]{1,0:T(8,128)(2,1)S(1)}, bf16[1024,128]{1,0:T(8,128)(2,1)S(1)}, u32[]{:S(2)}, u32[]{:S(2)}) %collective-permute-start.15) | collective-permute-done | bytes 262176 | tf_op jit(solution)/shard_map/ppermute | solution.py:128
  103.1 1.9 %collective-permute-start.16 = (bf16[512,128]{1,0:T(8,128)(2,1)}, bf16[512,128]{1,0:T(8,128)(2,1)}, u32[]{:S(2)}, u32[]{:S(2)}) collective-permute-start(bf16[512,128]{1,0:T(8,128)(2,1)} %slice.222), channel_id=1, source_target_pairs={{0,1},{1,2},{2,3},{3,4},{4,5},{5,6},{6,7},{7,0},{8,9},{9,10},{10,1... | collective-permute-start | bytes 393224 | tf_op jit(solution)/shard_map/ppermute | solution.py:122
  105.1 5.1 %collective-permute-start.17 = (bf16[512,128]{1,0:T(8,128)(2,1)S(1)}, bf16[512,128]{1,0:T(8,128)(2,1)S(1)}, u32[]{:S(2)}, u32[]{:S(2)}) collective-permute-start(bf16[512,128]{1,0:T(8,128)(2,1)S(1)} %slice.223), channel_id=1, source_target_pairs={{0,7},{1,0},{2,1},{3,2},{4,3},{5,4},{6,5},{7,6},{8,15},{9,8},{10,9... | collective-permute-start | bytes 393224 | tf_op jit(solution)/shard_map/ppermute | solution.py:123
  116.6 1.3 fusion.209
  118.0 1.9 %collective-permute-start.18 = (f32[32,17,256]{2,0,1:T(8,128)S(1)}, f32[32,17,256]{2,0,1:T(8,128)S(1)}, u32[]{:S(2)}, u32[]{:S(2)}) collective-permute-start(f32[32,17,256]{2,0,1:T(8,128)S(1)} %bitcast.132), channel_id=1, source_target_pairs={{0,8},{8,0},{1,9},{9,1},{2,10},{10,2},{3,11},{11,3},{4,12},{12,4},... | collective-permute-start | bytes 1671176 | tf_op jit(solution)/shard_map/ppermute | solution.py:106
  119.9 1.9 %collective-permute-done.18 = f32[32,17,256]{2,0,1:T(8,128)S(1)} collective-permute-done((f32[32,17,256]{2,0,1:T(8,128)S(1)}, f32[32,17,256]{2,0,1:T(8,128)S(1)}, u32[]{:S(2)}, u32[]{:S(2)}) %collective-permute-start.18) | collective-permute-done | bytes 557088 | tf_op jit(solution)/shard_map/ppermute | solution.py:106
  122.4 25.1 %all_to_all.5 = f32[32,17,256]{2,1,0:T(8,128)S(1)} all-to-all(f32[32,17,256]{2,1,0:T(8,128)S(1)} %copy.68), channel_id=1, replica_groups=mesh['x'=4,'z'=8,'core'=2,'orb'=8] {'x','z'}, dimensions={0} | all-to-all | bytes 1114112 | tf_op jit(solution)/shard_map/all_to_all | solution.py:107
  (100 shorter events, 18.5 us)
Async XLA Ops:
  1.7 15.9 %collective-permute-start = (bf16[4,16,16,128]{3,2,1,0:T(8,128)(2,1)S(1)}, bf16[4,16,16,128]{3,2,1,0:T(8,128)(2,1)S(1)}, u32[]{:S(2)}, u32[]{:S(2)}) collective-permute-start(bf16[4,16,16,128]{3,2,1,0:T(8,128)(2,1)S(1)} %convert_element_type.255), channel_id=1, source_target_pairs={{8,0},{16,8},{24,16},{32,24},{40,32},{48,40},{56,48},{64,56},{72,6... | collective-permute-start | bytes 786440 | tf_op jit(solution)/shard_map/ppermute | solution.py:25
  12.4 9.8 %collective-permute-start.1 = (bf16[4,16,16,128]{3,2,1,0:T(8,128)(2,1)S(1)}, bf16[4,16,16,128]{3,2,1,0:T(8,128)(2,1)S(1)}, u32[]{:S(2)}, u32[]{:S(2)}) collective-permute-start(bf16[4,16,16,128]{3,2,1,0:T(8,128)(2,1)S(1)} %convert_element_type.255), channel_id=1, source_target_pairs={{0,8},{8,16},{16,24},{24,32},{32,40},{40,48},{48,56},{56,64},{64,7... | collective-permute-start | bytes 786440 | tf_op jit(solution)/shard_map/ppermute | solution.py:24
  17.6 4.7 %copy-start = (f32[4,16,16,128]{3,2,1,0:T(8,128)S(1)}, f32[4,16,16,128]{3,2,1,0:T(8,128)}, u32[]{:S(2)}) copy-start(f32[4,16,16,128]{3,2,1,0:T(8,128)} %param.2) | copy-start | bytes 1572868
  17.6 4.7 %copy-start.1 = (f32[4,16,16]{2,1,0:T(8,128)S(1)}, f32[4,16,16]{2,1,0:T(8,128)}, u32[]{:S(2)}) copy-start(f32[4,16,16]{2,1,0:T(8,128)} %param.3) | copy-start | bytes 12292
  22.6 6.1 %collective-permute-start.2 = (bf16[4,16,16,128]{3,2,1,0:T(8,128)(2,1)S(1)}, bf16[4,16,16,128]{3,2,1,0:T(8,128)(2,1)S(1)}, u32[]{:S(2)}, u32[]{:S(2)}) collective-permute-start(bf16[4,16,16,128]{3,2,1,0:T(8,128)(2,1)S(1)} %get-tuple-element.11), channel_id=1, source_target_pairs={{8,0},{16,8},{24,16},{32,24},{40,32},{48,40},{56,48},{64,56},{72,6... | collective-permute-start | bytes 786440 | tf_op jit(solution)/shard_map/ppermute | solution.py:25
  24.8 9.8 %collective-permute-start.3 = (bf16[4,16,16,128]{3,2,1,0:T(8,128)(2,1)S(1)}, bf16[4,16,16,128]{3,2,1,0:T(8,128)(2,1)S(1)}, u32[]{:S(2)}, u32[]{:S(2)}) collective-permute-start(bf16[4,16,16,128]{3,2,1,0:T(8,128)(2,1)S(1)} %get-tuple-element.11), channel_id=1, source_target_pairs={{0,8},{8,16},{16,24},{24,32},{32,40},{40,48},{48,56},{56,64},{64,7... | collective-permute-start | bytes 786440 | tf_op jit(solution)/shard_map/ppermute | solution.py:24
  35.0 6.1 %collective-permute-start.4 = (bf16[4,16,16,128]{3,2,1,0:T(8,128)(2,1)S(1)}, bf16[4,16,16,128]{3,2,1,0:T(8,128)(2,1)S(1)}, u32[]{:S(2)}, u32[]{:S(2)}) collective-permute-start(bf16[4,16,16,128]{3,2,1,0:T(8,128)(2,1)S(1)} %get-tuple-element.9), channel_id=1, source_target_pairs={{8,0},{16,8},{24,16},{32,24},{40,32},{48,40},{56,48},{64,56},{72,6... | collective-permute-start | bytes 786440 | tf_op jit(solution)/shard_map/ppermute | solution.py:25
  37.0 9.8 %collective-permute-start.5 = (bf16[4,16,16,128]{3,2,1,0:T(8,128)(2,1)S(1)}, bf16[4,16,16,128]{3,2,1,0:T(8,128)(2,1)S(1)}, u32[]{:S(2)}, u32[]{:S(2)}) collective-permute-start(bf16[4,16,16,128]{3,2,1,0:T(8,128)(2,1)S(1)} %get-tuple-element.9), channel_id=1, source_target_pairs={{0,8},{8,16},{16,24},{24,32},{32,40},{40,48},{48,56},{56,64},{64,7... | collective-permute-start | bytes 786440 | tf_op jit(solution)/shard_map/ppermute | solution.py:24
  47.2 6.1 %collective-permute-start.6 = (bf16[4,16,16,128]{3,2,1,0:T(8,128)(2,1)S(1)}, bf16[4,16,16,128]{3,2,1,0:T(8,128)(2,1)S(1)}, u32[]{:S(2)}, u32[]{:S(2)}) collective-permute-start(bf16[4,16,16,128]{3,2,1,0:T(8,128)(2,1)S(1)} %get-tuple-element.7), channel_id=1, source_target_pairs={{8,0},{16,8},{24,16},{32,24},{40,32},{48,40},{56,48},{64,56},{72,6... | collective-permute-start | bytes 786440 | tf_op jit(solution)/shard_map/ppermute | solution.py:25
  49.2 9.8 %collective-permute-start.7 = (bf16[4,16,16,128]{3,2,1,0:T(8,128)(2,1)S(1)}, bf16[4,16,16,128]{3,2,1,0:T(8,128)(2,1)S(1)}, u32[]{:S(2)}, u32[]{:S(2)}) collective-permute-start(bf16[4,16,16,128]{3,2,1,0:T(8,128)(2,1)S(1)} %get-tuple-element.7), channel_id=1, source_target_pairs={{0,8},{8,16},{16,24},{24,32},{32,40},{40,48},{48,56},{56,64},{64,7... | collective-permute-start | bytes 786440 | tf_op jit(solution)/shard_map/ppermute | solution.py:24
  59.6 17.4 %collective-permute-start.9 = (bf16[4,16,16,128]{3,2,1,0:T(8,128)(2,1)S(1)}, bf16[4,16,16,128]{3,2,1,0:T(8,128)(2,1)S(1)}, u32[]{:S(2)}, u32[]{:S(2)}) collective-permute-start(bf16[4,16,16,128]{3,2,1,0:T(8,128)(2,1)S(1)} %get-tuple-element.6), channel_id=1, source_target_pairs={{0,8},{8,16},{16,24},{24,32},{32,40},{40,48},{48,56},{56,64},{64,7... | collective-permute-start | bytes 786440 | tf_op jit(solution)/shard_map/ppermute | solution.py:24
  61.5 15.5 %collective-permute-start.8 = (bf16[4,16,16,128]{3,2,1,0:T(8,128)(2,1)S(1)}, bf16[4,16,16,128]{3,2,1,0:T(8,128)(2,1)S(1)}, u32[]{:S(2)}, u32[]{:S(2)}) collective-permute-start(bf16[4,16,16,128]{3,2,1,0:T(8,128)(2,1)S(1)} %get-tuple-element.6), channel_id=1, source_target_pairs={{8,0},{16,8},{24,16},{32,24},{40,32},{48,40},{56,48},{64,56},{72,6... | collective-permute-start | bytes 786440 | tf_op jit(solution)/shard_map/ppermute | solution.py:25
  67.3 10.4 %collective-permute-start.10 = (bf16[1024,128]{1,0:T(8,128)(2,1)S(1)}, bf16[1024,128]{1,0:T(8,128)(2,1)S(1)}, u32[]{:S(2)}, u32[]{:S(2)}) collective-permute-start(bf16[1024,128]{1,0:T(8,128)(2,1)S(1)} %bitcast.114), channel_id=1, source_target_pairs={{0,7},{1,0},{2,1},{3,2},{4,3},{5,4},{6,5},{7,6},{8,15},{9,8},{10,9... | collective-permute-start | bytes 786440 | tf_op jit(solution)/shard_map/ppermute | solution.py:131
  72.7 10.9 %collective-permute-start.13 = (bf16[1024,128]{1,0:T(8,128)(2,1)S(1)}, bf16[1024,128]{1,0:T(8,128)(2,1)S(1)}, u32[]{:S(2)}, u32[]{:S(2)}) collective-permute-start(bf16[1024,128]{1,0:T(8,128)(2,1)S(1)} %bitcast.115), channel_id=1, source_target_pairs={{0,1},{1,2},{2,3},{3,4},{4,5},{5,6},{6,7},{7,0},{8,9},{9,10},{10,1... | collective-permute-start | bytes 786440 | tf_op jit(solution)/shard_map/ppermute | solution.py:128
  77.7 9.0 %collective-permute-start.11 = (bf16[1024,128]{1,0:T(8,128)(2,1)S(1)}, bf16[1024,128]{1,0:T(8,128)(2,1)S(1)}, u32[]{:S(2)}, u32[]{:S(2)}) collective-permute-start(bf16[1024,128]{1,0:T(8,128)(2,1)S(1)} %collective-permute-done.10), channel_id=1, source_target_pairs={{0,7},{1,0},{2,1},{3,2},{4,3},{5,4},{6,5},{7,6},{8,15},{9,8},{10,9... | collective-permute-start | bytes 786440 | tf_op jit(solution)/shard_map/ppermute | solution.py:131
  83.5 9.5 %collective-permute-start.14 = (bf16[1024,128]{1,0:T(8,128)(2,1)S(1)}, bf16[1024,128]{1,0:T(8,128)(2,1)S(1)}, u32[]{:S(2)}, u32[]{:S(2)}) collective-permute-start(bf16[1024,128]{1,0:T(8,128)(2,1)S(1)} %collective-permute-done.13), channel_id=1, source_target_pairs={{0,1},{1,2},{2,3},{3,4},{4,5},{5,6},{6,7},{7,0},{8,9},{9,10},{10,1... | collective-permute-start | bytes 786440 | tf_op jit(solution)/shard_map/ppermute | solution.py:128
  86.9 18.1 %collective-permute-start.12 = (bf16[1024,128]{1,0:T(8,128)(2,1)S(1)}, bf16[1024,128]{1,0:T(8,128)(2,1)S(1)}, u32[]{:S(2)}, u32[]{:S(2)}) collective-permute-start(bf16[1024,128]{1,0:T(8,128)(2,1)S(1)} %collective-permute-done.11), channel_id=1, source_target_pairs={{0,7},{1,0},{2,1},{3,2},{4,3},{5,4},{6,5},{7,6},{8,15},{9,8},{10,9... | collective-permute-start | bytes 786440 | tf_op jit(solution)/shard_map/ppermute | solution.py:131
  93.0 9.5 %collective-permute-start.15 = (bf16[1024,128]{1,0:T(8,128)(2,1)S(1)}, bf16[1024,128]{1,0:T(8,128)(2,1)S(1)}, u32[]{:S(2)}, u32[]{:S(2)}) collective-permute-start(bf16[1024,128]{1,0:T(8,128)(2,1)S(1)} %collective-permute-done.14), channel_id=1, source_target_pairs={{0,1},{1,2},{2,3},{3,4},{4,5},{5,6},{6,7},{7,0},{8,9},{9,10},{10,1... | collective-permute-start | bytes 786440 | tf_op jit(solution)/shard_map/ppermute | solution.py:128
  103.1 8.4 %collective-permute-start.16 = (bf16[512,128]{1,0:T(8,128)(2,1)}, bf16[512,128]{1,0:T(8,128)(2,1)}, u32[]{:S(2)}, u32[]{:S(2)}) collective-permute-start(bf16[512,128]{1,0:T(8,128)(2,1)} %slice.222), channel_id=1, source_target_pairs={{0,1},{1,2},{2,3},{3,4},{4,5},{5,6},{6,7},{7,0},{8,9},{9,10},{10,1... | collective-permute-start | bytes 393224 | tf_op jit(solution)/shard_map/ppermute | solution.py:122
  105.1 7.6 %collective-permute-start.17 = (bf16[512,128]{1,0:T(8,128)(2,1)S(1)}, bf16[512,128]{1,0:T(8,128)(2,1)S(1)}, u32[]{:S(2)}, u32[]{:S(2)}) collective-permute-start(bf16[512,128]{1,0:T(8,128)(2,1)S(1)} %slice.223), channel_id=1, source_target_pairs={{0,7},{1,0},{2,1},{3,2},{4,3},{5,4},{6,5},{7,6},{8,15},{9,8},{10,9... | collective-permute-start | bytes 393224 | tf_op jit(solution)/shard_map/ppermute | solution.py:123
  118.0 3.9 %collective-permute-start.18 = (f32[32,17,256]{2,0,1:T(8,128)S(1)}, f32[32,17,256]{2,0,1:T(8,128)S(1)}, u32[]{:S(2)}, u32[]{:S(2)}) collective-permute-start(f32[32,17,256]{2,0,1:T(8,128)S(1)} %bitcast.132), channel_id=1, source_target_pairs={{0,8},{8,0},{1,9},{9,1},{2,10},{10,2},{3,11},{11,3},{4,12},{12,4},... | collective-permute-start | bytes 1671176 | tf_op jit(solution)/shard_map/ppermute | solution.py:106
